TPU v7x, 256 devices: a whole 4x4x8 slice. The times are simulated.
256 devices in a mesh: req: 4 (over x), seq: 8 (over z_lo, y), tp: 8 (over z_hi, core).
Axes of the slice: x: 4, y: 4, z: 8 (z_hi: 4, z_lo: 2; z = z_hi * 2 + z_lo), core: 2. Of those that a mesh axis runs over, the one named last changes fastest.
Arguments:
- img_hidden: bfloat16 [16384, 3072], P(('req', 'seq'), 'tp'), parts along dimension 0, may hold values from -6 to 6
- txt_hidden: bfloat16 [2048, 3072], P(('req', 'seq'), 'tp'), parts along dimension 0, may hold values from -6 to 6
- img_mod: bfloat16 [12, 3072], P('req'), parts along dimension 0, may hold values from -3 to 3
- txt_mod: bfloat16 [12, 3072], P('req'), parts along dimension 0, may hold values from -3 to 3
- img_qkv: bfloat16 [3072, 3, 3072], P('seq', None, 'tp')
- txt_qkv: bfloat16 [3072, 3, 3072], P('seq', None, 'tp'), may hold values from -0.109375 to 0.109375
- qk_gains: float32 [4, 128], replicated, may hold values from 0.5 to 4.5, as said below
- img_out_w: bfloat16 [3072, 3072], P('tp', 'seq'), may hold values from -0.109375 to 0.109375
- txt_out_w: bfloat16 [3072, 3072], P('tp', 'seq'), may hold values from -0.109375 to 0.109375
- final_mod: bfloat16 [8, 3072], P('req'), parts along dimension 0, may hold values from -3 to 3
- final_w: bfloat16 [3072, 64], P('tp'), may hold values from -0.109375 to 0.109375
- conv_w: bfloat16 [3, 3, 64, 64], replicated, may hold values from -0.25 to 0.25
- latent: float32 [256, 4096], P(('req', 'seq'), 'tp'), parts along dimension 0, may hold values from -6 to 6
- text_len: int32 [4], P('req'), parts along dimension 0, may hold values from 1 to 512
- step_index: int32 [4], P('req'), parts along dimension 0, may hold values from 0 to 27
Outputs:
- img_next: bfloat16 [16384, 3072], P(('req', 'seq'), 'tp'), parts along dimension 0
- txt_next: bfloat16 [2048, 3072], P(('req', 'seq'), 'tp'), parts along dimension 0
- velocity: float32 [256, 4096], P(('req', 'seq'), 'tp'), parts along dimension 0
- latent_next: float32 [256, 4096], P(('req', 'seq'), 'tp'), parts along dimension 0
- denoised: float32 [256, 4096], P(('req', 'seq'), 'tp'), parts along dimension 0
There are 4 independent parts, one for each index of `req`. A program takes and returns all parts, laid end to end along the dimension named above; an argument that names none is the same for every part. Nothing has to cross between parts.
Inputs may be any that keep to these rules, and one draw needn't show every extreme that they name: `qk_gains`: positive gains.
All inputs are finite; a program needn't handle non-finite values.
Results may differ from a plain program's by a relative error of at most 0.014.
Values may be sent and summed in bfloat16 or wider, within the bound.
No kernel may reach another device: no remote copies, remote signals or barrier semaphores. Data moves between devices by JAX's collectives and lax.ppermute only.
A program may use at most 128 MiB of HBM per device.

v0:
```python
import math

import jax
import jax.numpy as jnp
from jax import lax
from jax.sharding import PartitionSpec as P

STEPS = 28


EPS = 1e-06
SHIFT_MU = 1.15
THETA = 10000.0


def extended(block, sides, width):
    for axis, dim in sides:
        count = lax.axis_size(axis)
        forward = [(i, i + 1) for i in range(count - 1)]
        backward = [(target, source) for source, target in forward]
        low = lax.ppermute(
            lax.slice_in_dim(block, block.shape[dim] - width, None, axis=dim), axis, forward
        )
        high = lax.ppermute(lax.slice_in_dim(block, 0, width, axis=dim), axis, backward)
        block = jnp.concatenate([low, block, high], axis=dim)
    return block


def modulate(hidden, mod_rows):
    values = hidden.astype(jnp.float32)
    mod_f = mod_rows.astype(jnp.float32)
    row_mean = jnp.mean(values, -1, keepdims=True)
    row_var = jnp.mean((values - row_mean) ** 2, -1, keepdims=True)
    normed = (values - row_mean) * lax.rsqrt(row_var + EPS)
    return (normed * (1.0 + mod_f[1]) + mod_f[0]).astype(jnp.bfloat16)


def rms_gain(values, gain_row):
    return values * lax.rsqrt(jnp.mean(values * values, -1, keepdims=True) + EPS) * gain_row


def rope_angles(row_pos, col_pos, head_dim):
    lead = head_dim // 16
    span = 7 * head_dim // 32
    freq = THETA ** (-jnp.arange(span, dtype=jnp.float32) / span)
    zero_part = jnp.zeros((row_pos.shape[0], lead), jnp.float32)
    return jnp.concatenate(
        [zero_part, row_pos[:, None] * freq[None], col_pos[:, None] * freq[None]], 1
    )


def apply_rope(values, angles):
    count, heads_n, head_dim = values.shape
    pairs = values.reshape(count, heads_n, head_dim // 2, 2)
    first = pairs[..., 0]
    second = pairs[..., 1]
    cosine = jnp.cos(angles)[:, None, :]
    sine = jnp.sin(angles)[:, None, :]
    turned = jnp.stack([first * cosine - second * sine, first * sine + second * cosine], -1)
    return turned.reshape(values.shape)


def split_heads(mixed, gain_q, gain_k, angles):
    head_dim = gain_q.shape[0]
    shaped = mixed.reshape(mixed.shape[0], 3, -1, head_dim)
    query = rms_gain(shaped[:, 0], gain_q)
    keyed = rms_gain(shaped[:, 1], gain_k)
    if angles is not None:
        query = apply_rope(query, angles)
        keyed = apply_rope(keyed, angles)
    return (
        query.astype(jnp.bfloat16),
        keyed.astype(jnp.bfloat16),
        shaped[:, 2].astype(jnp.bfloat16),
    )


def noise_level(tval):
    factor = math.exp(SHIFT_MU)
    return factor * tval / (factor * tval + 1.0 - tval)


def add_rows(normed, piece):
    flat_piece = piece.reshape(piece.shape[0], piece.shape[1] * piece.shape[2])
    return jnp.dot(normed, flat_piece, preferred_element_type=jnp.float32)


def per_device(
    img_hidden,
    txt_hidden,
    img_mod,
    txt_mod,
    img_qkv,
    txt_qkv,
    qk_gains,
    img_out_w,
    txt_out_w,
    final_mod,
    final_w,
    conv_w,
    latent,
    text_len,
    step_index,
):
    seq_count = lax.axis_size("seq")
    seq_at = lax.axis_index("seq")
    tp_at = lax.axis_index("tp")
    img_rows = img_hidden.shape[0]
    txt_rows = txt_hidden.shape[0]
    local_width = img_hidden.shape[1]
    img_full, txt_full = (
        lax.all_gather(img_hidden, "tp", axis=1, tiled=True),
        lax.all_gather(txt_hidden, "tp", axis=1, tiled=True),
    )
    full_width = img_full.shape[1]
    img_norm = modulate(img_full, img_mod)
    txt_norm = modulate(txt_full, txt_mod)
    img_mixed = add_rows(img_norm, lax.all_gather(img_qkv, "seq", axis=0, tiled=True))
    txt_mixed = add_rows(txt_norm, lax.all_gather(txt_qkv, "seq", axis=0, tiled=True))
    head_dim = qk_gains.shape[1]
    grid_side = latent.shape[0] * seq_count
    token_ids = seq_at * img_rows + jnp.arange(img_rows, dtype=jnp.int32)
    row_pos = (token_ids // grid_side).astype(jnp.float32)
    col_pos = (token_ids % grid_side).astype(jnp.float32)
    angles = rope_angles(row_pos, col_pos, head_dim)
    img_query, img_key, img_value = split_heads(img_mixed, qk_gains[0], qk_gains[1], angles)
    txt_query, txt_key, txt_value = split_heads(txt_mixed, qk_gains[2], qk_gains[3], None)
    local_len = txt_rows + img_rows
    heads_local = img_query.shape[1]
    queries = jnp.concatenate([txt_query, img_query], 0)
    keys_local = jnp.concatenate([txt_key, img_key], 0).reshape(local_len, heads_local * head_dim)
    values_local = jnp.concatenate([txt_value, img_value], 0).reshape(
        local_len, heads_local * head_dim
    )
    limit = text_len[0]
    score_scale = head_dim ** (-0.5)
    start_state = (
        jnp.full((heads_local, local_len), -1e30, jnp.float32),
        jnp.zeros((heads_local, local_len), jnp.float32),
        jnp.zeros((heads_local, local_len, head_dim), jnp.float32),
    )
    key_piece = lax.all_gather(keys_local, "seq", axis=0, tiled=True)
    value_piece = lax.all_gather(values_local, "seq", axis=0, tiled=True)
    blocks = key_piece.shape[0] // local_len

    def advance(block, state):
        peak, running, accum = state
        key_block = lax.dynamic_slice_in_dim(key_piece, block * local_len, local_len, 0).reshape(
            local_len, heads_local, head_dim
        )
        value_block = lax.dynamic_slice_in_dim(
            value_piece, block * local_len, local_len, 0
        ).reshape(local_len, heads_local, head_dim)
        within = jnp.arange(local_len, dtype=jnp.int32)
        text_pos = block * txt_rows + within
        usable = (within >= txt_rows) | (text_pos < limit)
        scores = (
            jnp.einsum("qhd,khd->hqk", queries, key_block, preferred_element_type=jnp.float32)
            * score_scale
        )
        scores = jnp.where(usable[None, None, :], scores, -1e30)
        new_peak = jnp.maximum(peak, jnp.max(scores, -1))
        rescale = jnp.exp(peak - new_peak)
        weights = jnp.exp(scores - new_peak[..., None])
        running = running * rescale + jnp.sum(weights, -1)
        accum = accum * rescale[..., None] + jnp.einsum(
            "hqk,khd->hqd",
            weights.astype(jnp.bfloat16),
            value_block,
            preferred_element_type=jnp.float32,
        )
        return (new_peak, running, accum)

    peak, running, accum = lax.fori_loop(0, blocks, advance, start_state)
    attn = (
        (accum / running[..., None])
        .astype(jnp.bfloat16)
        .transpose(1, 0, 2)
        .reshape(local_len, heads_local * head_dim)
    )
    txt_attn = attn[:txt_rows]
    img_attn = attn[txt_rows:]
    img_term = jnp.dot(
        img_attn,
        lax.all_gather(img_out_w, "seq", axis=1, tiled=True),
        preferred_element_type=jnp.float32,
    )
    txt_term = jnp.dot(
        txt_attn,
        lax.all_gather(txt_out_w, "seq", axis=1, tiled=True),
        preferred_element_type=jnp.float32,
    )
    img_out, txt_out = (
        lax.psum_scatter(
            img_term.astype(jnp.bfloat16), "tp", scatter_dimension=1, tiled=True
        ).astype(jnp.float32),
        lax.psum_scatter(
            txt_term.astype(jnp.bfloat16), "tp", scatter_dimension=1, tiled=True
        ).astype(jnp.float32),
    )
    img_gate = lax.dynamic_slice_in_dim(
        img_mod.astype(jnp.float32)[2], tp_at * local_width, local_width
    )
    txt_gate = lax.dynamic_slice_in_dim(
        txt_mod.astype(jnp.float32)[2], tp_at * local_width, local_width
    )
    img_next = (img_hidden.astype(jnp.float32) + img_gate * img_out).astype(jnp.bfloat16)
    text_valid = seq_at * txt_rows + jnp.arange(txt_rows, dtype=jnp.int32) < limit
    txt_base = txt_hidden.astype(jnp.float32)
    txt_next = jnp.where(text_valid[:, None], txt_base + txt_gate * txt_out, txt_base).astype(
        jnp.bfloat16
    )
    shift_row = lax.dynamic_slice_in_dim(final_mod[0], tp_at * local_width, local_width)
    scale_row = lax.dynamic_slice_in_dim(final_mod[1], tp_at * local_width, local_width)
    final_shift = shift_row.astype(jnp.float32)
    final_scale = scale_row.astype(jnp.float32)
    weight_final = final_w.astype(jnp.float32)
    values = img_next.astype(jnp.float32)
    row_sums, row_squares = lax.psum((jnp.sum(values, -1), jnp.sum(values * values, -1)), "tp")
    row_mean = row_sums / full_width
    row_var = row_squares / full_width - row_mean * row_mean
    normed = (values - row_mean[:, None]) * lax.rsqrt(row_var + EPS)[:, None] * (
        1.0 + final_scale
    ) + final_shift
    patch = lax.psum(jnp.dot(normed, weight_final, precision=lax.Precision.HIGHEST), "tp")
    channels = final_w.shape[1]
    band_rows = latent.shape[0]
    patch_band = patch.astype(jnp.bfloat16).reshape(band_rows, grid_side * channels)
    rimmed = extended(patch_band, (("seq", 0),), 1)
    col_width = latent.shape[1] // channels
    framed = jnp.pad(rimmed.reshape(band_rows + 2, grid_side, channels), ((0, 0), (1, 1), (0, 0)))
    window = lax.dynamic_slice_in_dim(framed, tp_at * col_width, col_width + 2, 1)
    velocity = jnp.zeros((band_rows, col_width, channels), jnp.float32)
    for row_shift in range(3):
        for col_shift in range(3):
            velocity = velocity + jnp.einsum(
                "rci,io->rco",
                window[row_shift : row_shift + band_rows, col_shift : col_shift + col_width],
                conv_w[row_shift, col_shift],
                preferred_element_type=jnp.float32,
            )
    velocity_flat = velocity.reshape(band_rows, col_width * channels)
    step_f = step_index[0].astype(jnp.float32)
    t_now = 1.0 - step_f / STEPS
    t_after = 1.0 - (step_f + 1.0) / STEPS
    delta = noise_level(t_after) - noise_level(t_now)
    latent_next = latent + delta * velocity_flat
    denoised = latent - noise_level(t_now) * velocity_flat
    return (img_next, txt_next, velocity_flat, latent_next, denoised)


def solution(mesh):
    placed = (
        P(("req", "seq"), "tp"),
        P(("req", "seq"), "tp"),
        P("req", None),
        P("req", None),
        P("seq", None, "tp"),
        P("seq", None, "tp"),
        P(),
        P("tp", "seq"),
        P("tp", "seq"),
        P("req", None),
        P("tp", None),
        P(),
        P(("req", "seq"), "tp"),
        P("req"),
        P("req"),
    )
    return jax.shard_map(
        per_device,
        mesh=mesh,
        in_specs=placed,
        out_specs=(
            P(("req", "seq"), "tp"),
            P(("req", "seq"), "tp"),
            P(("req", "seq"), "tp"),
            P(("req", "seq"), "tp"),
            P(("req", "seq"), "tp"),
        ),
        check_vma=False,
    )
```

profile of v0, /device:TPU:26, one launch (start us, length us, event | category | flops | bytes accessed | tf_op | source)
XLA Modules:
  0.0 589.2 jit_solution(14143399634798077735)
XLA Ops:
  8.0 2.3 copy.49
  10.4 2.3 copy.46
  14.3 19.3 %all_gather.24 = bf16[64,3072]{1,0:T(8,128)(2,1)S(1)} all-gather(bf16[64,384]{1,0:T(8,128)(2,1)S(1)} %copy-done.7), channel_id=1, replica_groups=mesh['req'=4,'seq'=8,'tp'=8] {'tp'}, dimensions={1}, use_global_device_ids=true | all-gather | bytes 442368 | tf_op jit(solution)/shard_map/all_gather | solution.py:113
  37.6 16.5 %all-gather.10.cloned.1.call-done = bf16[512,3072]{1,0:T(8,128)(2,1)} async-done(((bf16[512,384]{1,0:T(8,128)(2,1)}), bf16[512,3072]{1,0:T(8,128)(2,1)}) %all-gather.10.cloned.1.call-update) | async-done | bytes 3145744 | tf_op jit(solution)/shard_map/all_gather | solution.py:112
  54.1 2.5 convert_reduce_fusion
  57.2 1.0 fusion.18
  58.8 78.7 %all-gather.12.cloned.1.call-done = bf16[3072,3,384]{0,2,1:T(8,128)(2,1)} async-done(((bf16[384,3,384]{0,2,1:T(8,128)(2,1)}), bf16[3072,3,384]{0,2,1:T(8,128)(2,1)}) %all-gather.12.cloned.1.call-update) | async-done | bytes 7077904 | tf_op jit(solution)/shard_map/all_gather | solution.py:118
  137.4 6.4 %fusion.23 = f32[512,3,3,128]{0,3,2,1:T(8,128)S(1)} fusion(bf16[3,3,128,3072]{3,2,1,0:T(8,128)(2,1)} %bitcast.184, bf16[512,3072]{1,0:T(8,128)(2,1)S(1)} %copy-done.1, f32[3072]{0:T(1024)} %bitcast.183, f32[3072]{0:T(1024)} %bitcast.182, f32[512]{0:T(512)} %add_rsqrt_fusion.4, f32[512]{0:T(512)} %copy-done.16), kind=kOutput, calls=%fused_computation.35 | convolution fusion | flops 3633315840 | bytes 12611584 | tf_op jit(solution)/shard_map/dot_general | solution.py:85
  144.1 1.2 copy-done.4
  147.0 2.1 subtract_convert_fusion
  149.1 0.9 pad_maximum_fusion.3
  150.2 70.1 %all-gather.8.cloned.1.call-done = bf16[3072,3,384]{0,2,1:T(8,128)(2,1)} async-done(((bf16[384,3,384]{0,2,1:T(8,128)(2,1)}), bf16[3072,3,384]{0,2,1:T(8,128)(2,1)}) %all-gather.8.cloned.1.call-update) | async-done | bytes 7077904 | tf_op jit(solution)/shard_map/all_gather | solution.py:119
  220.3 5.3 fusion.43
  226.4 1.0 copy.51
  227.5 1.2 slice.301
  233.3 42.7 %all-gather.14.cloned.1.call-done = bf16[4608,384]{1,0:T(8,128)(2,1)} async-done(((bf16[576,384]{1,0:T(8,128)(2,1)}), bf16[4608,384]{1,0:T(8,128)(2,1)}) %all-gather.14.cloned.1.call-update) | async-done | bytes 3538960 | tf_op jit(solution)/shard_map/all_gather | solution.py:142
  276.0 50.1 %all-gather.16.cloned.1.call-done = bf16[4608,384]{1,0:T(8,128)(2,1)} async-done(((bf16[576,384]{1,0:T(8,128)(2,1)}), bf16[4608,384]{1,0:T(8,128)(2,1)}) %all-gather.16.cloned.1.call-update) | async-done | bytes 3538960 | tf_op jit(solution)/shard_map/all_gather | solution.py:143
  326.1 103.8 %while.18 = (s32[]{:T(128)}, f32[3,576]{1,0:T(4,128)S(1)}, f32[3,576]{1,0:T(4,128)S(1)}, f32[3,576,128]{2,1,0:T(8,128)S(1)}, s32[]{:T(128)}, /*index=5*/bf16[460...) while((s32[]{:T(128)}, f32[3,576]{1,0:T(4,128)S(1)}, ...), condition=%wide.region_11.12_spmd.clone, body=%wide.region_8.11_spmd.clone.sunk | while | flops 521231040 | bytes 18692560 | solution.py:174
  326.1 1.2 constant_dynamic-slice_fusion.7
  328.3 3.1 bitcast_reduce_fusion.2
  331.4 3.2 fusion.134
  334.9 4.1 fusion.136
  339.1 1.2 constant_dynamic-slice_fusion.7
  341.2 3.1 bitcast_reduce_fusion.2
  344.3 3.3 fusion.134
  347.9 4.1 fusion.136
  352.1 1.2 constant_dynamic-slice_fusion.7
  354.2 3.1 bitcast_reduce_fusion.2
  357.3 3.2 fusion.134
  360.8 4.1 fusion.136
  365.0 1.2 constant_dynamic-slice_fusion.7
  367.2 3.1 bitcast_reduce_fusion.2
  370.3 3.2 fusion.134
  373.8 4.1 fusion.136
  378.0 1.2 constant_dynamic-slice_fusion.7
  380.2 3.1 bitcast_reduce_fusion.2
  383.2 3.2 fusion.134
  386.8 4.1 fusion.136
  390.9 1.2 constant_dynamic-slice_fusion.7
  393.1 3.1 bitcast_reduce_fusion.2
  396.2 3.3 fusion.134
  399.8 4.2 fusion.136
  404.0 1.2 constant_dynamic-slice_fusion.7
  406.1 3.1 bitcast_reduce_fusion.2
  409.2 3.3 fusion.134
  412.8 4.1 fusion.136
  417.0 1.2 constant_dynamic-slice_fusion.7
  419.2 3.1 bitcast_reduce_fusion.2
  422.2 3.2 fusion.134
  425.8 4.1 fusion.136
  430.4 2.2 convolution_convert_fusion.1
  432.6 1.2 copy.72
  433.8 0.9 slice.209
  434.8 3.6 convolution_convert_fusion
  438.4 2.8 copy.70
  444.2 29.2 %reduce-scatter.9.cloned.1.call-done = bf16[384,64]{1,0:T(8,128)(2,1)} async-done(((bf16[3072,64]{1,0:T(8,128)(2,1)}), bf16[384,64]{1,0:T(8,128)(2,1)}) %reduce-scatter.9.cloned.1.call-update) | async-done | bytes 49168
  473.4 1.0 copy.73
  474.3 51.2 %reduce-scatter.7.cloned.1.call-done = bf16[384,512]{1,0:T(8,128)(2,1)} async-done(((bf16[3072,512]{1,0:T(8,128)(2,1)}), bf16[384,512]{1,0:T(8,128)(2,1)}) %reduce-scatter.7.cloned.1.call-update) | async-done | bytes 393232
  525.5 1.2 copy.71
  527.0 14.3 %all-reduce.1 = (f32[512]{0:T(512)S(1)}, f32[512]{0:T(512)S(1)}) all-reduce(f32[512]{0:T(512)S(1)} %get-tuple-element.193, f32[512]{0:T(512)S(1)} %get-tuple-element.192), channel_id=1, replica_groups=mesh['req'=4,'seq'=8,'tp'=8] {'tp'}, use_global_device_ids=true, to_apply=%region_17.18 | all-reduce | flops 1024 | bytes 8192 | tf_op jit(solution)/shard_map/psum | solution.py:219
  542.1 28.3 %all-reduce.3 = bf16[512,64]{0,1:T(8,128)(2,1)S(1)} all-reduce(f32[512,64]{0,1:T(8,128)S(1)} %fusion.38), channel_id=1, replica_groups=mesh['req'=4,'seq'=8,'tp'=8] {'tp'}, use_global_device_ids=true, to_apply=%region_18.19 | all-reduce | flops 32768 | bytes 196608 | tf_op jit(solution)/shard_map/psum | solution.py:225
  570.7 1.9 collective-permute-start
  572.8 3.9 collective-permute-start.1
  577.7 2.8 collective-permute-done.1
  (199 shorter events, 31.1 us)
Async XLA Ops:
  7.2 534.2 %copy-start = (bf16[384,64]{0,1:T(8,128)(2,1)S(1)}, bf16[384,64]{0,1:T(8,128)(2,1)}, u32[]{:S(2)}) copy-start(bf16[384,64]{0,1:T(8,128)(2,1)} %param.27) | copy-start | bytes 147460
  7.2 5.6 copy-start.10
  7.2 5.6 copy-start.20
  7.2 7.0 %copy-start.11 = (bf16[3,3072]{1,0:T(4,128)(2,1)S(1)}, bf16[3,3072]{1,0:T(4,128)(2,1)}, u32[]{:S(2)}) copy-start(bf16[3,3072]{1,0:T(4,128)(2,1)} %param.20) | copy-start | bytes 55300
  7.2 7.1 %copy-start.7 = (bf16[64,384]{1,0:T(8,128)(2,1)S(1)}, bf16[64,384]{1,0:T(8,128)(2,1)}, u32[]{:S(2)}) copy-start(bf16[64,384]{1,0:T(8,128)(2,1)} %param.18) | copy-start | bytes 147460
  7.2 46.9 %all-gather.10.cloned.1.call-start = ((), (), s32[]{:S(2)}) async-start(), calls=%async_computation.3 | async-start | bytes 3538944 | tf_op jit(solution)/shard_map/all_gather | solution.py:112
  8.0 129.5 %all-gather.12.cloned.1.call-start = ((), (), s32[]{:S(2)}) async-start(), calls=%async_computation.4 | async-start | bytes 7962624 | tf_op jit(solution)/shard_map/all_gather | solution.py:118
  10.3 209.9 %all-gather.8.cloned.1.call-start = ((), (), s32[]{:S(2)}) async-start(), calls=%async_computation.2 | async-start | bytes 7962624 | tf_op jit(solution)/shard_map/all_gather | solution.py:119
  12.7 263.3 %all-gather.14.cloned.1.call-start = ((), (), s32[]{:S(2)}) async-start(), calls=%async_computation.5 | async-start | bytes 3981312 | tf_op jit(solution)/shard_map/all_gather | solution.py:142
  33.6 0.7 copy-start.2
  34.4 3.3 copy-start.17
  54.1 3.1 copy-start.1
  56.6 0.6 copy-start.16
  143.9 1.5 copy-start.4
  143.9 2.5 copy-start.9
  146.3 74.0 %copy-start.3 = (bf16[64,3072]{1,0:T(8,128)(2,1)S(1)}, bf16[64,3072]{1,0:T(8,128)(2,1)}, u32[]{:S(2)}) copy-start(bf16[64,3072]{1,0:T(8,128)(2,1)} %copy-done.2) | copy-start | bytes 1179652
  146.3 74.0 %copy-start.13 = (f32[1,3072]{1,0:T(1,128)S(1)}, f32[1,3072]{1,0:T(1,128)}, u32[]{:S(2)}) copy-start(f32[1,3072]{1,0:T(1,128)} %get-tuple-element.238) | copy-start | bytes 36868
  146.3 74.0 %copy-start.18 = (f32[64]{0:T(128)S(1)}, f32[64]{0:T(128)}, u32[]{:S(2)}) copy-start(f32[64]{0:T(128)} %copy-done.17) | copy-start | bytes 772
  146.3 74.0 %copy-start.21 = (f32[64]{0:T(128)S(1)}, f32[64]{0:T(128)}, u32[]{:S(2)}) copy-start(f32[64]{0:T(128)} %add_rsqrt_fusion.6) | copy-start | bytes 772
  225.9 6.7 %copy-start.19 = (f32[128]{0:T(128)S(1)}, f32[128]{0:T(128)}, u32[]{:S(2)}) copy-start(f32[128]{0:T(128)} %get-tuple-element.245) | copy-start | bytes 1540
  227.4 98.7 %all-gather.16.cloned.1.call-start = ((), (), s32[]{:S(2)}) async-start(), calls=%async_computation.6 | async-start | bytes 3981312 | tf_op jit(solution)/shard_map/all_gather | solution.py:143
  229.8 200.6 %all-gather.20.cloned.1.call-start = ((), (), s32[]{:S(2)}) async-start(), calls=%async_computation.8 | async-start | bytes 2654208 | tf_op jit(solution)/shard_map/all_gather | solution.py:190
  230.4 204.4 %all-gather.18.cloned.1.call-start = ((), (), s32[]{:S(2)}) async-start(), calls=%async_computation.7 | async-start | bytes 2654208 | tf_op jit(solution)/shard_map/all_gather | solution.py:185
  231.1 242.2 %reduce-scatter.9.cloned.1.call-start = ((), (), s32[]{:S(2)}) async-start(), calls=%async_computation.10 | async-start | bytes 884736
  433.8 91.7 %reduce-scatter.7.cloned.1.call-start = ((), (), s32[]{:S(2)}) async-start(), calls=%async_computation.9 | async-start | bytes 3538944
  438.4 5.7 copy-start.14
  441.3 85.5 %copy-start.5 = (bf16[512,384]{1,0:T(8,128)(2,1)S(1)}, bf16[512,384]{1,0:T(8,128)(2,1)}, u32[]{:S(2)}) copy-start(bf16[512,384]{1,0:T(8,128)(2,1)} %param.17) | copy-start | bytes 1179652
  441.3 139.5 %copy-start.8 = (bf16[3,3,64,64]{3,2,1,0:T(8,128)(2,1)S(1)}, bf16[3,3,64,64]{3,2,1,0:T(8,128)(2,1)}, u32[]{:S(2)}) copy-start(bf16[3,3,64,64]{3,2,1,0:T(8,128)(2,1)} %param.28) | copy-start | bytes 221188
  441.3 140.8 %copy-start.15 = (f32[8,512]{1,0:T(8,128)S(1)}, f32[8,512]{1,0:T(8,128)}, u32[]{:S(2)}) copy-start(f32[8,512]{1,0:T(8,128)} %param.29) | copy-start | bytes 49156
  527.0 55.6 %copy-start.6 = (bf16[512,384]{1,0:T(8,128)(2,1)}, bf16[512,384]{1,0:T(8,128)(2,1)S(1)}, u32[]{:S(2)}) copy-start(bf16[512,384]{1,0:T(8,128)(2,1)S(1)} %get-tuple-element.216) | copy-start | bytes 1179652
  570.7 6.9 %collective-permute-start = (bf16[1,4096]{1,0:T(2,128)(2,1)S(1)}, bf16[1,4096]{1,0:T(2,128)(2,1)S(1)}, u32[]{:S(2)}, u32[]{:S(2)}) collective-permute-start(bf16[1,4096]{1,0:T(2,128)(2,1)S(1)} %slice.173), channel_id=1, source_target_pairs={{0,8},{8,16},{16,24},{24,32},{32,40},{40,48},{48,56},{1,9},{9,17},... | collective-permute-start | bytes 24584 | tf_op jit(solution)/shard_map/ppermute | solution.py:21
  572.8 7.7 %collective-permute-start.1 = (bf16[1,4096]{1,0:T(2,128)(2,1)S(1)}, bf16[1,4096]{1,0:T(2,128)(2,1)S(1)}, u32[]{:S(2)}, u32[]{:S(2)}) collective-permute-start(bf16[1,4096]{1,0:T(2,128)(2,1)S(1)} %slice.175), channel_id=1, source_target_pairs={{8,0},{16,8},{24,16},{32,24},{40,32},{48,40},{56,48},{9,1},{17,9},... | collective-permute-start | bytes 24584 | tf_op jit(solution)/shard_map/ppermute | solution.py:24
  582.0 0.6 copy-start.12
Sparse Core Ops, SparseCore 0:
  9.9 44.1 all-gather.9
  55.9 81.5 all-gather.11
  139.2 80.9 all-gather.7
  227.5 48.4 all-gather.13
  277.6 48.4 all-gather.15
  327.8 44.1 all-gather.19
  373.8 44.5 all-gather.17
  433.9 39.3 reduce-scatter.8
  476.1 49.3 reduce-scatter.6
where the time goes:
time: 591 us; the launch traced here: 589 us
  waiting for transfers between devices  343 us (58%)
  matrix products  77 us (13%)
  blocking collectives  62 us (10%)
  other arithmetic  46.2 us (8%)
  local copies, waits for them, and re-layouts  38 us (6%)
  between operations  15.9 us (3%)
  starting transfers between devices  6.39 us (1%)
    unnamed x11, waiting for transfers between devices  82.3 us
    all_gather x1, waiting for transfers between devices, per_device(): lax.all_gather(img_qkv, 'seq', axis=0, tiled=True)  78.7 us
    all_gather x1, waiting for transfers between devices, per_device(): lax.all_gather(txt_qkv, 'seq', axis=0, tiled=True)  70.1 us
    all_gather x1, waiting for transfers between devices, per_device(): value_piece = lax.all_gather(values_local, 'seq', axis=0, tiled=True)  50.1 us
    all_gather x1, waiting for transfers between devices, per_device(): key_piece = lax.all_gather(keys_local, 'seq', axis=0, tiled=True)  42.7 us
    dot_general x8, matrix products, advance(): jnp.einsum('hqk,khd->hqd', weights.astype(jnp.bfloat16), value_block, pre...  33 us
    psum x1, blocking collectives, per_device(): lax.psum(jnp.dot(normed, weight_final, precision=lax.Precision.HIGHEST),...  28.3 us
    reduce_sum x8, other arithmetic, advance(): running = running * rescale + jnp.sum(weights, -1)  26.1 us
  transfers between devices with their start and end apart: 11, of which 8 were waited for; matrix products, arithmetic and copies ran while one was open for 25% of the time, Pallas kernels for 0%

commit v1 on v0

--- a/solution.py
+++ b/solution.py
@@ -116,7 +116,10 @@
     img_norm = modulate(img_full, img_mod)
     txt_norm = modulate(txt_full, txt_mod)
     img_mixed = add_rows(img_norm, lax.all_gather(img_qkv, "seq", axis=0, tiled=True))
-    txt_mixed = add_rows(txt_norm, lax.all_gather(txt_qkv, "seq", axis=0, tiled=True))
+    txt_norm_rows = lax.all_to_all(txt_norm, "seq", 1, 0, tiled=True)
+    txt_mixed = lax.psum_scatter(
+        add_rows(txt_norm_rows, txt_qkv), "seq", scatter_dimension=0, tiled=True
+    )
     head_dim = qk_gains.shape[1]
     grid_side = latent.shape[0] * seq_count
     token_ids = seq_at * img_rows + jnp.arange(img_rows, dtype=jnp.int32)
@@ -186,18 +189,19 @@
         preferred_element_type=jnp.float32,
     )
     txt_term = jnp.dot(
-        txt_attn,
-        lax.all_gather(txt_out_w, "seq", axis=1, tiled=True),
+        lax.all_gather(txt_attn, "seq", axis=0, tiled=True),
+        txt_out_w,
         preferred_element_type=jnp.float32,
     )
-    img_out, txt_out = (
-        lax.psum_scatter(
-            img_term.astype(jnp.bfloat16), "tp", scatter_dimension=1, tiled=True
-        ).astype(jnp.float32),
-        lax.psum_scatter(
-            txt_term.astype(jnp.bfloat16), "tp", scatter_dimension=1, tiled=True
-        ).astype(jnp.float32),
-    )
+    txt_part = lax.psum_scatter(
+        txt_term.astype(jnp.bfloat16).astype(jnp.float32), "tp", scatter_dimension=0, tiled=True
+    )
+    side = lax.axis_size("tp")
+    swap = [(a * side + b, b * side + a) for a in range(side) for b in range(side)]
+    txt_out = lax.ppermute(txt_part, ("seq", "tp"), swap)
+    img_out = lax.psum_scatter(
+        img_term.astype(jnp.bfloat16), "tp", scatter_dimension=1, tiled=True
+    ).astype(jnp.float32)
     img_gate = lax.dynamic_slice_in_dim(
         img_mod.astype(jnp.float32)[2], tp_at * local_width, local_width
     )
@@ -216,14 +220,28 @@
     final_scale = scale_row.astype(jnp.float32)
     weight_final = final_w.astype(jnp.float32)
     values = img_next.astype(jnp.float32)
-    row_sums, row_squares = lax.psum((jnp.sum(values, -1), jnp.sum(values * values, -1)), "tp")
-    row_mean = row_sums / full_width
-    row_var = row_squares / full_width - row_mean * row_mean
-    normed = (values - row_mean[:, None]) * lax.rsqrt(row_var + EPS)[:, None] * (
-        1.0 + final_scale
-    ) + final_shift
-    patch = lax.psum(jnp.dot(normed, weight_final, precision=lax.Precision.HIGHEST), "tp")
     channels = final_w.shape[1]
+    final_gain = 1.0 + final_scale
+    high = lax.Precision.HIGHEST
+    lifted = jnp.dot(values * final_gain, weight_final, precision=high)
+    consts = jnp.stack(
+        [jnp.dot(final_gain, weight_final, precision=high), jnp.dot(final_shift, weight_final, precision=high)]
+    )
+    packed = jnp.concatenate(
+        [
+            jnp.concatenate([lifted, jnp.sum(values, -1)[:, None], jnp.sum(values * values, -1)[:, None]], 1),
+            jnp.pad(consts, ((0, 0), (0, 2))),
+        ],
+        0,
+    )
+    packed = lax.psum(packed, "tp")
+    lifted = packed[:img_rows, :channels]
+    row_mean = packed[:img_rows, channels] / full_width
+    row_var = packed[:img_rows, channels + 1] / full_width - row_mean * row_mean
+    row_scale = lax.rsqrt(row_var + EPS)[:, None]
+    patch = row_scale * (lifted - row_mean[:, None] * packed[img_rows, :channels]) + packed[
+        img_rows + 1, :channels
+    ]
     band_rows = latent.shape[0]
     patch_band = patch.astype(jnp.bfloat16).reshape(band_rows, grid_side * channels)
     rimmed = extended(patch_band, (("seq", 0),), 1)

time: 591 us -> 594 us (level)
  blocking collectives: 62 us -> 49.8 us
  starting transfers between devices: 6.39 us -> 16.2 us
    reduce_scatter x0 -> x2, waiting for transfers between devices: none -> 92.3 us  [the longest x1 57.5 us: per_device(): lax.psum_scatter(add_rows(txt_norm_rows, txt_qkv), 'seq', scatter_dimensi...]
    all_gather x2 -> x0, waiting for transfers between devices: 70.1 us -> none  [the longest x1 70.1 us: per_device(): lax.all_gather(txt_qkv, 'seq', axis=0, tiled=True)]
    psum x0 -> x1, waiting for transfers between devices: none -> 69.2 us  [per_device(): packed = lax.psum(packed, 'tp')]
    unnamed x11 -> x10, waiting for transfers between devices: 82.3 us -> 19.8 us
    psum x2 -> x0, blocking collectives: 42.7 us -> none  [the longest x1 28.3 us: per_device(): lax.psum(jnp.dot(normed, weight_final, precision=lax.Precision.HIGHEST),...]
    all_gather x0 -> x1, blocking collectives: none -> 31 us  [per_device(): lax.all_gather(txt_attn, 'seq', axis=0, tiled=True)]
    all_gather x1, waiting for transfers between devices: 78.7 us -> 61.5 us  [per_device(): lax.all_gather(img_qkv, 'seq', axis=0, tiled=True)]
    all_gather x1, waiting for transfers between devices: 16.5 us -> 0.01 us  [per_device(): lax.all_gather(img_hidden, 'tp', axis=1, tiled=True)]
  transfers between devices with their start and end apart: 11 -> 13, of which waited for: 8 -> 9; matrix products, arithmetic and copies ran while one was open for 25% -> 23% of each run, Pallas kernels for 0% -> 0%
where the time goes in v1:
time: 594 us; the launch traced here: 592 us
  waiting for transfers between devices  344 us (58%)
  matrix products  73.2 us (12%)
  other arithmetic  49.9 us (8%)
  blocking collectives  49.8 us (8%)
  local copies, waits for them, and re-layouts  40.4 us (7%)
  between operations  17.5 us (3%)
  starting transfers between devices  16.2 us (3%)
    psum x1, waiting for transfers between devices, per_device(): packed = lax.psum(packed, 'tp')  69.2 us
    all_gather x1, waiting for transfers between devices, per_device(): lax.all_gather(img_qkv, 'seq', axis=0, tiled=True)  61.5 us
    reduce_scatter x1, waiting for transfers between devices, per_device(): lax.psum_scatter(add_rows(txt_norm_rows, txt_qkv), 'seq', scatter_dimensi...  57.5 us
    all_gather x1, waiting for transfers between devices, per_device(): value_piece = lax.all_gather(values_local, 'seq', axis=0, tiled=True)  50.3 us
    all_gather x1, waiting for transfers between devices, per_device(): key_piece = lax.all_gather(keys_local, 'seq', axis=0, tiled=True)  43.4 us
    reduce_scatter x1, waiting for transfers between devices, per_device(): lax.psum_scatter(txt_term.astype(jnp.bfloat16).astype(jnp.float32), 'tp',...  34.9 us
    dot_general x8, matrix products, advance(): jnp.einsum('hqk,khd->hqd', weights.astype(jnp.bfloat16), value_block, pre...  33 us
    all_gather x1, blocking collectives, per_device(): lax.all_gather(txt_attn, 'seq', axis=0, tiled=True)  31 us
  transfers between devices with their start and end apart: 13, of which 9 were waited for; matrix products, arithmetic and copies ran while one was open for 23% of the time, Pallas kernels for 0%

profile of v1, /device:TPU:26, one launch (start us, length us, event | category | flops | bytes accessed | tf_op | source)
XLA Modules:
  0.0 591.7 jit_solution(8181375661822205329)
XLA Ops:
  8.0 1.4 fusion.103
  10.2 18.8 %all_gather.21 = bf16[64,3072]{1,0:T(8,128)(2,1)S(1)} all-gather(bf16[64,384]{1,0:T(8,128)(2,1)} %param.18), channel_id=1, replica_groups=mesh['req'=4,'seq'=8,'tp'=8] {'tp'}, dimensions={1}, use_global_device_ids=true | all-gather | bytes 442368 | tf_op jit(solution)/shard_map/all_gather | solution.py:113
  30.4 5.4 all-to-all-start
  35.8 2.5 copy.106
  38.3 4.1 all-to-all-done
  42.4 2.2 fusion.106
  45.2 2.2 copy.109
  49.9 1.2 fusion.44
  51.7 57.5 %reduce-scatter.6.cloned.1.call-done = f32[64,1152]{1,0:T(8,128)} async-done(((f32[512,1152]{1,0:T(8,128)}), f32[64,1152]{1,0:T(8,128)}) %reduce-scatter.6.cloned.1.call-update) | async-done | bytes 294928 | tf_op jit(solution)/shard_map/reduce_scatter | solution.py:120
  109.2 1.1 reshape.280
  111.0 2.5 convert_reduce_fusion
  115.4 61.5 %all-gather.8.cloned.1.call-done = bf16[3072,3,384]{0,2,1:T(8,128)(2,1)} async-done(((bf16[384,3,384]{0,2,1:T(8,128)(2,1)}), bf16[3072,3,384]{0,2,1:T(8,128)(2,1)}) %all-gather.8.cloned.1.call-update) | async-done | bytes 7077904 | tf_op jit(solution)/shard_map/all_gather | solution.py:118
  176.9 6.4 %fusion.23 = f32[512,3,3,128]{0,3,2,1:T(8,128)S(1)} fusion(bf16[3,3,128,3072]{3,2,1,0:T(8,128)(2,1)} %bitcast.197, bf16[512,3072]{1,0:T(8,128)(2,1)S(1)} %copy-done.1, f32[3072]{0:T(1024)} %bitcast.192, f32[3072]{0:T(1024)S(1)} %bitcast.191, f32[512]{0:T(512)} %add_rsqrt_fusion.5, f32[512]{0:T(512)S(1)} %broadcast_multiply_fusion.2), kind=kOutput, calls=%fused_computation.34 | convolution fusion | flops 3633315840 | bytes 12611584 | tf_op jit(solution)/shard_map/dot_general | solution.py:85
  183.6 1.1 copy-done.5
  186.5 2.1 subtract_convert_fusion
  191.0 1.2 slice.343
  196.1 43.4 %all-gather.10.cloned.1.call-done = bf16[4608,384]{1,0:T(8,128)(2,1)} async-done(((bf16[576,384]{1,0:T(8,128)(2,1)}), bf16[4608,384]{1,0:T(8,128)(2,1)}) %all-gather.10.cloned.1.call-update) | async-done | bytes 3538960 | tf_op jit(solution)/shard_map/all_gather | solution.py:145
  239.5 50.3 %all-gather.12.cloned.1.call-done = bf16[4608,384]{1,0:T(8,128)(2,1)} async-done(((bf16[576,384]{1,0:T(8,128)(2,1)}), bf16[4608,384]{1,0:T(8,128)(2,1)}) %all-gather.12.cloned.1.call-update) | async-done | bytes 3538960 | tf_op jit(solution)/shard_map/all_gather | solution.py:146
  289.8 104.1 %while.18 = (s32[]{:T(128)}, f32[3,576]{1,0:T(4,128)S(1)}, f32[3,576]{1,0:T(4,128)}, f32[3,576,128]{2,1,0:T(8,128)S(1)}, s32[]{:T(128)}, /*index=5*/bf16[4608,38...) while((s32[]{:T(128)}, f32[3,576]{1,0:T(4,128)S(1)}, ...), condition=%wide.region_12.13_spmd.clone, body=%wide.region_9.12_spmd.clone.sunk | while | flops 521231040 | bytes 18747912 | solution.py:177
  289.8 1.2 constant_dynamic-slice_fusion.7
  291.9 3.1 bitcast_reduce_fusion.2
  295.0 3.2 fusion.133
  298.6 4.1 fusion.135
  302.8 1.2 constant_dynamic-slice_fusion.7
  304.9 3.1 bitcast_reduce_fusion.2
  308.0 3.3 fusion.133
  311.6 4.1 fusion.135
  315.8 1.2 constant_dynamic-slice_fusion.7
  318.0 3.1 bitcast_reduce_fusion.2
  321.1 3.2 fusion.133
  324.7 4.2 fusion.135
  328.9 1.2 constant_dynamic-slice_fusion.7
  331.1 3.1 bitcast_reduce_fusion.2
  334.1 3.2 fusion.133
  337.7 4.1 fusion.135
  341.9 1.2 constant_dynamic-slice_fusion.7
  344.1 3.1 bitcast_reduce_fusion.2
  347.2 3.2 fusion.133
  350.7 4.1 fusion.135
  354.9 1.2 constant_dynamic-slice_fusion.7
  357.1 3.1 bitcast_reduce_fusion.2
  360.1 3.2 fusion.133
  363.7 4.1 fusion.135
  367.9 1.2 constant_dynamic-slice_fusion.7
  370.1 3.1 bitcast_reduce_fusion.2
  373.2 3.2 fusion.133
  376.7 4.1 fusion.135
  380.9 1.2 constant_dynamic-slice_fusion.7
  383.1 3.1 bitcast_reduce_fusion.2
  386.2 3.2 fusion.133
  389.7 4.1 fusion.135
  396.7 3.6 convolution_convert_fusion
  400.3 2.8 copy.131
  403.4 31.0 %all_gather.27 = bf16[512,384]{1,0:T(8,128)(2,1)S(1)} all-gather(bf16[64,384]{1,0:T(8,128)(2,1)S(1)} %copy.129), channel_id=1, replica_groups=mesh['req'=4,'seq'=8,'tp'=8] {'seq'}, dimensions={0}, use_global_device_ids=true | all-gather | bytes 442368 | tf_op jit(solution)/shard_map/all_gather | solution.py:192
  434.4 1.3 fusion.29
  436.9 18.7 %reduce-scatter.10.cloned.1.call-done = bf16[384,512]{1,0:T(8,128)(2,1)} async-done(((bf16[3072,512]{1,0:T(8,128)(2,1)}), bf16[384,512]{1,0:T(8,128)(2,1)}) %reduce-scatter.10.cloned.1.call-update) | async-done | bytes 393232
  455.6 1.2 copy.132
  460.6 34.9 %reduce-scatter.8.cloned.1.call-done = f32[64,384]{1,0:T(8,128)} async-done(((f32[512,384]{1,0:T(8,128)}), f32[64,384]{1,0:T(8,128)}) %reduce-scatter.8.cloned.1.call-update) | async-done | bytes 98320 | tf_op jit(solution)/shard_map/reduce_scatter | solution.py:196
  495.4 4.3 collective-permute-start
  499.7 69.2 %all-reduce.4.cloned.1.call-done = f32[514,66]{0,1:T(8,128)} async-done(((f32[514,66]{0,1:T(8,128)}), f32[514,66]{0,1:T(8,128)}) %all-reduce.4.cloned.1.call-update) | async-done | bytes 135712 | tf_op jit(solution)/shard_map/psum | solution.py:237
  569.7 1.0 slice_reduce_fusion.1
  571.9 2.5 collective-permute-start.1
  574.6 3.4 collective-permute-start.2
  579.0 3.3 collective-permute-done.2
  (241 shorter events, 38.1 us)
Async XLA Ops:
  8.0 426.4 %copy-start = (bf16[384,384]{1,0:T(8,128)(2,1)S(1)}, bf16[384,384]{1,0:T(8,128)(2,1)}, u32[]{:S(2)}) copy-start(bf16[384,384]{1,0:T(8,128)(2,1)} %param.25) | copy-start | bytes 884740
  30.4 14.8 %copy-start.8 = (bf16[384,3,384]{2,0,1:T(8,128)(2,1)S(1)}, bf16[384,3,384]{2,0,1:T(8,128)(2,1)}, u32[]{:S(2)}) copy-start(bf16[384,3,384]{2,0,1:T(8,128)(2,1)} %param.21) | copy-start | bytes 2654212
  30.4 11.9 %all-to-all-start = ((bf16[64,8,384]{2,0,1:T(8,128)(2,1)}), bf16[64,8,384]{2,0,1:T(8,128)(2,1)S(1)}, u32[]{:S(2)}, u32[]{:S(2)}) async-start(bf16[64,8,384]{2,0,1:T(8,128)(2,1)} %bitcast.155), calls=%async_computation | async-start | bytes 786432 | tf_op jit(solution)/shard_map/all_to_all | solution.py:119
  35.8 73.4 %reduce-scatter.6.cloned.1.call-start = ((), (), s32[]{:S(2)}) async-start(), calls=%async_computation.4 | async-start | bytes 2654208 | tf_op jit(solution)/shard_map/reduce_scatter | solution.py:120
  42.3 5.3 copy-start.18
  42.3 5.3 copy-start.23
  44.6 66.5 %all-gather.6.cloned.1.call-start = ((), (), s32[]{:S(2)}) async-start(), calls=%async_computation.5 | async-start | bytes 3538944 | tf_op jit(solution)/shard_map/all_gather | solution.py:112
  45.2 131.8 %all-gather.8.cloned.1.call-start = ((), (), s32[]{:S(2)}) async-start(), calls=%async_computation.6 | async-start | bytes 7962624 | tf_op jit(solution)/shard_map/all_gather | solution.py:118
  47.4 192.0 %all-gather.10.cloned.1.call-start = ((), (), s32[]{:S(2)}) async-start(), calls=%async_computation.7 | async-start | bytes 3981312 | tf_op jit(solution)/shard_map/all_gather | solution.py:145
  110.3 0.7 copy-start.3
  111.0 2.8 copy-start.1
  183.3 1.4 copy-start.5
  183.3 2.4 copy-start.17
  183.4 2.7 copy-start.16
  183.4 3.1 copy-start.9
  183.4 3.1 copy-start.10
  186.1 4.8 copy-start.4
  188.6 5.7 copy-start.22
  190.9 98.9 %all-gather.12.cloned.1.call-start = ((), (), s32[]{:S(2)}) async-start(), calls=%async_computation.8 | async-start | bytes 3981312 | tf_op jit(solution)/shard_map/all_gather | solution.py:146
  193.2 203.5 %all-gather.14.cloned.1.call-start = ((), (), s32[]{:S(2)}) async-start(), calls=%async_computation.9 | async-start | bytes 2654208 | tf_op jit(solution)/shard_map/all_gather | solution.py:188
  193.8 261.8 %reduce-scatter.10.cloned.1.call-start = ((), (), s32[]{:S(2)}) async-start(), calls=%async_computation.12 | async-start | bytes 3538944
  291.9 6.4 %copy-start.12 = (f32[3,576]{1,0:T(4,128)S(1)}, f32[3,576]{1,0:T(4,128)}, u32[]{:S(2)}) copy-start(f32[3,576]{1,0:T(4,128)} %get-tuple-element.355) | copy-start | bytes 20740 | tf_op jit(solution)/shard_map/while
  298.3 4.4 copy-start.13
  304.9 6.4 %copy-start.12 = (f32[3,576]{1,0:T(4,128)S(1)}, f32[3,576]{1,0:T(4,128)}, u32[]{:S(2)}) copy-start(f32[3,576]{1,0:T(4,128)} %get-tuple-element.355) | copy-start | bytes 20740 | tf_op jit(solution)/shard_map/while
  311.4 4.4 copy-start.13
  318.0 6.4 %copy-start.12 = (f32[3,576]{1,0:T(4,128)S(1)}, f32[3,576]{1,0:T(4,128)}, u32[]{:S(2)}) copy-start(f32[3,576]{1,0:T(4,128)} %get-tuple-element.355) | copy-start | bytes 20740 | tf_op jit(solution)/shard_map/while
  324.4 4.4 copy-start.13
  331.0 6.4 %copy-start.12 = (f32[3,576]{1,0:T(4,128)S(1)}, f32[3,576]{1,0:T(4,128)}, u32[]{:S(2)}) copy-start(f32[3,576]{1,0:T(4,128)} %get-tuple-element.355) | copy-start | bytes 20740 | tf_op jit(solution)/shard_map/while
  337.4 4.4 copy-start.13
  344.0 6.4 %copy-start.12 = (f32[3,576]{1,0:T(4,128)S(1)}, f32[3,576]{1,0:T(4,128)}, u32[]{:S(2)}) copy-start(f32[3,576]{1,0:T(4,128)} %get-tuple-element.355) | copy-start | bytes 20740 | tf_op jit(solution)/shard_map/while
  350.4 4.4 copy-start.13
  357.0 6.4 %copy-start.12 = (f32[3,576]{1,0:T(4,128)S(1)}, f32[3,576]{1,0:T(4,128)}, u32[]{:S(2)}) copy-start(f32[3,576]{1,0:T(4,128)} %get-tuple-element.355) | copy-start | bytes 20740 | tf_op jit(solution)/shard_map/while
  363.4 4.4 copy-start.13
  370.0 6.4 %copy-start.12 = (f32[3,576]{1,0:T(4,128)S(1)}, f32[3,576]{1,0:T(4,128)}, u32[]{:S(2)}) copy-start(f32[3,576]{1,0:T(4,128)} %get-tuple-element.355) | copy-start | bytes 20740 | tf_op jit(solution)/shard_map/while
  376.4 4.4 copy-start.13
  383.0 6.4 %copy-start.12 = (f32[3,576]{1,0:T(4,128)S(1)}, f32[3,576]{1,0:T(4,128)}, u32[]{:S(2)}) copy-start(f32[3,576]{1,0:T(4,128)} %get-tuple-element.355) | copy-start | bytes 20740 | tf_op jit(solution)/shard_map/while
  389.4 4.4 copy-start.13
  395.0 0.8 copy-start.2
  400.3 2.9 slice-start
  403.1 32.6 %copy-start.20 = (bf16[2,3072]{1,0:T(2,128)(2,1)S(1)}, bf16[2,3072]{1,0:T(2,128)(2,1)}, u32[]{:S(2)}) copy-start(bf16[2,3072]{1,0:T(2,128)(2,1)} %param.26) | copy-start | bytes 36868
  403.1 32.7 %copy-start.11 = (bf16[384,64]{0,1:T(8,128)(2,1)S(1)}, bf16[384,64]{0,1:T(8,128)(2,1)}, u32[]{:S(2)}) copy-start(bf16[384,64]{0,1:T(8,128)(2,1)} %param.27) | copy-start | bytes 147460
  403.1 53.7 %copy-start.6 = (bf16[512,384]{1,0:T(8,128)(2,1)S(1)}, bf16[512,384]{1,0:T(8,128)(2,1)}, u32[]{:S(2)}) copy-start(bf16[512,384]{1,0:T(8,128)(2,1)} %param.17) | copy-start | bytes 1179652
  403.1 174.9 %copy-start.14 = (bf16[64,384]{1,0:T(8,128)(2,1)S(1)}, bf16[64,384]{1,0:T(8,128)(2,1)}, u32[]{:S(2)}) copy-start(bf16[64,384]{1,0:T(8,128)(2,1)} %param.18) | copy-start | bytes 147460
  403.2 179.4 %copy-start.15 = (bf16[3,3,64,64]{3,2,1,0:T(8,128)(2,1)S(1)}, bf16[3,3,64,64]{3,2,1,0:T(8,128)(2,1)}, u32[]{:S(2)}) copy-start(bf16[3,3,64,64]{3,2,1,0:T(8,128)(2,1)} %param.28) | copy-start | bytes 221188
  403.2 180.6 %copy-start.21 = (f32[8,512]{1,0:T(8,128)S(1)}, f32[8,512]{1,0:T(8,128)}, u32[]{:S(2)}) copy-start(f32[8,512]{1,0:T(8,128)} %param.29) | copy-start | bytes 49156
  403.2 92.2 %reduce-scatter.8.cloned.1.call-start = ((), (), s32[]{:S(2)}) async-start(), calls=%async_computation.10 | async-start | bytes 884736 | tf_op jit(solution)/shard_map/reduce_scatter | solution.py:196
  435.7 133.1 %all-reduce.4.cloned.1.call-start = ((), (), s32[]{:S(2)}) async-start(), calls=%async_computation.11 | async-start | bytes 368640 | tf_op jit(solution)/shard_map/psum | solution.py:237
  457.1 127.3 %copy-start.7 = (bf16[512,384]{1,0:T(8,128)(2,1)}, bf16[512,384]{1,0:T(8,128)(2,1)S(1)}, u32[]{:S(2)}) copy-start(bf16[512,384]{1,0:T(8,128)(2,1)S(1)} %get-tuple-element.240) | copy-start | bytes 1179652
  495.4 82.6 %collective-permute-start = (f32[64,384]{1,0:T(8,128)}, f32[64,384]{1,0:T(8,128)S(1)}, u32[]{:S(2)}, u32[]{:S(2)}) collective-permute-start(f32[64,384]{1,0:T(8,128)} %reduce-scatter.8.cloned.1.call-done), channel_id=1, source_target_pairs={{0,0},{1,8},{2,16},{3,24},{4,32},{5,40},{6,48},{7,56},{8,1},{9,9},... | collective-permute-start | bytes 294920 | tf_op jit(solution)/shard_map/ppermute | solution.py:201
  571.9 6.9 %collective-permute-start.1 = (bf16[1,4096]{1,0:T(2,128)(2,1)S(1)}, bf16[1,4096]{1,0:T(2,128)(2,1)S(1)}, u32[]{:S(2)}, u32[]{:S(2)}) collective-permute-start(bf16[1,4096]{1,0:T(2,128)(2,1)S(1)} %slice.193), channel_id=1, source_target_pairs={{0,8},{8,16},{16,24},{24,32},{32,40},{40,48},{48,56},{1,9},{9,17},... | collective-permute-start | bytes 24584 | tf_op jit(solution)/shard_map/ppermute | solution.py:21
  574.6 7.7 %collective-permute-start.2 = (bf16[1,4096]{1,0:T(2,128)(2,1)S(1)}, bf16[1,4096]{1,0:T(2,128)(2,1)S(1)}, u32[]{:S(2)}, u32[]{:S(2)}) collective-permute-start(bf16[1,4096]{1,0:T(2,128)(2,1)S(1)} %slice.195), channel_id=1, source_target_pairs={{8,0},{16,8},{24,16},{32,24},{40,32},{48,40},{56,48},{9,1},{17,9},... | collective-permute-start | bytes 24584 | tf_op jit(solution)/shard_map/ppermute | solution.py:24
  583.8 0.6 copy-start.19
Sparse Core Ops, SparseCore 0:
  44.7 64.4 reduce-scatter.5
  191.0 48.4 all-gather.9
  241.3 48.4 all-gather.11
  291.4 44.1 all-gather.13
Sparse Core Ops, SparseCore 1:
  46.9 50.1 all-gather.5
  98.7 78.2 all-gather.7
  403.3 52.3 reduce-scatter.9
  458.2 37.2 reduce-scatter.7
  498.3 70.5 all-reduce.3

commit v2 on v1

--- a/solution.py
+++ b/solution.py
@@ -23,6 +23,31 @@
         )
         high = lax.ppermute(lax.slice_in_dim(block, 0, width, axis=dim), axis, backward)
         block = jnp.concatenate([low, block, high], axis=dim)
+    return block
+
+
+def tree_sum(block, axis):
+    count = lax.axis_size(axis)
+    step = 1
+    while step < count:
+        block = block + lax.ppermute(block, axis, [(i, i ^ step) for i in range(count)])
+        step *= 2
+    return block
+
+
+def halving_sum(block, axis, dim):
+    count = lax.axis_size(axis)
+    at = lax.axis_index(axis)
+    step = count // 2
+    while step >= 1:
+        half = block.shape[dim] // 2
+        low = lax.slice_in_dim(block, 0, half, axis=dim)
+        high = lax.slice_in_dim(block, half, None, axis=dim)
+        upper = (at // step) % 2 == 1
+        kept = jnp.where(upper, high, low)
+        sent = jnp.where(upper, low, high)
+        block = kept + lax.ppermute(sent, axis, [(i, i ^ step) for i in range(count)])
+        step //= 2
     return block
 
 
@@ -142,8 +167,12 @@
         jnp.zeros((heads_local, local_len), jnp.float32),
         jnp.zeros((heads_local, local_len, head_dim), jnp.float32),
     )
-    key_piece = lax.all_gather(keys_local, "seq", axis=0, tiled=True)
-    value_piece = lax.all_gather(values_local, "seq", axis=0, tiled=True)
+    kv_width = heads_local * head_dim
+    kv_piece = lax.all_gather(
+        jnp.concatenate([keys_local, values_local], 1), "seq", axis=0, tiled=True
+    )
+    key_piece = kv_piece[:, :kv_width]
+    value_piece = kv_piece[:, kv_width:]
     blocks = key_piece.shape[0] // local_len
 
     def advance(block, state):
@@ -189,16 +218,11 @@
         preferred_element_type=jnp.float32,
     )
     txt_term = jnp.dot(
-        lax.all_gather(txt_attn, "seq", axis=0, tiled=True),
-        txt_out_w,
+        txt_attn,
+        lax.all_gather(txt_out_w, "seq", axis=1, tiled=True),
         preferred_element_type=jnp.float32,
     )
-    txt_part = lax.psum_scatter(
-        txt_term.astype(jnp.bfloat16).astype(jnp.float32), "tp", scatter_dimension=0, tiled=True
-    )
-    side = lax.axis_size("tp")
-    swap = [(a * side + b, b * side + a) for a in range(side) for b in range(side)]
-    txt_out = lax.ppermute(txt_part, ("seq", "tp"), swap)
+    txt_out = halving_sum(txt_term.astype(jnp.bfloat16).astype(jnp.float32), "tp", 1)
     img_out = lax.psum_scatter(
         img_term.astype(jnp.bfloat16), "tp", scatter_dimension=1, tiled=True
     ).astype(jnp.float32)
@@ -234,7 +258,7 @@
         ],
         0,
     )
-    packed = lax.psum(packed, "tp")
+    packed = tree_sum(packed, "tp")
     lifted = packed[:img_rows, :channels]
     row_mean = packed[:img_rows, channels] / full_width
     row_var = packed[:img_rows, channels + 1] / full_width - row_mean * row_mean

time: 594 us -> 512 us (0.86)
  waiting for transfers between devices: 344 us -> 280 us
  blocking collectives: 49.8 us -> 18.8 us
  starting transfers between devices: 16.2 us -> 25 us
    psum x1 -> x0, waiting for transfers between devices: 69.2 us -> none  [per_device(): packed = lax.psum(packed, 'tp')]
    ppermute x1 -> x6, waiting for transfers between devices: 0.01 us -> 40.5 us  [the longest x3 27.4 us: halving_sum(): lax.ppermute(sent, axis, [(i, i ^ step) for i in range(count)])]
    reduce_scatter x1 -> x0, waiting for transfers between devices: 34.9 us -> none  [per_device(): lax.psum_scatter(txt_term.astype(jnp.bfloat16).astype(jnp.float32), 'tp',...]
    all_gather x1 -> x0, blocking collectives: 31 us -> none  [per_device(): lax.all_gather(txt_attn, 'seq', axis=0, tiled=True)]
    unnamed x10 -> x8, waiting for transfers between devices: 19.8 us -> 36.4 us
    all_gather x2, waiting for transfers between devices: 93.6 us -> 77.5 us  [the longest x1 77.5 us: per_device(): lax.all_gather(jnp.concatenate([keys_local, values_local], 1), 'seq', axi...]
    ppermute x1 -> x6, starting transfers between devices: 4.26 us -> 13.1 us  [the longest x3 7.5 us: halving_sum(): lax.ppermute(sent, axis, [(i, i ^ step) for i in range(count)])]
    slice x0 -> x1, local copies, waits for them, and re-layouts: none -> 6.73 us  [per_device(): value_piece = kv_piece[:, kv_width:]]
  transfers between devices with their start and end apart: 13 -> 16, of which waited for: 9 -> 10; matrix products, arithmetic and copies ran while one was open for 23% -> 28% of each run, Pallas kernels for 0% -> 0%
where the time goes in v2:
time: 512 us; the launch traced here: 507 us
  waiting for transfers between devices  280 us (55%)
  matrix products  73.9 us (14%)
  other arithmetic  46.6 us (9%)
  local copies, waits for them, and re-layouts  44.6 us (9%)
  starting transfers between devices  25 us (5%)
  blocking collectives  18.8 us (4%)
  between operations  17.7 us (3%)
    all_gather x1, waiting for transfers between devices, per_device(): lax.all_gather(jnp.concatenate([keys_local, values_local], 1), 'seq', axi...  77.5 us
    all_gather x1, waiting for transfers between devices, per_device(): lax.all_gather(img_qkv, 'seq', axis=0, tiled=True)  60.8 us
    reduce_scatter x1, waiting for transfers between devices, per_device(): lax.psum_scatter(add_rows(txt_norm_rows, txt_qkv), 'seq', scatter_dimensi...  57.6 us
    unnamed x8, waiting for transfers between devices  36.4 us
    dot_general x8, matrix products, advance(): jnp.einsum('hqk,khd->hqd', weights.astype(jnp.bfloat16), value_block, pre...  32.8 us
    ppermute x3, waiting for transfers between devices, halving_sum(): lax.ppermute(sent, axis, [(i, i ^ step) for i in range(count)])  27.4 us
    reduce_sum x8, other arithmetic, advance(): running = running * rescale + jnp.sum(weights, -1)  26.1 us
    dot_general x8, matrix products, advance(): jnp.einsum('qhd,khd->hqk', queries, key_block, preferred_element_type=jnp...  24.6 us
  transfers between devices with their start and end apart: 16, of which 10 were waited for; matrix products, arithmetic and copies ran while one was open for 28% of the time, Pallas kernels for 0%

profile of v2, /device:TPU:26, one launch (start us, length us, event | category | flops | bytes accessed | tf_op | source)
XLA Modules:
  0.0 506.7 jit_solution(16978659868541265932)
XLA Ops:
  8.0 1.4 fusion.105
  10.2 18.8 %all_gather.18 = bf16[64,3072]{1,0:T(8,128)(2,1)S(1)} all-gather(bf16[64,384]{1,0:T(8,128)(2,1)} %param.18), channel_id=1, replica_groups=mesh['req'=4,'seq'=8,'tp'=8] {'tp'}, dimensions={1}, use_global_device_ids=true | all-gather | bytes 442368 | tf_op jit(solution)/shard_map/all_gather | solution.py:138
  30.4 5.4 %all-to-all-start = ((bf16[64,8,384]{2,0,1:T(8,128)(2,1)}), bf16[64,8,384]{2,0,1:T(8,128)(2,1)S(1)}, u32[]{:S(2)}, u32[]{:S(2)}) async-start(bf16[64,8,384]{2,0,1:T(8,128)(2,1)} %bitcast.152), calls=%async_computation | async-start | bytes 786432 | tf_op jit(solution)/shard_map/all_to_all | solution.py:144
  35.8 2.5 copy.106
  38.3 4.1 all-to-all-done
  42.3 2.2 fusion.108
  45.2 2.2 copy.109
  51.6 57.6 %reduce-scatter.5.cloned.1.call-done = f32[64,1152]{1,0:T(8,128)} async-done(((f32[512,1152]{1,0:T(8,128)}), f32[64,1152]{1,0:T(8,128)}) %reduce-scatter.5.cloned.1.call-update) | async-done | bytes 294928 | tf_op jit(solution)/shard_map/reduce_scatter | solution.py:145
  111.6 2.5 convert_reduce_fusion
  116.2 60.8 %all-gather.8.cloned.1.call-done = bf16[3072,3,384]{0,2,1:T(8,128)(2,1)} async-done(((bf16[384,3,384]{0,2,1:T(8,128)(2,1)}), bf16[3072,3,384]{0,2,1:T(8,128)(2,1)}) %all-gather.8.cloned.1.call-update) | async-done | bytes 7077904 | tf_op jit(solution)/shard_map/all_gather | solution.py:143
  177.0 6.4 %fusion.24 = f32[512,3,3,128]{0,3,2,1:T(8,128)S(1)} fusion(bf16[3,3,128,3072]{3,2,1,0:T(8,128)(2,1)} %bitcast.194, bf16[512,3072]{1,0:T(8,128)(2,1)S(1)} %copy-done.1, f32[3072]{0:T(1024)} %bitcast.191, f32[3072]{0:T(1024)} %bitcast.190, f32[512]{0:T(512)} %add_rsqrt_fusion.5, f32[512]{0:T(512)} %copy-done.18), kind=kOutput, calls=%fused_computation.36 | convolution fusion | flops 3633315840 | bytes 12611584 | tf_op jit(solution)/shard_map/dot_general | solution.py:110
  185.4 2.1 subtract_convert_fusion
  189.1 1.3 copy.112
  194.1 77.5 %all-gather.10.cloned.1.call-done = bf16[4608,768]{1,0:T(8,128)(2,1)} async-done(((bf16[576,768]{1,0:T(8,128)(2,1)}), bf16[4608,768]{1,0:T(8,128)(2,1)}) %all-gather.10.cloned.1.call-update) | async-done | bytes 7077904 | tf_op jit(solution)/shard_map/all_gather | solution.py:171
  271.6 6.7 %fusion.102 = (bf16[4608,384]{1,0:T(8,128)(2,1)}, bf16[4608,384]{1,0:T(8,128)(2,1)}) fusion(bf16[4608,768]{1,0:T(8,128)(2,1)} %all-gather.10.cloned.1.call-done), kind=kLoop, calls=%fused_computation.198 | loop fusion | bytes 14155776 | tf_op jit(solution)/shard_map/slice | solution.py:175
  278.3 103.6 %while.18 = (s32[]{:T(128)}, f32[3,576]{1,0:T(4,128)S(1)}, f32[3,576]{1,0:T(4,128)S(1)}, f32[3,576,128]{2,1,0:T(8,128)S(1)}, s32[]{:T(128)}, /*index=5*/bf16[460...) while((s32[]{:T(128)}, f32[3,576]{1,0:T(4,128)S(1)}, ...), condition=%wide.region_12.13_spmd.clone, body=%wide.region_9.12_spmd.clone.sunk | while | flops 521231040 | bytes 18692560 | solution.py:206
  278.3 1.2 constant_dynamic-slice_fusion.7
  280.5 3.1 bitcast_reduce_fusion.2
  283.6 3.2 fusion.135
  287.1 4.1 fusion.137
  291.3 1.2 constant_dynamic-slice_fusion.7
  293.4 3.1 bitcast_reduce_fusion.2
  296.5 3.3 fusion.135
  300.1 4.1 fusion.137
  304.2 1.2 constant_dynamic-slice_fusion.7
  306.4 3.1 bitcast_reduce_fusion.2
  309.5 3.3 fusion.135
  313.0 4.1 fusion.137
  317.2 1.2 constant_dynamic-slice_fusion.7
  319.4 3.1 bitcast_reduce_fusion.2
  322.4 3.2 fusion.135
  326.0 4.1 fusion.137
  330.1 1.2 constant_dynamic-slice_fusion.7
  332.3 3.1 bitcast_reduce_fusion.2
  335.4 3.3 fusion.135
  338.9 4.1 fusion.137
  343.1 1.3 constant_dynamic-slice_fusion.7
  345.3 3.1 bitcast_reduce_fusion.2
  348.3 3.3 fusion.135
  351.9 4.1 fusion.137
  356.1 1.2 constant_dynamic-slice_fusion.7
  358.2 3.1 bitcast_reduce_fusion.2
  361.3 3.2 fusion.135
  364.9 4.1 fusion.137
  369.0 1.2 constant_dynamic-slice_fusion.7
  371.2 3.1 bitcast_reduce_fusion.2
  374.2 3.2 fusion.135
  377.8 4.1 fusion.137
  384.0 3.6 convolution_convert_fusion
  387.7 2.8 copy.132
  391.5 2.2 fusion.22
  393.8 5.3 %collective-permute-start = (f32[64,1536]{1,0:T(8,128)S(1)}, f32[64,1536]{1,0:T(8,128)S(1)}, u32[]{:S(2)}, u32[]{:S(2)}) collective-permute-start(f32[64,1536]{1,0:T(8,128)S(1)} %slice_select_fusion), channel_id=1, source_target_pairs={{0,4},{1,5},{2,6},{3,7},{4,0},{5,1},{6,2},{7,3},{8,12},{9,13},{10,... | collective-permute-start | bytes 1179656 | tf_op jit(solution)/shard_map/ppermute | solution.py:49
  401.5 13.6 %collective-permute-done = f32[64,1536]{1,0:T(8,128)S(1)} collective-permute-done((f32[64,1536]{1,0:T(8,128)S(1)}, f32[64,1536]{1,0:T(8,128)S(1)}, u32[]{:S(2)}, u32[]{:S(2)}) %collective-permute-start) | collective-permute-done | bytes 393248 | tf_op jit(solution)/shard_map/ppermute | solution.py:49
  415.2 34.6 %reduce-scatter.7.cloned.1.call-done = bf16[384,512]{1,0:T(8,128)(2,1)} async-done(((bf16[3072,512]{1,0:T(8,128)(2,1)}), bf16[384,512]{1,0:T(8,128)(2,1)}) %reduce-scatter.7.cloned.1.call-update) | async-done | bytes 393232
  449.8 1.2 copy.133
  451.9 2.0 collective-permute-start.3
  453.9 2.1 collective-permute-start.1
  457.1 13.8 %collective-permute-done.1 = f32[64,768]{1,0:T(8,128)S(1)} collective-permute-done((f32[64,768]{1,0:T(8,128)S(1)}, f32[64,768]{1,0:T(8,128)S(1)}, u32[]{:S(2)}, u32[]{:S(2)}) %collective-permute-start.1) | collective-permute-done | bytes 196640 | tf_op jit(solution)/shard_map/ppermute | solution.py:49
  470.9 3.0 collective-permute-done.4
  473.9 2.6 collective-permute-start.5
  476.6 10.2 %collective-permute-done.5 = f32[514,66]{0,1:T(8,128)S(1)} collective-permute-done((f32[514,66]{0,1:T(8,128)S(1)}, f32[514,66]{0,1:T(8,128)S(1)}, u32[]{:S(2)}, u32[]{:S(2)}) %collective-permute-start.5) | collective-permute-done | bytes 135728 | tf_op jit(solution)/shard_map/ppermute | solution.py:33
  487.4 1.9 collective-permute-start.6
  489.5 3.9 collective-permute-start.7
  494.4 2.8 collective-permute-done.7
  (216 shorter events, 38.0 us)
Async XLA Ops:
  8.0 383.3 %copy-start = (bf16[384,64]{0,1:T(8,128)(2,1)S(1)}, bf16[384,64]{0,1:T(8,128)(2,1)}, u32[]{:S(2)}) copy-start(bf16[384,64]{0,1:T(8,128)(2,1)} %param.27) | copy-start | bytes 147460
  30.4 14.8 %copy-start.8 = (bf16[384,3,384]{2,0,1:T(8,128)(2,1)S(1)}, bf16[384,3,384]{2,0,1:T(8,128)(2,1)}, u32[]{:S(2)}) copy-start(bf16[384,3,384]{2,0,1:T(8,128)(2,1)} %param.21) | copy-start | bytes 2654212
  30.4 11.9 %all-to-all-start = ((bf16[64,8,384]{2,0,1:T(8,128)(2,1)}), bf16[64,8,384]{2,0,1:T(8,128)(2,1)S(1)}, u32[]{:S(2)}, u32[]{:S(2)}) async-start(bf16[64,8,384]{2,0,1:T(8,128)(2,1)} %bitcast.152), calls=%async_computation | async-start | bytes 786432 | tf_op jit(solution)/shard_map/all_to_all | solution.py:144
  35.8 73.4 %reduce-scatter.5.cloned.1.call-start = ((), (), s32[]{:S(2)}) async-start(), calls=%async_computation.3 | async-start | bytes 2654208 | tf_op jit(solution)/shard_map/reduce_scatter | solution.py:145
  42.3 5.3 %copy-start.14 = (bf16[3,3072]{1,0:T(4,128)(2,1)S(1)}, bf16[3,3072]{1,0:T(4,128)(2,1)}, u32[]{:S(2)}) copy-start(bf16[3,3072]{1,0:T(4,128)(2,1)} %param.19) | copy-start | bytes 55300
  42.3 5.4 %copy-start.20 = (f32[4,128]{1,0:T(4,128)S(1)}, f32[4,128]{1,0:T(4,128)}, u32[]{:S(2)}) copy-start(f32[4,128]{1,0:T(4,128)} %param.23) | copy-start | bytes 6148
  44.6 66.9 %all-gather.6.cloned.1.call-start = ((), (), s32[]{:S(2)}) async-start(), calls=%async_computation.4 | async-start | bytes 3538944 | tf_op jit(solution)/shard_map/all_gather | solution.py:137
  45.2 131.8 %all-gather.8.cloned.1.call-start = ((), (), s32[]{:S(2)}) async-start(), calls=%async_computation.5 | async-start | bytes 7962624 | tf_op jit(solution)/shard_map/all_gather | solution.py:143
  47.5 224.2 %all-gather.10.cloned.1.call-start = ((), (), s32[]{:S(2)}) async-start(), calls=%async_computation.6 | async-start | bytes 7962624 | tf_op jit(solution)/shard_map/all_gather | solution.py:171
  110.3 1.3 copy-start.3
  111.5 3.1 copy-start.1
  114.1 0.5 copy-start.18
  183.4 1.3 copy-start.13
  183.4 1.7 copy-start.12
  184.7 3.9 copy-start.9
  187.5 4.5 copy-start.4
  187.5 4.7 copy-start.19
  190.5 193.6 %all-gather.12.cloned.1.call-start = ((), (), s32[]{:S(2)}) async-start(), calls=%async_computation.7 | async-start | bytes 2654208 | tf_op jit(solution)/shard_map/all_gather | solution.py:217
  191.2 200.2 %all-gather.14.cloned.1.call-start = ((), (), s32[]{:S(2)}) async-start(), calls=%async_computation.8 | async-start | bytes 2654208 | tf_op jit(solution)/shard_map/all_gather | solution.py:222
  191.8 258.0 %reduce-scatter.7.cloned.1.call-start = ((), (), s32[]{:S(2)}) async-start(), calls=%async_computation.9 | async-start | bytes 3538944
  194.1 84.3 %copy-start.7 = (f32[3,576,128]{2,1,0:T(8,128)S(1)}, f32[3,576,128]{2,1,0:T(8,128)}, u32[]{:S(2)}) copy-start(f32[3,576,128]{2,1,0:T(8,128)} %custom-call.2) | copy-start | bytes 2654212
  382.3 0.8 copy-start.2
  387.7 3.6 copy-start.16
  387.7 3.8 slice-start
  390.5 60.5 %copy-start.5 = (bf16[512,384]{1,0:T(8,128)(2,1)S(1)}, bf16[512,384]{1,0:T(8,128)(2,1)}, u32[]{:S(2)}) copy-start(bf16[512,384]{1,0:T(8,128)(2,1)} %param.17) | copy-start | bytes 1179652
  393.8 99.7 %copy-start.10 = (bf16[64,384]{1,0:T(8,128)(2,1)S(1)}, bf16[64,384]{1,0:T(8,128)(2,1)}, u32[]{:S(2)}) copy-start(bf16[64,384]{1,0:T(8,128)(2,1)} %param.18) | copy-start | bytes 147460
  393.8 21.3 %collective-permute-start = (f32[64,1536]{1,0:T(8,128)S(1)}, f32[64,1536]{1,0:T(8,128)S(1)}, u32[]{:S(2)}, u32[]{:S(2)}) collective-permute-start(f32[64,1536]{1,0:T(8,128)S(1)} %slice_select_fusion), channel_id=1, source_target_pairs={{0,4},{1,5},{2,6},{3,7},{4,0},{5,1},{6,2},{7,3},{8,12},{9,13},{10,... | collective-permute-start | bytes 1179656 | tf_op jit(solution)/shard_map/ppermute | solution.py:49
  401.5 95.9 %copy-start.11 = (bf16[3,3,64,64]{3,2,1,0:T(8,128)(2,1)S(1)}, bf16[3,3,64,64]{3,2,1,0:T(8,128)(2,1)}, u32[]{:S(2)}) copy-start(bf16[3,3,64,64]{3,2,1,0:T(8,128)(2,1)} %param.28) | copy-start | bytes 221188
  415.2 83.5 %copy-start.17 = (f32[8,512]{1,0:T(8,128)S(1)}, f32[8,512]{1,0:T(8,128)}, u32[]{:S(2)}) copy-start(f32[8,512]{1,0:T(8,128)} %param.29) | copy-start | bytes 49156
  451.3 48.0 %copy-start.6 = (bf16[512,384]{1,0:T(8,128)(2,1)}, bf16[512,384]{1,0:T(8,128)(2,1)S(1)}, u32[]{:S(2)}) copy-start(bf16[512,384]{1,0:T(8,128)(2,1)S(1)} %get-tuple-element.240) | copy-start | bytes 1179652
  451.9 4.1 collective-permute-start.3
  453.9 16.9 %collective-permute-start.1 = (f32[64,768]{1,0:T(8,128)S(1)}, f32[64,768]{1,0:T(8,128)S(1)}, u32[]{:S(2)}, u32[]{:S(2)}) collective-permute-start(f32[64,768]{1,0:T(8,128)S(1)} %slice_select_fusion.1), channel_id=1, source_target_pairs={{0,2},{1,3},{2,0},{3,1},{4,6},{5,7},{6,4},{7,5},{8,10},{9,11},{10,... | collective-permute-start | bytes 589832 | tf_op jit(solution)/shard_map/ppermute | solution.py:49
  456.0 17.8 %collective-permute-start.4 = (f32[514,66]{0,1:T(8,128)S(1)}, f32[514,66]{0,1:T(8,128)S(1)}, u32[]{:S(2)}, u32[]{:S(2)}) collective-permute-start(f32[514,66]{0,1:T(8,128)S(1)} %fusion.101), channel_id=1, source_target_pairs={{0,2},{1,3},{2,0},{3,1},{4,6},{5,7},{6,4},{7,5},{8,10},{9,11},{10,... | collective-permute-start | bytes 407096 | tf_op jit(solution)/shard_map/ppermute | solution.py:33
  473.9 12.9 %collective-permute-start.5 = (f32[514,66]{0,1:T(8,128)S(1)}, f32[514,66]{0,1:T(8,128)S(1)}, u32[]{:S(2)}, u32[]{:S(2)}) collective-permute-start(f32[514,66]{0,1:T(8,128)S(1)} %add.334), channel_id=1, source_target_pairs={{0,4},{1,5},{2,6},{3,7},{4,0},{5,1},{6,2},{7,3},{8,12},{9,13},{10,... | collective-permute-start | bytes 407096 | tf_op jit(solution)/shard_map/ppermute | solution.py:33
  476.5 16.9 %collective-permute-start.2 = (f32[64,384]{1,0:T(8,128)S(1)}, f32[64,384]{1,0:T(8,128)S(1)}, u32[]{:S(2)}, u32[]{:S(2)}) collective-permute-start(f32[64,384]{1,0:T(8,128)S(1)} %slice_select_fusion.2), channel_id=1, source_target_pairs={{0,1},{1,0},{2,3},{3,2},{4,5},{5,4},{6,7},{7,6},{8,9},{9,8},{10,11... | collective-permute-start | bytes 294920 | tf_op jit(solution)/shard_map/ppermute | solution.py:49
  487.4 6.9 %collective-permute-start.6 = (bf16[1,4096]{1,0:T(2,128)(2,1)S(1)}, bf16[1,4096]{1,0:T(2,128)(2,1)S(1)}, u32[]{:S(2)}, u32[]{:S(2)}) collective-permute-start(bf16[1,4096]{1,0:T(2,128)(2,1)S(1)} %slice.225), channel_id=1, source_target_pairs={{0,8},{8,16},{16,24},{24,32},{32,40},{40,48},{48,56},{1,9},{9,17},... | collective-permute-start | bytes 24584 | tf_op jit(solution)/shard_map/ppermute | solution.py:21
  489.5 7.7 %collective-permute-start.7 = (bf16[1,4096]{1,0:T(2,128)(2,1)S(1)}, bf16[1,4096]{1,0:T(2,128)(2,1)S(1)}, u32[]{:S(2)}, u32[]{:S(2)}) collective-permute-start(bf16[1,4096]{1,0:T(2,128)(2,1)S(1)} %slice.227), channel_id=1, source_target_pairs={{8,0},{16,8},{24,16},{32,24},{40,32},{48,40},{56,48},{9,1},{17,9},... | collective-permute-start | bytes 24584 | tf_op jit(solution)/shard_map/ppermute | solution.py:24
  498.7 0.6 copy-start.15
Sparse Core Ops, SparseCore 0:
  44.7 64.4 reduce-scatter.4
  190.6 80.9 all-gather.9
  273.4 44.1 all-gather.11
  319.2 44.5 all-gather.13
Sparse Core Ops, SparseCore 1:
  46.9 50.1 all-gather.5
  98.7 78.2 all-gather.7
  390.6 59.1 reduce-scatter.6

commit v3 on v2

--- a/solution.py
+++ b/solution.py
@@ -1,8 +1,10 @@
+import functools
 import math
 
 import jax
 import jax.numpy as jnp
 from jax import lax
+from jax.experimental import pallas as pl
 from jax.sharding import PartitionSpec as P
 
 STEPS = 28
@@ -49,6 +51,44 @@
         block = kept + lax.ppermute(sent, axis, [(i, i ^ step) for i in range(count)])
         step //= 2
     return block
+
+
+def attend_block(keep_ref, query_ref, key_ref, value_ref, out_ref, *, scale):
+    scores = (
+        lax.dot_general(
+            query_ref[...],
+            key_ref[...],
+            (((1,), (1,)), ((), ())),
+            preferred_element_type=jnp.float32,
+        )
+        * scale
+    )
+    scores = jnp.where(keep_ref[...] > 0.5, scores, -1e30)
+    peak = jnp.max(scores, -1, keepdims=True)
+    weights = jnp.exp(scores - peak)
+    summed = jnp.sum(weights, -1, keepdims=True)
+    mixed_v = jnp.dot(
+        weights.astype(jnp.bfloat16), value_ref[...], preferred_element_type=jnp.float32
+    )
+    out_ref[...] = (mixed_v / summed).astype(out_ref.dtype)
+
+
+def attention(keep, queries, keys, values, head_dim, q_tile):
+    rows = queries.shape[0]
+    total = keys.shape[0]
+    heads = queries.shape[1] // head_dim
+    return pl.pallas_call(
+        functools.partial(attend_block, scale=head_dim ** (-0.5)),
+        grid=(heads, rows // q_tile),
+        in_specs=[
+            pl.BlockSpec((1, total), lambda h, i: (0, 0)),
+            pl.BlockSpec((q_tile, head_dim), lambda h, i: (i, h)),
+            pl.BlockSpec((total, head_dim), lambda h, i: (0, h)),
+            pl.BlockSpec((total, head_dim), lambda h, i: (0, h)),
+        ],
+        out_specs=pl.BlockSpec((q_tile, head_dim), lambda h, i: (i, h)),
+        out_shape=jax.ShapeDtypeStruct(queries.shape, jnp.bfloat16),
+    )(keep, queries, keys, values)
 
 
 def modulate(hidden, mod_rows):
@@ -161,54 +201,23 @@
         local_len, heads_local * head_dim
     )
     limit = text_len[0]
-    score_scale = head_dim ** (-0.5)
-    start_state = (
-        jnp.full((heads_local, local_len), -1e30, jnp.float32),
-        jnp.zeros((heads_local, local_len), jnp.float32),
-        jnp.zeros((heads_local, local_len, head_dim), jnp.float32),
-    )
     kv_width = heads_local * head_dim
     kv_piece = lax.all_gather(
         jnp.concatenate([keys_local, values_local], 1), "seq", axis=0, tiled=True
     )
     key_piece = kv_piece[:, :kv_width]
     value_piece = kv_piece[:, kv_width:]
-    blocks = key_piece.shape[0] // local_len
-
-    def advance(block, state):
-        peak, running, accum = state
-        key_block = lax.dynamic_slice_in_dim(key_piece, block * local_len, local_len, 0).reshape(
-            local_len, heads_local, head_dim
-        )
-        value_block = lax.dynamic_slice_in_dim(
-            value_piece, block * local_len, local_len, 0
-        ).reshape(local_len, heads_local, head_dim)
-        within = jnp.arange(local_len, dtype=jnp.int32)
-        text_pos = block * txt_rows + within
-        usable = (within >= txt_rows) | (text_pos < limit)
-        scores = (
-            jnp.einsum("qhd,khd->hqk", queries, key_block, preferred_element_type=jnp.float32)
-            * score_scale
-        )
-        scores = jnp.where(usable[None, None, :], scores, -1e30)
-        new_peak = jnp.maximum(peak, jnp.max(scores, -1))
-        rescale = jnp.exp(peak - new_peak)
-        weights = jnp.exp(scores - new_peak[..., None])
-        running = running * rescale + jnp.sum(weights, -1)
-        accum = accum * rescale[..., None] + jnp.einsum(
-            "hqk,khd->hqd",
-            weights.astype(jnp.bfloat16),
-            value_block,
-            preferred_element_type=jnp.float32,
-        )
-        return (new_peak, running, accum)
-
-    peak, running, accum = lax.fori_loop(0, blocks, advance, start_state)
-    attn = (
-        (accum / running[..., None])
-        .astype(jnp.bfloat16)
-        .transpose(1, 0, 2)
-        .reshape(local_len, heads_local * head_dim)
+    slot = jnp.arange(key_piece.shape[0], dtype=jnp.int32)
+    within = slot % local_len
+    text_pos = (slot // local_len) * txt_rows + within
+    keep = ((within >= txt_rows) | (text_pos < limit)).astype(jnp.float32)[None, :]
+    attn = attention(
+        keep,
+        queries.reshape(local_len, kv_width),
+        key_piece,
+        value_piece,
+        head_dim,
+        local_len // 3,
     )
     txt_attn = attn[:txt_rows]
     img_attn = attn[txt_rows:]

time: 512 us -> 464 us (0.906)
  matrix products: 73.9 us -> 16.5 us
  waiting for transfers between devices: 280 us -> 316 us
  other arithmetic: 46.6 us -> 17.9 us
  Pallas kernels: 0 us -> 18.7 us
  local copies, waits for them, and re-layouts: 44.6 us -> 27.2 us
  starting transfers between devices: 25 us -> 30.5 us
    all_gather x1, waiting for transfers between devices: 0.01 us -> 58.6 us  [per_device(): lax.all_gather(txt_out_w, 'seq', axis=1, tiled=True)]
    dot_general x16 -> x0, matrix products: 57.4 us -> none  [the longest x8 32.8 us: advance(): jnp.einsum('hqk,khd->hqd', weights.astype(jnp.bfloat16), value_block, pre...]
    unnamed x8, waiting for transfers between devices: 36.4 us -> 1.82 us
    reduce_sum x8 -> x0, other arithmetic: 26.1 us -> none  [advance(): running = running * rescale + jnp.sum(weights, -1)]
    all_gather x1, waiting for transfers between devices: 0.01 us -> 20.5 us  [per_device(): lax.all_gather(img_out_w, 'seq', axis=1, tiled=True)]
    pallas_call x0 -> x1, Pallas kernels: none -> 18.7 us  [attention(): pl.pallas_call(functools.partial(attend_block, scale=head_dim ** (-0.5)),...]
    dynamic_slice x24 -> x0, local copies, waits for them, and re-layouts: 14.1 us -> none  [the longest x16 12 us: advance(): lax.dynamic_slice_in_dim(value_piece, block * local_len, local_len, 0)]
    ppermute x3, waiting for transfers between devices: 27.4 us -> 19.9 us  [halving_sum(): lax.ppermute(sent, axis, [(i, i ^ step) for i in range(count)])]
  transfers between devices with their start and end apart: 16 -> 16, of which waited for: 10 -> 11; matrix products, arithmetic and copies ran while one was open for 28% -> 8% of each run, Pallas kernels for 0% -> 4%
where the time goes in v3:
time: 464 us; the launch traced here: 463 us
  waiting for transfers between devices  316 us (68%)
  starting transfers between devices  30.5 us (7%)
  local copies, waits for them, and re-layouts  27.2 us (6%)
  blocking collectives  18.8 us (4%)
  Pallas kernels  18.7 us (4%)
  other arithmetic  17.9 us (4%)
  between operations  17.5 us (4%)
  matrix products  16.5 us (4%)
    all_gather x1, waiting for transfers between devices, per_device(): lax.all_gather(jnp.concatenate([keys_local, values_local], 1), 'seq', axi...  76 us
    all_gather x1, waiting for transfers between devices, per_device(): lax.all_gather(img_qkv, 'seq', axis=0, tiled=True)  60.9 us
    all_gather x1, waiting for transfers between devices, per_device(): lax.all_gather(txt_out_w, 'seq', axis=1, tiled=True)  58.6 us
    reduce_scatter x1, waiting for transfers between devices, per_device(): lax.psum_scatter(add_rows(txt_norm_rows, txt_qkv), 'seq', scatter_dimensi...  56.9 us
    all_gather x1, waiting for transfers between devices, per_device(): lax.all_gather(img_out_w, 'seq', axis=1, tiled=True)  20.5 us
    ppermute x3, waiting for transfers between devices, halving_sum(): lax.ppermute(sent, axis, [(i, i ^ step) for i in range(count)])  19.9 us
    all_gather x1, blocking collectives, per_device(): lax.all_gather(txt_hidden, 'tp', axis=1, tiled=True)  18.8 us
    pallas_call x1, Pallas kernels, attention(): pl.pallas_call(functools.partial(attend_block, scale=head_dim ** (-0.5)),...  18.7 us
  transfers between devices with their start and end apart: 16, of which 11 were waited for; matrix products, arithmetic and copies ran while one was open for 8% of the time, Pallas kernels for 4%

profile of v3, /device:TPU:26, one launch (start us, length us, event | category | flops | bytes accessed | tf_op | source)
XLA Modules:
  0.0 463.2 jit_solution(9607608980633032367)
XLA Ops:
  8.0 1.5 fusion.93
  9.5 0.7 convert_element_type.121
  10.2 18.8 %all_gather.18 = bf16[64,3072]{1,0:T(8,128)(2,1)S(1)} all-gather(bf16[64,384]{1,0:T(8,128)(2,1)} %param.16), channel_id=1, replica_groups=mesh['req'=4,'seq'=8,'tp'=8] {'tp'}, dimensions={1}, use_global_device_ids=true | all-gather | bytes 442368 | tf_op jit(solution)/shard_map/all_gather | solution.py:178
  29.7 0.8 copy.104
  30.5 5.2 %all-to-all-start = ((bf16[64,8,384]{2,0,1:T(8,128)(2,1)}), bf16[64,8,384]{2,0,1:T(8,128)(2,1)S(1)}, u32[]{:S(2)}, u32[]{:S(2)}) async-start(bf16[64,8,384]{2,0,1:T(8,128)(2,1)} %bitcast.139), calls=%async_computation | async-start | bytes 786432 | tf_op jit(solution)/shard_map/all_to_all | solution.py:184
  35.7 2.4 copy.73
  38.1 4.2 all-to-all-done
  42.2 2.2 fusion.96
  44.6 0.5 all-gather.6.cloned.1.call-update
  45.1 2.2 copy.76
  47.6 0.8 mul.373
  48.4 0.8 mul.400
  49.2 0.6 broadcast_bitcast_fusion
  49.8 1.2 fusion.28
  51.0 0.6 fusion.94
  51.6 0.6 slice_add_fusion
  52.2 56.9 %reduce-scatter.5.cloned.1.call-done = f32[64,1152]{1,0:T(8,128)} async-done(((f32[512,1152]{1,0:T(8,128)}), f32[64,1152]{1,0:T(8,128)}) %reduce-scatter.5.cloned.1.call-update) | async-done | bytes 294928 | tf_op jit(solution)/shard_map/reduce_scatter | solution.py:185
  109.1 1.1 reshape.324
  110.5 0.6 add_rsqrt_fusion
  111.3 2.5 convert_reduce_fusion
  113.9 0.5 copy-done.17
  114.4 1.0 fusion.2
  115.4 0.6 add_rsqrt_fusion.5
  116.0 60.9 %all-gather.8.cloned.1.call-done = bf16[3072,3,384]{0,2,1:T(8,128)(2,1)} async-done(((bf16[384,3,384]{0,2,1:T(8,128)(2,1)}), bf16[3072,3,384]{0,2,1:T(8,128)(2,1)}) %all-gather.8.cloned.1.call-update) | async-done | bytes 7077904 | tf_op jit(solution)/shard_map/all_gather | solution.py:183
  176.9 6.4 %fusion.8 = f32[512,3,3,128]{0,3,2,1:T(8,128)S(1)} fusion(bf16[3,3,128,3072]{3,2,1,0:T(8,128)(2,1)} %bitcast.166, bf16[512,3072]{1,0:T(8,128)(2,1)S(1)} %copy-done.1, f32[3072]{0:T(1024)} %bitcast.163, f32[3072]{0:T(1024)} %bitcast.162, f32[512]{0:T(512)} %add_rsqrt_fusion.5, f32[512]{0:T(512)} %copy-done.17), kind=kOutput, calls=%fused_computation.12 | convolution fusion | flops 3633315840 | bytes 12611584 | tf_op jit(solution)/shard_map/dot_general | solution.py:150
  183.7 0.5 squeeze.59
  184.1 0.5 squeeze.61
  184.6 0.3 multiply_multiply_fusion.1
  185.0 0.3 multiply_multiply_fusion
  185.4 2.1 subtract_convert_fusion
  187.5 0.9 pad_maximum_fusion.2
  189.0 1.0 maximum_maximum_fusion
  190.0 0.7 all-gather.12.cloned.1.call-update
  190.8 0.5 all-gather.14.cloned.1.call-update
  192.2 0.7 or_convert_fusion.keep_ref
  193.1 0.9 pad_maximum_fusion.1
  194.4 0.8 pad_maximum_fusion.query_ref
  195.2 76.0 %all-gather.10.cloned.1.call-done = bf16[4608,768]{1,0:T(8,128)(2,1)} async-done(((bf16[576,768]{1,0:T(8,128)(2,1)}), bf16[4608,768]{1,0:T(8,128)(2,1)}) %all-gather.10.cloned.1.call-update) | async-done | bytes 7077904 | tf_op jit(solution)/shard_map/all_gather | solution.py:205
  271.1 6.7 %fusion.91 = (bf16[4608,384]{1,0:T(8,128)(2,1)}, bf16[4608,384]{1,0:T(8,128)(2,1)}) fusion(bf16[4608,768]{1,0:T(8,128)(2,1)} %all-gather.10.cloned.1.call-done), kind=kLoop, calls=%fused_computation.184 | loop fusion | bytes 14155776 | tf_op jit(solution)/shard_map/slice | solution.py:209
  277.9 18.7 %shard_map.182 = bf16[576,384]{1,0:T(8,128)(2,1)} custom-call(f32[1,4608]{1,0:T(1,128)} %or_convert_fusion.keep_ref, bf16[576,384]{1,0:T(8,128)(2,1)} %pad_maximum_fusion.query_ref, bf16[4608,384]{1,0:T(8,128)(2,1)} %get-tuple-element.17.key_ref, bf16[4608,384]{1,0:T(8,128)(2,1)} %get-tuple-element.16.value_ref), custom_call_target="tpu_custom_call" | custom-call | tf_op jit(solution)/shard_map/pallas_call | solution.py:80
  296.6 20.5 %all-gather.12.cloned.1.call-done = bf16[384,3072]{1,0:T(8,128)(2,1)} async-done(((bf16[384,384]{1,0:T(8,128)(2,1)}), bf16[384,3072]{1,0:T(8,128)(2,1)}) %all-gather.12.cloned.1.call-update) | async-done | bytes 2359312 | tf_op jit(solution)/shard_map/all_gather | solution.py:226
  317.1 3.6 convolution_convert_fusion
  320.7 2.8 copy.88
  323.6 0.6 copy-done.14
  324.4 58.6 %all-gather.14.cloned.1.call-done = bf16[384,3072]{1,0:T(8,128)(2,1)} async-done(((bf16[384,384]{1,0:T(8,128)(2,1)}), bf16[384,3072]{1,0:T(8,128)(2,1)}) %all-gather.14.cloned.1.call-update) | async-done | bytes 2359312 | tf_op jit(solution)/shard_map/all_gather | solution.py:231
  383.0 2.3 fusion.6
  385.3 6.5 %collective-permute-start = (f32[64,1536]{1,0:T(8,128)S(1)}, f32[64,1536]{1,0:T(8,128)S(1)}, u32[]{:S(2)}, u32[]{:S(2)}) collective-permute-start(f32[64,1536]{1,0:T(8,128)S(1)} %slice_select_fusion), channel_id=1, source_target_pairs={{0,4},{1,5},{2,6},{3,7},{4,0},{5,1},{6,2},{7,3},{8,12},{9,13},{10,... | collective-permute-start | bytes 1179656 | tf_op jit(solution)/shard_map/ppermute | solution.py:51
  392.8 0.7 fusion.78
  393.5 0.7 fusion.79
  394.2 7.4 %collective-permute-done = f32[64,1536]{1,0:T(8,128)S(1)} collective-permute-done((f32[64,1536]{1,0:T(8,128)S(1)}, f32[64,1536]{1,0:T(8,128)S(1)}, u32[]{:S(2)}, u32[]{:S(2)}) %collective-permute-start) | collective-permute-done | bytes 393248 | tf_op jit(solution)/shard_map/ppermute | solution.py:51
  401.7 1.2 copy.89
  402.9 0.3 convert_reduce_fusion.1
  403.3 0.6 fusion.20
  404.0 7.2 %collective-permute-start.1 = (f32[64,768]{1,0:T(8,128)S(1)}, f32[64,768]{1,0:T(8,128)S(1)}, u32[]{:S(2)}, u32[]{:S(2)}) collective-permute-start(f32[64,768]{1,0:T(8,128)S(1)} %slice_select_fusion.1), channel_id=1, source_target_pairs={{0,2},{1,3},{2,0},{3,1},{4,6},{5,7},{6,4},{7,5},{8,10},{9,11},{10,... | collective-permute-start | bytes 589832 | tf_op jit(solution)/shard_map/ppermute | solution.py:51
  411.3 1.4 collective-permute-start.4
  412.6 12.5 %collective-permute-done.1 = f32[64,768]{1,0:T(8,128)S(1)} collective-permute-done((f32[64,768]{1,0:T(8,128)S(1)}, f32[64,768]{1,0:T(8,128)S(1)}, u32[]{:S(2)}, u32[]{:S(2)}) %collective-permute-start.1) | collective-permute-done | bytes 196640 | tf_op jit(solution)/shard_map/ppermute | solution.py:51
  425.2 3.7 collective-permute-done.4
  428.9 3.5 collective-permute-start.5
  432.5 10.8 %collective-permute-done.5 = f32[514,66]{0,1:T(8,128)S(1)} collective-permute-done((f32[514,66]{0,1:T(8,128)S(1)}, f32[514,66]{0,1:T(8,128)S(1)}, u32[]{:S(2)}, u32[]{:S(2)}) %collective-permute-start.5) | collective-permute-done | bytes 135728 | tf_op jit(solution)/shard_map/ppermute | solution.py:35
  443.9 1.9 collective-permute-start.6
  446.0 3.9 collective-permute-start.7
  450.0 0.7 fusion.29
  451.0 2.8 collective-permute-done.7
  455.2 0.6 multiply_subtract_fusion
  (123 shorter events, 6.7 us)
Async XLA Ops:
  8.0 316.3 %copy-start = (bf16[384,64]{0,1:T(8,128)(2,1)S(1)}, bf16[384,64]{0,1:T(8,128)(2,1)}, u32[]{:S(2)}) copy-start(bf16[384,64]{0,1:T(8,128)(2,1)} %param.25) | copy-start | bytes 147460
  8.0 27.7 %copy-start.4 = (bf16[384,3,384]{2,0,1:T(8,128)(2,1)S(1)}, bf16[384,3,384]{2,0,1:T(8,128)(2,1)}, u32[]{:S(2)}) copy-start(bf16[384,3,384]{2,0,1:T(8,128)(2,1)} %param.20) | copy-start | bytes 2654212
  30.5 11.8 %all-to-all-start = ((bf16[64,8,384]{2,0,1:T(8,128)(2,1)}), bf16[64,8,384]{2,0,1:T(8,128)(2,1)S(1)}, u32[]{:S(2)}, u32[]{:S(2)}) async-start(bf16[64,8,384]{2,0,1:T(8,128)(2,1)} %bitcast.139), calls=%async_computation | async-start | bytes 786432 | tf_op jit(solution)/shard_map/all_to_all | solution.py:184
  35.7 73.5 %reduce-scatter.5.cloned.1.call-start = ((), (), s32[]{:S(2)}) async-start(), calls=%async_computation.3 | async-start | bytes 2654208 | tf_op jit(solution)/shard_map/reduce_scatter | solution.py:185
  42.2 2.9 copy-start.5
  44.5 3.1 copy-start.12
  44.5 3.1 copy-start.18
  44.5 66.8 %all-gather.6.cloned.1.call-start = ((), (), s32[]{:S(2)}) async-start(), calls=%async_computation.4 | async-start | bytes 3538944 | tf_op jit(solution)/shard_map/all_gather | solution.py:177
  45.1 131.8 %all-gather.8.cloned.1.call-start = ((), (), s32[]{:S(2)}) async-start(), calls=%async_computation.5 | async-start | bytes 7962624 | tf_op jit(solution)/shard_map/all_gather | solution.py:183
  47.4 223.8 %all-gather.10.cloned.1.call-start = ((), (), s32[]{:S(2)}) async-start(), calls=%async_computation.6 | async-start | bytes 7962624 | tf_op jit(solution)/shard_map/all_gather | solution.py:205
  111.3 3.1 copy-start.1
  113.9 0.5 copy-start.17
  183.3 1.3 copy-start.10
  183.6 1.4 copy-start.9
  183.6 1.7 copy-start.6
  187.5 5.5 %copy-start.11 = (f32[64,3]{1,0:T(8,128)S(1)}, f32[64,3]{1,0:T(8,128)}, u32[]{:S(2)}) copy-start(f32[64,3]{1,0:T(8,128)} %get-tuple-element.55) | copy-start | bytes 2308
  188.4 4.7 %copy-start.16 = (f32[384]{0:T(512)S(1)}, f32[384]{0:T(512)}, u32[]{:S(2)}) copy-start(f32[384]{0:T(512)} %get-tuple-element.51) | copy-start | bytes 4612
  190.0 127.1 %all-gather.12.cloned.1.call-start = ((), (), s32[]{:S(2)}) async-start(), calls=%async_computation.7 | async-start | bytes 2654208 | tf_op jit(solution)/shard_map/all_gather | solution.py:226
  190.7 192.3 %all-gather.14.cloned.1.call-start = ((), (), s32[]{:S(2)}) async-start(), calls=%async_computation.8 | async-start | bytes 2654208 | tf_op jit(solution)/shard_map/all_gather | solution.py:231
  191.3 210.4 %reduce-scatter.7.cloned.1.call-start = ((), (), s32[]{:S(2)}) async-start(), calls=%async_computation.9 | async-start | bytes 3538944
  323.5 0.7 copy-start.14
  324.4 78.5 %copy-start.2 = (bf16[512,384]{1,0:T(8,128)(2,1)S(1)}, bf16[512,384]{1,0:T(8,128)(2,1)}, u32[]{:S(2)}) copy-start(bf16[512,384]{1,0:T(8,128)(2,1)} %param.15) | copy-start | bytes 1179652
  385.3 16.3 %collective-permute-start = (f32[64,1536]{1,0:T(8,128)S(1)}, f32[64,1536]{1,0:T(8,128)S(1)}, u32[]{:S(2)}, u32[]{:S(2)}) collective-permute-start(f32[64,1536]{1,0:T(8,128)S(1)} %slice_select_fusion), channel_id=1, source_target_pairs={{0,4},{1,5},{2,6},{3,7},{4,0},{5,1},{6,2},{7,3},{8,12},{9,13},{10,... | collective-permute-start | bytes 1179656 | tf_op jit(solution)/shard_map/ppermute | solution.py:51
  402.9 47.1 %copy-start.7 = (bf16[64,384]{1,0:T(8,128)(2,1)S(1)}, bf16[64,384]{1,0:T(8,128)(2,1)}, u32[]{:S(2)}) copy-start(bf16[64,384]{1,0:T(8,128)(2,1)} %param.16) | copy-start | bytes 147460
  402.9 51.1 %copy-start.8 = (bf16[3,3,64,64]{3,2,1,0:T(8,128)(2,1)S(1)}, bf16[3,3,64,64]{3,2,1,0:T(8,128)(2,1)}, u32[]{:S(2)}) copy-start(bf16[3,3,64,64]{3,2,1,0:T(8,128)(2,1)} %param.26) | copy-start | bytes 221188
  403.2 51.6 %copy-start.3 = (bf16[512,384]{1,0:T(8,128)(2,1)}, bf16[512,384]{1,0:T(8,128)(2,1)S(1)}, u32[]{:S(2)}) copy-start(bf16[512,384]{1,0:T(8,128)(2,1)S(1)} %get-tuple-element.15) | copy-start | bytes 1179652
  403.3 52.0 %copy-start.15 = (f32[8,512]{1,0:T(8,128)S(1)}, f32[8,512]{1,0:T(8,128)}, u32[]{:S(2)}) copy-start(f32[8,512]{1,0:T(8,128)} %param.27) | copy-start | bytes 49156
  403.9 7.3 %collective-permute-start.3 = (f32[514,66]{0,1:T(8,128)S(1)}, f32[514,66]{0,1:T(8,128)S(1)}, u32[]{:S(2)}, u32[]{:S(2)}) collective-permute-start(f32[514,66]{0,1:T(8,128)S(1)} %select_maximum_fusion), channel_id=1, source_target_pairs={{0,1},{1,0},{2,3},{3,2},{4,5},{5,4},{6,7},{7,6},{8,9},{9,8},{10,11... | collective-permute-start | bytes 407096 | tf_op jit(solution)/shard_map/ppermute | solution.py:35
  404.0 21.1 %collective-permute-start.1 = (f32[64,768]{1,0:T(8,128)S(1)}, f32[64,768]{1,0:T(8,128)S(1)}, u32[]{:S(2)}, u32[]{:S(2)}) collective-permute-start(f32[64,768]{1,0:T(8,128)S(1)} %slice_select_fusion.1), channel_id=1, source_target_pairs={{0,2},{1,3},{2,0},{3,1},{4,6},{5,7},{6,4},{7,5},{8,10},{9,11},{10,... | collective-permute-start | bytes 589832 | tf_op jit(solution)/shard_map/ppermute | solution.py:51
  411.3 17.6 %collective-permute-start.4 = (f32[514,66]{0,1:T(8,128)S(1)}, f32[514,66]{0,1:T(8,128)S(1)}, u32[]{:S(2)}, u32[]{:S(2)}) collective-permute-start(f32[514,66]{0,1:T(8,128)S(1)} %fusion.90), channel_id=1, source_target_pairs={{0,2},{1,3},{2,0},{3,1},{4,6},{5,7},{6,4},{7,5},{8,10},{9,11},{10,... | collective-permute-start | bytes 407096 | tf_op jit(solution)/shard_map/ppermute | solution.py:35
  428.9 14.4 %collective-permute-start.5 = (f32[514,66]{0,1:T(8,128)S(1)}, f32[514,66]{0,1:T(8,128)S(1)}, u32[]{:S(2)}, u32[]{:S(2)}) collective-permute-start(f32[514,66]{0,1:T(8,128)S(1)} %add.315), channel_id=1, source_target_pairs={{0,4},{1,5},{2,6},{3,7},{4,0},{5,1},{6,2},{7,3},{8,12},{9,13},{10,... | collective-permute-start | bytes 407096 | tf_op jit(solution)/shard_map/ppermute | solution.py:35
  432.4 17.6 %collective-permute-start.2 = (f32[64,384]{1,0:T(8,128)S(1)}, f32[64,384]{1,0:T(8,128)S(1)}, u32[]{:S(2)}, u32[]{:S(2)}) collective-permute-start(f32[64,384]{1,0:T(8,128)S(1)} %slice_select_fusion.2), channel_id=1, source_target_pairs={{0,1},{1,0},{2,3},{3,2},{4,5},{5,4},{6,7},{7,6},{8,9},{9,8},{10,11... | collective-permute-start | bytes 294920 | tf_op jit(solution)/shard_map/ppermute | solution.py:51
  443.9 6.9 %collective-permute-start.6 = (bf16[1,4096]{1,0:T(2,128)(2,1)S(1)}, bf16[1,4096]{1,0:T(2,128)(2,1)S(1)}, u32[]{:S(2)}, u32[]{:S(2)}) collective-permute-start(bf16[1,4096]{1,0:T(2,128)(2,1)S(1)} %slice.217), channel_id=1, source_target_pairs={{0,8},{8,16},{16,24},{24,32},{32,40},{40,48},{48,56},{1,9},{9,17},... | collective-permute-start | bytes 24584 | tf_op jit(solution)/shard_map/ppermute | solution.py:23
  446.0 7.7 %collective-permute-start.7 = (bf16[1,4096]{1,0:T(2,128)(2,1)S(1)}, bf16[1,4096]{1,0:T(2,128)(2,1)S(1)}, u32[]{:S(2)}, u32[]{:S(2)}) collective-permute-start(bf16[1,4096]{1,0:T(2,128)(2,1)S(1)} %slice.219), channel_id=1, source_target_pairs={{8,0},{16,8},{24,16},{32,24},{40,32},{48,40},{56,48},{9,1},{17,9},... | collective-permute-start | bytes 24584 | tf_op jit(solution)/shard_map/ppermute | solution.py:26
  455.2 0.6 copy-start.13
Sparse Core Ops, SparseCore 0:
  44.6 64.4 reduce-scatter.4
  190.1 80.9 all-gather.9
  272.9 44.1 all-gather.11
  318.8 64.1 all-gather.13
Sparse Core Ops, SparseCore 1:
  46.8 50.1 all-gather.5
  98.6 78.2 all-gather.7
  323.7 72.1 reduce-scatter.6

commit v4 on v3

--- a/solution.py
+++ b/solution.py
@@ -89,6 +89,57 @@
         out_specs=pl.BlockSpec((q_tile, head_dim), lambda h, i: (i, h)),
         out_shape=jax.ShapeDtypeStruct(queries.shape, jnp.bfloat16),
     )(keep, queries, keys, values)
+
+
+def bit_of(value, step):
+    return (value // step) % 2
+
+
+def doubling_gather(block, axis, dim, order):
+    count = lax.axis_size(axis)
+    at = lax.axis_index(axis)
+    stacked = block[None]
+    for step in order:
+        other = lax.ppermute(stacked, axis, [(i, i ^ step) for i in range(count)])
+        upper = bit_of(at, step) == 1
+        stacked = jnp.stack([jnp.where(upper, other, stacked), jnp.where(upper, stacked, other)])
+        stacked = stacked.reshape((-1,) + block.shape)
+    rank = len(order)
+    source = [sum(((p >> k) & 1) * order[k] for k in range(rank)) for p in range(count)]
+    place = [source.index(d) for d in range(count)]
+    picked = jnp.stack([stacked[p] for p in place], 0)
+    moved = jnp.moveaxis(picked, 0, dim)
+    shape = list(block.shape)
+    shape[dim] *= count
+    return moved.reshape(shape)
+
+
+def halving_scatter(block, axis, dim, order):
+    count = lax.axis_size(axis)
+    at = lax.axis_index(axis)
+    rank = len(order)
+    width = block.shape[dim] // count
+    pieces = [lax.slice_in_dim(block, d * width, (d + 1) * width, axis=dim) for d in range(count)]
+    slots = [sum(((d // order[k]) % 2) << (rank - 1 - k) for k in range(rank)) for d in range(count)]
+    arranged = [None] * count
+    for d in range(count):
+        arranged[slots[d]] = pieces[d]
+    block = jnp.concatenate(arranged, dim)
+    for step in order:
+        half = block.shape[dim] // 2
+        low = lax.slice_in_dim(block, 0, half, axis=dim)
+        high = lax.slice_in_dim(block, half, None, axis=dim)
+        upper = bit_of(at, step) == 1
+        kept = jnp.where(upper, high, low)
+        sent = jnp.where(upper, low, high)
+        block = kept + lax.ppermute(sent, axis, [(i, i ^ step) for i in range(count)])
+    return block
+
+
+def transpose_devices(block):
+    side = lax.axis_size("tp")
+    swap = [(a * side + b, b * side + a) for a in range(side) for b in range(side)]
+    return lax.ppermute(block, ("seq", "tp"), swap)
 
 
 def modulate(hidden, mod_rows):
@@ -173,18 +224,17 @@
     img_rows = img_hidden.shape[0]
     txt_rows = txt_hidden.shape[0]
     local_width = img_hidden.shape[1]
-    img_full, txt_full = (
-        lax.all_gather(img_hidden, "tp", axis=1, tiled=True),
-        lax.all_gather(txt_hidden, "tp", axis=1, tiled=True),
-    )
+    tp_order = (4, 2, 1)
+    seq_order = (2, 1, 4)
+    img_full = doubling_gather(img_hidden, "tp", 1, tp_order)
+    txt_full = doubling_gather(txt_hidden, "tp", 1, tp_order)
+    img_out_full = doubling_gather(img_out_w, "seq", 1, seq_order)
     full_width = img_full.shape[1]
     img_norm = modulate(img_full, img_mod)
     txt_norm = modulate(txt_full, txt_mod)
     img_mixed = add_rows(img_norm, lax.all_gather(img_qkv, "seq", axis=0, tiled=True))
     txt_norm_rows = lax.all_to_all(txt_norm, "seq", 1, 0, tiled=True)
-    txt_mixed = lax.psum_scatter(
-        add_rows(txt_norm_rows, txt_qkv), "seq", scatter_dimension=0, tiled=True
-    )
+    txt_mixed = halving_scatter(add_rows(txt_norm_rows, txt_qkv), "seq", 0, (4, 1, 2))
     head_dim = qk_gains.shape[1]
     grid_side = latent.shape[0] * seq_count
     token_ids = seq_at * img_rows + jnp.arange(img_rows, dtype=jnp.int32)
@@ -223,15 +273,17 @@
     img_attn = attn[txt_rows:]
     img_term = jnp.dot(
         img_attn,
-        lax.all_gather(img_out_w, "seq", axis=1, tiled=True),
+        img_out_full,
         preferred_element_type=jnp.float32,
     )
     txt_term = jnp.dot(
-        txt_attn,
-        lax.all_gather(txt_out_w, "seq", axis=1, tiled=True),
+        doubling_gather(txt_attn, "seq", 0, seq_order),
+        txt_out_w,
         preferred_element_type=jnp.float32,
     )
-    txt_out = halving_sum(txt_term.astype(jnp.bfloat16).astype(jnp.float32), "tp", 1)
+    txt_out = transpose_devices(
+        halving_scatter(txt_term.astype(jnp.bfloat16).astype(jnp.float32), "tp", 0, (1, 2, 4))
+    )
     img_out = lax.psum_scatter(
         img_term.astype(jnp.bfloat16), "tp", scatter_dimension=1, tiled=True
     ).astype(jnp.float32)

time: 464 us -> 477 us (1.028); the launches traced: 463 us -> 468 us
  waiting for transfers between devices: 316 us -> 255 us
  starting transfers between devices: 30.5 us -> 68.3 us
  local copies, waits for them, and re-layouts: 27.2 us -> 59.5 us
  blocking collectives: 18.8 us -> 0 us
  other arithmetic: 17.9 us -> 36.2 us
    ppermute x3 -> x19, waiting for transfers between devices: 19.9 us -> 170 us  [the longest x12 124 us: doubling_gather(): other = lax.ppermute(stacked, axis, [(i, i ^ step) for i in range(count)])]
    all_gather x3 -> x0, waiting for transfers between devices: 79.1 us -> none  [the longest x1 58.6 us: per_device(): lax.all_gather(txt_out_w, 'seq', axis=1, tiled=True)]
    all_gather x1, waiting for transfers between devices: 60.9 us -> 0.02 us  [per_device(): lax.all_gather(img_qkv, 'seq', axis=0, tiled=True)]
    reduce_scatter x1 -> x0, waiting for transfers between devices: 56.9 us -> none  [per_device(): lax.psum_scatter(add_rows(txt_norm_rows, txt_qkv), 'seq', scatter_dimensi...]
    all_gather x1, waiting for transfers between devices: 76 us -> 20.3 us  [per_device(): lax.all_gather(jnp.concatenate([keys_local, values_local], 1), 'seq', axi...]
    ppermute x3 -> x19, starting transfers between devices: 13.8 us -> 50.4 us  [the longest x12 39.1 us: doubling_gather(): other = lax.ppermute(stacked, axis, [(i, i ^ step) for i in range(count)])]
    unnamed x8 -> x4, waiting for transfers between devices: 1.82 us -> 23.2 us
    all_gather x1 -> x0, blocking collectives: 18.8 us -> none  [per_device(): lax.all_gather(txt_hidden, 'tp', axis=1, tiled=True)]
  transfers between devices with their start and end apart: 16 -> 28, of which waited for: 11 -> 19; matrix products, arithmetic and copies ran while one was open for 8% -> 16% of each run, Pallas kernels for 4% -> 0%
where the time goes in v4:
time: 477 us; the launch traced here: 468 us
  waiting for transfers between devices  255 us (53%)
  starting transfers between devices  68.3 us (14%)
  local copies, waits for them, and re-layouts  59.5 us (12%)
  other arithmetic  36.2 us (8%)
  Pallas kernels  18.7 us (4%)
  between operations  16.6 us (3%)
  matrix products  13.9 us (3%)
    ppermute x12, waiting for transfers between devices, doubling_gather(): other = lax.ppermute(stacked, axis, [(i, i ^ step) for i in range(count)])  124 us
    ppermute x6, waiting for transfers between devices, halving_scatter(): lax.ppermute(sent, axis, [(i, i ^ step) for i in range(count)])  46.2 us
    ppermute x12, starting transfers between devices, doubling_gather(): other = lax.ppermute(stacked, axis, [(i, i ^ step) for i in range(count)])  39.1 us
    ppermute x3, waiting for transfers between devices, tree_sum(): lax.ppermute(block, axis, [(i, i ^ step) for i in range(count)])  24 us
    unnamed x90, local copies, waits for them, and re-layouts  23.7 us
    unnamed x4, waiting for transfers between devices  23.2 us
    all_gather x1, waiting for transfers between devices, per_device(): lax.all_gather(jnp.concatenate([keys_local, values_local], 1), 'seq', axi...  20.3 us
    pallas_call x1, Pallas kernels, attention(): pl.pallas_call(functools.partial(attend_block, scale=head_dim ** (-0.5)),...  18.7 us
  transfers between devices with their start and end apart: 28, of which 19 were waited for; matrix products, arithmetic and copies ran while one was open for 16% of the time, Pallas kernels for 0%

profile of v4, /device:TPU:26, one launch (start us, length us, event | category | flops | bytes accessed | tf_op | source)
XLA Modules:
  0.0 468.3 jit_solution(11457501983727777757)
XLA Ops:
  7.3 7.3 %collective-permute-start = (bf16[1,64,384]{2,1,0:T(8,128)(2,1)}, bf16[1,64,384]{2,1,0:T(8,128)(2,1)S(1)}, u32[]{:S(2)}, u32[]{:S(2)}) collective-permute-start(bf16[1,64,384]{2,1,0:T(8,128)(2,1)} %bitcast.285), channel_id=1, source_target_pairs={{0,4},{1,5},{2,6},{3,7},{4,0},{5,1},{6,2},{7,3},{8,12},{9,13},{10,... | collective-permute-start | bytes 147464 | tf_op jit(solution)/shard_map/ppermute | solution.py:103
  14.6 2.3 collective-permute-done
  17.7 2.6 collective-permute-start.1
  20.3 2.3 copy.111
  22.6 1.8 collective-permute-done.1
  24.6 5.0 %collective-permute-start.6 = (bf16[1,512,384]{2,1,0:T(8,128)(2,1)S(1)}, bf16[1,512,384]{2,1,0:T(8,128)(2,1)S(1)}, u32[]{:S(2)}, u32[]{:S(2)}) collective-permute-start(bf16[1,512,384]{2,1,0:T(8,128)(2,1)S(1)} %bitcast.272), channel_id=1, source_target_pairs={{0,4},{1,5},{2,6},{3,7},{4,0},{5,1},{6,2},{7,3},{8,12},{9,13},{10,... | collective-permute-start | bytes 1179656 | tf_op jit(solution)/shard_map/ppermute | solution.py:103
  29.8 2.4 copy.100
  33.0 1.0 fusion.18
  34.0 6.0 %all-to-all-start = ((bf16[64,8,384]{2,0,1:T(8,128)(2,1)}), bf16[64,8,384]{2,0,1:T(8,128)(2,1)S(1)}, u32[]{:S(2)}, u32[]{:S(2)}) async-start(bf16[64,8,384]{2,0,1:T(8,128)(2,1)} %fusion.18), calls=%async_computation | async-start | bytes 786432 | tf_op jit(solution)/shard_map/all_to_all | solution.py:236
  41.5 7.6 %collective-permute-done.6 = bf16[1,512,384]{2,1,0:T(8,128)(2,1)S(1)} collective-permute-done((bf16[1,512,384]{2,1,0:T(8,128)(2,1)S(1)}, bf16[1,512,384]{2,1,0:T(8,128)(2,1)S(1)}, u32[]{:S(2)}, u32[]{:S(2)}) %collective-permute-start.6) | collective-permute-done | bytes 393248 | tf_op jit(solution)/shard_map/ppermute | solution.py:103
  49.4 14.6 %collective-permute-start.7 = (bf16[2,512,384]{2,1,0:T(8,128)(2,1)S(1)}, bf16[2,512,384]{2,1,0:T(8,128)(2,1)}, u32[]{:S(2)}, u32[]{:S(2)}) collective-permute-start(bf16[2,512,384]{2,1,0:T(8,128)(2,1)S(1)} %maximum_bitcast_fusion), channel_id=1, source_target_pairs={{0,2},{1,3},{2,0},{3,1},{4,6},{5,7},{6,4},{7,5},{8,10},{9,11},{10,... | collective-permute-start | bytes 2359304 | tf_op jit(solution)/shard_map/ppermute | solution.py:103
  64.0 15.1 %all-to-all-done = bf16[64,8,384]{2,0,1:T(8,128)(2,1)S(1)} async-done(((bf16[64,8,384]{2,0,1:T(8,128)(2,1)}), bf16[64,8,384]{2,0,1:T(8,128)(2,1)S(1)}, u32[]{:S(2)}, u32[]{:S(2)}) %all-to-all-start) | async-done | bytes 393248 | tf_op jit(solution)/shard_map/all_to_all | solution.py:236
  80.3 18.4 %collective-permute-done.7 = bf16[2,512,384]{2,1,0:T(8,128)(2,1)} collective-permute-done((bf16[2,512,384]{2,1,0:T(8,128)(2,1)S(1)}, bf16[2,512,384]{2,1,0:T(8,128)(2,1)}, u32[]{:S(2)}, u32[]{:S(2)}) %collective-permute-start.7) | collective-permute-done | bytes 786464 | tf_op jit(solution)/shard_map/ppermute | solution.py:103
  98.7 1.3 select_bitcast_fusion.5
  100.4 1.2 fusion.26
  101.6 45.8 %collective-permute-done.3 = f32[256,1152]{1,0:T(8,128)S(1)} collective-permute-done((f32[256,1152]{1,0:T(8,128)S(1)}, f32[256,1152]{1,0:T(8,128)S(1)}, u32[]{:S(2)}, u32[]{:S(2)}) %collective-permute-start.3) | collective-permute-done | bytes 1179680 | tf_op jit(solution)/shard_map/ppermute | solution.py:135
  147.6 1.0 slice_select_fusion
  149.9 1.6 copy.128
  151.5 1.5 copy.129
  153.0 1.5 copy.130
  154.5 1.5 copy.131
  156.0 1.5 copy.132
  157.5 1.5 copy.133
  159.1 1.5 copy.134
  160.6 1.5 copy.135
  162.1 15.9 %stack.162 = bf16[8,512,384]{2,0,1:T(8,128)(2,1)S(1)} concatenate(bf16[1,512,384]{2,0,1:T(2,128)(2,1)} %copy.128, bf16[1,512,384]{2,0,1:T(2,128)(2,1)} %copy.129, bf16[1,512,384]{2,0,1:T(2,128)(2,1)} %copy.130, bf16[1,512,384]{2,0,1:T(2,128)(2,1)} %copy.131, bf16[1,512,384]{2,0,1:T(2,128)(2,1)} %copy.132, bf16[1,512,384]{2,0,1:T(2,128)(2,1)} %copy.133, ...), dimensions={0} | concatenate | bytes 6291456 | tf_op jit(solution)/shard_map/stack | solution.py:110
  178.0 1.3 convert_reduce_fusion
  179.2 7.4 %fusion.2 = f32[512]{0:T(512)S(1)} fusion(bf16[8,512,384]{2,0,1:T(8,128)(2,1)S(1)} %stack.162, f32[512]{0:T(512)S(1)} %broadcast_multiply_fusion.2), kind=kLoop, calls=%fused_computation.4 | loop fusion | flops 6290944 | bytes 3149824 | tf_op jit(solution)/shard_map/reduce_sum | solution.py:149
  186.7 1.2 select_add_fusion.1
  189.6 3.4 fusion.6
  193.0 5.9 %reshape.436 = bf16[512,3072,1,1]{1,0,2,3:T(8,128)(2,1)} reshape(bf16[512,8,384]{2,1,0:T(8,128)(2,1)} %fusion.6) | data formatting | bytes 6291456 | tf_op jit(solution)/shard_map/convert_element_type | solution.py:151
  198.9 1.0 select_add_fusion.3
  200.1 1.4 multiply_reduce_fusion.2
  201.7 7.1 %fusion.7 = f32[512,3,3,128]{0,3,2,1:T(8,128)S(1)} fusion(bf16[3,3,128,3072]{3,2,1,0:T(8,128)(2,1)} %bitcast.293, bf16[512,3072,1,1]{1,0,2,3:T(8,128)(2,1)} %reshape.436), kind=kOutput, calls=%fused_computation.11 | convolution fusion | flops 3623878656 | bytes 12582912 | tf_op jit(solution)/shard_map/dot_general | solution.py:201
  211.2 2.7 subtract_convert_fusion
  215.4 1.0 maximum_maximum_fusion
  216.5 3.6 collective-permute-start.9
  220.0 7.4 %collective-permute-done.9 = bf16[1,384,384]{2,1,0:T(8,128)(2,1)S(1)} collective-permute-done((bf16[1,384,384]{2,1,0:T(8,128)(2,1)S(1)}, bf16[1,384,384]{2,1,0:T(8,128)(2,1)S(1)}, u32[]{:S(2)}, u32[]{:S(2)}) %collective-permute-start.9) | collective-permute-done | bytes 294944 | tf_op jit(solution)/shard_map/ppermute | solution.py:103
  227.5 2.2 collective-permute-start.10
  229.7 20.2 %collective-permute-done.10 = bf16[2,384,384]{2,1,0:T(8,128)(2,1)S(1)} collective-permute-done((bf16[2,384,384]{2,1,0:T(8,128)(2,1)S(1)}, bf16[2,384,384]{2,1,0:T(8,128)(2,1)S(1)}, u32[]{:S(2)}, u32[]{:S(2)}) %collective-permute-start.10) | collective-permute-done | bytes 589856 | tf_op jit(solution)/shard_map/ppermute | solution.py:103
  251.1 2.8 collective-permute-start.11
  255.2 44.3 %collective-permute-done.11 = bf16[4,384,384]{1,2,0:T(8,128)(2,1)S(1)} collective-permute-done((bf16[4,384,384]{1,2,0:T(8,128)(2,1)S(1)}, bf16[4,384,384]{1,2,0:T(8,128)(2,1)S(1)}, u32[]{:S(2)}, u32[]{:S(2)}) %collective-permute-start.11) | collective-permute-done | bytes 1179680 | tf_op jit(solution)/shard_map/ppermute | solution.py:103
  301.0 0.9 copy-done.26
  304.0 20.3 %all-gather.5.cloned.1.call-done = bf16[4608,768]{1,0:T(8,128)(2,1)} async-done(((bf16[576,768]{1,0:T(8,128)(2,1)}), bf16[4608,768]{1,0:T(8,128)(2,1)}) %all-gather.5.cloned.1.call-update) | async-done | bytes 7077904 | tf_op jit(solution)/shard_map/all_gather | solution.py:255
  324.3 6.7 %fusion.90 = (bf16[4608,384]{1,0:T(8,128)(2,1)}, bf16[4608,384]{1,0:T(8,128)(2,1)}) fusion(bf16[4608,768]{1,0:T(8,128)(2,1)} %all-gather.5.cloned.1.call-done), kind=kLoop, calls=%fused_computation.258 | loop fusion | bytes 14155776 | tf_op jit(solution)/shard_map/slice | solution.py:259
  331.0 18.7 %shard_map.182 = bf16[576,384]{1,0:T(8,128)(2,1)} custom-call(f32[1,4608]{1,0:T(1,128)} %or_convert_fusion.keep_ref, bf16[576,384]{1,0:T(8,128)(2,1)} %pad_maximum_fusion.10.query_ref, bf16[4608,384]{1,0:T(8,128)(2,1)} %get-tuple-element.21.key_ref, bf16[4608,384]{1,0:T(8,128)(2,1)} %get-tuple-element.20.value_ref), custom_call_target="tpu_custom_call" | custom-call | tf_op jit(solution)/shard_map/pallas_call | solution.py:80
  349.7 3.6 convolution_convert_fusion
  353.4 2.8 copy.126
  357.0 5.6 %collective-permute-done.12 = bf16[1,64,384]{2,1,0:T(8,128)(2,1)S(1)} collective-permute-done((bf16[1,64,384]{2,1,0:T(8,128)(2,1)S(1)}, bf16[1,64,384]{2,1,0:T(8,128)(2,1)S(1)}, u32[]{:S(2)}, u32[]{:S(2)}) %collective-permute-start.12) | collective-permute-done | bytes 49184 | tf_op jit(solution)/shard_map/ppermute | solution.py:103
  363.7 4.5 collective-permute-done.13
  368.8 11.4 %collective-permute-done.14 = bf16[4,64,384]{2,1,0:T(8,128)(2,1)S(1)} collective-permute-done((bf16[4,64,384]{2,1,0:T(8,128)(2,1)S(1)}, bf16[4,64,384]{2,1,0:T(8,128)(2,1)S(1)}, u32[]{:S(2)}, u32[]{:S(2)}) %collective-permute-start.14) | collective-permute-done | bytes 196640 | tf_op jit(solution)/shard_map/ppermute | solution.py:103
  382.9 4.8 %collective-permute-start.16 = (f32[128,384]{1,0:T(8,128)S(1)}, f32[128,384]{1,0:T(8,128)S(1)}, u32[]{:S(2)}, u32[]{:S(2)}) collective-permute-start(f32[128,384]{1,0:T(8,128)S(1)} %slice_select_fusion.2), channel_id=1, source_target_pairs={{0,2},{1,3},{2,0},{3,1},{4,6},{5,7},{6,4},{7,5},{8,10},{9,11},{10,... | collective-permute-start | bytes 589832 | tf_op jit(solution)/shard_map/ppermute | solution.py:135
  387.7 23.1 %reduce-scatter.4.cloned.1.call-done = bf16[384,512]{1,0:T(8,128)(2,1)} async-done(((bf16[3072,512]{1,0:T(8,128)(2,1)}), bf16[384,512]{1,0:T(8,128)(2,1)}) %reduce-scatter.4.cloned.1.call-update) | async-done | bytes 393232
  410.8 1.2 copy.127
  413.0 4.0 collective-permute-start.19
  417.0 1.0 collective-permute-done.19
  418.4 3.9 collective-permute-start.17
  422.2 11.9 %collective-permute-done.20 = f32[514,66]{0,1:T(8,128)S(1)} collective-permute-done((f32[514,66]{0,1:T(8,128)S(1)}, f32[514,66]{0,1:T(8,128)S(1)}, u32[]{:S(2)}, u32[]{:S(2)}) %collective-permute-start.20) | collective-permute-done | bytes 135728 | tf_op jit(solution)/shard_map/ppermute | solution.py:35
  434.2 1.7 collective-permute-start.21
  435.9 2.1 collective-permute-start.18
  438.0 11.1 %collective-permute-done.21 = f32[514,66]{0,1:T(8,128)S(1)} collective-permute-done((f32[514,66]{0,1:T(8,128)S(1)}, f32[514,66]{0,1:T(8,128)S(1)}, u32[]{:S(2)}, u32[]{:S(2)}) %collective-permute-start.21) | collective-permute-done | bytes 135728 | tf_op jit(solution)/shard_map/ppermute | solution.py:35
  449.7 1.9 collective-permute-start.22
  451.8 3.9 collective-permute-start.23
  456.7 2.8 collective-permute-done.23
  (236 shorter events, 27.2 us)
Async XLA Ops:
  7.2 373.3 %copy-start = (bf16[384,384]{1,0:T(8,128)(2,1)S(1)}, bf16[384,384]{1,0:T(8,128)(2,1)}, u32[]{:S(2)}) copy-start(bf16[384,384]{1,0:T(8,128)(2,1)} %param.23) | copy-start | bytes 884740
  7.2 17.4 %copy-start.6 = (bf16[512,384]{1,0:T(8,128)(2,1)S(1)}, bf16[512,384]{1,0:T(8,128)(2,1)}, u32[]{:S(2)}) copy-start(bf16[512,384]{1,0:T(8,128)(2,1)} %param.15) | copy-start | bytes 1179652
  7.2 22.4 %copy-start.21 = (bf16[3,3072]{1,0:T(4,128)(2,1)S(1)}, bf16[3,3072]{1,0:T(4,128)(2,1)}, u32[]{:S(2)}) copy-start(bf16[3,3072]{1,0:T(4,128)(2,1)} %param.17) | copy-start | bytes 55300
  7.2 22.4 %copy-start.23 = (bf16[3,3072]{1,0:T(4,128)(2,1)S(1)}, bf16[3,3072]{1,0:T(4,128)(2,1)}, u32[]{:S(2)}) copy-start(bf16[3,3072]{1,0:T(4,128)(2,1)} %param.18) | copy-start | bytes 55300
  7.2 22.6 %copy-start.9 = (bf16[384,3,384]{2,0,1:T(8,128)(2,1)S(1)}, bf16[384,3,384]{2,0,1:T(8,128)(2,1)}, u32[]{:S(2)}) copy-start(bf16[384,3,384]{2,0,1:T(8,128)(2,1)} %param.20) | copy-start | bytes 2654212
  7.2 194.5 %all-gather.3.cloned.1.call-start = ((), (), s32[]{:S(2)}) async-start(), calls=%async_computation.2 | async-start | bytes 7962624 | tf_op jit(solution)/shard_map/all_gather | solution.py:235
  7.3 9.6 %collective-permute-start = (bf16[1,64,384]{2,1,0:T(8,128)(2,1)}, bf16[1,64,384]{2,1,0:T(8,128)(2,1)S(1)}, u32[]{:S(2)}, u32[]{:S(2)}) collective-permute-start(bf16[1,64,384]{2,1,0:T(8,128)(2,1)} %bitcast.285), channel_id=1, source_target_pairs={{0,4},{1,5},{2,6},{3,7},{4,0},{5,1},{6,2},{7,3},{8,12},{9,13},{10,... | collective-permute-start | bytes 147464 | tf_op jit(solution)/shard_map/ppermute | solution.py:103
  17.7 6.8 %collective-permute-start.1 = (bf16[2,64,384]{2,1,0:T(8,128)(2,1)S(1)}, bf16[2,64,384]{2,1,0:T(8,128)(2,1)S(1)}, u32[]{:S(2)}, u32[]{:S(2)}) collective-permute-start(bf16[2,64,384]{2,1,0:T(8,128)(2,1)S(1)} %maximum_bitcast_fusion.2), channel_id=1, source_target_pairs={{0,2},{1,3},{2,0},{3,1},{4,6},{5,7},{6,4},{7,5},{8,10},{9,11},{10,... | collective-permute-start | bytes 294920 | tf_op jit(solution)/shard_map/ppermute | solution.py:103
  24.5 7.8 %collective-permute-start.2 = (bf16[4,64,384]{2,1,0:T(8,128)(2,1)S(1)}, bf16[4,64,384]{2,1,0:T(8,128)(2,1)S(1)}, u32[]{:S(2)}, u32[]{:S(2)}) collective-permute-start(bf16[4,64,384]{2,1,0:T(8,128)(2,1)S(1)} %bitcast.273), channel_id=1, source_target_pairs={{0,1},{1,0},{2,3},{3,2},{4,5},{5,4},{6,7},{7,6},{8,9},{9,8},{10,11... | collective-permute-start | bytes 589832 | tf_op jit(solution)/shard_map/ppermute | solution.py:103
  24.6 24.6 %collective-permute-start.6 = (bf16[1,512,384]{2,1,0:T(8,128)(2,1)S(1)}, bf16[1,512,384]{2,1,0:T(8,128)(2,1)S(1)}, u32[]{:S(2)}, u32[]{:S(2)}) collective-permute-start(bf16[1,512,384]{2,1,0:T(8,128)(2,1)S(1)} %bitcast.272), channel_id=1, source_target_pairs={{0,4},{1,5},{2,6},{3,7},{4,0},{5,1},{6,2},{7,3},{8,12},{9,13},{10,... | collective-permute-start | bytes 1179656 | tf_op jit(solution)/shard_map/ppermute | solution.py:103
  32.3 7.7 %copy-start.28 = (f32[4,128]{1,0:T(4,128)S(1)}, f32[4,128]{1,0:T(4,128)}, u32[]{:S(2)}) copy-start(f32[4,128]{1,0:T(4,128)} %param.21) | copy-start | bytes 6148
  34.0 45.1 %all-to-all-start = ((bf16[64,8,384]{2,0,1:T(8,128)(2,1)}), bf16[64,8,384]{2,0,1:T(8,128)(2,1)S(1)}, u32[]{:S(2)}, u32[]{:S(2)}) async-start(bf16[64,8,384]{2,0,1:T(8,128)(2,1)} %fusion.18), calls=%async_computation | async-start | bytes 786432 | tf_op jit(solution)/shard_map/all_to_all | solution.py:236
  40.0 284.3 %all-gather.5.cloned.1.call-start = ((), (), s32[]{:S(2)}) async-start(), calls=%async_computation.3 | async-start | bytes 7962624 | tf_op jit(solution)/shard_map/all_gather | solution.py:255
  49.4 49.4 %collective-permute-start.7 = (bf16[2,512,384]{2,1,0:T(8,128)(2,1)S(1)}, bf16[2,512,384]{2,1,0:T(8,128)(2,1)}, u32[]{:S(2)}, u32[]{:S(2)}) collective-permute-start(bf16[2,512,384]{2,1,0:T(8,128)(2,1)S(1)} %maximum_bitcast_fusion), channel_id=1, source_target_pairs={{0,2},{1,3},{2,0},{3,1},{4,6},{5,7},{6,4},{7,5},{8,10},{9,11},{10,... | collective-permute-start | bytes 2359304 | tf_op jit(solution)/shard_map/ppermute | solution.py:103
  80.2 67.3 %collective-permute-start.3 = (f32[256,1152]{1,0:T(8,128)S(1)}, f32[256,1152]{1,0:T(8,128)S(1)}, u32[]{:S(2)}, u32[]{:S(2)}) collective-permute-start(f32[256,1152]{1,0:T(8,128)S(1)} %broadcast_select_fusion), channel_id=1, source_target_pairs={{0,32},{8,40},{16,48},{24,56},{32,0},{40,8},{48,16},{56,24},{1,33}... | collective-permute-start | bytes 3538952 | tf_op jit(solution)/shard_map/ppermute | solution.py:135
  100.2 48.5 %collective-permute-start.8 = (bf16[4,512,384]{2,1,0:T(8,128)(2,1)S(1)}, bf16[4,512,384]{2,1,0:T(8,128)(2,1)S(1)}, u32[]{:S(2)}, u32[]{:S(2)}) collective-permute-start(bf16[4,512,384]{2,1,0:T(8,128)(2,1)S(1)} %bitcast.252), channel_id=1, source_target_pairs={{0,1},{1,0},{2,3},{3,2},{4,5},{5,4},{6,7},{7,6},{8,9},{9,8},{10,11... | collective-permute-start | bytes 4718600 | tf_op jit(solution)/shard_map/ppermute | solution.py:103
  147.6 1.6 copy-start.1
  148.6 38.1 %collective-permute-start.4 = (f32[128,1152]{1,0:T(8,128)}, f32[128,1152]{1,0:T(8,128)}, u32[]{:S(2)}, u32[]{:S(2)}) collective-permute-start(f32[128,1152]{1,0:T(8,128)} %slice_select_fusion), channel_id=1, source_target_pairs={{0,8},{8,0},{16,24},{24,16},{32,40},{40,32},{48,56},{56,48},{1,9},... | collective-permute-start | bytes 1769480 | tf_op jit(solution)/shard_map/ppermute | solution.py:135
  179.2 7.4 %copy-start.2 = (f32[256,1152]{1,0:T(8,128)S(1)}, f32[256,1152]{1,0:T(8,128)}, u32[]{:S(2)}) copy-start(f32[256,1152]{1,0:T(8,128)} %copy-done.1) | copy-start | bytes 3538948
  187.8 0.8 copy-start.3
  189.4 9.5 %collective-permute-start.5 = (f32[64,1152]{1,0:T(8,128)}, f32[64,1152]{1,0:T(8,128)}, u32[]{:S(2)}, u32[]{:S(2)}) collective-permute-start(f32[64,1152]{1,0:T(8,128)} %slice_select_fusion.1), channel_id=1, source_target_pairs={{0,16},{8,24},{16,0},{24,8},{32,48},{40,56},{48,32},{56,40},{1,17}... | collective-permute-start | bytes 884744 | tf_op jit(solution)/shard_map/ppermute | solution.py:135
  193.0 5.9 %copy-start.4 = (f32[128,1152]{1,0:T(8,128)S(1)}, f32[128,1152]{1,0:T(8,128)}, u32[]{:S(2)}) copy-start(f32[128,1152]{1,0:T(8,128)} %copy-done.3) | copy-start | bytes 1769476
  209.1 1.1 copy-start.18
  209.2 1.4 copy-start.17
  210.2 0.9 copy-start.11
  210.2 1.0 copy-start.12
  214.8 1.7 copy-start.14
  216.4 194.4 %reduce-scatter.4.cloned.1.call-start = ((), (), s32[]{:S(2)}) async-start(), calls=%async_computation.4 | async-start | bytes 3538944
  216.5 10.9 %collective-permute-start.9 = (bf16[1,384,384]{2,1,0:T(8,128)(2,1)S(1)}, bf16[1,384,384]{2,1,0:T(8,128)(2,1)S(1)}, u32[]{:S(2)}, u32[]{:S(2)}) collective-permute-start(bf16[1,384,384]{2,1,0:T(8,128)(2,1)S(1)} %bitcast.282), channel_id=1, source_target_pairs={{0,16},{8,24},{16,0},{24,8},{32,48},{40,56},{48,32},{56,40},{1,17}... | collective-permute-start | bytes 884744 | tf_op jit(solution)/shard_map/ppermute | solution.py:103
  227.5 22.4 %collective-permute-start.10 = (bf16[2,384,384]{2,1,0:T(8,128)(2,1)S(1)}, bf16[2,384,384]{2,1,0:T(8,128)(2,1)S(1)}, u32[]{:S(2)}, u32[]{:S(2)}) collective-permute-start(bf16[2,384,384]{2,1,0:T(8,128)(2,1)S(1)} %maximum_bitcast_fusion.1), channel_id=1, source_target_pairs={{0,8},{8,0},{16,24},{24,16},{32,40},{40,32},{48,56},{56,48},{1,9},... | collective-permute-start | bytes 1769480 | tf_op jit(solution)/shard_map/ppermute | solution.py:103
  251.1 48.5 %collective-permute-start.11 = (bf16[4,384,384]{1,2,0:T(8,128)(2,1)S(1)}, bf16[4,384,384]{1,2,0:T(8,128)(2,1)S(1)}, u32[]{:S(2)}, u32[]{:S(2)}) collective-permute-start(bf16[4,384,384]{1,2,0:T(8,128)(2,1)S(1)} %copy.117), channel_id=1, source_target_pairs={{0,32},{8,40},{16,48},{24,56},{32,0},{40,8},{48,16},{56,24},{1,33}... | collective-permute-start | bytes 3538952 | tf_op jit(solution)/shard_map/ppermute | solution.py:103
  300.1 0.8 copy-start.19
  300.1 0.9 copy-start.10
  300.1 1.8 copy-start.8
  300.5 1.4 copy-start.26
  356.2 12.6 %copy-start.25 = (bf16[2,3072]{1,0:T(2,128)(2,1)S(1)}, bf16[2,3072]{1,0:T(2,128)(2,1)}, u32[]{:S(2)}) copy-start(bf16[2,3072]{1,0:T(2,128)(2,1)} %param.24) | copy-start | bytes 36868
  357.0 5.6 %collective-permute-start.12 = (bf16[1,64,384]{2,1,0:T(8,128)(2,1)S(1)}, bf16[1,64,384]{2,1,0:T(8,128)(2,1)S(1)}, u32[]{:S(2)}, u32[]{:S(2)}) collective-permute-start(bf16[1,64,384]{2,1,0:T(8,128)(2,1)S(1)} %slice_bitcast_fusion), channel_id=1, source_target_pairs={{0,16},{8,24},{16,0},{24,8},{32,48},{40,56},{48,32},{56,40},{1,17}... | collective-permute-start | bytes 147464 | tf_op jit(solution)/shard_map/ppermute | solution.py:103
  363.5 4.7 %collective-permute-start.13 = (bf16[2,64,384]{2,1,0:T(8,128)(2,1)S(1)}, bf16[2,64,384]{2,1,0:T(8,128)(2,1)S(1)}, u32[]{:S(2)}, u32[]{:S(2)}) collective-permute-start(bf16[2,64,384]{2,1,0:T(8,128)(2,1)S(1)} %maximum_bitcast_fusion.3), channel_id=1, source_target_pairs={{0,8},{8,0},{16,24},{24,16},{32,40},{40,32},{48,56},{56,48},{1,9},... | collective-permute-start | bytes 294920 | tf_op jit(solution)/shard_map/ppermute | solution.py:103
  368.2 12.0 %collective-permute-start.14 = (bf16[4,64,384]{2,1,0:T(8,128)(2,1)S(1)}, bf16[4,64,384]{2,1,0:T(8,128)(2,1)S(1)}, u32[]{:S(2)}, u32[]{:S(2)}) collective-permute-start(bf16[4,64,384]{2,1,0:T(8,128)(2,1)S(1)} %bitcast.274), channel_id=1, source_target_pairs={{0,32},{8,40},{16,48},{24,56},{32,0},{40,8},{48,16},{56,24},{1,33}... | collective-permute-start | bytes 589832 | tf_op jit(solution)/shard_map/ppermute | solution.py:103
  380.4 0.8 copy-start.13
  380.4 0.9 copy-start.22
  380.4 1.0 copy-start.24
  381.0 31.1 %copy-start.7 = (bf16[512,384]{1,0:T(8,128)(2,1)S(1)}, bf16[512,384]{1,0:T(8,128)(2,1)}, u32[]{:S(2)}) copy-start(bf16[512,384]{1,0:T(8,128)(2,1)} %param.15) | copy-start | bytes 1179652
  381.0 1.8 collective-permute-start.15
  382.9 34.0 %collective-permute-start.16 = (f32[128,384]{1,0:T(8,128)S(1)}, f32[128,384]{1,0:T(8,128)S(1)}, u32[]{:S(2)}, u32[]{:S(2)}) collective-permute-start(f32[128,384]{1,0:T(8,128)S(1)} %slice_select_fusion.2), channel_id=1, source_target_pairs={{0,2},{1,3},{2,0},{3,1},{4,6},{5,7},{6,4},{7,5},{8,10},{9,11},{10,... | collective-permute-start | bytes 589832 | tf_op jit(solution)/shard_map/ppermute | solution.py:135
  412.4 44.1 %copy-start.5 = (bf16[512,384]{1,0:T(8,128)(2,1)}, bf16[512,384]{1,0:T(8,128)(2,1)S(1)}, u32[]{:S(2)}) copy-start(bf16[512,384]{1,0:T(8,128)(2,1)S(1)} %get-tuple-element.19) | copy-start | bytes 1179652
  412.4 43.4 %copy-start.15 = (bf16[64,384]{1,0:T(8,128)(2,1)S(1)}, bf16[64,384]{1,0:T(8,128)(2,1)}, u32[]{:S(2)}) copy-start(bf16[64,384]{1,0:T(8,128)(2,1)} %param.16) | copy-start | bytes 147460
  413.0 46.8 %copy-start.16 = (bf16[3,3,64,64]{3,2,1,0:T(8,128)(2,1)S(1)}, bf16[3,3,64,64]{3,2,1,0:T(8,128)(2,1)}, u32[]{:S(2)}) copy-start(bf16[3,3,64,64]{3,2,1,0:T(8,128)(2,1)} %param.26) | copy-start | bytes 221188
  413.0 5.0 %collective-permute-start.19 = (f32[514,66]{0,1:T(8,128)S(1)}, f32[514,66]{0,1:T(8,128)S(1)}, u32[]{:S(2)}, u32[]{:S(2)}) collective-permute-start(f32[514,66]{0,1:T(8,128)S(1)} %select_maximum_fusion), channel_id=1, source_target_pairs={{0,1},{1,0},{2,3},{3,2},{4,5},{5,4},{6,7},{7,6},{8,9},{9,8},{10,11... | collective-permute-start | bytes 407096 | tf_op jit(solution)/shard_map/ppermute | solution.py:35
  417.0 44.0 %copy-start.27 = (f32[8,512]{1,0:T(8,128)S(1)}, f32[8,512]{1,0:T(8,128)}, u32[]{:S(2)}) copy-start(f32[8,512]{1,0:T(8,128)} %param.27) | copy-start | bytes 49156
  418.1 16.1 %collective-permute-start.20 = (f32[514,66]{0,1:T(8,128)S(1)}, f32[514,66]{0,1:T(8,128)S(1)}, u32[]{:S(2)}, u32[]{:S(2)}) collective-permute-start(f32[514,66]{0,1:T(8,128)S(1)} %fusion.89), channel_id=1, source_target_pairs={{0,2},{1,3},{2,0},{3,1},{4,6},{5,7},{6,4},{7,5},{8,10},{9,11},{10,... | collective-permute-start | bytes 407096 | tf_op jit(solution)/shard_map/ppermute | solution.py:35
  418.4 17.5 %collective-permute-start.17 = (f32[64,384]{1,0:T(8,128)S(1)}, f32[64,384]{1,0:T(8,128)S(1)}, u32[]{:S(2)}, u32[]{:S(2)}) collective-permute-start(f32[64,384]{1,0:T(8,128)S(1)} %slice_select_fusion.3), channel_id=1, source_target_pairs={{0,4},{1,5},{2,6},{3,7},{4,0},{5,1},{6,2},{7,3},{8,12},{9,13},{10,... | collective-permute-start | bytes 294920 | tf_op jit(solution)/shard_map/ppermute | solution.py:135
  434.2 15.0 %collective-permute-start.21 = (f32[514,66]{0,1:T(8,128)S(1)}, f32[514,66]{0,1:T(8,128)S(1)}, u32[]{:S(2)}, u32[]{:S(2)}) collective-permute-start(f32[514,66]{0,1:T(8,128)S(1)} %add.354), channel_id=1, source_target_pairs={{0,4},{1,5},{2,6},{3,7},{4,0},{5,1},{6,2},{7,3},{8,12},{9,13},{10,... | collective-permute-start | bytes 407096 | tf_op jit(solution)/shard_map/ppermute | solution.py:35
  435.9 19.9 %collective-permute-start.18 = (f32[64,384]{1,0:T(8,128)S(1)}, f32[64,384]{1,0:T(8,128)S(1)}, u32[]{:S(2)}, u32[]{:S(2)}) collective-permute-start(f32[64,384]{1,0:T(8,128)S(1)} %select_add_fusion.5), channel_id=1, source_target_pairs={{0,0},{1,8},{2,16},{3,24},{4,32},{5,40},{6,48},{7,56},{8,1},{9,9},... | collective-permute-start | bytes 294920 | tf_op jit(solution)/shard_map/ppermute | solution.py:142
  449.7 6.9 %collective-permute-start.22 = (bf16[1,4096]{1,0:T(2,128)(2,1)S(1)}, bf16[1,4096]{1,0:T(2,128)(2,1)S(1)}, u32[]{:S(2)}, u32[]{:S(2)}) collective-permute-start(bf16[1,4096]{1,0:T(2,128)(2,1)S(1)} %slice.425), channel_id=1, source_target_pairs={{0,8},{8,16},{16,24},{24,32},{32,40},{40,48},{48,56},{1,9},{9,17},... | collective-permute-start | bytes 24584 | tf_op jit(solution)/shard_map/ppermute | solution.py:23
  451.8 7.7 %collective-permute-start.23 = (bf16[1,4096]{1,0:T(2,128)(2,1)S(1)}, bf16[1,4096]{1,0:T(2,128)(2,1)S(1)}, u32[]{:S(2)}, u32[]{:S(2)}) collective-permute-start(bf16[1,4096]{1,0:T(2,128)(2,1)S(1)} %slice.427), channel_id=1, source_target_pairs={{8,0},{16,8},{24,16},{32,24},{40,32},{48,40},{56,48},{9,1},{17,9},... | collective-permute-start | bytes 24584 | tf_op jit(solution)/shard_map/ppermute | solution.py:26
  461.0 0.6 copy-start.20
Sparse Core Ops, SparseCore 0:
  22.7 144.2 all-gather.2
  216.5 107.6 all-gather.4
  356.4 54.4 reduce-scatter.3

commit v5 on v4

--- a/solution.py
+++ b/solution.py
@@ -224,17 +224,21 @@
     img_rows = img_hidden.shape[0]
     txt_rows = txt_hidden.shape[0]
     local_width = img_hidden.shape[1]
-    tp_order = (4, 2, 1)
-    seq_order = (2, 1, 4)
-    img_full = doubling_gather(img_hidden, "tp", 1, tp_order)
-    txt_full = doubling_gather(txt_hidden, "tp", 1, tp_order)
-    img_out_full = doubling_gather(img_out_w, "seq", 1, seq_order)
+    img_full, txt_full = (
+        lax.all_gather(img_hidden, "tp", axis=1, tiled=True),
+        lax.all_gather(txt_hidden, "tp", axis=1, tiled=True),
+    )
     full_width = img_full.shape[1]
     img_norm = modulate(img_full, img_mod)
     txt_norm = modulate(txt_full, txt_mod)
-    img_mixed = add_rows(img_norm, lax.all_gather(img_qkv, "seq", axis=0, tiled=True))
+    img_weights = lax.all_gather(img_qkv, "seq", axis=0, tiled=True)
+    img_weights, img_out_w = lax.optimization_barrier((img_weights, img_out_w))
+    img_out_full = lax.all_gather(img_out_w, "seq", axis=1, tiled=True)
+    img_mixed = add_rows(img_norm, img_weights)
     txt_norm_rows = lax.all_to_all(txt_norm, "seq", 1, 0, tiled=True)
-    txt_mixed = halving_scatter(add_rows(txt_norm_rows, txt_qkv), "seq", 0, (4, 1, 2))
+    txt_mixed = lax.psum_scatter(
+        add_rows(txt_norm_rows, txt_qkv), "seq", scatter_dimension=0, tiled=True
+    )
     head_dim = qk_gains.shape[1]
     grid_side = latent.shape[0] * seq_count
     token_ids = seq_at * img_rows + jnp.arange(img_rows, dtype=jnp.int32)
@@ -277,7 +281,7 @@
         preferred_element_type=jnp.float32,
     )
     txt_term = jnp.dot(
-        doubling_gather(txt_attn, "seq", 0, seq_order),
+        doubling_gather(txt_attn, "seq", 0, (2, 1, 4)),
         txt_out_w,
         preferred_element_type=jnp.float32,
     )

time: 477 us -> 437 us (0.916); the launches traced: 468 us -> 436 us
  starting transfers between devices: 68.3 us -> 30.8 us
  waiting for transfers between devices: 255 us -> 290 us
  local copies, waits for them, and re-layouts: 59.5 us -> 25.8 us
  blocking collectives: 0 us -> 18.8 us
  other arithmetic: 36.2 us -> 19.4 us
    ppermute x12 -> x3, waiting for transfers between devices: 124 us -> 18.4 us  [doubling_gather(): other = lax.ppermute(stacked, axis, [(i, i ^ step) for i in range(count)])]
    all_gather x1 -> x3, waiting for transfers between devices: 0.02 us -> 80.9 us  [the longest x1 60.3 us: per_device(): img_weights = lax.all_gather(img_qkv, 'seq', axis=0, tiled=True)]
    reduce_scatter x0 -> x1, waiting for transfers between devices: none -> 57.4 us  [per_device(): lax.psum_scatter(add_rows(txt_norm_rows, txt_qkv), 'seq', scatter_dimensi...]
    all_gather x1, waiting for transfers between devices: 20.3 us -> 76.6 us  [per_device(): lax.all_gather(jnp.concatenate([keys_local, values_local], 1), 'seq', axi...]
    ppermute x6 -> x3, waiting for transfers between devices: 46.2 us -> 0.01 us  [halving_scatter(): lax.ppermute(sent, axis, [(i, i ^ step) for i in range(count)])]
    ppermute x12 -> x3, starting transfers between devices: 39.1 us -> 4.2 us  [doubling_gather(): other = lax.ppermute(stacked, axis, [(i, i ^ step) for i in range(count)])]
    all_gather x0 -> x1, blocking collectives: none -> 18.8 us  [per_device(): lax.all_gather(txt_hidden, 'tp', axis=1, tiled=True)]
    another operation x4 -> x1, local copies, waits for them, and re-layouts: 16 us -> 0.01 us  [doubling_gather(): picked = jnp.stack([stacked[p] for p in place], 0)]
  transfers between devices with their start and end apart: 28 -> 19, of which waited for: 19 -> 13; matrix products, arithmetic and copies ran while one was open for 16% -> 7% of each run, Pallas kernels for 0% -> 4%
where the time goes in v5:
time: 437 us; the launch traced here: 436 us
  waiting for transfers between devices  290 us (66%)
  starting transfers between devices  30.8 us (7%)
  local copies, waits for them, and re-layouts  25.8 us (6%)
  other arithmetic  19.4 us (4%)
  blocking collectives  18.8 us (4%)
  Pallas kernels  18.7 us (4%)
  between operations  17.7 us (4%)
  matrix products  14.6 us (3%)
    all_gather x1, waiting for transfers between devices, per_device(): lax.all_gather(jnp.concatenate([keys_local, values_local], 1), 'seq', axi...  76.6 us
    all_gather x1, waiting for transfers between devices, per_device(): img_weights = lax.all_gather(img_qkv, 'seq', axis=0, tiled=True)  60.3 us
    reduce_scatter x1, waiting for transfers between devices, per_device(): lax.psum_scatter(add_rows(txt_norm_rows, txt_qkv), 'seq', scatter_dimensi...  57.4 us
    unnamed x7, waiting for transfers between devices  27.9 us
    ppermute x3, waiting for transfers between devices, tree_sum(): lax.ppermute(block, axis, [(i, i ^ step) for i in range(count)])  21.5 us
    all_gather x1, waiting for transfers between devices, per_device(): img_out_full = lax.all_gather(img_out_w, 'seq', axis=1, tiled=True)  20.5 us
    all_gather x1, blocking collectives, per_device(): lax.all_gather(txt_hidden, 'tp', axis=1, tiled=True)  18.8 us
    pallas_call x1, Pallas kernels, attention(): pl.pallas_call(functools.partial(attend_block, scale=head_dim ** (-0.5)),...  18.7 us
  transfers between devices with their start and end apart: 19, of which 13 were waited for; matrix products, arithmetic and copies ran while one was open for 7% of the time, Pallas kernels for 4%

profile of v5, /device:TPU:26, one launch (start us, length us, event | category | flops | bytes accessed | tf_op | source)
XLA Modules:
  0.0 435.5 jit_solution(2923945732717388132)
XLA Ops:
  8.0 0.9 fusion.94
  8.9 0.7 convert_element_type.121
  9.6 18.8 %all_gather.15 = bf16[64,3072]{1,0:T(8,128)(2,1)S(1)} all-gather(bf16[64,384]{1,0:T(8,128)(2,1)} %param.16), channel_id=1, replica_groups=mesh['req'=4,'seq'=8,'tp'=8] {'tp'}, dimensions={1}, use_global_device_ids=true | all-gather | bytes 442368 | tf_op jit(solution)/shard_map/all_gather | solution.py:229
  29.1 0.8 copy.104
  29.9 5.2 %all-to-all-start = ((bf16[64,8,384]{2,0,1:T(8,128)(2,1)}), bf16[64,8,384]{2,0,1:T(8,128)(2,1)S(1)}, u32[]{:S(2)}, u32[]{:S(2)}) async-start(bf16[64,8,384]{2,0,1:T(8,128)(2,1)} %bitcast.169), calls=%async_computation | async-start | bytes 786432 | tf_op jit(solution)/shard_map/all_to_all | solution.py:238
  35.1 2.4 copy.73
  37.5 4.2 all-to-all-done
  41.7 2.2 fusion.97
  44.0 0.5 all-gather.5.cloned.1.call-update
  44.6 2.2 copy.76
  47.1 0.7 mul.373
  47.8 0.8 mul.400
  48.7 1.2 fusion.29
  49.9 0.6 fusion.95
  50.5 0.6 slice_add_fusion
  51.1 57.4 %reduce-scatter.5.cloned.1.call-done = f32[64,1152]{1,0:T(8,128)} async-done(((f32[512,1152]{1,0:T(8,128)}), f32[64,1152]{1,0:T(8,128)}) %reduce-scatter.5.cloned.1.call-update) | async-done | bytes 294928 | tf_op jit(solution)/shard_map/reduce_scatter | solution.py:239
  108.6 1.1 reshape.336
  109.7 0.8 multiply_reduce_fusion.2
  110.5 0.6 add_rsqrt_fusion
  111.3 2.5 convert_reduce_fusion
  113.8 0.6 copy-done.19
  114.4 1.0 fusion.2
  115.4 0.6 add_rsqrt_fusion.5
  116.0 60.3 %all-gather.7.cloned.1.call-done = bf16[3072,3,384]{0,2,1:T(8,128)(2,1)} async-done(((bf16[384,3,384]{0,2,1:T(8,128)(2,1)}), bf16[3072,3,384]{0,2,1:T(8,128)(2,1)}) %all-gather.7.cloned.1.call-update) | async-done | bytes 7077904 | tf_op jit(solution)/shard_map/all_gather | solution.py:234
  176.3 6.4 %fusion.7 = f32[512,3,3,128]{0,3,2,1:T(8,128)S(1)} fusion(bf16[3,3,128,3072]{3,2,1,0:T(8,128)(2,1)} %bitcast.205, bf16[512,3072]{1,0:T(8,128)(2,1)S(1)} %copy-done.1, f32[3072]{0:T(1024)} %bitcast.202, f32[3072]{0:T(1024)} %bitcast.201, f32[512]{0:T(512)} %add_rsqrt_fusion.5, f32[512]{0:T(512)} %copy-done.19), kind=kOutput, calls=%fused_computation.10 | convolution fusion | flops 3633315840 | bytes 12611584 | tf_op jit(solution)/shard_map/dot_general | solution.py:201
  184.8 2.1 subtract_convert_fusion
  186.9 0.9 pad_maximum_fusion.2
  188.4 1.0 maximum_maximum_fusion
  189.5 0.7 all-gather.11.cloned.1.call-update
  191.1 0.7 or_convert_fusion.keep_ref
  191.9 0.9 pad_maximum_fusion.1
  193.2 0.8 pad_maximum_fusion.query_ref
  194.0 76.6 %all-gather.9.cloned.1.call-done = bf16[4608,768]{1,0:T(8,128)(2,1)} async-done(((bf16[576,768]{1,0:T(8,128)(2,1)}), bf16[4608,768]{1,0:T(8,128)(2,1)}) %all-gather.9.cloned.1.call-update) | async-done | bytes 7077904 | tf_op jit(solution)/shard_map/all_gather | solution.py:259
  270.6 6.7 %fusion.91 = (bf16[4608,384]{1,0:T(8,128)(2,1)}, bf16[4608,384]{1,0:T(8,128)(2,1)}) fusion(bf16[4608,768]{1,0:T(8,128)(2,1)} %all-gather.9.cloned.1.call-done), kind=kLoop, calls=%fused_computation.203 | loop fusion | bytes 14155776 | tf_op jit(solution)/shard_map/slice | solution.py:263
  277.3 18.7 %shard_map.182 = bf16[576,384]{1,0:T(8,128)(2,1)} custom-call(f32[1,4608]{1,0:T(1,128)} %or_convert_fusion.keep_ref, bf16[576,384]{1,0:T(8,128)(2,1)} %pad_maximum_fusion.query_ref, bf16[4608,384]{1,0:T(8,128)(2,1)} %get-tuple-element.21.key_ref, bf16[4608,384]{1,0:T(8,128)(2,1)} %get-tuple-element.20.value_ref), custom_call_target="tpu_custom_call" | custom-call | tf_op jit(solution)/shard_map/pallas_call | solution.py:80
  296.0 20.5 %all-gather.11.cloned.1.call-done = bf16[384,3072]{1,0:T(8,128)(2,1)} async-done(((bf16[384,384]{1,0:T(8,128)(2,1)}), bf16[384,3072]{1,0:T(8,128)(2,1)}) %all-gather.11.cloned.1.call-update) | async-done | bytes 2359312 | tf_op jit(solution)/shard_map/all_gather | solution.py:236
  316.6 3.6 convolution_convert_fusion
  320.2 2.8 copy.88
  323.0 0.8 slice_bitcast_fusion
  323.8 1.5 collective-permute-start
  325.4 4.5 %collective-permute-done = bf16[1,64,384]{2,1,0:T(8,128)(2,1)S(1)} collective-permute-done((bf16[1,64,384]{2,1,0:T(8,128)(2,1)S(1)}, bf16[1,64,384]{2,1,0:T(8,128)(2,1)S(1)}, u32[]{:S(2)}, u32[]{:S(2)}) %collective-permute-start) | collective-permute-done | bytes 49184 | tf_op jit(solution)/shard_map/ppermute | solution.py:103
  329.8 0.8 select_bitcast_fusion.5
  330.7 1.2 collective-permute-start.1
  331.9 3.5 collective-permute-done.1
  335.5 1.5 collective-permute-start.2
  337.0 10.4 %collective-permute-done.2 = bf16[4,64,384]{2,1,0:T(8,128)(2,1)S(1)} collective-permute-done((bf16[4,64,384]{2,1,0:T(8,128)(2,1)S(1)}, bf16[4,64,384]{2,1,0:T(8,128)(2,1)S(1)}, u32[]{:S(2)}, u32[]{:S(2)}) %collective-permute-start.2) | collective-permute-done | bytes 196640 | tf_op jit(solution)/shard_map/ppermute | solution.py:103
  349.5 0.7 fusion.78
  350.4 2.7 collective-permute-start.4
  353.0 26.7 %reduce-scatter.7.cloned.1.call-done = bf16[384,512]{1,0:T(8,128)(2,1)} async-done(((bf16[3072,512]{1,0:T(8,128)(2,1)}), bf16[384,512]{1,0:T(8,128)(2,1)}) %reduce-scatter.7.cloned.1.call-update) | async-done | bytes 393232
  379.7 1.2 copy.89
  381.3 0.6 fusion.20
  381.9 1.1 collective-permute-start.7
  383.1 1.0 collective-permute-done.7
  384.1 2.2 collective-permute-start.8
  386.3 3.0 collective-permute-start.5
  389.3 10.9 %collective-permute-done.8 = f32[514,66]{0,1:T(8,128)S(1)} collective-permute-done((f32[514,66]{0,1:T(8,128)S(1)}, f32[514,66]{0,1:T(8,128)S(1)}, u32[]{:S(2)}, u32[]{:S(2)}) %collective-permute-start.8) | collective-permute-done | bytes 135728 | tf_op jit(solution)/shard_map/ppermute | solution.py:35
  400.2 3.9 collective-permute-start.9
  404.1 1.9 collective-permute-start.6
  406.1 9.6 %collective-permute-done.9 = f32[514,66]{0,1:T(8,128)S(1)} collective-permute-done((f32[514,66]{0,1:T(8,128)S(1)}, f32[514,66]{0,1:T(8,128)S(1)}, u32[]{:S(2)}, u32[]{:S(2)}) %collective-permute-start.9) | collective-permute-done | bytes 135728 | tf_op jit(solution)/shard_map/ppermute | solution.py:35
  416.3 1.9 collective-permute-start.10
  418.4 3.9 collective-permute-start.11
  422.3 0.7 fusion.30
  423.3 2.8 collective-permute-done.11
  427.6 0.6 multiply_subtract_fusion
  (148 shorter events, 9.1 us)
Async XLA Ops:
  8.0 339.7 %copy-start = (bf16[384,384]{1,0:T(8,128)(2,1)S(1)}, bf16[384,384]{1,0:T(8,128)(2,1)}, u32[]{:S(2)}) copy-start(bf16[384,384]{1,0:T(8,128)(2,1)} %param.23) | copy-start | bytes 884740
  8.0 27.1 %copy-start.4 = (bf16[384,3,384]{2,0,1:T(8,128)(2,1)S(1)}, bf16[384,3,384]{2,0,1:T(8,128)(2,1)}, u32[]{:S(2)}) copy-start(bf16[384,3,384]{2,0,1:T(8,128)(2,1)} %param.20) | copy-start | bytes 2654212
  29.9 11.8 %all-to-all-start = ((bf16[64,8,384]{2,0,1:T(8,128)(2,1)}), bf16[64,8,384]{2,0,1:T(8,128)(2,1)S(1)}, u32[]{:S(2)}, u32[]{:S(2)}) async-start(bf16[64,8,384]{2,0,1:T(8,128)(2,1)} %bitcast.169), calls=%async_computation | async-start | bytes 786432 | tf_op jit(solution)/shard_map/all_to_all | solution.py:238
  35.1 73.5 %reduce-scatter.5.cloned.1.call-start = ((), (), s32[]{:S(2)}) async-start(), calls=%async_computation.3 | async-start | bytes 2654208 | tf_op jit(solution)/shard_map/reduce_scatter | solution.py:239
  41.7 2.9 copy-start.5
  43.9 3.1 copy-start.15
  43.9 3.1 copy-start.20
  43.9 67.4 %all-gather.5.cloned.1.call-start = ((), (), s32[]{:S(2)}) async-start(), calls=%async_computation.4 | async-start | bytes 3538944 | tf_op jit(solution)/shard_map/all_gather | solution.py:228
  44.5 131.8 %all-gather.7.cloned.1.call-start = ((), (), s32[]{:S(2)}) async-start(), calls=%async_computation.5 | async-start | bytes 7962624 | tf_op jit(solution)/shard_map/all_gather | solution.py:234
  46.8 223.8 %all-gather.9.cloned.1.call-start = ((), (), s32[]{:S(2)}) async-start(), calls=%async_computation.6 | async-start | bytes 7962624 | tf_op jit(solution)/shard_map/all_gather | solution.py:259
  111.3 3.1 copy-start.1
  113.8 0.6 copy-start.19
  182.7 1.3 copy-start.13
  183.0 1.4 copy-start.12
  183.1 1.7 copy-start.7
  183.1 1.7 copy-start.8
  186.9 4.9 %copy-start.14 = (f32[64,3]{1,0:T(8,128)S(1)}, f32[64,3]{1,0:T(8,128)}, u32[]{:S(2)}) copy-start(f32[64,3]{1,0:T(8,128)} %get-tuple-element.73) | copy-start | bytes 2308
  186.9 5.0 %copy-start.6 = (f32[64,1,3,128]{3,2,1,0:T(4,128)S(1)}, f32[64,1,3,128]{3,2,1,0:T(4,128)}, u32[]{:S(2)}) copy-start(f32[64,1,3,128]{3,2,1,0:T(4,128)} %get-tuple-element.41) | copy-start | bytes 294916
  189.4 127.2 %all-gather.11.cloned.1.call-start = ((), (), s32[]{:S(2)}) async-start(), calls=%async_computation.7 | async-start | bytes 2654208 | tf_op jit(solution)/shard_map/all_gather | solution.py:236
  190.2 189.5 %reduce-scatter.7.cloned.1.call-start = ((), (), s32[]{:S(2)}) async-start(), calls=%async_computation.8 | async-start | bytes 3538944
  323.0 13.9 %copy-start.17 = (bf16[2,3072]{1,0:T(2,128)(2,1)S(1)}, bf16[2,3072]{1,0:T(2,128)(2,1)}, u32[]{:S(2)}) copy-start(bf16[2,3072]{1,0:T(2,128)(2,1)} %param.24) | copy-start | bytes 36868
  323.8 6.0 %collective-permute-start = (bf16[1,64,384]{2,1,0:T(8,128)(2,1)S(1)}, bf16[1,64,384]{2,1,0:T(8,128)(2,1)S(1)}, u32[]{:S(2)}, u32[]{:S(2)}) collective-permute-start(bf16[1,64,384]{2,1,0:T(8,128)(2,1)S(1)} %slice_bitcast_fusion), channel_id=1, source_target_pairs={{0,16},{8,24},{16,0},{24,8},{32,48},{40,56},{48,32},{56,40},{1,17}... | collective-permute-start | bytes 147464 | tf_op jit(solution)/shard_map/ppermute | solution.py:103
  330.7 4.7 %collective-permute-start.1 = (bf16[2,64,384]{2,1,0:T(8,128)(2,1)S(1)}, bf16[2,64,384]{2,1,0:T(8,128)(2,1)S(1)}, u32[]{:S(2)}, u32[]{:S(2)}) collective-permute-start(bf16[2,64,384]{2,1,0:T(8,128)(2,1)S(1)} %maximum_bitcast_fusion), channel_id=1, source_target_pairs={{0,8},{8,0},{16,24},{24,16},{32,40},{40,32},{48,56},{56,48},{1,9},... | collective-permute-start | bytes 294920 | tf_op jit(solution)/shard_map/ppermute | solution.py:103
  335.5 12.0 %collective-permute-start.2 = (bf16[4,64,384]{2,1,0:T(8,128)(2,1)S(1)}, bf16[4,64,384]{2,1,0:T(8,128)(2,1)S(1)}, u32[]{:S(2)}, u32[]{:S(2)}) collective-permute-start(bf16[4,64,384]{2,1,0:T(8,128)(2,1)S(1)} %bitcast.185), channel_id=1, source_target_pairs={{0,32},{8,40},{16,48},{24,56},{32,0},{40,8},{48,16},{56,24},{1,33}... | collective-permute-start | bytes 589832 | tf_op jit(solution)/shard_map/ppermute | solution.py:103
  337.0 11.3 %copy-start.9 = (bf16[384,64]{0,1:T(8,128)(2,1)S(1)}, bf16[384,64]{0,1:T(8,128)(2,1)}, u32[]{:S(2)}) copy-start(bf16[384,64]{0,1:T(8,128)(2,1)} %param.25) | copy-start | bytes 147460
  348.1 32.8 %copy-start.2 = (bf16[512,384]{1,0:T(8,128)(2,1)S(1)}, bf16[512,384]{1,0:T(8,128)(2,1)}, u32[]{:S(2)}) copy-start(bf16[512,384]{1,0:T(8,128)(2,1)} %param.15) | copy-start | bytes 1179652
  348.2 2.0 collective-permute-start.3
  350.4 32.7 %collective-permute-start.4 = (f32[128,384]{1,0:T(8,128)S(1)}, f32[128,384]{1,0:T(8,128)S(1)}, u32[]{:S(2)}, u32[]{:S(2)}) collective-permute-start(f32[128,384]{1,0:T(8,128)S(1)} %slice_select_fusion), channel_id=1, source_target_pairs={{0,2},{1,3},{2,0},{3,1},{4,6},{5,7},{6,4},{7,5},{8,10},{9,11},{10,... | collective-permute-start | bytes 589832 | tf_op jit(solution)/shard_map/ppermute | solution.py:135
  379.7 42.6 %copy-start.10 = (bf16[64,384]{1,0:T(8,128)(2,1)S(1)}, bf16[64,384]{1,0:T(8,128)(2,1)}, u32[]{:S(2)}) copy-start(bf16[64,384]{1,0:T(8,128)(2,1)} %param.16) | copy-start | bytes 147460
  380.9 45.4 %copy-start.11 = (bf16[3,3,64,64]{3,2,1,0:T(8,128)(2,1)S(1)}, bf16[3,3,64,64]{3,2,1,0:T(8,128)(2,1)}, u32[]{:S(2)}) copy-start(bf16[3,3,64,64]{3,2,1,0:T(8,128)(2,1)} %param.26) | copy-start | bytes 221188
  381.2 47.0 %copy-start.3 = (bf16[512,384]{1,0:T(8,128)(2,1)}, bf16[512,384]{1,0:T(8,128)(2,1)S(1)}, u32[]{:S(2)}) copy-start(bf16[512,384]{1,0:T(8,128)(2,1)S(1)} %get-tuple-element.19) | copy-start | bytes 1179652
  381.3 46.3 %copy-start.18 = (f32[8,512]{1,0:T(8,128)S(1)}, f32[8,512]{1,0:T(8,128)}, u32[]{:S(2)}) copy-start(f32[8,512]{1,0:T(8,128)} %param.27) | copy-start | bytes 49156
  381.9 2.2 collective-permute-start.7
  384.1 16.1 %collective-permute-start.8 = (f32[514,66]{0,1:T(8,128)S(1)}, f32[514,66]{0,1:T(8,128)S(1)}, u32[]{:S(2)}, u32[]{:S(2)}) collective-permute-start(f32[514,66]{0,1:T(8,128)S(1)} %fusion.90), channel_id=1, source_target_pairs={{0,2},{1,3},{2,0},{3,1},{4,6},{5,7},{6,4},{7,5},{8,10},{9,11},{10,... | collective-permute-start | bytes 407096 | tf_op jit(solution)/shard_map/ppermute | solution.py:35
  386.3 17.8 %collective-permute-start.5 = (f32[64,384]{1,0:T(8,128)S(1)}, f32[64,384]{1,0:T(8,128)S(1)}, u32[]{:S(2)}, u32[]{:S(2)}) collective-permute-start(f32[64,384]{1,0:T(8,128)S(1)} %slice_select_fusion.1), channel_id=1, source_target_pairs={{0,4},{1,5},{2,6},{3,7},{4,0},{5,1},{6,2},{7,3},{8,12},{9,13},{10,... | collective-permute-start | bytes 294920 | tf_op jit(solution)/shard_map/ppermute | solution.py:135
  400.2 15.5 %collective-permute-start.9 = (f32[514,66]{0,1:T(8,128)S(1)}, f32[514,66]{0,1:T(8,128)S(1)}, u32[]{:S(2)}, u32[]{:S(2)}) collective-permute-start(f32[514,66]{0,1:T(8,128)S(1)} %add.330), channel_id=1, source_target_pairs={{0,4},{1,5},{2,6},{3,7},{4,0},{5,1},{6,2},{7,3},{8,12},{9,13},{10,... | collective-permute-start | bytes 407096 | tf_op jit(solution)/shard_map/ppermute | solution.py:35
  404.1 18.2 %collective-permute-start.6 = (f32[64,384]{1,0:T(8,128)S(1)}, f32[64,384]{1,0:T(8,128)S(1)}, u32[]{:S(2)}, u32[]{:S(2)}) collective-permute-start(f32[64,384]{1,0:T(8,128)S(1)} %select_add_fusion.2), channel_id=1, source_target_pairs={{0,0},{1,8},{2,16},{3,24},{4,32},{5,40},{6,48},{7,56},{8,1},{9,9},... | collective-permute-start | bytes 294920 | tf_op jit(solution)/shard_map/ppermute | solution.py:142
  416.3 6.9 %collective-permute-start.10 = (bf16[1,4096]{1,0:T(2,128)(2,1)S(1)}, bf16[1,4096]{1,0:T(2,128)(2,1)S(1)}, u32[]{:S(2)}, u32[]{:S(2)}) collective-permute-start(bf16[1,4096]{1,0:T(2,128)(2,1)S(1)} %slice.275), channel_id=1, source_target_pairs={{0,8},{8,16},{16,24},{24,32},{32,40},{40,48},{48,56},{1,9},{9,17},... | collective-permute-start | bytes 24584 | tf_op jit(solution)/shard_map/ppermute | solution.py:23
  418.4 7.7 %collective-permute-start.11 = (bf16[1,4096]{1,0:T(2,128)(2,1)S(1)}, bf16[1,4096]{1,0:T(2,128)(2,1)S(1)}, u32[]{:S(2)}, u32[]{:S(2)}) collective-permute-start(bf16[1,4096]{1,0:T(2,128)(2,1)S(1)} %slice.277), channel_id=1, source_target_pairs={{8,0},{16,8},{24,16},{32,24},{40,32},{48,40},{56,48},{9,1},{17,9},... | collective-permute-start | bytes 24584 | tf_op jit(solution)/shard_map/ppermute | solution.py:26
  427.6 0.6 copy-start.16
Sparse Core Ops, SparseCore 0:
  44.0 64.4 reduce-scatter.4
  189.5 80.9 all-gather.8
  272.4 44.1 all-gather.10
Sparse Core Ops, SparseCore 1:
  46.2 50.1 all-gather.4
  98.0 78.2 all-gather.6
  323.1 56.5 reduce-scatter.6

commit v6 on v5

--- a/solution.py
+++ b/solution.py
@@ -53,42 +53,47 @@
     return block
 
 
-def attend_block(keep_ref, query_ref, key_ref, value_ref, out_ref, *, scale):
-    scores = (
-        lax.dot_general(
-            query_ref[...],
-            key_ref[...],
-            (((1,), (1,)), ((), ())),
-            preferred_element_type=jnp.float32,
-        )
-        * scale
-    )
-    scores = jnp.where(keep_ref[...] > 0.5, scores, -1e30)
-    peak = jnp.max(scores, -1, keepdims=True)
-    weights = jnp.exp(scores - peak)
-    summed = jnp.sum(weights, -1, keepdims=True)
+def attend_block(keep_ref, query_ref, tkey_ref, tvalue_ref, ikey_ref, ivalue_ref, out_ref, *, scale):
+    query = query_ref[...]
+    contract = (((1,), (1,)), ((), ()))
+    text_scores = (
+        lax.dot_general(query, tkey_ref[...], contract, preferred_element_type=jnp.float32) * scale
+    )
+    text_scores = jnp.where(keep_ref[...] > 0.5, text_scores, -1e30)
+    img_scores = (
+        lax.dot_general(query, ikey_ref[...], contract, preferred_element_type=jnp.float32) * scale
+    )
+    peak = jnp.maximum(
+        jnp.max(text_scores, -1, keepdims=True), jnp.max(img_scores, -1, keepdims=True)
+    )
+    text_weights = jnp.exp(text_scores - peak)
+    img_weights = jnp.exp(img_scores - peak)
+    summed = jnp.sum(text_weights, -1, keepdims=True) + jnp.sum(img_weights, -1, keepdims=True)
     mixed_v = jnp.dot(
-        weights.astype(jnp.bfloat16), value_ref[...], preferred_element_type=jnp.float32
-    )
+        text_weights.astype(jnp.bfloat16), tvalue_ref[...], preferred_element_type=jnp.float32
+    ) + jnp.dot(img_weights.astype(jnp.bfloat16), ivalue_ref[...], preferred_element_type=jnp.float32)
     out_ref[...] = (mixed_v / summed).astype(out_ref.dtype)
 
 
-def attention(keep, queries, keys, values, head_dim, q_tile):
+def attention(keep, queries, text_kv, img_kv, head_dim, q_tile):
     rows = queries.shape[0]
-    total = keys.shape[0]
+    text_total = text_kv.shape[0]
+    img_total = img_kv.shape[0]
     heads = queries.shape[1] // head_dim
     return pl.pallas_call(
         functools.partial(attend_block, scale=head_dim ** (-0.5)),
         grid=(heads, rows // q_tile),
         in_specs=[
-            pl.BlockSpec((1, total), lambda h, i: (0, 0)),
+            pl.BlockSpec((1, text_total), lambda h, i: (0, 0)),
             pl.BlockSpec((q_tile, head_dim), lambda h, i: (i, h)),
-            pl.BlockSpec((total, head_dim), lambda h, i: (0, h)),
-            pl.BlockSpec((total, head_dim), lambda h, i: (0, h)),
+            pl.BlockSpec((text_total, head_dim), lambda h, i: (0, h)),
+            pl.BlockSpec((text_total, head_dim), lambda h, i: (0, h + heads)),
+            pl.BlockSpec((img_total, head_dim), lambda h, i: (0, h)),
+            pl.BlockSpec((img_total, head_dim), lambda h, i: (0, h + heads)),
         ],
         out_specs=pl.BlockSpec((q_tile, head_dim), lambda h, i: (i, h)),
         out_shape=jax.ShapeDtypeStruct(queries.shape, jnp.bfloat16),
-    )(keep, queries, keys, values)
+    )(keep, queries, text_kv, text_kv, img_kv, img_kv)
 
 
 def bit_of(value, step):
@@ -235,6 +240,7 @@
     img_weights, img_out_w = lax.optimization_barrier((img_weights, img_out_w))
     img_out_full = lax.all_gather(img_out_w, "seq", axis=1, tiled=True)
     img_mixed = add_rows(img_norm, img_weights)
+    txt_norm, img_norm = lax.optimization_barrier((txt_norm, img_norm))
     txt_norm_rows = lax.all_to_all(txt_norm, "seq", 1, 0, tiled=True)
     txt_mixed = lax.psum_scatter(
         add_rows(txt_norm_rows, txt_qkv), "seq", scatter_dimension=0, tiled=True
@@ -249,30 +255,27 @@
     txt_query, txt_key, txt_value = split_heads(txt_mixed, qk_gains[2], qk_gains[3], None)
     local_len = txt_rows + img_rows
     heads_local = img_query.shape[1]
-    queries = jnp.concatenate([txt_query, img_query], 0)
-    keys_local = jnp.concatenate([txt_key, img_key], 0).reshape(local_len, heads_local * head_dim)
-    values_local = jnp.concatenate([txt_value, img_value], 0).reshape(
-        local_len, heads_local * head_dim
+    kv_width = heads_local * head_dim
+    queries = jnp.concatenate([txt_query, img_query], 0).reshape(local_len, kv_width)
+    img_kv = lax.all_gather(
+        jnp.concatenate(
+            [img_key.reshape(img_rows, kv_width), img_value.reshape(img_rows, kv_width)], 1
+        ),
+        "seq",
+        axis=0,
+        tiled=True,
+    )
+    text_kv = lax.all_gather(
+        jnp.concatenate(
+            [txt_key.reshape(txt_rows, kv_width), txt_value.reshape(txt_rows, kv_width)], 1
+        ),
+        "seq",
+        axis=0,
+        tiled=True,
     )
     limit = text_len[0]
-    kv_width = heads_local * head_dim
-    kv_piece = lax.all_gather(
-        jnp.concatenate([keys_local, values_local], 1), "seq", axis=0, tiled=True
-    )
-    key_piece = kv_piece[:, :kv_width]
-    value_piece = kv_piece[:, kv_width:]
-    slot = jnp.arange(key_piece.shape[0], dtype=jnp.int32)
-    within = slot % local_len
-    text_pos = (slot // local_len) * txt_rows + within
-    keep = ((within >= txt_rows) | (text_pos < limit)).astype(jnp.float32)[None, :]
-    attn = attention(
-        keep,
-        queries.reshape(local_len, kv_width),
-        key_piece,
-        value_piece,
-        head_dim,
-        local_len // 3,
-    )
+    keep = (jnp.arange(text_kv.shape[0], dtype=jnp.int32) < limit).astype(jnp.float32)[None, :]
+    attn = attention(keep, queries, text_kv, img_kv, head_dim, local_len // 3)
     txt_attn = attn[:txt_rows]
     img_attn = attn[txt_rows:]
     img_term = jnp.dot(

time: 437 us -> 433 us (level)
  blocking collectives: 18.8 us -> 52.1 us
  waiting for transfers between devices: 290 us -> 263 us
  local copies, waits for them, and re-layouts: 25.8 us -> 15.5 us
    all_gather x1, waiting for transfers between devices: 76.6 us -> 42.1 us  [per_device(): lax.all_gather(jnp.concatenate([img_key.reshape(img_rows, kv_width), img_...]
    all_gather x0 -> x1, blocking collectives: none -> 33.6 us  [per_device(): lax.all_gather(jnp.concatenate([txt_key.reshape(txt_rows, kv_width), txt_...]
    all_gather x1, waiting for transfers between devices: 0.03 us -> 26.5 us  [per_device(): lax.all_gather(img_hidden, 'tp', axis=1, tiled=True)]
    reduce_scatter x1, waiting for transfers between devices: 57.4 us -> 31.2 us  [per_device(): lax.psum_scatter(add_rows(txt_norm_rows, txt_qkv), 'seq', scatter_dimensi...]
    slice x1 -> x0, local copies, waits for them, and re-layouts: 6.71 us -> none  [per_device(): value_piece = kv_piece[:, kv_width:]]
    all_gather x1, waiting for transfers between devices: 20.5 us -> 25.6 us  [per_device(): img_out_full = lax.all_gather(img_out_w, 'seq', axis=1, tiled=True)]
    all_to_all x1, waiting for transfers between devices: 4.19 us -> 8.92 us  [per_device(): txt_norm_rows = lax.all_to_all(txt_norm, 'seq', 1, 0, tiled=True)]
    all_gather x1, waiting for transfers between devices: 60.3 us -> 55.9 us  [per_device(): img_weights = lax.all_gather(img_qkv, 'seq', axis=0, tiled=True)]
  transfers between devices with their start and end apart: 19 -> 19, of which waited for: 13 -> 15; matrix products, arithmetic and copies ran while one was open for 7% -> 10% of each run, Pallas kernels for 4% -> 5%
where the time goes in v6:
time: 433 us; the launch traced here: 432 us
  waiting for transfers between devices  263 us (61%)
  blocking collectives  52.1 us (12%)
  starting transfers between devices  29.8 us (7%)
  Pallas kernels  20.1 us (5%)
  other arithmetic  19.9 us (5%)
  between operations  16.3 us (4%)
  local copies, waits for them, and re-layouts  15.5 us (4%)
  matrix products  15.3 us (4%)
    all_gather x1, waiting for transfers between devices, per_device(): img_weights = lax.all_gather(img_qkv, 'seq', axis=0, tiled=True)  55.9 us
    all_gather x1, waiting for transfers between devices, per_device(): lax.all_gather(jnp.concatenate([img_key.reshape(img_rows, kv_width), img_...  42.1 us
    all_gather x1, blocking collectives, per_device(): lax.all_gather(jnp.concatenate([txt_key.reshape(txt_rows, kv_width), txt_...  33.6 us
    reduce_scatter x1, waiting for transfers between devices, per_device(): lax.psum_scatter(add_rows(txt_norm_rows, txt_qkv), 'seq', scatter_dimensi...  31.2 us
    unnamed x7, waiting for transfers between devices  28.8 us
    all_gather x1, waiting for transfers between devices, per_device(): lax.all_gather(img_hidden, 'tp', axis=1, tiled=True)  26.5 us
    all_gather x1, waiting for transfers between devices, per_device(): img_out_full = lax.all_gather(img_out_w, 'seq', axis=1, tiled=True)  25.6 us
    ppermute x3, waiting for transfers between devices, tree_sum(): lax.ppermute(block, axis, [(i, i ^ step) for i in range(count)])  22.5 us
  transfers between devices with their start and end apart: 19, of which 15 were waited for; matrix products, arithmetic and copies ran while one was open for 10% of the time, Pallas kernels for 5%

profile of v6, /device:TPU:26, one launch (start us, length us, event | category | flops | bytes accessed | tf_op | source)
XLA Modules:
  0.0 432.3 jit_solution(3357476717469114944)
XLA Ops:
  7.3 0.7 all-gather.5.cloned.1.call-update
  8.0 2.3 copy.76
  10.3 0.7 convert_element_type.118
  11.1 18.6 %all_gather.18 = bf16[64,3072]{1,0:T(8,128)(2,1)S(1)} all-gather(bf16[64,384]{1,0:T(8,128)(2,1)S(1)} %copy-done.6), channel_id=1, replica_groups=mesh['req'=4,'seq'=8,'tp'=8] {'tp'}, dimensions={1}, use_global_device_ids=true | all-gather | bytes 442368 | tf_op jit(solution)/shard_map/all_gather | solution.py:234
  30.4 26.5 %all-gather.5.cloned.1.call-done = bf16[512,3072]{1,0:T(8,128)(2,1)} async-done(((bf16[512,384]{1,0:T(8,128)(2,1)}), bf16[512,3072]{1,0:T(8,128)(2,1)}) %all-gather.5.cloned.1.call-update) | async-done | bytes 3145744 | tf_op jit(solution)/shard_map/all_gather | solution.py:233
  56.9 2.5 convert_reduce_fusion
  59.5 0.3 copy-done.1
  59.8 1.0 fusion.2
  60.7 3.5 fusion.5
  64.3 0.8 copy.104
  65.1 5.6 %all-to-all-start = ((bf16[64,8,384]{2,0,1:T(8,128)(2,1)}), bf16[64,8,384]{2,0,1:T(8,128)(2,1)S(1)}, u32[]{:S(2)}, u32[]{:S(2)}) async-start(bf16[64,8,384]{2,0,1:T(8,128)(2,1)} %bitcast.169), calls=%async_computation | async-start | bytes 786432 | tf_op jit(solution)/shard_map/all_to_all | solution.py:244
  70.7 2.4 copy.73
  73.1 8.9 %all-to-all-done = bf16[64,8,384]{2,0,1:T(8,128)(2,1)S(1)} async-done(((bf16[64,8,384]{2,0,1:T(8,128)(2,1)}), bf16[64,8,384]{2,0,1:T(8,128)(2,1)S(1)}, u32[]{:S(2)}, u32[]{:S(2)}) %all-to-all-start) | async-done | bytes 393248 | tf_op jit(solution)/shard_map/all_to_all | solution.py:244
  82.0 2.2 fusion.89
  84.9 0.5 fusion.24
  85.4 55.9 %all-gather.7.cloned.1.call-done = bf16[3072,3,384]{0,2,1:T(8,128)(2,1)} async-done(((bf16[384,3,384]{0,2,1:T(8,128)(2,1)}), bf16[3072,3,384]{0,2,1:T(8,128)(2,1)}) %all-gather.7.cloned.1.call-update) | async-done | bytes 7077904 | tf_op jit(solution)/shard_map/all_gather | solution.py:239
  141.3 7.1 %fusion.6 = f32[512,3,3,128]{0,3,2,1:T(8,128)S(1)} fusion(bf16[3,3,128,3072]{3,2,1,0:T(8,128)(2,1)} %bitcast.205, bf16[512,3072]{1,0:T(8,128)(2,1)} %fusion.5), kind=kOutput, calls=%fused_computation.9 | convolution fusion | flops 3623878656 | bytes 12582912 | tf_op jit(solution)/shard_map/dot_general | solution.py:206
  148.4 0.3 multiply_reduce_fusion
  148.7 0.5 squeeze.59
  149.2 0.5 squeeze.61
  149.7 0.3 multiply_multiply_fusion.1
  150.0 0.3 multiply_multiply_fusion
  150.4 2.1 subtract_convert_fusion
  152.5 0.9 pad_maximum_fusion.3
  154.0 1.0 pad_maximum_fusion
  155.1 0.5 all-gather.11.cloned.1.call-update
  156.3 0.6 compare_convert_fusion.keep_ref
  156.9 31.2 %reduce-scatter.5.cloned.1.call-done = f32[64,1152]{1,0:T(8,128)} async-done(((f32[512,1152]{1,0:T(8,128)}), f32[64,1152]{1,0:T(8,128)}) %reduce-scatter.5.cloned.1.call-update) | async-done | bytes 294928 | tf_op jit(solution)/shard_map/reduce_scatter | solution.py:245
  188.1 1.1 reshape.280
  189.8 33.6 %all_gather.21.tkey_ref.tvalue_ref = bf16[512,768]{1,0:T(8,128)(2,1)} all-gather(bf16[64,768]{1,0:T(8,128)(2,1)S(1)} %pad_maximum_fusion.9), channel_id=1, replica_groups=mesh['req'=4,'seq'=8,'tp'=8] {'seq'}, dimensions={0}, use_global_device_ids=true | all-gather | bytes 884736 | tf_op jit(solution)/shard_map/all_gather | solution.py:268
  223.4 0.9 pad_maximum_fusion.2
  224.7 0.8 pad_maximum_fusion.1.query_ref
  225.5 42.1 %all-gather.9.cloned.1.call-done.ikey_ref.ivalue_ref = bf16[4096,768]{1,0:T(8,128)(2,1)} async-done(((bf16[512,768]{1,0:T(8,128)(2,1)}), bf16[4096,768]{1,0:T(8,128)(2,1)}) %all-gather.9.cloned.1.call-update) | async-done | bytes 6291472 | tf_op jit(solution)/shard_map/all_gather | solution.py:260
  267.6 20.1 %shard_map.182 = bf16[576,384]{1,0:T(8,128)(2,1)} custom-call(f32[1,512]{1,0:T(1,128)} %compare_convert_fusion.keep_ref, bf16[576,384]{1,0:T(8,128)(2,1)} %pad_maximum_fusion.1.query_ref, bf16[512,768]{1,0:T(8,128)(2,1)} %all_gather.21.tkey_ref.tvalue_ref, bf16[512,768]{1,0:T(8,128)(2,1)} %all_gather.21.tkey_ref.tvalue_ref, ...), custom_call_target="tpu_custom_call" | custom-call | tf_op jit(solution)/shard_map/pallas_call | solution.py:83
  287.7 25.6 %all-gather.11.cloned.1.call-done = bf16[384,3072]{1,0:T(8,128)(2,1)} async-done(((bf16[384,384]{1,0:T(8,128)(2,1)}), bf16[384,3072]{1,0:T(8,128)(2,1)}) %all-gather.11.cloned.1.call-update) | async-done | bytes 2359312 | tf_op jit(solution)/shard_map/all_gather | solution.py:241
  313.3 3.6 convolution_convert_fusion
  316.9 2.8 copy.88
  319.7 0.8 slice_bitcast_fusion
  320.5 1.6 collective-permute-start
  322.1 4.5 %collective-permute-done = bf16[1,64,384]{2,1,0:T(8,128)(2,1)S(1)} collective-permute-done((bf16[1,64,384]{2,1,0:T(8,128)(2,1)S(1)}, bf16[1,64,384]{2,1,0:T(8,128)(2,1)S(1)}, u32[]{:S(2)}, u32[]{:S(2)}) %collective-permute-start) | collective-permute-done | bytes 49184 | tf_op jit(solution)/shard_map/ppermute | solution.py:108
  326.6 0.8 select_bitcast_fusion.5
  327.4 1.2 collective-permute-start.1
  328.6 3.5 collective-permute-done.1
  332.2 1.5 collective-permute-start.2
  333.7 10.4 %collective-permute-done.2 = bf16[4,64,384]{2,1,0:T(8,128)(2,1)S(1)} collective-permute-done((bf16[4,64,384]{2,1,0:T(8,128)(2,1)S(1)}, bf16[4,64,384]{2,1,0:T(8,128)(2,1)S(1)}, u32[]{:S(2)}, u32[]{:S(2)}) %collective-permute-start.2) | collective-permute-done | bytes 196640 | tf_op jit(solution)/shard_map/ppermute | solution.py:108
  344.4 0.4 fusion.8
  346.3 0.4 collective-permute-done.3
  346.8 2.6 collective-permute-start.4
  349.5 27.5 %reduce-scatter.7.cloned.1.call-done = bf16[384,512]{1,0:T(8,128)(2,1)} async-done(((bf16[3072,512]{1,0:T(8,128)(2,1)}), bf16[384,512]{1,0:T(8,128)(2,1)}) %reduce-scatter.7.cloned.1.call-update) | async-done | bytes 393232
  377.0 1.2 copy.89
  378.6 0.6 fusion.15
  379.2 0.9 collective-permute-start.7
  380.1 1.0 collective-permute-done.7
  381.2 2.2 collective-permute-start.8
  383.4 2.2 collective-permute-start.5
  385.6 11.0 %collective-permute-done.8 = f32[514,66]{0,1:T(8,128)S(1)} collective-permute-done((f32[514,66]{0,1:T(8,128)S(1)}, f32[514,66]{0,1:T(8,128)S(1)}, u32[]{:S(2)}, u32[]{:S(2)}) %collective-permute-start.8) | collective-permute-done | bytes 135728 | tf_op jit(solution)/shard_map/ppermute | solution.py:35
  396.6 3.9 collective-permute-start.9
  400.5 1.9 collective-permute-start.6
  402.4 10.5 %collective-permute-done.9 = f32[514,66]{0,1:T(8,128)S(1)} collective-permute-done((f32[514,66]{0,1:T(8,128)S(1)}, f32[514,66]{0,1:T(8,128)S(1)}, u32[]{:S(2)}, u32[]{:S(2)}) %collective-permute-start.9) | collective-permute-done | bytes 135728 | tf_op jit(solution)/shard_map/ppermute | solution.py:35
  413.5 1.9 collective-permute-start.10
  415.6 3.9 collective-permute-start.11
  419.5 0.7 fusion.25
  420.5 2.8 collective-permute-done.11
  424.8 0.6 multiply_subtract_fusion
  (136 shorter events, 7.1 us)
Async XLA Ops:
  7.2 337.2 %copy-start = (bf16[384,384]{1,0:T(8,128)(2,1)S(1)}, bf16[384,384]{1,0:T(8,128)(2,1)}, u32[]{:S(2)}) copy-start(bf16[384,384]{1,0:T(8,128)(2,1)} %param.23) | copy-start | bytes 884740
  7.2 22.9 %copy-start.8 = (bf16[3,3072]{1,0:T(4,128)(2,1)S(1)}, bf16[3,3072]{1,0:T(4,128)(2,1)}, u32[]{:S(2)}) copy-start(bf16[3,3072]{1,0:T(4,128)(2,1)} %param.17) | copy-start | bytes 55300
  7.2 3.9 copy-start.9
  7.2 3.9 copy-start.6
  7.2 49.7 %all-gather.5.cloned.1.call-start = ((), (), s32[]{:S(2)}) async-start(), calls=%async_computation.3 | async-start | bytes 3538944 | tf_op jit(solution)/shard_map/all_gather | solution.py:233
  7.9 133.3 %all-gather.7.cloned.1.call-start = ((), (), s32[]{:S(2)}) async-start(), calls=%async_computation.5 | async-start | bytes 7962624 | tf_op jit(solution)/shard_map/all_gather | solution.py:239
  56.9 2.8 copy-start.1
  60.7 9.9 %copy-start.4 = (bf16[384,3,384]{2,0,1:T(8,128)(2,1)S(1)}, bf16[384,3,384]{2,0,1:T(8,128)(2,1)}, u32[]{:S(2)}) copy-start(bf16[384,3,384]{2,0,1:T(8,128)(2,1)} %param.20) | copy-start | bytes 2654212
  65.1 16.9 %all-to-all-start = ((bf16[64,8,384]{2,0,1:T(8,128)(2,1)}), bf16[64,8,384]{2,0,1:T(8,128)(2,1)S(1)}, u32[]{:S(2)}, u32[]{:S(2)}) async-start(bf16[64,8,384]{2,0,1:T(8,128)(2,1)} %bitcast.169), calls=%async_computation | async-start | bytes 786432 | tf_op jit(solution)/shard_map/all_to_all | solution.py:244
  70.7 117.5 %reduce-scatter.5.cloned.1.call-start = ((), (), s32[]{:S(2)}) async-start(), calls=%async_computation.4 | async-start | bytes 2654208 | tf_op jit(solution)/shard_map/reduce_scatter | solution.py:245
  73.0 11.4 %copy-start.13 = (f32[4,128]{1,0:T(4,128)S(1)}, f32[4,128]{1,0:T(4,128)}, u32[]{:S(2)}) copy-start(f32[4,128]{1,0:T(4,128)} %param.21) | copy-start | bytes 6148
  84.2 183.4 %all-gather.9.cloned.1.call-start = ((), (), s32[]{:S(2)}) async-start(), calls=%async_computation.6 | async-start | bytes 7077888 | tf_op jit(solution)/shard_map/all_gather | solution.py:260
  155.0 158.3 %all-gather.11.cloned.1.call-start = ((), (), s32[]{:S(2)}) async-start(), calls=%async_computation.7 | async-start | bytes 2654208 | tf_op jit(solution)/shard_map/all_gather | solution.py:241
  155.6 221.4 %reduce-scatter.7.cloned.1.call-start = ((), (), s32[]{:S(2)}) async-start(), calls=%async_computation.8 | async-start | bytes 3538944
  319.7 14.0 %copy-start.11 = (bf16[2,3072]{1,0:T(2,128)(2,1)S(1)}, bf16[2,3072]{1,0:T(2,128)(2,1)}, u32[]{:S(2)}) copy-start(bf16[2,3072]{1,0:T(2,128)(2,1)} %param.24) | copy-start | bytes 36868
  320.5 6.0 %collective-permute-start = (bf16[1,64,384]{2,1,0:T(8,128)(2,1)S(1)}, bf16[1,64,384]{2,1,0:T(8,128)(2,1)S(1)}, u32[]{:S(2)}, u32[]{:S(2)}) collective-permute-start(bf16[1,64,384]{2,1,0:T(8,128)(2,1)S(1)} %slice_bitcast_fusion), channel_id=1, source_target_pairs={{0,16},{8,24},{16,0},{24,8},{32,48},{40,56},{48,32},{56,40},{1,17}... | collective-permute-start | bytes 147464 | tf_op jit(solution)/shard_map/ppermute | solution.py:108
  327.4 4.7 %collective-permute-start.1 = (bf16[2,64,384]{2,1,0:T(8,128)(2,1)S(1)}, bf16[2,64,384]{2,1,0:T(8,128)(2,1)S(1)}, u32[]{:S(2)}, u32[]{:S(2)}) collective-permute-start(bf16[2,64,384]{2,1,0:T(8,128)(2,1)S(1)} %maximum_bitcast_fusion), channel_id=1, source_target_pairs={{0,8},{8,0},{16,24},{24,16},{32,40},{40,32},{48,56},{56,48},{1,9},... | collective-permute-start | bytes 294920 | tf_op jit(solution)/shard_map/ppermute | solution.py:108
  332.2 12.0 %collective-permute-start.2 = (bf16[4,64,384]{2,1,0:T(8,128)(2,1)S(1)}, bf16[4,64,384]{2,1,0:T(8,128)(2,1)S(1)}, u32[]{:S(2)}, u32[]{:S(2)}) collective-permute-start(bf16[4,64,384]{2,1,0:T(8,128)(2,1)S(1)} %bitcast.185), channel_id=1, source_target_pairs={{0,32},{8,40},{16,48},{24,56},{32,0},{40,8},{48,16},{56,24},{1,33}... | collective-permute-start | bytes 589832 | tf_op jit(solution)/shard_map/ppermute | solution.py:108
  333.7 11.3 %copy-start.5 = (bf16[384,64]{0,1:T(8,128)(2,1)S(1)}, bf16[384,64]{0,1:T(8,128)(2,1)}, u32[]{:S(2)}) copy-start(bf16[384,64]{0,1:T(8,128)(2,1)} %param.25) | copy-start | bytes 147460
  344.8 33.4 %copy-start.2 = (bf16[512,384]{1,0:T(8,128)(2,1)S(1)}, bf16[512,384]{1,0:T(8,128)(2,1)}, u32[]{:S(2)}) copy-start(bf16[512,384]{1,0:T(8,128)(2,1)} %param.15) | copy-start | bytes 1179652
  344.9 1.8 collective-permute-start.3
  346.8 33.3 %collective-permute-start.4 = (f32[128,384]{1,0:T(8,128)S(1)}, f32[128,384]{1,0:T(8,128)S(1)}, u32[]{:S(2)}, u32[]{:S(2)}) collective-permute-start(f32[128,384]{1,0:T(8,128)S(1)} %slice_select_fusion), channel_id=1, source_target_pairs={{0,2},{1,3},{2,0},{3,1},{4,6},{5,7},{6,4},{7,5},{8,10},{9,11},{10,... | collective-permute-start | bytes 589832 | tf_op jit(solution)/shard_map/ppermute | solution.py:140
  378.2 45.3 %copy-start.7 = (bf16[3,3,64,64]{3,2,1,0:T(8,128)(2,1)S(1)}, bf16[3,3,64,64]{3,2,1,0:T(8,128)(2,1)}, u32[]{:S(2)}) copy-start(bf16[3,3,64,64]{3,2,1,0:T(8,128)(2,1)} %param.26) | copy-start | bytes 221188
  378.5 46.9 %copy-start.3 = (bf16[512,384]{1,0:T(8,128)(2,1)}, bf16[512,384]{1,0:T(8,128)(2,1)S(1)}, u32[]{:S(2)}) copy-start(bf16[512,384]{1,0:T(8,128)(2,1)S(1)} %get-tuple-element.21) | copy-start | bytes 1179652
  378.5 46.2 %copy-start.12 = (f32[8,512]{1,0:T(8,128)S(1)}, f32[8,512]{1,0:T(8,128)}, u32[]{:S(2)}) copy-start(f32[8,512]{1,0:T(8,128)} %param.27) | copy-start | bytes 49156
  379.2 2.0 collective-permute-start.7
  381.2 15.4 %collective-permute-start.8 = (f32[514,66]{0,1:T(8,128)S(1)}, f32[514,66]{0,1:T(8,128)S(1)}, u32[]{:S(2)}, u32[]{:S(2)}) collective-permute-start(f32[514,66]{0,1:T(8,128)S(1)} %fusion.83), channel_id=1, source_target_pairs={{0,2},{1,3},{2,0},{3,1},{4,6},{5,7},{6,4},{7,5},{8,10},{9,11},{10,... | collective-permute-start | bytes 407096 | tf_op jit(solution)/shard_map/ppermute | solution.py:35
  383.4 17.1 %collective-permute-start.5 = (f32[64,384]{1,0:T(8,128)S(1)}, f32[64,384]{1,0:T(8,128)S(1)}, u32[]{:S(2)}, u32[]{:S(2)}) collective-permute-start(f32[64,384]{1,0:T(8,128)S(1)} %slice_select_fusion.1), channel_id=1, source_target_pairs={{0,4},{1,5},{2,6},{3,7},{4,0},{5,1},{6,2},{7,3},{8,12},{9,13},{10,... | collective-permute-start | bytes 294920 | tf_op jit(solution)/shard_map/ppermute | solution.py:140
  396.6 16.3 %collective-permute-start.9 = (f32[514,66]{0,1:T(8,128)S(1)}, f32[514,66]{0,1:T(8,128)S(1)}, u32[]{:S(2)}, u32[]{:S(2)}) collective-permute-start(f32[514,66]{0,1:T(8,128)S(1)} %add.295), channel_id=1, source_target_pairs={{0,4},{1,5},{2,6},{3,7},{4,0},{5,1},{6,2},{7,3},{8,12},{9,13},{10,... | collective-permute-start | bytes 407096 | tf_op jit(solution)/shard_map/ppermute | solution.py:35
  400.5 19.0 %collective-permute-start.6 = (f32[64,384]{1,0:T(8,128)S(1)}, f32[64,384]{1,0:T(8,128)S(1)}, u32[]{:S(2)}, u32[]{:S(2)}) collective-permute-start(f32[64,384]{1,0:T(8,128)S(1)} %select_add_fusion.2), channel_id=1, source_target_pairs={{0,0},{1,8},{2,16},{3,24},{4,32},{5,40},{6,48},{7,56},{8,1},{9,9},... | collective-permute-start | bytes 294920 | tf_op jit(solution)/shard_map/ppermute | solution.py:147
  413.5 6.9 %collective-permute-start.10 = (bf16[1,4096]{1,0:T(2,128)(2,1)S(1)}, bf16[1,4096]{1,0:T(2,128)(2,1)S(1)}, u32[]{:S(2)}, u32[]{:S(2)}) collective-permute-start(bf16[1,4096]{1,0:T(2,128)(2,1)S(1)} %slice.267), channel_id=1, source_target_pairs={{0,8},{8,16},{16,24},{24,32},{32,40},{40,48},{48,56},{1,9},{9,17},... | collective-permute-start | bytes 24584 | tf_op jit(solution)/shard_map/ppermute | solution.py:23
  415.6 7.7 %collective-permute-start.11 = (bf16[1,4096]{1,0:T(2,128)(2,1)S(1)}, bf16[1,4096]{1,0:T(2,128)(2,1)S(1)}, u32[]{:S(2)}, u32[]{:S(2)}) collective-permute-start(bf16[1,4096]{1,0:T(2,128)(2,1)S(1)} %slice.269), channel_id=1, source_target_pairs={{8,0},{16,8},{24,16},{32,24},{40,32},{48,40},{56,48},{9,1},{17,9},... | collective-permute-start | bytes 24584 | tf_op jit(solution)/shard_map/ppermute | solution.py:26
  424.8 0.6 copy-start.10
Sparse Core Ops, SparseCore 0:
  9.9 46.9 all-gather.4
  58.7 82.4 all-gather.6
  143.8 44.2 reduce-scatter.4
  189.8 77.7 all-gather.8
  269.2 43.9 all-gather.10
  319.8 57.1 reduce-scatter.6

commit v7 on v6

--- a/solution.py
+++ b/solution.py
@@ -237,8 +237,6 @@
     img_norm = modulate(img_full, img_mod)
     txt_norm = modulate(txt_full, txt_mod)
     img_weights = lax.all_gather(img_qkv, "seq", axis=0, tiled=True)
-    img_weights, img_out_w = lax.optimization_barrier((img_weights, img_out_w))
-    img_out_full = lax.all_gather(img_out_w, "seq", axis=1, tiled=True)
     img_mixed = add_rows(img_norm, img_weights)
     txt_norm, img_norm = lax.optimization_barrier((txt_norm, img_norm))
     txt_norm_rows = lax.all_to_all(txt_norm, "seq", 1, 0, tiled=True)
@@ -273,6 +271,8 @@
         axis=0,
         tiled=True,
     )
+    img_kv, img_out_w = lax.optimization_barrier((img_kv, img_out_w))
+    img_out_full = doubling_gather(img_out_w, "seq", 1, (2, 1, 4))
     limit = text_len[0]
     keep = (jnp.arange(text_kv.shape[0], dtype=jnp.int32) < limit).astype(jnp.float32)[None, :]
     attn = attention(keep, queries, text_kv, img_kv, head_dim, local_len // 3)

time: 433 us -> 479 us (1.11)
  waiting for transfers between devices: 263 us -> 288 us
  blocking collectives: 52.1 us -> 66.4 us
  local copies, waits for them, and re-layouts: 15.5 us -> 21.7 us
    all_gather x1 -> x0, waiting for transfers between devices: 25.6 us -> none  [per_device(): img_out_full = lax.all_gather(img_out_w, 'seq', axis=1, tiled=True)]
    all_gather x1, waiting for transfers between devices: 55.9 us -> 74.4 us  [per_device(): img_weights = lax.all_gather(img_qkv, 'seq', axis=0, tiled=True)]
    all_gather x1, waiting for transfers between devices: 26.5 us -> 44.2 us  [per_device(): lax.all_gather(img_hidden, 'tp', axis=1, tiled=True)]
    all_gather x1, blocking collectives: 33.6 us -> 49.3 us  [per_device(): lax.all_gather(jnp.concatenate([txt_key.reshape(txt_rows, kv_width), txt_...]
    ppermute x3 -> x6, waiting for transfers between devices: 18.4 us -> 29.6 us  [doubling_gather(): other = lax.ppermute(stacked, axis, [(i, i ^ step) for i in range(count)])]
    reduce_scatter x1, waiting for transfers between devices: 31.2 us -> 39.6 us  [per_device(): lax.psum_scatter(add_rows(txt_norm_rows, txt_qkv), 'seq', scatter_dimensi...]
    unnamed x7 -> x6, waiting for transfers between devices: 28.8 us -> 27 us
    unnamed x39 -> x57, local copies, waits for them, and re-layouts: 9.13 us -> 10.4 us
  transfers between devices with their start and end apart: 19 -> 21, of which waited for: 15 -> 14; matrix products, arithmetic and copies ran while one was open for 10% -> 7% of each run, Pallas kernels for 5% -> 4%
where the time goes in v7:
time: 479 us
  waiting for transfers between devices  288 us (60%)
  blocking collectives  66.4 us (14%)
  starting transfers between devices  30 us (6%)
  other arithmetic  23.5 us (5%)
  local copies, waits for them, and re-layouts  21.7 us (5%)
  Pallas kernels  20.1 us (4%)
  between operations  16.1 us (3%)
  matrix products  12.6 us (3%)
    all_gather x1, waiting for transfers between devices, per_device(): img_weights = lax.all_gather(img_qkv, 'seq', axis=0, tiled=True)  74.4 us
    all_gather x1, blocking collectives, per_device(): lax.all_gather(jnp.concatenate([txt_key.reshape(txt_rows, kv_width), txt_...  49.3 us
    all_gather x1, waiting for transfers between devices, per_device(): lax.all_gather(img_hidden, 'tp', axis=1, tiled=True)  44.2 us
    reduce_scatter x1, waiting for transfers between devices, per_device(): lax.psum_scatter(add_rows(txt_norm_rows, txt_qkv), 'seq', scatter_dimensi...  39.6 us
    all_gather x1, waiting for transfers between devices, per_device(): lax.all_gather(jnp.concatenate([img_key.reshape(img_rows, kv_width), img_...  39.6 us
    ppermute x6, waiting for transfers between devices, doubling_gather(): other = lax.ppermute(stacked, axis, [(i, i ^ step) for i in range(count)])  29.6 us
    unnamed x6, waiting for transfers between devices  27 us
    ppermute x3, waiting for transfers between devices, tree_sum(): lax.ppermute(block, axis, [(i, i ^ step) for i in range(count)])  21.9 us
  transfers between devices with their start and end apart: 21, of which 14 were waited for; matrix products, arithmetic and copies ran while one was open for 7% of the time, Pallas kernels for 4%

profile of v7, /device:TPU:26, one launch (start us, length us, event | category | flops | bytes accessed | tf_op | source)
XLA Modules:
  0.0 478.5 jit_solution(13694529297237209758)
XLA Ops:
  7.2 0.7 all-gather.4.cloned.1.call-update
  8.0 2.3 copy.88
  10.8 1.2 fusion.24
  12.0 0.6 fusion.87
  12.7 44.2 %all-gather.4.cloned.1.call-done = bf16[512,3072]{1,0:T(8,128)(2,1)} async-done(((bf16[512,384]{1,0:T(8,128)(2,1)}), bf16[512,3072]{1,0:T(8,128)(2,1)}) %all-gather.4.cloned.1.call-update) | async-done | bytes 3145744 | tf_op jit(solution)/shard_map/all_gather | solution.py:233
  56.9 2.5 convert_reduce_fusion
  59.7 1.0 fusion.2
  60.7 1.8 fusion.5
  62.5 74.4 %all-gather.6.cloned.1.call-done = bf16[3072,3,384]{0,2,1:T(8,128)(2,1)} async-done(((bf16[384,3,384]{0,2,1:T(8,128)(2,1)}), bf16[3072,3,384]{0,2,1:T(8,128)(2,1)}) %all-gather.6.cloned.1.call-update) | async-done | bytes 7077904 | tf_op jit(solution)/shard_map/all_gather | solution.py:239
  137.0 6.1 %fusion.6 = f32[512,3,3,128]{0,3,2,1:T(8,128)S(1)} fusion(bf16[3,3,128,3072]{3,2,1,0:T(8,128)(2,1)} %bitcast.241, bf16[512,3072]{1,0:T(8,128)(2,1)S(1)} %fusion.5), kind=kOutput, calls=%fused_computation.9 | convolution fusion | flops 3623878656 | bytes 12582912 | tf_op jit(solution)/shard_map/dot_general | solution.py:206
  145.3 2.7 subtract_convert_fusion.1
  148.0 0.9 pad_maximum_fusion.5
  149.6 1.0 pad_maximum_fusion.2
  150.7 17.1 %all_gather.15 = bf16[64,3072]{1,0:T(8,128)(2,1)S(1)} all-gather(bf16[64,384]{1,0:T(8,128)(2,1)S(1)} %copy-done.12), channel_id=1, replica_groups=mesh['req'=4,'seq'=8,'tp'=8] {'tp'}, dimensions={1}, use_global_device_ids=true | all-gather | bytes 442368 | tf_op jit(solution)/shard_map/all_gather | solution.py:234
  168.2 0.6 fusion.86
  169.1 0.8 copy.119
  169.9 6.0 %all-to-all-start = ((bf16[64,8,384]{2,0,1:T(8,128)(2,1)}), bf16[64,8,384]{2,0,1:T(8,128)(2,1)S(1)}, u32[]{:S(2)}, u32[]{:S(2)}) async-start(bf16[64,8,384]{2,0,1:T(8,128)(2,1)} %bitcast.195), calls=%async_computation | async-start | bytes 786432 | tf_op jit(solution)/shard_map/all_to_all | solution.py:242
  175.9 2.4 copy.85
  178.3 9.1 %all-to-all-done = bf16[64,8,384]{2,0,1:T(8,128)(2,1)S(1)} async-done(((bf16[64,8,384]{2,0,1:T(8,128)(2,1)}), bf16[64,8,384]{2,0,1:T(8,128)(2,1)S(1)}, u32[]{:S(2)}, u32[]{:S(2)}) %all-to-all-start) | async-done | bytes 393248 | tf_op jit(solution)/shard_map/all_to_all | solution.py:242
  187.4 2.3 fusion.89
  189.7 39.6 %all-gather.8.cloned.1.call-done.ikey_ref.ivalue_ref = bf16[4096,768]{1,0:T(8,128)(2,1)} async-done(((bf16[512,768]{1,0:T(8,128)(2,1)}), bf16[4096,768]{1,0:T(8,128)(2,1)}) %all-gather.8.cloned.1.call-update) | async-done | bytes 6291472 | tf_op jit(solution)/shard_map/all_gather | solution.py:258
  229.3 0.7 collective-permute-start
  230.0 9.7 %collective-permute-done = bf16[1,384,384]{2,1,0:T(8,128)(2,1)S(1)} collective-permute-done((bf16[1,384,384]{2,1,0:T(8,128)(2,1)S(1)}, bf16[1,384,384]{2,1,0:T(8,128)(2,1)S(1)}, u32[]{:S(2)}, u32[]{:S(2)}) %collective-permute-start) | collective-permute-done | bytes 294944 | tf_op jit(solution)/shard_map/ppermute | solution.py:108
  241.2 0.6 broadcast_bitcast_fusion
  241.8 39.6 %reduce-scatter.5.cloned.1.call-done = f32[64,1152]{1,0:T(8,128)} async-done(((f32[512,1152]{1,0:T(8,128)}), f32[64,1152]{1,0:T(8,128)}) %reduce-scatter.5.cloned.1.call-update) | async-done | bytes 294928 | tf_op jit(solution)/shard_map/reduce_scatter | solution.py:243
  281.4 1.1 reshape.292
  282.5 0.9 multiply_reduce_fusion.2
  283.7 0.8 copy.94
  284.5 1.0 collective-permute-start.2
  285.6 0.9 slice.499
  286.6 0.9 fusion.27
  287.7 0.9 fusion.29
  288.7 49.3 %all_gather.18.tkey_ref.tvalue_ref = bf16[512,768]{1,0:T(8,128)(2,1)} all-gather(bf16[64,768]{1,0:T(8,128)(2,1)S(1)} %pad_maximum_fusion.11), channel_id=1, replica_groups=mesh['req'=4,'seq'=8,'tp'=8] {'seq'}, dimensions={0}, use_global_device_ids=true | all-gather | bytes 884736 | tf_op jit(solution)/shard_map/all_gather | solution.py:266
  338.0 0.9 pad_maximum_fusion.4
  339.2 0.9 pad_maximum_fusion.3.query_ref
  340.1 20.1 %shard_map.182 = bf16[576,384]{1,0:T(8,128)(2,1)} custom-call(f32[1,512]{1,0:T(1,128)} %compare_convert_fusion.keep_ref, bf16[576,384]{1,0:T(8,128)(2,1)} %pad_maximum_fusion.3.query_ref, bf16[512,768]{1,0:T(8,128)(2,1)} %all_gather.18.tkey_ref.tvalue_ref, bf16[512,768]{1,0:T(8,128)(2,1)} %all_gather.18.tkey_ref.tvalue_ref, ...), custom_call_target="tpu_custom_call" | custom-call | tf_op jit(solution)/shard_map/pallas_call | solution.py:83
  360.2 1.5 select_bitcast_fusion.1
  363.0 1.8 convolution_convert_fusion
  364.8 2.8 copy.103
  367.7 0.8 slice_bitcast_fusion
  368.5 0.6 collective-permute-start.3
  369.1 5.0 %collective-permute-done.3 = bf16[1,64,384]{2,1,0:T(8,128)(2,1)S(1)} collective-permute-done((bf16[1,64,384]{2,1,0:T(8,128)(2,1)S(1)}, bf16[1,64,384]{2,1,0:T(8,128)(2,1)S(1)}, u32[]{:S(2)}, u32[]{:S(2)}) %collective-permute-start.3) | collective-permute-done | bytes 49184 | tf_op jit(solution)/shard_map/ppermute | solution.py:108
  374.1 0.8 select_bitcast_fusion.11
  375.0 4.6 collective-permute-done.4
  379.7 0.7 collective-permute-start.5
  380.4 10.4 %collective-permute-done.5 = bf16[4,64,384]{2,1,0:T(8,128)(2,1)S(1)} collective-permute-done((bf16[4,64,384]{2,1,0:T(8,128)(2,1)S(1)}, bf16[4,64,384]{2,1,0:T(8,128)(2,1)S(1)}, u32[]{:S(2)}, u32[]{:S(2)}) %collective-permute-start.5) | collective-permute-done | bytes 196640 | tf_op jit(solution)/shard_map/ppermute | solution.py:108
  392.9 0.7 fusion.71
  393.6 0.7 fusion.72
  394.5 2.5 collective-permute-start.7
  397.0 26.3 %reduce-scatter.7.cloned.1.call-done = bf16[384,512]{1,0:T(8,128)(2,1)} async-done(((bf16[3072,512]{1,0:T(8,128)(2,1)}), bf16[384,512]{1,0:T(8,128)(2,1)}) %reduce-scatter.7.cloned.1.call-update) | async-done | bytes 393232
  423.2 1.2 copy.104
  425.4 1.3 collective-permute-start.10
  426.8 1.0 collective-permute-done.10
  427.8 1.1 collective-permute-start.11
  428.9 3.7 collective-permute-start.8
  432.7 10.7 %collective-permute-done.11 = f32[514,66]{0,1:T(8,128)S(1)} collective-permute-done((f32[514,66]{0,1:T(8,128)S(1)}, f32[514,66]{0,1:T(8,128)S(1)}, u32[]{:S(2)}, u32[]{:S(2)}) %collective-permute-start.11) | collective-permute-done | bytes 135728 | tf_op jit(solution)/shard_map/ppermute | solution.py:35
  443.4 4.0 collective-permute-start.12
  447.5 1.9 collective-permute-start.9
  449.4 10.1 %collective-permute-done.12 = f32[514,66]{0,1:T(8,128)S(1)} collective-permute-done((f32[514,66]{0,1:T(8,128)S(1)}, f32[514,66]{0,1:T(8,128)S(1)}, u32[]{:S(2)}, u32[]{:S(2)}) %collective-permute-start.12) | collective-permute-done | bytes 135728 | tf_op jit(solution)/shard_map/ppermute | solution.py:35
  460.1 1.9 collective-permute-start.13
  462.2 3.9 collective-permute-start.14
  466.1 0.7 fusion.25
  467.1 2.8 collective-permute-done.14
  471.4 0.6 multiply_subtract_fusion
  (165 shorter events, 12.5 us)
Async XLA Ops:
  7.2 383.9 %copy-start = (bf16[384,384]{1,0:T(8,128)(2,1)S(1)}, bf16[384,384]{1,0:T(8,128)(2,1)}, u32[]{:S(2)}) copy-start(bf16[384,384]{1,0:T(8,128)(2,1)} %param.23) | copy-start | bytes 884740
  7.2 3.2 copy-start.14
  7.2 3.2 copy-start.19
  7.2 49.7 %all-gather.4.cloned.1.call-start = ((), (), s32[]{:S(2)}) async-start(), calls=%async_computation.3 | async-start | bytes 3538944 | tf_op jit(solution)/shard_map/all_gather | solution.py:233
  7.9 129.0 %all-gather.6.cloned.1.call-start = ((), (), s32[]{:S(2)}) async-start(), calls=%async_computation.5 | async-start | bytes 7962624 | tf_op jit(solution)/shard_map/all_gather | solution.py:239
  10.3 219.0 %all-gather.8.cloned.1.call-start = ((), (), s32[]{:S(2)}) async-start(), calls=%async_computation.6 | async-start | bytes 7077888 | tf_op jit(solution)/shard_map/all_gather | solution.py:258
  56.9 2.8 copy-start.1
  144.4 0.9 copy-start.8
  144.4 1.0 copy-start.9
  148.9 1.7 copy-start.15
  149.0 1.7 copy-start.12
  150.6 25.3 %copy-start.6 = (bf16[384,3,384]{2,0,1:T(8,128)(2,1)S(1)}, bf16[384,3,384]{2,0,1:T(8,128)(2,1)}, u32[]{:S(2)}) copy-start(bf16[384,3,384]{2,0,1:T(8,128)(2,1)} %param.20) | copy-start | bytes 2654212
  169.9 17.5 %all-to-all-start = ((bf16[64,8,384]{2,0,1:T(8,128)(2,1)}), bf16[64,8,384]{2,0,1:T(8,128)(2,1)S(1)}, u32[]{:S(2)}, u32[]{:S(2)}) async-start(bf16[64,8,384]{2,0,1:T(8,128)(2,1)} %bitcast.195), calls=%async_computation | async-start | bytes 786432 | tf_op jit(solution)/shard_map/all_to_all | solution.py:242
  175.9 105.5 %reduce-scatter.5.cloned.1.call-start = ((), (), s32[]{:S(2)}) async-start(), calls=%async_computation.4 | async-start | bytes 2654208 | tf_op jit(solution)/shard_map/reduce_scatter | solution.py:243
  187.4 41.9 %copy-start.11 = (bf16[384,384]{1,0:T(8,128)(2,1)S(1)}, bf16[384,384]{1,0:T(8,128)(2,1)}, u32[]{:S(2)}) copy-start(bf16[384,384]{1,0:T(8,128)(2,1)} %param.22) | copy-start | bytes 884740
  189.7 233.6 %reduce-scatter.7.cloned.1.call-start = ((), (), s32[]{:S(2)}) async-start(), calls=%async_computation.7 | async-start | bytes 3538944
  229.3 10.4 %collective-permute-start = (bf16[1,384,384]{2,1,0:T(8,128)(2,1)S(1)}, bf16[1,384,384]{2,1,0:T(8,128)(2,1)S(1)}, u32[]{:S(2)}, u32[]{:S(2)}) collective-permute-start(bf16[1,384,384]{2,1,0:T(8,128)(2,1)S(1)} %bitcast.227), channel_id=1, source_target_pairs={{0,16},{8,24},{16,0},{24,8},{32,48},{40,56},{48,32},{56,40},{1,17}... | collective-permute-start | bytes 884744 | tf_op jit(solution)/shard_map/ppermute | solution.py:108
  239.8 43.5 %collective-permute-start.1 = (bf16[2,384,384]{2,1,0:T(8,128)(2,1)S(1)}, bf16[2,384,384]{2,1,0:T(8,128)(2,1)S(1)}, u32[]{:S(2)}, u32[]{:S(2)}) collective-permute-start(bf16[2,384,384]{2,1,0:T(8,128)(2,1)S(1)} %maximum_bitcast_fusion), channel_id=1, source_target_pairs={{0,8},{8,0},{16,24},{24,16},{32,40},{40,32},{48,56},{56,48},{1,9},... | collective-permute-start | bytes 1769480 | tf_op jit(solution)/shard_map/ppermute | solution.py:108
  282.5 1.2 copy-start.5
  283.7 54.3 %copy-start.4 = (bf16[512,3,64,1]{0,3,2,1:T(2,128)(2,1)S(1)}, bf16[512,3,64,1]{0,3,2,1:T(2,128)(2,1)}, u32[]{:S(2)}) copy-start(bf16[512,3,64,1]{0,3,2,1:T(2,128)(2,1)} %get-tuple-element.29) | copy-start | bytes 589828
  284.5 75.7 %collective-permute-start.2 = (bf16[4,384,384]{1,2,0:T(8,128)(2,1)S(1)}, bf16[4,384,384]{1,2,0:T(8,128)(2,1)}, u32[]{:S(2)}, u32[]{:S(2)}) collective-permute-start(bf16[4,384,384]{1,2,0:T(8,128)(2,1)S(1)} %copy.94), channel_id=1, source_target_pairs={{0,32},{8,40},{16,48},{24,56},{32,0},{40,8},{48,16},{56,24},{1,33}... | collective-permute-start | bytes 3538952 | tf_op jit(solution)/shard_map/ppermute | solution.py:108
  361.9 1.0 copy-start.7
  367.6 12.8 %copy-start.17 = (bf16[2,3072]{1,0:T(2,128)(2,1)S(1)}, bf16[2,3072]{1,0:T(2,128)(2,1)}, u32[]{:S(2)}) copy-start(bf16[2,3072]{1,0:T(2,128)(2,1)} %param.24) | copy-start | bytes 36868
  368.5 5.6 %collective-permute-start.3 = (bf16[1,64,384]{2,1,0:T(8,128)(2,1)S(1)}, bf16[1,64,384]{2,1,0:T(8,128)(2,1)S(1)}, u32[]{:S(2)}, u32[]{:S(2)}) collective-permute-start(bf16[1,64,384]{2,1,0:T(8,128)(2,1)S(1)} %slice_bitcast_fusion), channel_id=1, source_target_pairs={{0,16},{8,24},{16,0},{24,8},{32,48},{40,56},{48,32},{56,40},{1,17}... | collective-permute-start | bytes 147464 | tf_op jit(solution)/shard_map/ppermute | solution.py:108
  374.9 4.7 collective-permute-start.4
  379.7 11.1 %collective-permute-start.5 = (bf16[4,64,384]{2,1,0:T(8,128)(2,1)S(1)}, bf16[4,64,384]{2,1,0:T(8,128)(2,1)S(1)}, u32[]{:S(2)}, u32[]{:S(2)}) collective-permute-start(bf16[4,64,384]{2,1,0:T(8,128)(2,1)S(1)} %bitcast.219), channel_id=1, source_target_pairs={{0,32},{8,40},{16,48},{24,56},{32,0},{40,8},{48,16},{56,24},{1,33}... | collective-permute-start | bytes 589832 | tf_op jit(solution)/shard_map/ppermute | solution.py:108
  391.0 0.8 copy-start.10
  391.5 32.9 %copy-start.2 = (bf16[512,384]{1,0:T(8,128)(2,1)S(1)}, bf16[512,384]{1,0:T(8,128)(2,1)}, u32[]{:S(2)}) copy-start(bf16[512,384]{1,0:T(8,128)(2,1)} %param.15) | copy-start | bytes 1179652
  391.6 2.8 collective-permute-start.6
  394.5 32.3 %collective-permute-start.7 = (f32[128,384]{1,0:T(8,128)S(1)}, f32[128,384]{1,0:T(8,128)S(1)}, u32[]{:S(2)}, u32[]{:S(2)}) collective-permute-start(f32[128,384]{1,0:T(8,128)S(1)} %slice_select_fusion), channel_id=1, source_target_pairs={{0,2},{1,3},{2,0},{3,1},{4,6},{5,7},{6,4},{7,5},{8,10},{9,11},{10,... | collective-permute-start | bytes 589832 | tf_op jit(solution)/shard_map/ppermute | solution.py:140
  424.8 42.1 %copy-start.3 = (bf16[512,384]{1,0:T(8,128)(2,1)}, bf16[512,384]{1,0:T(8,128)(2,1)S(1)}, u32[]{:S(2)}) copy-start(bf16[512,384]{1,0:T(8,128)(2,1)S(1)} %get-tuple-element.21) | copy-start | bytes 1179652
  425.4 44.8 %copy-start.13 = (bf16[3,3,64,64]{3,2,1,0:T(8,128)(2,1)S(1)}, bf16[3,3,64,64]{3,2,1,0:T(8,128)(2,1)}, u32[]{:S(2)}) copy-start(bf16[3,3,64,64]{3,2,1,0:T(8,128)(2,1)} %param.26) | copy-start | bytes 221188
  425.4 2.4 collective-permute-start.10
  426.8 44.6 %copy-start.18 = (f32[8,512]{1,0:T(8,128)S(1)}, f32[8,512]{1,0:T(8,128)}, u32[]{:S(2)}) copy-start(f32[8,512]{1,0:T(8,128)} %param.27) | copy-start | bytes 49156
  427.8 15.6 %collective-permute-start.11 = (f32[514,66]{0,1:T(8,128)S(1)}, f32[514,66]{0,1:T(8,128)S(1)}, u32[]{:S(2)}, u32[]{:S(2)}) collective-permute-start(f32[514,66]{0,1:T(8,128)S(1)} %fusion.83), channel_id=1, source_target_pairs={{0,2},{1,3},{2,0},{3,1},{4,6},{5,7},{6,4},{7,5},{8,10},{9,11},{10,... | collective-permute-start | bytes 407096 | tf_op jit(solution)/shard_map/ppermute | solution.py:35
  428.9 18.5 %collective-permute-start.8 = (f32[64,384]{1,0:T(8,128)S(1)}, f32[64,384]{1,0:T(8,128)S(1)}, u32[]{:S(2)}, u32[]{:S(2)}) collective-permute-start(f32[64,384]{1,0:T(8,128)S(1)} %slice_select_fusion.1), channel_id=1, source_target_pairs={{0,4},{1,5},{2,6},{3,7},{4,0},{5,1},{6,2},{7,3},{8,12},{9,13},{10,... | collective-permute-start | bytes 294920 | tf_op jit(solution)/shard_map/ppermute | solution.py:140
  443.4 16.1 %collective-permute-start.12 = (f32[514,66]{0,1:T(8,128)S(1)}, f32[514,66]{0,1:T(8,128)S(1)}, u32[]{:S(2)}, u32[]{:S(2)}) collective-permute-start(f32[514,66]{0,1:T(8,128)S(1)} %add.298), channel_id=1, source_target_pairs={{0,4},{1,5},{2,6},{3,7},{4,0},{5,1},{6,2},{7,3},{8,12},{9,13},{10,... | collective-permute-start | bytes 407096 | tf_op jit(solution)/shard_map/ppermute | solution.py:35
  447.5 18.7 %collective-permute-start.9 = (f32[64,384]{1,0:T(8,128)S(1)}, f32[64,384]{1,0:T(8,128)S(1)}, u32[]{:S(2)}, u32[]{:S(2)}) collective-permute-start(f32[64,384]{1,0:T(8,128)S(1)} %select_add_fusion.2), channel_id=1, source_target_pairs={{0,0},{1,8},{2,16},{3,24},{4,32},{5,40},{6,48},{7,56},{8,1},{9,9},... | collective-permute-start | bytes 294920 | tf_op jit(solution)/shard_map/ppermute | solution.py:147
  460.1 6.9 %collective-permute-start.13 = (bf16[1,4096]{1,0:T(2,128)(2,1)S(1)}, bf16[1,4096]{1,0:T(2,128)(2,1)S(1)}, u32[]{:S(2)}, u32[]{:S(2)}) collective-permute-start(bf16[1,4096]{1,0:T(2,128)(2,1)S(1)} %slice.297), channel_id=1, source_target_pairs={{0,8},{8,16},{16,24},{24,32},{32,40},{40,48},{48,56},{1,9},{9,17},... | collective-permute-start | bytes 24584 | tf_op jit(solution)/shard_map/ppermute | solution.py:23
  462.2 7.7 %collective-permute-start.14 = (bf16[1,4096]{1,0:T(2,128)(2,1)S(1)}, bf16[1,4096]{1,0:T(2,128)(2,1)S(1)}, u32[]{:S(2)}, u32[]{:S(2)}) collective-permute-start(bf16[1,4096]{1,0:T(2,128)(2,1)S(1)} %slice.299), channel_id=1, source_target_pairs={{8,0},{16,8},{24,16},{32,24},{40,32},{48,40},{56,48},{9,1},{17,9},... | collective-permute-start | bytes 24584 | tf_op jit(solution)/shard_map/ppermute | solution.py:26
  471.4 0.6 copy-start.16
Sparse Core Ops, SparseCore 0:
  9.9 46.9 all-gather.3
  58.7 78.2 all-gather.5
  150.7 78.5 all-gather.7
  231.7 49.6 reduce-scatter.4
  367.8 55.4 reduce-scatter.6

commit v8 on v6

--- a/solution.py
+++ b/solution.py
@@ -242,9 +242,7 @@
     img_mixed = add_rows(img_norm, img_weights)
     txt_norm, img_norm = lax.optimization_barrier((txt_norm, img_norm))
     txt_norm_rows = lax.all_to_all(txt_norm, "seq", 1, 0, tiled=True)
-    txt_mixed = lax.psum_scatter(
-        add_rows(txt_norm_rows, txt_qkv), "seq", scatter_dimension=0, tiled=True
-    )
+    txt_mixed = halving_scatter(add_rows(txt_norm_rows, txt_qkv), "seq", 0, (4, 1, 2))
     head_dim = qk_gains.shape[1]
     grid_side = latent.shape[0] * seq_count
     token_ids = seq_at * img_rows + jnp.arange(img_rows, dtype=jnp.int32)

time: 433 us -> 451 us (1.042)
  waiting for transfers between devices: 263 us -> 274 us
  starting transfers between devices: 29.8 us -> 37.5 us
    ppermute x3 -> x6, waiting for transfers between devices: 0.45 us -> 77.3 us  [halving_scatter(): lax.ppermute(sent, axis, [(i, i ^ step) for i in range(count)])]
    all_gather x1, waiting for transfers between devices: 42.1 us -> 0.01 us  [per_device(): lax.all_gather(jnp.concatenate([img_key.reshape(img_rows, kv_width), img_...]
    reduce_scatter x1 -> x0, waiting for transfers between devices: 31.2 us -> none  [per_device(): lax.psum_scatter(add_rows(txt_norm_rows, txt_qkv), 'seq', scatter_dimensi...]
    all_gather x1, waiting for transfers between devices: 25.6 us -> 0.01 us  [per_device(): img_out_full = lax.all_gather(img_out_w, 'seq', axis=1, tiled=True)]
    all_gather x1, waiting for transfers between devices: 55.9 us -> 74.4 us  [per_device(): img_weights = lax.all_gather(img_qkv, 'seq', axis=0, tiled=True)]
    all_gather x1, waiting for transfers between devices: 26.5 us -> 44.3 us  [per_device(): lax.all_gather(img_hidden, 'tp', axis=1, tiled=True)]
    ppermute x3 -> x6, starting transfers between devices: 4.91 us -> 12 us  [halving_scatter(): lax.ppermute(sent, axis, [(i, i ^ step) for i in range(count)])]
    unnamed x7 -> x6, waiting for transfers between devices: 28.8 us -> 27.5 us
  transfers between devices with their start and end apart: 19 -> 21, of which waited for: 15 -> 14; matrix products, arithmetic and copies ran while one was open for 10% -> 6% of each run, Pallas kernels for 5% -> 4%
where the time goes in v8:
time: 451 us; the launch traced here: 449 us
  waiting for transfers between devices  274 us (61%)
  blocking collectives  49.7 us (11%)
  starting transfers between devices  37.5 us (8%)
  other arithmetic  20.8 us (5%)
  Pallas kernels  20.1 us (4%)
  local copies, waits for them, and re-layouts  17.3 us (4%)
  between operations  16.1 us (4%)
  matrix products  12.9 us (3%)
    ppermute x6, waiting for transfers between devices, halving_scatter(): lax.ppermute(sent, axis, [(i, i ^ step) for i in range(count)])  77.3 us
    all_gather x1, waiting for transfers between devices, per_device(): img_weights = lax.all_gather(img_qkv, 'seq', axis=0, tiled=True)  74.4 us
    all_gather x1, waiting for transfers between devices, per_device(): lax.all_gather(img_hidden, 'tp', axis=1, tiled=True)  44.3 us
    all_gather x1, blocking collectives, per_device(): lax.all_gather(jnp.concatenate([txt_key.reshape(txt_rows, kv_width), txt_...  32.6 us
    unnamed x6, waiting for transfers between devices  27.5 us
    ppermute x3, waiting for transfers between devices, tree_sum(): lax.ppermute(block, axis, [(i, i ^ step) for i in range(count)])  21.2 us
    pallas_call x1, Pallas kernels, attention(): pl.pallas_call(functools.partial(attend_block, scale=head_dim ** (-0.5)),...  20.1 us
    ppermute x3, waiting for transfers between devices, doubling_gather(): other = lax.ppermute(stacked, axis, [(i, i ^ step) for i in range(count)])  17.5 us
  transfers between devices with their start and end apart: 21, of which 14 were waited for; matrix products, arithmetic and copies ran while one was open for 6% of the time, Pallas kernels for 4%

profile of v8, /device:TPU:26, one launch (start us, length us, event | category | flops | bytes accessed | tf_op | source)
XLA Modules:
  0.0 448.5 jit_solution(557667955143928662)
XLA Ops:
  7.2 0.7 all-gather.5.cloned.1.call-update
  8.0 2.3 copy.76
  10.4 0.5 slice_bitcast_fusion.1
  11.3 1.2 fusion.24
  12.6 44.3 %all-gather.5.cloned.1.call-done = bf16[512,3072]{1,0:T(8,128)(2,1)} async-done(((bf16[512,384]{1,0:T(8,128)(2,1)}), bf16[512,3072]{1,0:T(8,128)(2,1)}) %all-gather.5.cloned.1.call-update) | async-done | bytes 3145744 | tf_op jit(solution)/shard_map/all_gather | solution.py:233
  56.9 2.5 convert_reduce_fusion
  59.7 1.0 fusion.2
  60.7 1.8 fusion.5
  62.5 74.4 %all-gather.7.cloned.1.call-done = bf16[3072,3,384]{0,2,1:T(8,128)(2,1)} async-done(((bf16[384,3,384]{0,2,1:T(8,128)(2,1)}), bf16[3072,3,384]{0,2,1:T(8,128)(2,1)}) %all-gather.7.cloned.1.call-update) | async-done | bytes 7077904 | tf_op jit(solution)/shard_map/all_gather | solution.py:239
  137.0 6.1 %fusion.6 = f32[512,3,3,128]{0,3,2,1:T(8,128)S(1)} fusion(bf16[3,3,128,3072]{3,2,1,0:T(8,128)(2,1)} %bitcast.205, bf16[512,3072]{1,0:T(8,128)(2,1)S(1)} %fusion.5), kind=kOutput, calls=%fused_computation.9 | convolution fusion | flops 3623878656 | bytes 12582912 | tf_op jit(solution)/shard_map/dot_general | solution.py:206
  143.4 0.5 squeeze.59
  143.9 0.5 squeeze.61
  144.4 0.3 multiply_multiply_fusion.1
  144.8 0.3 multiply_multiply_fusion
  145.1 2.8 subtract_convert_fusion
  148.0 0.9 pad_maximum_fusion.9
  149.5 1.0 pad_maximum_fusion.6
  150.6 17.1 %all_gather.18 = bf16[64,3072]{1,0:T(8,128)(2,1)S(1)} all-gather(bf16[64,384]{1,0:T(8,128)(2,1)S(1)} %copy-done.11), channel_id=1, replica_groups=mesh['req'=4,'seq'=8,'tp'=8] {'tp'}, dimensions={1}, use_global_device_ids=true | all-gather | bytes 442368 | tf_op jit(solution)/shard_map/all_gather | solution.py:234
  168.1 0.6 fusion.87
  169.0 0.8 copy.104
  169.8 6.0 %all-to-all-start = ((bf16[64,8,384]{2,0,1:T(8,128)(2,1)}), bf16[64,8,384]{2,0,1:T(8,128)(2,1)S(1)}, u32[]{:S(2)}, u32[]{:S(2)}) async-start(bf16[64,8,384]{2,0,1:T(8,128)(2,1)} %bitcast.169), calls=%async_computation | async-start | bytes 786432 | tf_op jit(solution)/shard_map/all_to_all | solution.py:244
  175.8 2.4 copy.73
  178.2 9.1 %all-to-all-done = bf16[64,8,384]{2,0,1:T(8,128)(2,1)S(1)} async-done(((bf16[64,8,384]{2,0,1:T(8,128)(2,1)}), bf16[64,8,384]{2,0,1:T(8,128)(2,1)S(1)}, u32[]{:S(2)}, u32[]{:S(2)}) %all-to-all-start) | async-done | bytes 393248 | tf_op jit(solution)/shard_map/all_to_all | solution.py:244
  187.2 0.8 fusion.90
  188.2 0.7 copy-done.2
  189.1 0.7 collective-permute-start
  189.8 53.2 %collective-permute-done = f32[256,1152]{1,0:T(8,128)} collective-permute-done((f32[256,1152]{1,0:T(8,128)S(1)}, f32[256,1152]{1,0:T(8,128)}, u32[]{:S(2)}, u32[]{:S(2)}) %collective-permute-start) | collective-permute-done | bytes 1179680 | tf_op jit(solution)/shard_map/ppermute | solution.py:140
  243.0 1.5 select_add_fusion
  245.5 14.2 %collective-permute-done.1 = f32[128,1152]{1,0:T(8,128)S(1)} collective-permute-done((f32[128,1152]{1,0:T(8,128)S(1)}, f32[128,1152]{1,0:T(8,128)S(1)}, u32[]{:S(2)}, u32[]{:S(2)}) %collective-permute-start.1) | collective-permute-done | bytes 589856 | tf_op jit(solution)/shard_map/ppermute | solution.py:140
  259.8 5.7 %collective-permute-start.2 = (f32[64,1152]{1,0:T(8,128)S(1)}, f32[64,1152]{1,0:T(8,128)S(1)}, u32[]{:S(2)}, u32[]{:S(2)}) collective-permute-start(f32[64,1152]{1,0:T(8,128)S(1)} %slice_select_fusion.1), channel_id=1, source_target_pairs={{0,16},{8,24},{16,0},{24,8},{32,48},{40,56},{48,32},{56,40},{1,17}... | collective-permute-start | bytes 884744 | tf_op jit(solution)/shard_map/ppermute | solution.py:140
  265.5 0.6 compare_convert_fusion.keep_ref
  266.1 9.9 %collective-permute-done.2 = f32[64,1152]{1,0:T(8,128)S(1)} collective-permute-done((f32[64,1152]{1,0:T(8,128)S(1)}, f32[64,1152]{1,0:T(8,128)S(1)}, u32[]{:S(2)}, u32[]{:S(2)}) %collective-permute-start.2) | collective-permute-done | bytes 294944 | tf_op jit(solution)/shard_map/ppermute | solution.py:140
  276.8 32.6 %all_gather.21.tkey_ref.tvalue_ref = bf16[512,768]{1,0:T(8,128)(2,1)} all-gather(bf16[64,768]{1,0:T(8,128)(2,1)S(1)} %pad_maximum_fusion.15), channel_id=1, replica_groups=mesh['req'=4,'seq'=8,'tp'=8] {'seq'}, dimensions={0}, use_global_device_ids=true | all-gather | bytes 884736 | tf_op jit(solution)/shard_map/all_gather | solution.py:266
  309.4 0.9 pad_maximum_fusion.8
  310.6 0.8 pad_maximum_fusion.7.query_ref
  311.5 20.1 %shard_map.182 = bf16[576,384]{1,0:T(8,128)(2,1)} custom-call(f32[1,512]{1,0:T(1,128)} %compare_convert_fusion.keep_ref, bf16[576,384]{1,0:T(8,128)(2,1)} %pad_maximum_fusion.7.query_ref, bf16[512,768]{1,0:T(8,128)(2,1)} %all_gather.21.tkey_ref.tvalue_ref, bf16[512,768]{1,0:T(8,128)(2,1)} %all_gather.21.tkey_ref.tvalue_ref, ...), custom_call_target="tpu_custom_call" | custom-call | tf_op jit(solution)/shard_map/pallas_call | solution.py:83
  331.6 3.6 convolution_convert_fusion
  335.2 2.8 copy.88
  338.0 0.8 slice_bitcast_fusion
  338.8 1.9 collective-permute-start.3
  340.8 3.7 collective-permute-done.3
  344.4 0.8 select_bitcast_fusion.5
  345.4 4.6 %collective-permute-done.4 = bf16[2,64,384]{2,1,0:T(8,128)(2,1)S(1)} collective-permute-done((bf16[2,64,384]{2,1,0:T(8,128)(2,1)S(1)}, bf16[2,64,384]{2,1,0:T(8,128)(2,1)S(1)}, u32[]{:S(2)}, u32[]{:S(2)}) %collective-permute-start.4) | collective-permute-done | bytes 98336 | tf_op jit(solution)/shard_map/ppermute | solution.py:108
  350.0 2.2 collective-permute-start.5
  352.3 9.2 %collective-permute-done.5 = bf16[4,64,384]{2,1,0:T(8,128)(2,1)S(1)} collective-permute-done((bf16[4,64,384]{2,1,0:T(8,128)(2,1)S(1)}, bf16[4,64,384]{2,1,0:T(8,128)(2,1)S(1)}, u32[]{:S(2)}, u32[]{:S(2)}) %collective-permute-start.5) | collective-permute-done | bytes 196640 | tf_op jit(solution)/shard_map/ppermute | solution.py:108
  361.8 0.4 fusion.8
  363.7 0.7 fusion.72
  364.5 2.3 collective-permute-start.7
  366.8 26.7 %reduce-scatter.4.cloned.1.call-done = bf16[384,512]{1,0:T(8,128)(2,1)} async-done(((bf16[3072,512]{1,0:T(8,128)(2,1)}), bf16[384,512]{1,0:T(8,128)(2,1)}) %reduce-scatter.4.cloned.1.call-update) | async-done | bytes 393232
  393.5 1.2 copy.89
  395.1 0.6 fusion.15
  395.7 2.0 collective-permute-start.10
  397.7 1.0 collective-permute-done.10
  398.7 1.1 collective-permute-start.11
  399.9 3.1 collective-permute-start.8
  403.0 10.7 %collective-permute-done.11 = f32[514,66]{0,1:T(8,128)S(1)} collective-permute-done((f32[514,66]{0,1:T(8,128)S(1)}, f32[514,66]{0,1:T(8,128)S(1)}, u32[]{:S(2)}, u32[]{:S(2)}) %collective-permute-start.11) | collective-permute-done | bytes 135728 | tf_op jit(solution)/shard_map/ppermute | solution.py:35
  413.7 4.2 collective-permute-start.12
  418.0 1.9 collective-permute-start.9
  419.9 9.5 %collective-permute-done.12 = f32[514,66]{0,1:T(8,128)S(1)} collective-permute-done((f32[514,66]{0,1:T(8,128)S(1)}, f32[514,66]{0,1:T(8,128)S(1)}, u32[]{:S(2)}, u32[]{:S(2)}) %collective-permute-start.12) | collective-permute-done | bytes 135728 | tf_op jit(solution)/shard_map/ppermute | solution.py:35
  430.1 1.9 collective-permute-start.13
  432.2 3.9 collective-permute-start.14
  436.1 0.7 fusion.25
  437.1 2.8 collective-permute-done.14
  441.4 0.6 multiply_subtract_fusion
  (161 shorter events, 8.4 us)
Async XLA Ops:
  7.2 354.6 %copy-start = (bf16[384,384]{1,0:T(8,128)(2,1)S(1)}, bf16[384,384]{1,0:T(8,128)(2,1)}, u32[]{:S(2)}) copy-start(bf16[384,384]{1,0:T(8,128)(2,1)} %param.23) | copy-start | bytes 884740
  7.2 3.2 copy-start.14
  7.2 3.2 copy-start.19
  7.2 49.7 %all-gather.5.cloned.1.call-start = ((), (), s32[]{:S(2)}) async-start(), calls=%async_computation.2 | async-start | bytes 3538944 | tf_op jit(solution)/shard_map/all_gather | solution.py:233
  7.9 129.0 %all-gather.7.cloned.1.call-start = ((), (), s32[]{:S(2)}) async-start(), calls=%async_computation.3 | async-start | bytes 7962624 | tf_op jit(solution)/shard_map/all_gather | solution.py:239
  10.3 301.2 %all-gather.9.cloned.1.call-start = ((), (), s32[]{:S(2)}) async-start(), calls=%async_computation.4 | async-start | bytes 7077888 | tf_op jit(solution)/shard_map/all_gather | solution.py:258
  56.9 2.8 copy-start.1
  143.9 1.2 copy-start.8
  143.9 1.2 copy-start.9
  148.8 1.7 copy-start.15
  148.9 1.7 copy-start.11
  150.5 25.3 %copy-start.7 = (bf16[384,3,384]{2,0,1:T(8,128)(2,1)S(1)}, bf16[384,3,384]{2,0,1:T(8,128)(2,1)}, u32[]{:S(2)}) copy-start(bf16[384,3,384]{2,0,1:T(8,128)(2,1)} %param.20) | copy-start | bytes 2654212
  169.8 17.5 %all-to-all-start = ((bf16[64,8,384]{2,0,1:T(8,128)(2,1)}), bf16[64,8,384]{2,0,1:T(8,128)(2,1)S(1)}, u32[]{:S(2)}, u32[]{:S(2)}) async-start(bf16[64,8,384]{2,0,1:T(8,128)(2,1)} %bitcast.169), calls=%async_computation | async-start | bytes 786432 | tf_op jit(solution)/shard_map/all_to_all | solution.py:244
  175.8 155.8 %all-gather.11.cloned.1.call-start = ((), (), s32[]{:S(2)}) async-start(), calls=%async_computation.5 | async-start | bytes 2654208 | tf_op jit(solution)/shard_map/all_gather | solution.py:241
  188.2 0.7 copy-start.2
  189.1 53.9 %collective-permute-start = (f32[256,1152]{1,0:T(8,128)S(1)}, f32[256,1152]{1,0:T(8,128)}, u32[]{:S(2)}, u32[]{:S(2)}) collective-permute-start(f32[256,1152]{1,0:T(8,128)S(1)} %broadcast_select_fusion), channel_id=1, source_target_pairs={{0,32},{8,40},{16,48},{24,56},{32,0},{40,8},{48,16},{56,24},{1,33}... | collective-permute-start | bytes 3538952 | tf_op jit(solution)/shard_map/ppermute | solution.py:140
  244.6 21.5 %copy-start.20 = (f32[128]{0:T(128)S(1)}, f32[128]{0:T(128)}, u32[]{:S(2)}) copy-start(f32[128]{0:T(128)} %get-tuple-element.67) | copy-start | bytes 1540
  244.6 149.0 %reduce-scatter.4.cloned.1.call-start = ((), (), s32[]{:S(2)}) async-start(), calls=%async_computation.6 | async-start | bytes 3538944
  244.7 14.9 %collective-permute-start.1 = (f32[128,1152]{1,0:T(8,128)S(1)}, f32[128,1152]{1,0:T(8,128)S(1)}, u32[]{:S(2)}, u32[]{:S(2)}) collective-permute-start(f32[128,1152]{1,0:T(8,128)S(1)} %slice_select_fusion), channel_id=1, source_target_pairs={{0,8},{8,0},{16,24},{24,16},{32,40},{40,32},{48,56},{56,48},{1,9},... | collective-permute-start | bytes 1769480 | tf_op jit(solution)/shard_map/ppermute | solution.py:140
  259.8 16.2 %collective-permute-start.2 = (f32[64,1152]{1,0:T(8,128)S(1)}, f32[64,1152]{1,0:T(8,128)S(1)}, u32[]{:S(2)}, u32[]{:S(2)}) collective-permute-start(f32[64,1152]{1,0:T(8,128)S(1)} %slice_select_fusion.1), channel_id=1, source_target_pairs={{0,16},{8,24},{16,0},{24,8},{32,48},{40,56},{48,32},{56,40},{1,17}... | collective-permute-start | bytes 884744 | tf_op jit(solution)/shard_map/ppermute | solution.py:140
  266.1 43.3 %copy-start.5 = (bf16[512,3,64,1]{0,3,2,1:T(2,128)(2,1)S(1)}, bf16[512,3,64,1]{0,3,2,1:T(2,128)(2,1)}, u32[]{:S(2)}) copy-start(bf16[512,3,64,1]{0,3,2,1:T(2,128)(2,1)} %get-tuple-element.48) | copy-start | bytes 589828
  266.1 43.3 %copy-start.6 = (bf16[512,3,64,1]{0,3,2,1:T(2,128)(2,1)S(1)}, bf16[512,3,64,1]{0,3,2,1:T(2,128)(2,1)}, u32[]{:S(2)}) copy-start(bf16[512,3,64,1]{0,3,2,1:T(2,128)(2,1)} %get-tuple-element.49) | copy-start | bytes 589828
  338.0 14.3 %copy-start.17 = (bf16[2,3072]{1,0:T(2,128)(2,1)S(1)}, bf16[2,3072]{1,0:T(2,128)(2,1)}, u32[]{:S(2)}) copy-start(bf16[2,3072]{1,0:T(2,128)(2,1)} %param.24) | copy-start | bytes 36868
  338.8 5.6 %collective-permute-start.3 = (bf16[1,64,384]{2,1,0:T(8,128)(2,1)S(1)}, bf16[1,64,384]{2,1,0:T(8,128)(2,1)S(1)}, u32[]{:S(2)}, u32[]{:S(2)}) collective-permute-start(bf16[1,64,384]{2,1,0:T(8,128)(2,1)S(1)} %slice_bitcast_fusion), channel_id=1, source_target_pairs={{0,16},{8,24},{16,0},{24,8},{32,48},{40,56},{48,32},{56,40},{1,17}... | collective-permute-start | bytes 147464 | tf_op jit(solution)/shard_map/ppermute | solution.py:108
  345.3 4.7 %collective-permute-start.4 = (bf16[2,64,384]{2,1,0:T(8,128)(2,1)S(1)}, bf16[2,64,384]{2,1,0:T(8,128)(2,1)S(1)}, u32[]{:S(2)}, u32[]{:S(2)}) collective-permute-start(bf16[2,64,384]{2,1,0:T(8,128)(2,1)S(1)} %maximum_bitcast_fusion), channel_id=1, source_target_pairs={{0,8},{8,0},{16,24},{24,16},{32,40},{40,32},{48,56},{56,48},{1,9},... | collective-permute-start | bytes 294920 | tf_op jit(solution)/shard_map/ppermute | solution.py:108
  350.0 11.5 %collective-permute-start.5 = (bf16[4,64,384]{2,1,0:T(8,128)(2,1)S(1)}, bf16[4,64,384]{2,1,0:T(8,128)(2,1)S(1)}, u32[]{:S(2)}, u32[]{:S(2)}) collective-permute-start(bf16[4,64,384]{2,1,0:T(8,128)(2,1)S(1)} %bitcast.185), channel_id=1, source_target_pairs={{0,32},{8,40},{16,48},{24,56},{32,0},{40,8},{48,16},{56,24},{1,33}... | collective-permute-start | bytes 589832 | tf_op jit(solution)/shard_map/ppermute | solution.py:108
  361.7 0.8 copy-start.10
  362.3 32.5 %copy-start.3 = (bf16[512,384]{1,0:T(8,128)(2,1)S(1)}, bf16[512,384]{1,0:T(8,128)(2,1)}, u32[]{:S(2)}) copy-start(bf16[512,384]{1,0:T(8,128)(2,1)} %param.15) | copy-start | bytes 1179652
  362.3 2.1 collective-permute-start.6
  364.5 33.1 %collective-permute-start.7 = (f32[128,384]{1,0:T(8,128)S(1)}, f32[128,384]{1,0:T(8,128)S(1)}, u32[]{:S(2)}, u32[]{:S(2)}) collective-permute-start(f32[128,384]{1,0:T(8,128)S(1)} %slice_select_fusion.2), channel_id=1, source_target_pairs={{0,2},{1,3},{2,0},{3,1},{4,6},{5,7},{6,4},{7,5},{8,10},{9,11},{10,... | collective-permute-start | bytes 589832 | tf_op jit(solution)/shard_map/ppermute | solution.py:140
  395.1 41.8 %copy-start.4 = (bf16[512,384]{1,0:T(8,128)(2,1)}, bf16[512,384]{1,0:T(8,128)(2,1)S(1)}, u32[]{:S(2)}) copy-start(bf16[512,384]{1,0:T(8,128)(2,1)S(1)} %get-tuple-element.21) | copy-start | bytes 1179652
  395.1 41.1 %copy-start.12 = (bf16[64,384]{1,0:T(8,128)(2,1)S(1)}, bf16[64,384]{1,0:T(8,128)(2,1)}, u32[]{:S(2)}) copy-start(bf16[64,384]{1,0:T(8,128)(2,1)} %param.16) | copy-start | bytes 147460
  395.7 44.5 %copy-start.13 = (bf16[3,3,64,64]{3,2,1,0:T(8,128)(2,1)S(1)}, bf16[3,3,64,64]{3,2,1,0:T(8,128)(2,1)}, u32[]{:S(2)}) copy-start(bf16[3,3,64,64]{3,2,1,0:T(8,128)(2,1)} %param.26) | copy-start | bytes 221188
  395.7 3.0 collective-permute-start.10
  397.7 43.7 %copy-start.18 = (f32[8,512]{1,0:T(8,128)S(1)}, f32[8,512]{1,0:T(8,128)}, u32[]{:S(2)}) copy-start(f32[8,512]{1,0:T(8,128)} %param.27) | copy-start | bytes 49156
  398.7 15.0 %collective-permute-start.11 = (f32[514,66]{0,1:T(8,128)S(1)}, f32[514,66]{0,1:T(8,128)S(1)}, u32[]{:S(2)}, u32[]{:S(2)}) collective-permute-start(f32[514,66]{0,1:T(8,128)S(1)} %fusion.83), channel_id=1, source_target_pairs={{0,2},{1,3},{2,0},{3,1},{4,6},{5,7},{6,4},{7,5},{8,10},{9,11},{10,... | collective-permute-start | bytes 407096 | tf_op jit(solution)/shard_map/ppermute | solution.py:35
  399.9 18.1 %collective-permute-start.8 = (f32[64,384]{1,0:T(8,128)S(1)}, f32[64,384]{1,0:T(8,128)S(1)}, u32[]{:S(2)}, u32[]{:S(2)}) collective-permute-start(f32[64,384]{1,0:T(8,128)S(1)} %slice_select_fusion.3), channel_id=1, source_target_pairs={{0,4},{1,5},{2,6},{3,7},{4,0},{5,1},{6,2},{7,3},{8,12},{9,13},{10,... | collective-permute-start | bytes 294920 | tf_op jit(solution)/shard_map/ppermute | solution.py:140
  413.7 15.7 %collective-permute-start.12 = (f32[514,66]{0,1:T(8,128)S(1)}, f32[514,66]{0,1:T(8,128)S(1)}, u32[]{:S(2)}, u32[]{:S(2)}) collective-permute-start(f32[514,66]{0,1:T(8,128)S(1)} %add.308), channel_id=1, source_target_pairs={{0,4},{1,5},{2,6},{3,7},{4,0},{5,1},{6,2},{7,3},{8,12},{9,13},{10,... | collective-permute-start | bytes 407096 | tf_op jit(solution)/shard_map/ppermute | solution.py:35
  418.0 18.1 %collective-permute-start.9 = (f32[64,384]{1,0:T(8,128)S(1)}, f32[64,384]{1,0:T(8,128)S(1)}, u32[]{:S(2)}, u32[]{:S(2)}) collective-permute-start(f32[64,384]{1,0:T(8,128)S(1)} %select_add_fusion.5), channel_id=1, source_target_pairs={{0,0},{1,8},{2,16},{3,24},{4,32},{5,40},{6,48},{7,56},{8,1},{9,9},... | collective-permute-start | bytes 294920 | tf_op jit(solution)/shard_map/ppermute | solution.py:147
  430.1 6.9 %collective-permute-start.13 = (bf16[1,4096]{1,0:T(2,128)(2,1)S(1)}, bf16[1,4096]{1,0:T(2,128)(2,1)S(1)}, u32[]{:S(2)}, u32[]{:S(2)}) collective-permute-start(bf16[1,4096]{1,0:T(2,128)(2,1)S(1)} %slice.323), channel_id=1, source_target_pairs={{0,8},{8,16},{16,24},{24,32},{32,40},{40,48},{48,56},{1,9},{9,17},... | collective-permute-start | bytes 24584 | tf_op jit(solution)/shard_map/ppermute | solution.py:23
  432.2 7.7 %collective-permute-start.14 = (bf16[1,4096]{1,0:T(2,128)(2,1)S(1)}, bf16[1,4096]{1,0:T(2,128)(2,1)S(1)}, u32[]{:S(2)}, u32[]{:S(2)}) collective-permute-start(bf16[1,4096]{1,0:T(2,128)(2,1)S(1)} %slice.325), channel_id=1, source_target_pairs={{8,0},{16,8},{24,16},{32,24},{40,32},{48,40},{56,48},{9,1},{17,9},... | collective-permute-start | bytes 24584 | tf_op jit(solution)/shard_map/ppermute | solution.py:26
  441.4 0.6 copy-start.16
Sparse Core Ops, SparseCore 0:
  9.9 46.9 all-gather.4
  58.7 78.2 all-gather.6
  150.6 103.8 all-gather.8
  256.1 48.1 all-gather.10
  338.2 55.3 reduce-scatter.3

commit v9 on v8

--- a/solution.py
+++ b/solution.py
@@ -239,10 +239,22 @@
     img_weights = lax.all_gather(img_qkv, "seq", axis=0, tiled=True)
     img_weights, img_out_w = lax.optimization_barrier((img_weights, img_out_w))
     img_out_full = lax.all_gather(img_out_w, "seq", axis=1, tiled=True)
-    img_mixed = add_rows(img_norm, img_weights)
-    txt_norm, img_norm = lax.optimization_barrier((txt_norm, img_norm))
     txt_norm_rows = lax.all_to_all(txt_norm, "seq", 1, 0, tiled=True)
     txt_mixed = halving_scatter(add_rows(txt_norm_rows, txt_qkv), "seq", 0, (4, 1, 2))
+    head_dim = qk_gains.shape[1]
+    txt_query, txt_key, txt_value = split_heads(txt_mixed, qk_gains[2], qk_gains[3], None)
+    heads_local = txt_query.shape[1]
+    kv_width = heads_local * head_dim
+    text_kv = lax.all_gather(
+        jnp.concatenate(
+            [txt_key.reshape(txt_rows, kv_width), txt_value.reshape(txt_rows, kv_width)], 1
+        ),
+        "seq",
+        axis=0,
+        tiled=True,
+    )
+    text_kv, txt_query, img_norm = lax.optimization_barrier((text_kv, txt_query, img_norm))
+    img_mixed = add_rows(img_norm, img_weights)
     head_dim = qk_gains.shape[1]
     grid_side = latent.shape[0] * seq_count
     token_ids = seq_at * img_rows + jnp.arange(img_rows, dtype=jnp.int32)
@@ -250,7 +262,6 @@
     col_pos = (token_ids % grid_side).astype(jnp.float32)
     angles = rope_angles(row_pos, col_pos, head_dim)
     img_query, img_key, img_value = split_heads(img_mixed, qk_gains[0], qk_gains[1], angles)
-    txt_query, txt_key, txt_value = split_heads(txt_mixed, qk_gains[2], qk_gains[3], None)
     local_len = txt_rows + img_rows
     heads_local = img_query.shape[1]
     kv_width = heads_local * head_dim
@@ -258,14 +269,6 @@
     img_kv = lax.all_gather(
         jnp.concatenate(
             [img_key.reshape(img_rows, kv_width), img_value.reshape(img_rows, kv_width)], 1
-        ),
-        "seq",
-        axis=0,
-        tiled=True,
-    )
-    text_kv = lax.all_gather(
-        jnp.concatenate(
-            [txt_key.reshape(txt_rows, kv_width), txt_value.reshape(txt_rows, kv_width)], 1
         ),
         "seq",
         axis=0,

time: 451 us -> 434 us (0.962)
  waiting for transfers between devices: 274 us -> 258 us
    all_gather x1, waiting for transfers between devices: 74.4 us -> 0.02 us  [per_device(): img_weights = lax.all_gather(img_qkv, 'seq', axis=0, tiled=True)]
    all_gather x1, waiting for transfers between devices: 0.01 us -> 67.7 us  [per_device(): lax.all_gather(jnp.concatenate([img_key.reshape(img_rows, kv_width), img_...]
    all_gather x1, waiting for transfers between devices: 44.3 us -> 0.01 us  [per_device(): lax.all_gather(img_hidden, 'tp', axis=1, tiled=True)]
    all_gather x1, waiting for transfers between devices: 0.01 us -> 25.8 us  [per_device(): img_out_full = lax.all_gather(img_out_w, 'seq', axis=1, tiled=True)]
    all_to_all x1, waiting for transfers between devices: 9.09 us -> 15.8 us  [per_device(): txt_norm_rows = lax.all_to_all(txt_norm, 'seq', 1, 0, tiled=True)]
    unnamed x53 -> x51, local copies, waits for them, and re-layouts: 9.95 us -> 9.23 us
  transfers between devices with their start and end apart: 21 -> 21, of which waited for: 14 -> 14; matrix products, arithmetic and copies ran while one was open for 6% -> 7% of each run, Pallas kernels for 4% -> 5%
where the time goes in v9:
time: 434 us; the launch traced here: 433 us
  waiting for transfers between devices  258 us (59%)
  blocking collectives  52 us (12%)
  starting transfers between devices  33 us (8%)
  other arithmetic  21.1 us (5%)
  Pallas kernels  20.1 us (5%)
  local copies, waits for them, and re-layouts  19.4 us (4%)
  between operations  16.1 us (4%)
  matrix products  12.9 us (3%)
    ppermute x6, waiting for transfers between devices, halving_scatter(): lax.ppermute(sent, axis, [(i, i ^ step) for i in range(count)])  79.4 us
    all_gather x1, waiting for transfers between devices, per_device(): lax.all_gather(jnp.concatenate([img_key.reshape(img_rows, kv_width), img_...  67.7 us
    all_gather x1, blocking collectives, per_device(): lax.all_gather(jnp.concatenate([txt_key.reshape(txt_rows, kv_width), txt_...  33.3 us
    unnamed x6, waiting for transfers between devices  28 us
    all_gather x1, waiting for transfers between devices, per_device(): img_out_full = lax.all_gather(img_out_w, 'seq', axis=1, tiled=True)  25.8 us
    ppermute x3, waiting for transfers between devices, tree_sum(): lax.ppermute(block, axis, [(i, i ^ step) for i in range(count)])  20.3 us
    pallas_call x1, Pallas kernels, attention(): pl.pallas_call(functools.partial(attend_block, scale=head_dim ** (-0.5)),...  20.1 us
    all_gather x1, blocking collectives, per_device(): lax.all_gather(txt_hidden, 'tp', axis=1, tiled=True)  18.7 us
  transfers between devices with their start and end apart: 21, of which 14 were waited for; matrix products, arithmetic and copies ran while one was open for 7% of the time, Pallas kernels for 5%

profile of v9, /device:TPU:26, one launch (start us, length us, event | category | flops | bytes accessed | tf_op | source)
XLA Modules:
  0.0 432.6 jit_solution(12739883898807902064)
XLA Ops:
  7.2 0.7 all-gather.5.cloned.1.call-update
  8.0 2.3 copy.82
  10.3 18.7 %all_gather.18 = bf16[64,3072]{1,0:T(8,128)(2,1)S(1)} all-gather(bf16[64,384]{1,0:T(8,128)(2,1)S(1)} %copy-done.8), channel_id=1, replica_groups=mesh['req'=4,'seq'=8,'tp'=8] {'tp'}, dimensions={1}, use_global_device_ids=true | all-gather | bytes 442368 | tf_op jit(solution)/shard_map/all_gather | solution.py:234
  29.5 0.6 fusion.86
  30.3 0.8 copy.105
  31.1 5.3 %all-to-all-start = ((bf16[64,8,384]{2,0,1:T(8,128)(2,1)}), bf16[64,8,384]{2,0,1:T(8,128)(2,1)S(1)}, u32[]{:S(2)}, u32[]{:S(2)}) async-start(bf16[64,8,384]{2,0,1:T(8,128)(2,1)} %bitcast.163), calls=%async_computation | async-start | bytes 786432 | tf_op jit(solution)/shard_map/all_to_all | solution.py:242
  36.4 2.4 copy.77
  38.8 15.8 %all-to-all-done = bf16[64,8,384]{2,0,1:T(8,128)(2,1)S(1)} async-done(((bf16[64,8,384]{2,0,1:T(8,128)(2,1)}), bf16[64,8,384]{2,0,1:T(8,128)(2,1)S(1)}, u32[]{:S(2)}, u32[]{:S(2)}) %all-to-all-start) | async-done | bytes 393248 | tf_op jit(solution)/shard_map/all_to_all | solution.py:242
  54.6 0.8 fusion.89
  55.6 1.1 broadcast_select_fusion
  56.8 1.8 collective-permute-start
  58.8 0.6 slice_add_fusion
  59.4 37.8 %collective-permute-done = f32[256,1152]{1,0:T(8,128)} collective-permute-done((f32[256,1152]{1,0:T(8,128)}, f32[256,1152]{1,0:T(8,128)}, u32[]{:S(2)}, u32[]{:S(2)}) %collective-permute-start) | collective-permute-done | bytes 1179680 | tf_op jit(solution)/shard_map/ppermute | solution.py:140
  97.2 1.4 select_add_fusion
  98.8 0.6 fusion.87
  99.5 27.9 %collective-permute-done.1 = f32[128,1152]{1,0:T(8,128)S(1)} collective-permute-done((f32[128,1152]{1,0:T(8,128)S(1)}, f32[128,1152]{1,0:T(8,128)S(1)}, u32[]{:S(2)}, u32[]{:S(2)}) %collective-permute-start.1) | collective-permute-done | bytes 589856 | tf_op jit(solution)/shard_map/ppermute | solution.py:140
  127.6 0.7 mul.359
  128.4 0.8 mul.377
  129.1 1.2 fusion.24
  130.3 13.7 %collective-permute-done.2 = f32[64,1152]{1,0:T(8,128)S(1)} collective-permute-done((f32[64,1152]{1,0:T(8,128)S(1)}, f32[64,1152]{1,0:T(8,128)S(1)}, u32[]{:S(2)}, u32[]{:S(2)}) %collective-permute-start.2) | collective-permute-done | bytes 294944 | tf_op jit(solution)/shard_map/ppermute | solution.py:140
  144.9 33.3 %all_gather.19.tkey_ref.tvalue_ref = bf16[512,768]{1,0:T(8,128)(2,1)} all-gather(bf16[64,768]{1,0:T(8,128)(2,1)S(1)} %pad_maximum_fusion.15), channel_id=1, replica_groups=mesh['req'=4,'seq'=8,'tp'=8] {'seq'}, dimensions={0}, use_global_device_ids=true | all-gather | bytes 884736 | tf_op jit(solution)/shard_map/all_gather | solution.py:248
  178.2 2.5 convert_reduce_fusion
  181.0 1.0 fusion.2
  182.0 1.8 fusion.5
  183.8 6.1 %fusion.6 = f32[512,3,3,128]{0,3,2,1:T(8,128)S(1)} fusion(bf16[3,3,128,3072]{3,2,1,0:T(8,128)(2,1)} %bitcast.198, bf16[512,3072]{1,0:T(8,128)(2,1)S(1)} %fusion.5), kind=kOutput, calls=%fused_computation.9 | convolution fusion | flops 3623878656 | bytes 12582912 | tf_op jit(solution)/shard_map/dot_general | solution.py:206
  190.3 0.5 squeeze.60
  192.1 2.1 subtract_convert_fusion
  194.1 0.9 pad_maximum_fusion.9
  195.6 1.0 pad_maximum_fusion.6
  196.8 0.5 all-gather.11.cloned.1.call-update
  198.2 0.6 compare_convert_fusion.keep_ref
  198.9 0.9 pad_maximum_fusion.8
  200.2 1.0 copy.86.query_ref
  201.2 67.7 %all-gather.9.cloned.1.call-done.ikey_ref.ivalue_ref = bf16[4096,768]{1,0:T(8,128)(2,1)} async-done(((bf16[512,768]{1,0:T(8,128)(2,1)}), bf16[4096,768]{1,0:T(8,128)(2,1)}) %all-gather.9.cloned.1.call-update) | async-done | bytes 6291472 | tf_op jit(solution)/shard_map/all_gather | solution.py:269
  268.9 20.1 %shard_map.182 = bf16[576,384]{1,0:T(8,128)(2,1)} custom-call(f32[1,512]{1,0:T(1,128)} %compare_convert_fusion.keep_ref, bf16[576,384]{1,0:T(8,128)(2,1)} %copy.86.query_ref, bf16[512,768]{1,0:T(8,128)(2,1)} %all_gather.19.tkey_ref.tvalue_ref, bf16[512,768]{1,0:T(8,128)(2,1)} %all_gather.19.tkey_ref.tvalue_ref, ...), custom_call_target="tpu_custom_call" | custom-call | tf_op jit(solution)/shard_map/pallas_call | solution.py:83
  289.0 25.8 %all-gather.11.cloned.1.call-done = bf16[384,3072]{1,0:T(8,128)(2,1)} async-done(((bf16[384,384]{1,0:T(8,128)(2,1)}), bf16[384,3072]{1,0:T(8,128)(2,1)}) %all-gather.11.cloned.1.call-update) | async-done | bytes 2359312 | tf_op jit(solution)/shard_map/all_gather | solution.py:241
  314.7 3.6 convolution_convert_fusion
  318.3 2.8 copy.93
  321.2 0.8 slice_bitcast_fusion.1
  322.0 1.6 collective-permute-start.3
  323.5 4.5 %collective-permute-done.3 = bf16[1,64,384]{2,1,0:T(8,128)(2,1)S(1)} collective-permute-done((bf16[1,64,384]{2,1,0:T(8,128)(2,1)S(1)}, bf16[1,64,384]{2,1,0:T(8,128)(2,1)S(1)}, u32[]{:S(2)}, u32[]{:S(2)}) %collective-permute-start.3) | collective-permute-done | bytes 49184 | tf_op jit(solution)/shard_map/ppermute | solution.py:108
  328.0 0.8 select_bitcast_fusion.5
  328.9 1.2 collective-permute-start.4
  330.0 3.5 collective-permute-done.4
  333.6 1.5 collective-permute-start.5
  335.2 10.5 %collective-permute-done.5 = bf16[4,64,384]{2,1,0:T(8,128)(2,1)S(1)} collective-permute-done((bf16[4,64,384]{2,1,0:T(8,128)(2,1)S(1)}, bf16[4,64,384]{2,1,0:T(8,128)(2,1)S(1)}, u32[]{:S(2)}, u32[]{:S(2)}) %collective-permute-start.5) | collective-permute-done | bytes 196640 | tf_op jit(solution)/shard_map/ppermute | solution.py:108
  347.8 0.7 fusion.69
  348.5 0.7 fusion.70
  349.3 2.6 collective-permute-start.7
  351.9 26.7 %reduce-scatter.4.cloned.1.call-done = bf16[384,512]{1,0:T(8,128)(2,1)} async-done(((bf16[3072,512]{1,0:T(8,128)(2,1)}), bf16[384,512]{1,0:T(8,128)(2,1)}) %reduce-scatter.4.cloned.1.call-update) | async-done | bytes 393232
  378.6 1.2 copy.94
  380.1 0.6 fusion.15
  380.9 1.3 collective-permute-done.10
  382.3 1.4 collective-permute-start.11
  383.8 4.5 %collective-permute-start.8 = (f32[64,384]{1,0:T(8,128)S(1)}, f32[64,384]{1,0:T(8,128)S(1)}, u32[]{:S(2)}, u32[]{:S(2)}) collective-permute-start(f32[64,384]{1,0:T(8,128)S(1)} %slice_select_fusion.3), channel_id=1, source_target_pairs={{0,4},{1,5},{2,6},{3,7},{4,0},{5,1},{6,2},{7,3},{8,12},{9,13},{10,... | collective-permute-start | bytes 294920 | tf_op jit(solution)/shard_map/ppermute | solution.py:140
  388.3 9.9 %collective-permute-done.11 = f32[514,66]{0,1:T(8,128)S(1)} collective-permute-done((f32[514,66]{0,1:T(8,128)S(1)}, f32[514,66]{0,1:T(8,128)S(1)}, u32[]{:S(2)}, u32[]{:S(2)}) %collective-permute-start.11) | collective-permute-done | bytes 135728 | tf_op jit(solution)/shard_map/ppermute | solution.py:35
  398.2 4.3 %collective-permute-start.12 = (f32[514,66]{0,1:T(8,128)S(1)}, f32[514,66]{0,1:T(8,128)S(1)}, u32[]{:S(2)}, u32[]{:S(2)}) collective-permute-start(f32[514,66]{0,1:T(8,128)S(1)} %add.308), channel_id=1, source_target_pairs={{0,4},{1,5},{2,6},{3,7},{4,0},{5,1},{6,2},{7,3},{8,12},{9,13},{10,... | collective-permute-start | bytes 407096 | tf_op jit(solution)/shard_map/ppermute | solution.py:35
  402.6 1.9 collective-permute-start.9
  404.5 9.1 %collective-permute-done.12 = f32[514,66]{0,1:T(8,128)S(1)} collective-permute-done((f32[514,66]{0,1:T(8,128)S(1)}, f32[514,66]{0,1:T(8,128)S(1)}, u32[]{:S(2)}, u32[]{:S(2)}) %collective-permute-start.12) | collective-permute-done | bytes 135728 | tf_op jit(solution)/shard_map/ppermute | solution.py:35
  414.2 1.9 collective-permute-start.13
  416.3 4.1 collective-permute-start.14
  420.4 0.7 fusion.25
  421.4 2.6 collective-permute-done.14
  425.5 0.6 multiply_subtract_fusion
  (161 shorter events, 10.0 us)
Async XLA Ops:
  7.2 338.7 %copy-start = (bf16[384,384]{1,0:T(8,128)(2,1)S(1)}, bf16[384,384]{1,0:T(8,128)(2,1)}, u32[]{:S(2)}) copy-start(bf16[384,384]{1,0:T(8,128)(2,1)} %param.23) | copy-start | bytes 884740
  7.2 3.1 copy-start.8
  7.2 22.3 %copy-start.12 = (bf16[3,3072]{1,0:T(4,128)(2,1)S(1)}, bf16[3,3072]{1,0:T(4,128)(2,1)}, u32[]{:S(2)}) copy-start(bf16[3,3072]{1,0:T(4,128)(2,1)} %param.18) | copy-start | bytes 55300
  7.2 171.0 %all-gather.5.cloned.1.call-start = ((), (), s32[]{:S(2)}) async-start(), calls=%async_computation.2 | async-start | bytes 3538944 | tf_op jit(solution)/shard_map/all_gather | solution.py:233
  7.9 175.9 %all-gather.7.cloned.1.call-start = ((), (), s32[]{:S(2)}) async-start(), calls=%async_computation.3 | async-start | bytes 7962624 | tf_op jit(solution)/shard_map/all_gather | solution.py:239
  10.3 26.2 %copy-start.4 = (bf16[384,3,384]{2,0,1:T(8,128)(2,1)S(1)}, bf16[384,3,384]{2,0,1:T(8,128)(2,1)}, u32[]{:S(2)}) copy-start(bf16[384,3,384]{2,0,1:T(8,128)(2,1)} %param.20) | copy-start | bytes 2654212
  31.1 23.5 %all-to-all-start = ((bf16[64,8,384]{2,0,1:T(8,128)(2,1)}), bf16[64,8,384]{2,0,1:T(8,128)(2,1)S(1)}, u32[]{:S(2)}, u32[]{:S(2)}) async-start(bf16[64,8,384]{2,0,1:T(8,128)(2,1)} %bitcast.163), calls=%async_computation | async-start | bytes 786432 | tf_op jit(solution)/shard_map/all_to_all | solution.py:242
  36.4 232.5 %all-gather.9.cloned.1.call-start = ((), (), s32[]{:S(2)}) async-start(), calls=%async_computation.4 | async-start | bytes 7077888 | tf_op jit(solution)/shard_map/all_gather | solution.py:269
  55.6 3.0 copy-start.13
  55.6 3.0 copy-start.19
  56.8 40.4 %collective-permute-start = (f32[256,1152]{1,0:T(8,128)}, f32[256,1152]{1,0:T(8,128)}, u32[]{:S(2)}, u32[]{:S(2)}) collective-permute-start(f32[256,1152]{1,0:T(8,128)} %broadcast_select_fusion), channel_id=1, source_target_pairs={{0,32},{8,40},{16,48},{24,56},{32,0},{40,8},{48,16},{56,24},{1,33}... | collective-permute-start | bytes 3538952 | tf_op jit(solution)/shard_map/ppermute | solution.py:140
  98.7 28.7 %collective-permute-start.1 = (f32[128,1152]{1,0:T(8,128)S(1)}, f32[128,1152]{1,0:T(8,128)S(1)}, u32[]{:S(2)}, u32[]{:S(2)}) collective-permute-start(f32[128,1152]{1,0:T(8,128)S(1)} %slice_select_fusion), channel_id=1, source_target_pairs={{0,8},{8,0},{16,24},{24,16},{32,40},{40,32},{48,56},{56,48},{1,9},... | collective-permute-start | bytes 1769480 | tf_op jit(solution)/shard_map/ppermute | solution.py:140
  127.5 16.5 %collective-permute-start.2 = (f32[64,1152]{1,0:T(8,128)S(1)}, f32[64,1152]{1,0:T(8,128)S(1)}, u32[]{:S(2)}, u32[]{:S(2)}) collective-permute-start(f32[64,1152]{1,0:T(8,128)S(1)} %slice_select_fusion.1), channel_id=1, source_target_pairs={{0,16},{8,24},{16,0},{24,8},{32,48},{40,56},{48,32},{56,40},{1,17}... | collective-permute-start | bytes 884744 | tf_op jit(solution)/shard_map/ppermute | solution.py:140
  178.2 2.8 copy-start.1
  180.7 1.3 copy-start.16
  180.7 1.3 copy-start.17
  190.2 1.1 copy-start.11
  190.3 1.4 copy-start.10
  190.8 1.2 copy-start.5
  190.8 1.2 copy-start.6
  196.7 118.0 %all-gather.11.cloned.1.call-start = ((), (), s32[]{:S(2)}) async-start(), calls=%async_computation.5 | async-start | bytes 2654208 | tf_op jit(solution)/shard_map/all_gather | solution.py:241
  197.3 181.3 %reduce-scatter.4.cloned.1.call-start = ((), (), s32[]{:S(2)}) async-start(), calls=%async_computation.6 | async-start | bytes 3538944
  321.2 14.0 %copy-start.15 = (bf16[2,3072]{1,0:T(2,128)(2,1)S(1)}, bf16[2,3072]{1,0:T(2,128)(2,1)}, u32[]{:S(2)}) copy-start(bf16[2,3072]{1,0:T(2,128)(2,1)} %param.24) | copy-start | bytes 36868
  322.0 6.0 %collective-permute-start.3 = (bf16[1,64,384]{2,1,0:T(8,128)(2,1)S(1)}, bf16[1,64,384]{2,1,0:T(8,128)(2,1)S(1)}, u32[]{:S(2)}, u32[]{:S(2)}) collective-permute-start(bf16[1,64,384]{2,1,0:T(8,128)(2,1)S(1)} %slice_bitcast_fusion.1), channel_id=1, source_target_pairs={{0,16},{8,24},{16,0},{24,8},{32,48},{40,56},{48,32},{56,40},{1,17}... | collective-permute-start | bytes 147464 | tf_op jit(solution)/shard_map/ppermute | solution.py:108
  328.9 4.7 %collective-permute-start.4 = (bf16[2,64,384]{2,1,0:T(8,128)(2,1)S(1)}, bf16[2,64,384]{2,1,0:T(8,128)(2,1)S(1)}, u32[]{:S(2)}, u32[]{:S(2)}) collective-permute-start(bf16[2,64,384]{2,1,0:T(8,128)(2,1)S(1)} %maximum_bitcast_fusion), channel_id=1, source_target_pairs={{0,8},{8,0},{16,24},{24,16},{32,40},{40,32},{48,56},{56,48},{1,9},... | collective-permute-start | bytes 294920 | tf_op jit(solution)/shard_map/ppermute | solution.py:108
  333.6 12.0 %collective-permute-start.5 = (bf16[4,64,384]{2,1,0:T(8,128)(2,1)S(1)}, bf16[4,64,384]{2,1,0:T(8,128)(2,1)S(1)}, u32[]{:S(2)}, u32[]{:S(2)}) collective-permute-start(bf16[4,64,384]{2,1,0:T(8,128)(2,1)S(1)} %bitcast.180), channel_id=1, source_target_pairs={{0,32},{8,40},{16,48},{24,56},{32,0},{40,8},{48,16},{56,24},{1,33}... | collective-permute-start | bytes 589832 | tf_op jit(solution)/shard_map/ppermute | solution.py:108
  345.8 0.8 copy-start.7
  346.3 33.5 %copy-start.2 = (bf16[512,384]{1,0:T(8,128)(2,1)S(1)}, bf16[512,384]{1,0:T(8,128)(2,1)}, u32[]{:S(2)}) copy-start(bf16[512,384]{1,0:T(8,128)(2,1)} %param.15) | copy-start | bytes 1179652
  346.4 2.8 collective-permute-start.6
  349.3 31.6 %collective-permute-start.7 = (f32[128,384]{1,0:T(8,128)S(1)}, f32[128,384]{1,0:T(8,128)S(1)}, u32[]{:S(2)}, u32[]{:S(2)}) collective-permute-start(f32[128,384]{1,0:T(8,128)S(1)} %slice_select_fusion.2), channel_id=1, source_target_pairs={{0,2},{1,3},{2,0},{3,1},{4,6},{5,7},{6,4},{7,5},{8,10},{9,11},{10,... | collective-permute-start | bytes 589832 | tf_op jit(solution)/shard_map/ppermute | solution.py:140
  380.1 41.0 %copy-start.3 = (bf16[512,384]{1,0:T(8,128)(2,1)}, bf16[512,384]{1,0:T(8,128)(2,1)S(1)}, u32[]{:S(2)}) copy-start(bf16[512,384]{1,0:T(8,128)(2,1)S(1)} %get-tuple-element.23) | copy-start | bytes 1179652
  380.7 43.5 %copy-start.9 = (bf16[3,3,64,64]{3,2,1,0:T(8,128)(2,1)S(1)}, bf16[3,3,64,64]{3,2,1,0:T(8,128)(2,1)}, u32[]{:S(2)}) copy-start(bf16[3,3,64,64]{3,2,1,0:T(8,128)(2,1)} %param.26) | copy-start | bytes 221188
  380.8 1.5 collective-permute-start.10
  380.9 44.5 %copy-start.18 = (f32[8,512]{1,0:T(8,128)S(1)}, f32[8,512]{1,0:T(8,128)}, u32[]{:S(2)}) copy-start(f32[8,512]{1,0:T(8,128)} %param.27) | copy-start | bytes 49156
  382.3 15.9 %collective-permute-start.11 = (f32[514,66]{0,1:T(8,128)S(1)}, f32[514,66]{0,1:T(8,128)S(1)}, u32[]{:S(2)}, u32[]{:S(2)}) collective-permute-start(f32[514,66]{0,1:T(8,128)S(1)} %fusion.81), channel_id=1, source_target_pairs={{0,2},{1,3},{2,0},{3,1},{4,6},{5,7},{6,4},{7,5},{8,10},{9,11},{10,... | collective-permute-start | bytes 407096 | tf_op jit(solution)/shard_map/ppermute | solution.py:35
  383.8 18.8 %collective-permute-start.8 = (f32[64,384]{1,0:T(8,128)S(1)}, f32[64,384]{1,0:T(8,128)S(1)}, u32[]{:S(2)}, u32[]{:S(2)}) collective-permute-start(f32[64,384]{1,0:T(8,128)S(1)} %slice_select_fusion.3), channel_id=1, source_target_pairs={{0,4},{1,5},{2,6},{3,7},{4,0},{5,1},{6,2},{7,3},{8,12},{9,13},{10,... | collective-permute-start | bytes 294920 | tf_op jit(solution)/shard_map/ppermute | solution.py:140
  398.2 15.4 %collective-permute-start.12 = (f32[514,66]{0,1:T(8,128)S(1)}, f32[514,66]{0,1:T(8,128)S(1)}, u32[]{:S(2)}, u32[]{:S(2)}) collective-permute-start(f32[514,66]{0,1:T(8,128)S(1)} %add.308), channel_id=1, source_target_pairs={{0,4},{1,5},{2,6},{3,7},{4,0},{5,1},{6,2},{7,3},{8,12},{9,13},{10,... | collective-permute-start | bytes 407096 | tf_op jit(solution)/shard_map/ppermute | solution.py:35
  402.6 17.9 %collective-permute-start.9 = (f32[64,384]{1,0:T(8,128)S(1)}, f32[64,384]{1,0:T(8,128)S(1)}, u32[]{:S(2)}, u32[]{:S(2)}) collective-permute-start(f32[64,384]{1,0:T(8,128)S(1)} %select_add_fusion.5), channel_id=1, source_target_pairs={{0,0},{1,8},{2,16},{3,24},{4,32},{5,40},{6,48},{7,56},{8,1},{9,9},... | collective-permute-start | bytes 294920 | tf_op jit(solution)/shard_map/ppermute | solution.py:147
  414.2 7.1 %collective-permute-start.13 = (bf16[1,4096]{1,0:T(2,128)(2,1)S(1)}, bf16[1,4096]{1,0:T(2,128)(2,1)S(1)}, u32[]{:S(2)}, u32[]{:S(2)}) collective-permute-start(bf16[1,4096]{1,0:T(2,128)(2,1)S(1)} %slice.323), channel_id=1, source_target_pairs={{0,8},{8,16},{16,24},{24,32},{32,40},{40,48},{48,56},{1,9},{9,17},... | collective-permute-start | bytes 24584 | tf_op jit(solution)/shard_map/ppermute | solution.py:23
  416.3 7.7 %collective-permute-start.14 = (bf16[1,4096]{1,0:T(2,128)(2,1)S(1)}, bf16[1,4096]{1,0:T(2,128)(2,1)S(1)}, u32[]{:S(2)}, u32[]{:S(2)}) collective-permute-start(bf16[1,4096]{1,0:T(2,128)(2,1)S(1)} %slice.325), channel_id=1, source_target_pairs={{8,0},{16,8},{24,16},{32,24},{40,32},{48,40},{56,48},{9,1},{17,9},... | collective-permute-start | bytes 24584 | tf_op jit(solution)/shard_map/ppermute | solution.py:26
  425.5 0.6 copy-start.14
Sparse Core Ops, SparseCore 0:
  9.9 51.1 all-gather.4
  62.9 106.1 all-gather.6
  196.8 72.0 all-gather.8
  270.5 44.1 all-gather.10
  321.3 57.2 reduce-scatter.3

commit v10 on v6

--- a/solution.py
+++ b/solution.py
@@ -145,6 +145,21 @@
     side = lax.axis_size("tp")
     swap = [(a * side + b, b * side + a) for a in range(side) for b in range(side)]
     return lax.ppermute(block, ("seq", "tp"), swap)
+
+
+def direct_sum(block, axis):
+    count = lax.axis_size(axis)
+    at = lax.axis_index(axis)
+    received = [block] + [
+        lax.ppermute(block, axis, [(i, (i + shift) % count) for i in range(count)])
+        for shift in range(1, count)
+    ]
+    stacked = jnp.stack(received)
+    total = None
+    for source in range(count):
+        piece = lax.dynamic_index_in_dim(stacked, (at - source) % count, 0, keepdims=False)
+        total = piece if total is None else total + piece
+    return total
 
 
 def modulate(hidden, mod_rows):
@@ -326,7 +341,7 @@
         ],
         0,
     )
-    packed = tree_sum(packed, "tp")
+    packed = direct_sum(packed, "tp")
     lifted = packed[:img_rows, :channels]
     row_mean = packed[:img_rows, channels] / full_width
     row_var = packed[:img_rows, channels + 1] / full_width - row_mean * row_mean

time: 433 us -> 450 us (1.039)
  starting transfers between devices: 29.8 us -> 46.6 us
    ppermute x3, waiting for transfers between devices: 0.45 us -> 15.6 us  [halving_scatter(): lax.ppermute(sent, axis, [(i, i ^ step) for i in range(count)])]
    unnamed x7, waiting for transfers between devices: 28.8 us -> 14 us
    ppermute x1, starting transfers between devices: 1.92 us -> 10.7 us  [extended(): lax.ppermute(lax.slice_in_dim(block, block.shape[dim] - width, None, axis...]
    ppermute x3 -> x7, starting transfers between devices: 6.95 us -> 14.4 us  [direct_sum(): lax.ppermute(block, axis, [(i, (i + shift) % count) for i in range(count)])]
    ppermute x3 -> x7, waiting for transfers between devices: 22.5 us -> 19.5 us  [direct_sum(): lax.ppermute(block, axis, [(i, (i + shift) % count) for i in range(count)])]
    unnamed x39 -> x45, local copies, waits for them, and re-layouts: 9.13 us -> 9.28 us
  transfers between devices with their start and end apart: 19 -> 23, of which waited for: 15 -> 19; matrix products, arithmetic and copies ran while one was open for 10% -> 9% of each run, Pallas kernels for 5% -> 4%
where the time goes in v10:
time: 450 us; the launch traced here: 449 us
  waiting for transfers between devices  263 us (58%)
  blocking collectives  52.2 us (12%)
  starting transfers between devices  46.6 us (10%)
  Pallas kernels  20.1 us (4%)
  other arithmetic  19.2 us (4%)
  between operations  16.6 us (4%)
  local copies, waits for them, and re-layouts  15.7 us (3%)
  matrix products  15.3 us (3%)
    all_gather x1, waiting for transfers between devices, per_device(): img_weights = lax.all_gather(img_qkv, 'seq', axis=0, tiled=True)  56.2 us
    all_gather x1, waiting for transfers between devices, per_device(): lax.all_gather(jnp.concatenate([img_key.reshape(img_rows, kv_width), img_...  42.2 us
    all_gather x1, blocking collectives, per_device(): lax.all_gather(jnp.concatenate([txt_key.reshape(txt_rows, kv_width), txt_...  33.6 us
    reduce_scatter x1, waiting for transfers between devices, per_device(): lax.psum_scatter(add_rows(txt_norm_rows, txt_qkv), 'seq', scatter_dimensi...  31.3 us
    all_gather x1, waiting for transfers between devices, per_device(): lax.all_gather(img_hidden, 'tp', axis=1, tiled=True)  27 us
    all_gather x1, waiting for transfers between devices, per_device(): img_out_full = lax.all_gather(img_out_w, 'seq', axis=1, tiled=True)  25.6 us
    pallas_call x1, Pallas kernels, attention(): pl.pallas_call(functools.partial(attend_block, scale=head_dim ** (-0.5)),...  20.1 us
    ppermute x7, waiting for transfers between devices, direct_sum(): lax.ppermute(block, axis, [(i, (i + shift) % count) for i in range(count)])  19.5 us
  transfers between devices with their start and end apart: 23, of which 19 were waited for; matrix products, arithmetic and copies ran while one was open for 9% of the time, Pallas kernels for 4%

profile of v10, /device:TPU:26, one launch (start us, length us, event | category | flops | bytes accessed | tf_op | source)
XLA Modules:
  0.0 448.9 jit_solution(15714891420466936999)
XLA Ops:
  7.3 0.7 all-gather.5.cloned.1.call-update
  8.0 2.3 copy.76
  10.4 18.6 %all_gather.18 = bf16[64,3072]{1,0:T(8,128)(2,1)S(1)} all-gather(bf16[64,384]{1,0:T(8,128)(2,1)S(1)} %copy-done.6), channel_id=1, replica_groups=mesh['req'=4,'seq'=8,'tp'=8] {'tp'}, dimensions={1}, use_global_device_ids=true | all-gather | bytes 442368 | tf_op jit(solution)/shard_map/all_gather | solution.py:249
  29.7 27.0 %all-gather.5.cloned.1.call-done = bf16[512,3072]{1,0:T(8,128)(2,1)} async-done(((bf16[512,384]{1,0:T(8,128)(2,1)}), bf16[512,3072]{1,0:T(8,128)(2,1)}) %all-gather.5.cloned.1.call-update) | async-done | bytes 3145744 | tf_op jit(solution)/shard_map/all_gather | solution.py:248
  56.7 2.5 convert_reduce_fusion
  59.5 1.0 fusion.2
  60.5 3.5 fusion.5
  64.0 0.8 copy.104
  64.8 5.4 %all-to-all-start = ((bf16[64,8,384]{2,0,1:T(8,128)(2,1)}), bf16[64,8,384]{2,0,1:T(8,128)(2,1)S(1)}, u32[]{:S(2)}, u32[]{:S(2)}) async-start(bf16[64,8,384]{2,0,1:T(8,128)(2,1)} %bitcast.187), calls=%async_computation | async-start | bytes 786432 | tf_op jit(solution)/shard_map/all_to_all | solution.py:259
  70.2 2.4 copy.73
  72.6 8.9 %all-to-all-done = bf16[64,8,384]{2,0,1:T(8,128)(2,1)S(1)} async-done(((bf16[64,8,384]{2,0,1:T(8,128)(2,1)}), bf16[64,8,384]{2,0,1:T(8,128)(2,1)S(1)}, u32[]{:S(2)}, u32[]{:S(2)}) %all-to-all-start) | async-done | bytes 393248 | tf_op jit(solution)/shard_map/all_to_all | solution.py:259
  81.5 2.2 fusion.88
  84.5 0.5 fusion.24
  85.0 56.2 %all-gather.7.cloned.1.call-done = bf16[3072,3,384]{0,2,1:T(8,128)(2,1)} async-done(((bf16[384,3,384]{0,2,1:T(8,128)(2,1)}), bf16[3072,3,384]{0,2,1:T(8,128)(2,1)}) %all-gather.7.cloned.1.call-update) | async-done | bytes 7077904 | tf_op jit(solution)/shard_map/all_gather | solution.py:254
  141.2 7.1 %fusion.6 = f32[512,3,3,128]{0,3,2,1:T(8,128)S(1)} fusion(bf16[3,3,128,3072]{3,2,1,0:T(8,128)(2,1)} %bitcast.223, bf16[512,3072]{1,0:T(8,128)(2,1)} %fusion.5), kind=kOutput, calls=%fused_computation.9 | convolution fusion | flops 3623878656 | bytes 12582912 | tf_op jit(solution)/shard_map/dot_general | solution.py:221
  148.6 0.5 squeeze.74
  149.1 0.5 squeeze.76
  150.3 2.1 subtract_convert_fusion
  152.4 0.9 pad_maximum_fusion.3
  153.9 1.0 pad_maximum_fusion
  155.0 0.5 all-gather.11.cloned.1.call-update
  156.3 0.6 compare_convert_fusion.keep_ref
  156.8 31.3 %reduce-scatter.5.cloned.1.call-done = f32[64,1152]{1,0:T(8,128)} async-done(((f32[512,1152]{1,0:T(8,128)}), f32[64,1152]{1,0:T(8,128)}) %reduce-scatter.5.cloned.1.call-update) | async-done | bytes 294928 | tf_op jit(solution)/shard_map/reduce_scatter | solution.py:260
  188.1 1.1 reshape.284
  189.8 33.6 %all_gather.21.tkey_ref.tvalue_ref = bf16[512,768]{1,0:T(8,128)(2,1)} all-gather(bf16[64,768]{1,0:T(8,128)(2,1)S(1)} %pad_maximum_fusion.9), channel_id=1, replica_groups=mesh['req'=4,'seq'=8,'tp'=8] {'seq'}, dimensions={0}, use_global_device_ids=true | all-gather | bytes 884736 | tf_op jit(solution)/shard_map/all_gather | solution.py:283
  223.4 0.9 pad_maximum_fusion.2
  224.7 0.8 pad_maximum_fusion.1.query_ref
  225.6 42.2 %all-gather.9.cloned.1.call-done.ikey_ref.ivalue_ref = bf16[4096,768]{1,0:T(8,128)(2,1)} async-done(((bf16[512,768]{1,0:T(8,128)(2,1)}), bf16[4096,768]{1,0:T(8,128)(2,1)}) %all-gather.9.cloned.1.call-update) | async-done | bytes 6291472 | tf_op jit(solution)/shard_map/all_gather | solution.py:275
  267.7 20.1 %shard_map.182 = bf16[576,384]{1,0:T(8,128)(2,1)} custom-call(f32[1,512]{1,0:T(1,128)} %compare_convert_fusion.keep_ref, bf16[576,384]{1,0:T(8,128)(2,1)} %pad_maximum_fusion.1.query_ref, bf16[512,768]{1,0:T(8,128)(2,1)} %all_gather.21.tkey_ref.tvalue_ref, bf16[512,768]{1,0:T(8,128)(2,1)} %all_gather.21.tkey_ref.tvalue_ref, ...), custom_call_target="tpu_custom_call" | custom-call | tf_op jit(solution)/shard_map/pallas_call | solution.py:83
  287.9 25.6 %all-gather.11.cloned.1.call-done = bf16[384,3072]{1,0:T(8,128)(2,1)} async-done(((bf16[384,384]{1,0:T(8,128)(2,1)}), bf16[384,3072]{1,0:T(8,128)(2,1)}) %all-gather.11.cloned.1.call-update) | async-done | bytes 2359312 | tf_op jit(solution)/shard_map/all_gather | solution.py:256
  313.4 3.6 convolution_convert_fusion
  317.0 2.8 copy.88
  319.9 0.8 slice_bitcast_fusion
  320.7 1.6 collective-permute-start
  322.3 4.5 collective-permute-done
  326.7 0.8 select_bitcast_fusion.5
  327.6 1.2 collective-permute-start.1
  328.7 3.5 collective-permute-done.1
  332.3 1.5 collective-permute-start.2
  334.1 10.2 %collective-permute-done.2 = bf16[4,64,384]{2,1,0:T(8,128)(2,1)S(1)} collective-permute-done((bf16[4,64,384]{2,1,0:T(8,128)(2,1)S(1)}, bf16[4,64,384]{2,1,0:T(8,128)(2,1)S(1)}, u32[]{:S(2)}, u32[]{:S(2)}) %collective-permute-start.2) | collective-permute-done | bytes 196640 | tf_op jit(solution)/shard_map/ppermute | solution.py:108
  344.6 0.4 fusion.8
  345.6 1.4 collective-permute-done.3
  347.0 2.6 collective-permute-start.4
  350.6 14.2 %collective-permute-done.4 = f32[128,384]{1,0:T(8,128)S(1)} collective-permute-done((f32[128,384]{1,0:T(8,128)S(1)}, f32[128,384]{1,0:T(8,128)S(1)}, u32[]{:S(2)}, u32[]{:S(2)}) %collective-permute-start.4) | collective-permute-done | bytes 196640 | tf_op jit(solution)/shard_map/ppermute | solution.py:140
  364.8 5.0 %collective-permute-start.5 = (f32[64,384]{1,0:T(8,128)S(1)}, f32[64,384]{1,0:T(8,128)S(1)}, u32[]{:S(2)}, u32[]{:S(2)}) collective-permute-start(f32[64,384]{1,0:T(8,128)S(1)} %slice_select_fusion.1), channel_id=1, source_target_pairs={{0,4},{1,5},{2,6},{3,7},{4,0},{5,1},{6,2},{7,3},{8,12},{9,13},{10,... | collective-permute-start | bytes 294920 | tf_op jit(solution)/shard_map/ppermute | solution.py:140
  369.8 12.7 %reduce-scatter.7.cloned.1.call-done = bf16[384,512]{1,0:T(8,128)(2,1)} async-done(((bf16[3072,512]{1,0:T(8,128)(2,1)}), bf16[384,512]{1,0:T(8,128)(2,1)}) %reduce-scatter.7.cloned.1.call-update) | async-done | bytes 393232
  382.6 1.2 copy.89
  384.1 0.6 fusion.15
  384.7 2.0 collective-permute-start.7
  386.7 1.9 collective-permute-start.6
  388.6 0.4 collective-permute-start.8
  389.1 3.3 collective-permute-start.9
  392.3 3.4 collective-permute-start.10
  395.7 3.0 collective-permute-start.11
  398.8 2.4 collective-permute-start.12
  401.2 6.9 %collective-permute-done.9 = f32[514,66]{0,1:T(8,128)S(1)} collective-permute-done((f32[514,66]{0,1:T(8,128)S(1)}, f32[514,66]{0,1:T(8,128)S(1)}, u32[]{:S(2)}, u32[]{:S(2)}) %collective-permute-start.9) | collective-permute-done | bytes 135728 | tf_op jit(solution)/shard_map/ppermute | solution.py:154
  408.1 10.5 %collective-permute-done.10 = f32[514,66]{0,1:T(8,128)S(1)} collective-permute-done((f32[514,66]{0,1:T(8,128)S(1)}, f32[514,66]{0,1:T(8,128)S(1)}, u32[]{:S(2)}, u32[]{:S(2)}) %collective-permute-start.10) | collective-permute-done | bytes 135728 | tf_op jit(solution)/shard_map/ppermute | solution.py:154
  418.7 0.9 collective-permute-done.11
  419.8 0.9 collective-permute-done.13
  421.4 10.7 %collective-permute-start.14 = (bf16[1,4096]{1,0:T(2,128)(2,1)S(1)}, bf16[1,4096]{1,0:T(2,128)(2,1)S(1)}, u32[]{:S(2)}, u32[]{:S(2)}) collective-permute-start(bf16[1,4096]{1,0:T(2,128)(2,1)S(1)} %slice.267), channel_id=1, source_target_pairs={{0,8},{8,16},{16,24},{24,32},{32,40},{40,48},{48,56},{1,9},{9,17},... | collective-permute-start | bytes 24584 | tf_op jit(solution)/shard_map/ppermute | solution.py:23
  432.3 1.9 collective-permute-start.15
  434.2 0.7 fusion.25
  435.2 4.8 %collective-permute-done.15 = bf16[1,4096]{1,0:T(2,128)(2,1)S(1)} collective-permute-done((bf16[1,4096]{1,0:T(2,128)(2,1)S(1)}, bf16[1,4096]{1,0:T(2,128)(2,1)S(1)}, u32[]{:S(2)}, u32[]{:S(2)}) %collective-permute-start.15) | collective-permute-done | bytes 8224 | tf_op jit(solution)/shard_map/ppermute | solution.py:26
  441.5 0.6 multiply_subtract_fusion
  (150 shorter events, 8.9 us)
Async XLA Ops:
  7.2 337.4 %copy-start = (bf16[384,384]{1,0:T(8,128)(2,1)S(1)}, bf16[384,384]{1,0:T(8,128)(2,1)}, u32[]{:S(2)}) copy-start(bf16[384,384]{1,0:T(8,128)(2,1)} %param.23) | copy-start | bytes 884740
  7.2 3.1 copy-start.8
  7.2 3.2 copy-start.9
  7.2 3.2 copy-start.6
  7.2 49.5 %all-gather.5.cloned.1.call-start = ((), (), s32[]{:S(2)}) async-start(), calls=%async_computation.3 | async-start | bytes 3538944 | tf_op jit(solution)/shard_map/all_gather | solution.py:248
  7.9 133.3 %all-gather.7.cloned.1.call-start = ((), (), s32[]{:S(2)}) async-start(), calls=%async_computation.5 | async-start | bytes 7962624 | tf_op jit(solution)/shard_map/all_gather | solution.py:254
  56.7 2.8 copy-start.1
  60.5 9.7 %copy-start.4 = (bf16[384,3,384]{2,0,1:T(8,128)(2,1)S(1)}, bf16[384,3,384]{2,0,1:T(8,128)(2,1)}, u32[]{:S(2)}) copy-start(bf16[384,3,384]{2,0,1:T(8,128)(2,1)} %param.20) | copy-start | bytes 2654212
  64.8 16.7 %all-to-all-start = ((bf16[64,8,384]{2,0,1:T(8,128)(2,1)}), bf16[64,8,384]{2,0,1:T(8,128)(2,1)S(1)}, u32[]{:S(2)}, u32[]{:S(2)}) async-start(bf16[64,8,384]{2,0,1:T(8,128)(2,1)} %bitcast.187), calls=%async_computation | async-start | bytes 786432 | tf_op jit(solution)/shard_map/all_to_all | solution.py:259
  70.2 117.9 %reduce-scatter.5.cloned.1.call-start = ((), (), s32[]{:S(2)}) async-start(), calls=%async_computation.4 | async-start | bytes 2654208 | tf_op jit(solution)/shard_map/reduce_scatter | solution.py:260
  81.5 2.5 copy-start.13
  83.8 184.0 %all-gather.9.cloned.1.call-start = ((), (), s32[]{:S(2)}) async-start(), calls=%async_computation.6 | async-start | bytes 7077888 | tf_op jit(solution)/shard_map/all_gather | solution.py:275
  155.0 158.5 %all-gather.11.cloned.1.call-start = ((), (), s32[]{:S(2)}) async-start(), calls=%async_computation.7 | async-start | bytes 2654208 | tf_op jit(solution)/shard_map/all_gather | solution.py:256
  155.6 227.0 %reduce-scatter.7.cloned.1.call-start = ((), (), s32[]{:S(2)}) async-start(), calls=%async_computation.8 | async-start | bytes 3538944
  319.9 14.0 %copy-start.11 = (bf16[2,3072]{1,0:T(2,128)(2,1)S(1)}, bf16[2,3072]{1,0:T(2,128)(2,1)}, u32[]{:S(2)}) copy-start(bf16[2,3072]{1,0:T(2,128)(2,1)} %param.24) | copy-start | bytes 36868
  320.7 6.0 %collective-permute-start = (bf16[1,64,384]{2,1,0:T(8,128)(2,1)S(1)}, bf16[1,64,384]{2,1,0:T(8,128)(2,1)S(1)}, u32[]{:S(2)}, u32[]{:S(2)}) collective-permute-start(bf16[1,64,384]{2,1,0:T(8,128)(2,1)S(1)} %slice_bitcast_fusion), channel_id=1, source_target_pairs={{0,16},{8,24},{16,0},{24,8},{32,48},{40,56},{48,32},{56,40},{1,17}... | collective-permute-start | bytes 147464 | tf_op jit(solution)/shard_map/ppermute | solution.py:108
  327.6 4.7 %collective-permute-start.1 = (bf16[2,64,384]{2,1,0:T(8,128)(2,1)S(1)}, bf16[2,64,384]{2,1,0:T(8,128)(2,1)S(1)}, u32[]{:S(2)}, u32[]{:S(2)}) collective-permute-start(bf16[2,64,384]{2,1,0:T(8,128)(2,1)S(1)} %maximum_bitcast_fusion), channel_id=1, source_target_pairs={{0,8},{8,0},{16,24},{24,16},{32,40},{40,32},{48,56},{56,48},{1,9},... | collective-permute-start | bytes 294920 | tf_op jit(solution)/shard_map/ppermute | solution.py:108
  332.3 12.0 %collective-permute-start.2 = (bf16[4,64,384]{2,1,0:T(8,128)(2,1)S(1)}, bf16[4,64,384]{2,1,0:T(8,128)(2,1)S(1)}, u32[]{:S(2)}, u32[]{:S(2)}) collective-permute-start(bf16[4,64,384]{2,1,0:T(8,128)(2,1)S(1)} %bitcast.203), channel_id=1, source_target_pairs={{0,32},{8,40},{16,48},{24,56},{32,0},{40,8},{48,16},{56,24},{1,33}... | collective-permute-start | bytes 589832 | tf_op jit(solution)/shard_map/ppermute | solution.py:108
  344.5 0.8 copy-start.5
  345.1 38.7 %copy-start.2 = (bf16[512,384]{1,0:T(8,128)(2,1)S(1)}, bf16[512,384]{1,0:T(8,128)(2,1)}, u32[]{:S(2)}) copy-start(bf16[512,384]{1,0:T(8,128)(2,1)} %param.15) | copy-start | bytes 1179652
  345.1 1.8 collective-permute-start.3
  347.0 17.8 %collective-permute-start.4 = (f32[128,384]{1,0:T(8,128)S(1)}, f32[128,384]{1,0:T(8,128)S(1)}, u32[]{:S(2)}, u32[]{:S(2)}) collective-permute-start(f32[128,384]{1,0:T(8,128)S(1)} %slice_select_fusion), channel_id=1, source_target_pairs={{0,2},{1,3},{2,0},{3,1},{4,6},{5,7},{6,4},{7,5},{8,10},{9,11},{10,... | collective-permute-start | bytes 589832 | tf_op jit(solution)/shard_map/ppermute | solution.py:140
  364.8 21.9 %collective-permute-start.5 = (f32[64,384]{1,0:T(8,128)S(1)}, f32[64,384]{1,0:T(8,128)S(1)}, u32[]{:S(2)}, u32[]{:S(2)}) collective-permute-start(f32[64,384]{1,0:T(8,128)S(1)} %slice_select_fusion.1), channel_id=1, source_target_pairs={{0,4},{1,5},{2,6},{3,7},{4,0},{5,1},{6,2},{7,3},{8,12},{9,13},{10,... | collective-permute-start | bytes 294920 | tf_op jit(solution)/shard_map/ppermute | solution.py:140
  384.1 36.8 %copy-start.3 = (bf16[512,384]{1,0:T(8,128)(2,1)}, bf16[512,384]{1,0:T(8,128)(2,1)S(1)}, u32[]{:S(2)}) copy-start(bf16[512,384]{1,0:T(8,128)(2,1)S(1)} %get-tuple-element.21) | copy-start | bytes 1179652
  384.7 11.0 %collective-permute-start.7 = (f32[514,66]{0,1:T(8,128)S(1)}, f32[514,66]{0,1:T(8,128)S(1)}, u32[]{:S(2)}, u32[]{:S(2)}) collective-permute-start(f32[514,66]{0,1:T(8,128)S(1)} %select_maximum_fusion), channel_id=1, source_target_pairs={{0,1},{1,2},{2,3},{3,4},{4,5},{5,6},{6,7},{7,0},{8,9},{9,10},{10,1... | collective-permute-start | bytes 407096 | tf_op jit(solution)/shard_map/ppermute | solution.py:154
  386.7 47.5 %collective-permute-start.6 = (f32[64,384]{1,0:T(8,128)S(1)}, f32[64,384]{1,0:T(8,128)S(1)}, u32[]{:S(2)}, u32[]{:S(2)}) collective-permute-start(f32[64,384]{1,0:T(8,128)S(1)} %select_add_fusion.2), channel_id=1, source_target_pairs={{0,0},{1,8},{2,16},{3,24},{4,32},{5,40},{6,48},{7,56},{8,1},{9,9},... | collective-permute-start | bytes 294920 | tf_op jit(solution)/shard_map/ppermute | solution.py:147
  388.6 10.2 %collective-permute-start.8 = (f32[514,66]{0,1:T(8,128)S(1)}, f32[514,66]{0,1:T(8,128)S(1)}, u32[]{:S(2)}, u32[]{:S(2)}) collective-permute-start(f32[514,66]{0,1:T(8,128)S(1)} %select_maximum_fusion), channel_id=1, source_target_pairs={{0,2},{1,3},{2,4},{3,5},{4,6},{5,7},{6,0},{7,1},{8,10},{9,11},{10,... | collective-permute-start | bytes 407096 | tf_op jit(solution)/shard_map/ppermute | solution.py:154
  389.1 19.1 %collective-permute-start.9 = (f32[514,66]{0,1:T(8,128)S(1)}, f32[514,66]{0,1:T(8,128)S(1)}, u32[]{:S(2)}, u32[]{:S(2)}) collective-permute-start(f32[514,66]{0,1:T(8,128)S(1)} %select_maximum_fusion), channel_id=1, source_target_pairs={{0,3},{1,4},{2,5},{3,6},{4,7},{5,0},{6,1},{7,2},{8,11},{9,12},{10,... | collective-permute-start | bytes 407096 | tf_op jit(solution)/shard_map/ppermute | solution.py:154
  392.3 26.4 %collective-permute-start.10 = (f32[514,66]{0,1:T(8,128)S(1)}, f32[514,66]{0,1:T(8,128)S(1)}, u32[]{:S(2)}, u32[]{:S(2)}) collective-permute-start(f32[514,66]{0,1:T(8,128)S(1)} %select_maximum_fusion), channel_id=1, source_target_pairs={{0,4},{1,5},{2,6},{3,7},{4,0},{5,1},{6,2},{7,3},{8,12},{9,13},{10,... | collective-permute-start | bytes 407096 | tf_op jit(solution)/shard_map/ppermute | solution.py:154
  395.7 23.9 %collective-permute-start.11 = (f32[514,66]{0,1:T(8,128)S(1)}, f32[514,66]{0,1:T(8,128)S(1)}, u32[]{:S(2)}, u32[]{:S(2)}) collective-permute-start(f32[514,66]{0,1:T(8,128)S(1)} %select_maximum_fusion), channel_id=1, source_target_pairs={{0,5},{1,6},{2,7},{3,0},{4,1},{5,2},{6,3},{7,4},{8,13},{9,14},{10,... | collective-permute-start | bytes 407096 | tf_op jit(solution)/shard_map/ppermute | solution.py:154
  398.8 21.0 %collective-permute-start.12 = (f32[514,66]{0,1:T(8,128)S(1)}, f32[514,66]{0,1:T(8,128)S(1)}, u32[]{:S(2)}, u32[]{:S(2)}) collective-permute-start(f32[514,66]{0,1:T(8,128)S(1)} %select_maximum_fusion), channel_id=1, source_target_pairs={{0,6},{1,7},{2,0},{3,1},{4,2},{5,3},{6,4},{7,5},{8,14},{9,15},{10,... | collective-permute-start | bytes 407096 | tf_op jit(solution)/shard_map/ppermute | solution.py:154
  401.2 39.0 %copy-start.7 = (bf16[3,3,64,64]{3,2,1,0:T(8,128)(2,1)S(1)}, bf16[3,3,64,64]{3,2,1,0:T(8,128)(2,1)}, u32[]{:S(2)}) copy-start(bf16[3,3,64,64]{3,2,1,0:T(8,128)(2,1)} %param.26) | copy-start | bytes 221188
  408.1 12.6 %collective-permute-start.13 = (f32[514,66]{0,1:T(8,128)S(1)}, f32[514,66]{0,1:T(8,128)S(1)}, u32[]{:S(2)}, u32[]{:S(2)}) collective-permute-start(f32[514,66]{0,1:T(8,128)S(1)} %select_maximum_fusion), channel_id=1, source_target_pairs={{0,7},{1,0},{2,1},{3,2},{4,3},{5,4},{6,5},{7,6},{8,15},{9,8},{10,9... | collective-permute-start | bytes 407096 | tf_op jit(solution)/shard_map/ppermute | solution.py:154
  418.7 22.7 %copy-start.12 = (f32[8,512]{1,0:T(8,128)S(1)}, f32[8,512]{1,0:T(8,128)}, u32[]{:S(2)}) copy-start(f32[8,512]{1,0:T(8,128)} %param.27) | copy-start | bytes 49156
  421.4 13.6 %collective-permute-start.14 = (bf16[1,4096]{1,0:T(2,128)(2,1)S(1)}, bf16[1,4096]{1,0:T(2,128)(2,1)S(1)}, u32[]{:S(2)}, u32[]{:S(2)}) collective-permute-start(bf16[1,4096]{1,0:T(2,128)(2,1)S(1)} %slice.267), channel_id=1, source_target_pairs={{0,8},{8,16},{16,24},{24,32},{32,40},{40,48},{48,56},{1,9},{9,17},... | collective-permute-start | bytes 24584 | tf_op jit(solution)/shard_map/ppermute | solution.py:23
  432.3 7.7 %collective-permute-start.15 = (bf16[1,4096]{1,0:T(2,128)(2,1)S(1)}, bf16[1,4096]{1,0:T(2,128)(2,1)S(1)}, u32[]{:S(2)}, u32[]{:S(2)}) collective-permute-start(bf16[1,4096]{1,0:T(2,128)(2,1)S(1)} %slice.269), channel_id=1, source_target_pairs={{8,0},{16,8},{24,16},{32,24},{40,32},{48,40},{56,48},{9,1},{17,9},... | collective-permute-start | bytes 24584 | tf_op jit(solution)/shard_map/ppermute | solution.py:26
  441.5 0.6 copy-start.10
Sparse Core Ops, SparseCore 0:
  9.9 46.7 all-gather.4
  58.5 82.6 all-gather.6
  143.8 44.2 reduce-scatter.4
  189.8 77.9 all-gather.8
  269.4 43.9 all-gather.10
  320.0 62.5 reduce-scatter.6

commit v11 on v8

--- a/solution.py
+++ b/solution.py
@@ -242,7 +242,9 @@
     img_mixed = add_rows(img_norm, img_weights)
     txt_norm, img_norm = lax.optimization_barrier((txt_norm, img_norm))
     txt_norm_rows = lax.all_to_all(txt_norm, "seq", 1, 0, tiled=True)
-    txt_mixed = halving_scatter(add_rows(txt_norm_rows, txt_qkv), "seq", 0, (4, 1, 2))
+    txt_mixed = lax.psum_scatter(
+        add_rows(txt_norm_rows, txt_qkv).astype(jnp.bfloat16), "seq", scatter_dimension=0, tiled=True
+    ).astype(jnp.float32)
     head_dim = qk_gains.shape[1]
     grid_side = latent.shape[0] * seq_count
     token_ids = seq_at * img_rows + jnp.arange(img_rows, dtype=jnp.int32)

time: 451 us -> 429 us (0.951)
  waiting for transfers between devices: 274 us -> 259 us
  starting transfers between devices: 37.5 us -> 29.5 us
    ppermute x6 -> x3, waiting for transfers between devices: 77.3 us -> 0.45 us  [halving_scatter(): lax.ppermute(sent, axis, [(i, i ^ step) for i in range(count)])]
    all_gather x1, waiting for transfers between devices: 0.01 us -> 42.1 us  [per_device(): lax.all_gather(jnp.concatenate([img_key.reshape(img_rows, kv_width), img_...]
    reduce_scatter x0 -> x1, waiting for transfers between devices: none -> 27.1 us  [per_device(): lax.psum_scatter(add_rows(txt_norm_rows, txt_qkv).astype(jnp.bfloat16), '...]
    all_gather x1, waiting for transfers between devices: 0.01 us -> 25.6 us  [per_device(): img_out_full = lax.all_gather(img_out_w, 'seq', axis=1, tiled=True)]
    all_gather x1, waiting for transfers between devices: 44.3 us -> 26.5 us  [per_device(): lax.all_gather(img_hidden, 'tp', axis=1, tiled=True)]
    all_gather x1, waiting for transfers between devices: 74.4 us -> 57.2 us  [per_device(): img_weights = lax.all_gather(img_qkv, 'seq', axis=0, tiled=True)]
    ppermute x6 -> x3, starting transfers between devices: 12 us -> 4.79 us  [halving_scatter(): lax.ppermute(sent, axis, [(i, i ^ step) for i in range(count)])]
    unnamed x6 -> x7, waiting for transfers between devices: 27.5 us -> 28.5 us
  transfers between devices with their start and end apart: 21 -> 19, of which waited for: 14 -> 15; matrix products, arithmetic and copies ran while one was open for 6% -> 10% of each run, Pallas kernels for 4% -> 5%
where the time goes in v11:
time: 429 us; the launch traced here: 427 us
  waiting for transfers between devices  259 us (60%)
  blocking collectives  52.1 us (12%)
  starting transfers between devices  29.5 us (7%)
  Pallas kernels  20.1 us (5%)
  other arithmetic  19.9 us (5%)
  between operations  16.3 us (4%)
  local copies, waits for them, and re-layouts  15.4 us (4%)
  matrix products  14.9 us (3%)
    all_gather x1, waiting for transfers between devices, per_device(): img_weights = lax.all_gather(img_qkv, 'seq', axis=0, tiled=True)  57.2 us
    all_gather x1, waiting for transfers between devices, per_device(): lax.all_gather(jnp.concatenate([img_key.reshape(img_rows, kv_width), img_...  42.1 us
    all_gather x1, blocking collectives, per_device(): lax.all_gather(jnp.concatenate([txt_key.reshape(txt_rows, kv_width), txt_...  33.5 us
    unnamed x7, waiting for transfers between devices  28.5 us
    reduce_scatter x1, waiting for transfers between devices, per_device(): lax.psum_scatter(add_rows(txt_norm_rows, txt_qkv).astype(jnp.bfloat16), '...  27.1 us
    all_gather x1, waiting for transfers between devices, per_device(): lax.all_gather(img_hidden, 'tp', axis=1, tiled=True)  26.5 us
    all_gather x1, waiting for transfers between devices, per_device(): img_out_full = lax.all_gather(img_out_w, 'seq', axis=1, tiled=True)  25.6 us
    ppermute x3, waiting for transfers between devices, tree_sum(): lax.ppermute(block, axis, [(i, i ^ step) for i in range(count)])  22.5 us
  transfers between devices with their start and end apart: 19, of which 15 were waited for; matrix products, arithmetic and copies ran while one was open for 10% of the time, Pallas kernels for 5%

profile of v11, /device:TPU:26, one launch (start us, length us, event | category | flops | bytes accessed | tf_op | source)
XLA Modules:
  0.0 427.3 jit_solution(7289120784598842753)
XLA Ops:
  7.3 0.7 all-gather.5.cloned.1.call-update
  8.0 2.3 copy.75
  10.3 0.7 convert_element_type.122
  11.1 18.6 %all_gather.18 = bf16[64,3072]{1,0:T(8,128)(2,1)S(1)} all-gather(bf16[64,384]{1,0:T(8,128)(2,1)S(1)} %copy-done.6), channel_id=1, replica_groups=mesh['req'=4,'seq'=8,'tp'=8] {'tp'}, dimensions={1}, use_global_device_ids=true | all-gather | bytes 442368 | tf_op jit(solution)/shard_map/all_gather | solution.py:234
  30.4 26.5 %all-gather.5.cloned.1.call-done = bf16[512,3072]{1,0:T(8,128)(2,1)} async-done(((bf16[512,384]{1,0:T(8,128)(2,1)}), bf16[512,3072]{1,0:T(8,128)(2,1)}) %all-gather.5.cloned.1.call-update) | async-done | bytes 3145744 | tf_op jit(solution)/shard_map/all_gather | solution.py:233
  56.9 2.5 convert_reduce_fusion
  59.5 0.3 copy-done.1
  59.8 1.0 fusion.2
  60.8 3.5 fusion.5
  64.3 0.8 copy.103
  65.1 5.6 %all-to-all-start = ((bf16[64,8,384]{2,0,1:T(8,128)(2,1)}), bf16[64,8,384]{2,0,1:T(8,128)(2,1)S(1)}, u32[]{:S(2)}, u32[]{:S(2)}) async-start(bf16[64,8,384]{2,0,1:T(8,128)(2,1)} %bitcast.169), calls=%async_computation | async-start | bytes 786432 | tf_op jit(solution)/shard_map/all_to_all | solution.py:244
  71.0 2.4 copy.72
  73.5 0.5 fusion.24
  74.0 8.0 %all-to-all-done = bf16[64,8,384]{2,0,1:T(8,128)(2,1)S(1)} async-done(((bf16[64,8,384]{2,0,1:T(8,128)(2,1)}), bf16[64,8,384]{2,0,1:T(8,128)(2,1)S(1)}, u32[]{:S(2)}, u32[]{:S(2)}) %all-to-all-start) | async-done | bytes 393248 | tf_op jit(solution)/shard_map/all_to_all | solution.py:244
  82.0 1.8 convolution_convert_fusion.1
  84.1 57.2 %all-gather.7.cloned.1.call-done = bf16[3072,3,384]{0,2,1:T(8,128)(2,1)} async-done(((bf16[384,3,384]{0,2,1:T(8,128)(2,1)}), bf16[3072,3,384]{0,2,1:T(8,128)(2,1)}) %all-gather.7.cloned.1.call-update) | async-done | bytes 7077904 | tf_op jit(solution)/shard_map/all_gather | solution.py:239
  141.2 7.1 %fusion.6 = f32[512,3,3,128]{0,3,2,1:T(8,128)S(1)} fusion(bf16[3,3,128,3072]{3,2,1,0:T(8,128)(2,1)} %bitcast.205, bf16[512,3072]{1,0:T(8,128)(2,1)} %fusion.5), kind=kOutput, calls=%fused_computation.9 | convolution fusion | flops 3623878656 | bytes 12582912 | tf_op jit(solution)/shard_map/dot_general | solution.py:206
  148.4 0.3 multiply_reduce_fusion
  148.7 0.5 squeeze.59
  149.1 0.5 squeeze.61
  149.6 0.3 multiply_multiply_fusion.1
  150.0 0.3 multiply_multiply_fusion
  150.4 2.1 subtract_convert_fusion
  152.4 0.9 pad_maximum_fusion.3
  153.9 1.0 pad_maximum_fusion
  155.0 0.5 all-gather.11.cloned.1.call-update
  156.3 0.6 compare_convert_fusion.keep_ref
  156.9 27.1 %reduce-scatter.5.cloned.1.call-done = bf16[64,1152]{1,0:T(8,128)(2,1)} async-done(((bf16[512,1152]{1,0:T(8,128)(2,1)}), bf16[64,1152]{1,0:T(8,128)(2,1)}) %reduce-scatter.5.cloned.1.call-update) | async-done | bytes 147472 | tf_op jit(solution)/shard_map/reduce_scatter | solution.py:245
  183.9 1.0 reshape.283
  185.6 33.5 %all_gather.21.tkey_ref.tvalue_ref = bf16[512,768]{1,0:T(8,128)(2,1)} all-gather(bf16[64,768]{1,0:T(8,128)(2,1)S(1)} %pad_maximum_fusion.9), channel_id=1, replica_groups=mesh['req'=4,'seq'=8,'tp'=8] {'seq'}, dimensions={0}, use_global_device_ids=true | all-gather | bytes 884736 | tf_op jit(solution)/shard_map/all_gather | solution.py:268
  219.1 0.9 pad_maximum_fusion.2
  220.4 0.8 pad_maximum_fusion.1.query_ref
  221.3 42.1 %all-gather.9.cloned.1.call-done.ikey_ref.ivalue_ref = bf16[4096,768]{1,0:T(8,128)(2,1)} async-done(((bf16[512,768]{1,0:T(8,128)(2,1)}), bf16[4096,768]{1,0:T(8,128)(2,1)}) %all-gather.9.cloned.1.call-update) | async-done | bytes 6291472 | tf_op jit(solution)/shard_map/all_gather | solution.py:260
  263.4 20.1 %shard_map.182 = bf16[576,384]{1,0:T(8,128)(2,1)} custom-call(f32[1,512]{1,0:T(1,128)} %compare_convert_fusion.keep_ref, bf16[576,384]{1,0:T(8,128)(2,1)} %pad_maximum_fusion.1.query_ref, bf16[512,768]{1,0:T(8,128)(2,1)} %all_gather.21.tkey_ref.tvalue_ref, bf16[512,768]{1,0:T(8,128)(2,1)} %all_gather.21.tkey_ref.tvalue_ref, ...), custom_call_target="tpu_custom_call" | custom-call | tf_op jit(solution)/shard_map/pallas_call | solution.py:83
  283.5 25.6 %all-gather.11.cloned.1.call-done = bf16[384,3072]{1,0:T(8,128)(2,1)} async-done(((bf16[384,384]{1,0:T(8,128)(2,1)}), bf16[384,3072]{1,0:T(8,128)(2,1)}) %all-gather.11.cloned.1.call-update) | async-done | bytes 2359312 | tf_op jit(solution)/shard_map/all_gather | solution.py:241
  309.1 3.6 convolution_convert_fusion
  312.7 2.8 copy.87
  315.5 0.8 slice_bitcast_fusion
  316.3 1.6 collective-permute-start
  317.9 4.5 %collective-permute-done = bf16[1,64,384]{2,1,0:T(8,128)(2,1)S(1)} collective-permute-done((bf16[1,64,384]{2,1,0:T(8,128)(2,1)S(1)}, bf16[1,64,384]{2,1,0:T(8,128)(2,1)S(1)}, u32[]{:S(2)}, u32[]{:S(2)}) %collective-permute-start) | collective-permute-done | bytes 49184 | tf_op jit(solution)/shard_map/ppermute | solution.py:108
  322.3 0.8 select_bitcast_fusion.5
  323.2 1.2 collective-permute-start.1
  324.4 3.5 collective-permute-done.1
  328.0 1.5 collective-permute-start.2
  329.5 10.4 %collective-permute-done.2 = bf16[4,64,384]{2,1,0:T(8,128)(2,1)S(1)} collective-permute-done((bf16[4,64,384]{2,1,0:T(8,128)(2,1)S(1)}, bf16[4,64,384]{2,1,0:T(8,128)(2,1)S(1)}, u32[]{:S(2)}, u32[]{:S(2)}) %collective-permute-start.2) | collective-permute-done | bytes 196640 | tf_op jit(solution)/shard_map/ppermute | solution.py:108
  340.2 0.4 fusion.8
  342.1 0.4 collective-permute-done.3
  342.6 2.6 collective-permute-start.4
  345.2 27.2 %reduce-scatter.7.cloned.1.call-done = bf16[384,512]{1,0:T(8,128)(2,1)} async-done(((bf16[3072,512]{1,0:T(8,128)(2,1)}), bf16[384,512]{1,0:T(8,128)(2,1)}) %reduce-scatter.7.cloned.1.call-update) | async-done | bytes 393232
  372.4 1.2 copy.88
  373.9 0.6 fusion.15
  374.5 2.1 collective-permute-start.7
  376.6 1.0 collective-permute-done.7
  377.7 1.2 collective-permute-start.8
  378.9 2.1 collective-permute-start.5
  381.0 10.6 %collective-permute-done.8 = f32[514,66]{0,1:T(8,128)S(1)} collective-permute-done((f32[514,66]{0,1:T(8,128)S(1)}, f32[514,66]{0,1:T(8,128)S(1)}, u32[]{:S(2)}, u32[]{:S(2)}) %collective-permute-start.8) | collective-permute-done | bytes 135728 | tf_op jit(solution)/shard_map/ppermute | solution.py:35
  391.7 3.4 collective-permute-start.9
  395.1 1.9 collective-permute-start.6
  397.1 10.8 %collective-permute-done.9 = f32[514,66]{0,1:T(8,128)S(1)} collective-permute-done((f32[514,66]{0,1:T(8,128)S(1)}, f32[514,66]{0,1:T(8,128)S(1)}, u32[]{:S(2)}, u32[]{:S(2)}) %collective-permute-start.9) | collective-permute-done | bytes 135728 | tf_op jit(solution)/shard_map/ppermute | solution.py:35
  408.5 1.9 collective-permute-start.10
  410.6 3.9 collective-permute-start.11
  414.5 0.7 fusion.25
  415.5 2.8 collective-permute-done.11
  419.8 0.6 multiply_subtract_fusion
  (138 shorter events, 7.2 us)
Async XLA Ops:
  7.2 333.0 %copy-start = (bf16[384,384]{1,0:T(8,128)(2,1)S(1)}, bf16[384,384]{1,0:T(8,128)(2,1)}, u32[]{:S(2)}) copy-start(bf16[384,384]{1,0:T(8,128)(2,1)} %param.23) | copy-start | bytes 884740
  7.2 22.9 %copy-start.8 = (bf16[3,3072]{1,0:T(4,128)(2,1)S(1)}, bf16[3,3072]{1,0:T(4,128)(2,1)}, u32[]{:S(2)}) copy-start(bf16[3,3072]{1,0:T(4,128)(2,1)} %param.17) | copy-start | bytes 55300
  7.2 3.9 copy-start.9
  7.2 3.9 copy-start.6
  7.2 49.7 %all-gather.5.cloned.1.call-start = ((), (), s32[]{:S(2)}) async-start(), calls=%async_computation.3 | async-start | bytes 3538944 | tf_op jit(solution)/shard_map/all_gather | solution.py:233
  7.9 133.3 %all-gather.7.cloned.1.call-start = ((), (), s32[]{:S(2)}) async-start(), calls=%async_computation.5 | async-start | bytes 7962624 | tf_op jit(solution)/shard_map/all_gather | solution.py:239
  56.9 2.8 copy-start.1
  60.7 9.9 %copy-start.13 = (f32[4,128]{1,0:T(4,128)S(1)}, f32[4,128]{1,0:T(4,128)}, u32[]{:S(2)}) copy-start(f32[4,128]{1,0:T(4,128)} %param.21) | copy-start | bytes 6148
  60.7 10.2 %copy-start.4 = (bf16[384,3,384]{2,0,1:T(8,128)(2,1)S(1)}, bf16[384,3,384]{2,0,1:T(8,128)(2,1)}, u32[]{:S(2)}) copy-start(bf16[384,3,384]{2,0,1:T(8,128)(2,1)} %param.20) | copy-start | bytes 2654212
  65.1 16.9 %all-to-all-start = ((bf16[64,8,384]{2,0,1:T(8,128)(2,1)}), bf16[64,8,384]{2,0,1:T(8,128)(2,1)S(1)}, u32[]{:S(2)}, u32[]{:S(2)}) async-start(bf16[64,8,384]{2,0,1:T(8,128)(2,1)} %bitcast.169), calls=%async_computation | async-start | bytes 786432 | tf_op jit(solution)/shard_map/all_to_all | solution.py:244
  70.7 113.3 %reduce-scatter.5.cloned.1.call-start = ((), (), s32[]{:S(2)}) async-start(), calls=%async_computation.4 | async-start | bytes 1327104 | tf_op jit(solution)/shard_map/reduce_scatter | solution.py:245
  83.8 179.5 %all-gather.9.cloned.1.call-start = ((), (), s32[]{:S(2)}) async-start(), calls=%async_computation.6 | async-start | bytes 7077888 | tf_op jit(solution)/shard_map/all_gather | solution.py:260
  155.0 154.1 %all-gather.11.cloned.1.call-start = ((), (), s32[]{:S(2)}) async-start(), calls=%async_computation.7 | async-start | bytes 2654208 | tf_op jit(solution)/shard_map/all_gather | solution.py:241
  155.6 216.8 %reduce-scatter.7.cloned.1.call-start = ((), (), s32[]{:S(2)}) async-start(), calls=%async_computation.8 | async-start | bytes 3538944
  315.5 14.0 %copy-start.11 = (bf16[2,3072]{1,0:T(2,128)(2,1)S(1)}, bf16[2,3072]{1,0:T(2,128)(2,1)}, u32[]{:S(2)}) copy-start(bf16[2,3072]{1,0:T(2,128)(2,1)} %param.24) | copy-start | bytes 36868
  316.3 6.0 %collective-permute-start = (bf16[1,64,384]{2,1,0:T(8,128)(2,1)S(1)}, bf16[1,64,384]{2,1,0:T(8,128)(2,1)S(1)}, u32[]{:S(2)}, u32[]{:S(2)}) collective-permute-start(bf16[1,64,384]{2,1,0:T(8,128)(2,1)S(1)} %slice_bitcast_fusion), channel_id=1, source_target_pairs={{0,16},{8,24},{16,0},{24,8},{32,48},{40,56},{48,32},{56,40},{1,17}... | collective-permute-start | bytes 147464 | tf_op jit(solution)/shard_map/ppermute | solution.py:108
  323.2 4.7 %collective-permute-start.1 = (bf16[2,64,384]{2,1,0:T(8,128)(2,1)S(1)}, bf16[2,64,384]{2,1,0:T(8,128)(2,1)S(1)}, u32[]{:S(2)}, u32[]{:S(2)}) collective-permute-start(bf16[2,64,384]{2,1,0:T(8,128)(2,1)S(1)} %maximum_bitcast_fusion), channel_id=1, source_target_pairs={{0,8},{8,0},{16,24},{24,16},{32,40},{40,32},{48,56},{56,48},{1,9},... | collective-permute-start | bytes 294920 | tf_op jit(solution)/shard_map/ppermute | solution.py:108
  328.0 12.0 %collective-permute-start.2 = (bf16[4,64,384]{2,1,0:T(8,128)(2,1)S(1)}, bf16[4,64,384]{2,1,0:T(8,128)(2,1)S(1)}, u32[]{:S(2)}, u32[]{:S(2)}) collective-permute-start(bf16[4,64,384]{2,1,0:T(8,128)(2,1)S(1)} %bitcast.185), channel_id=1, source_target_pairs={{0,32},{8,40},{16,48},{24,56},{32,0},{40,8},{48,16},{56,24},{1,33}... | collective-permute-start | bytes 589832 | tf_op jit(solution)/shard_map/ppermute | solution.py:108
  329.5 11.3 %copy-start.5 = (bf16[384,64]{0,1:T(8,128)(2,1)S(1)}, bf16[384,64]{0,1:T(8,128)(2,1)}, u32[]{:S(2)}) copy-start(bf16[384,64]{0,1:T(8,128)(2,1)} %param.25) | copy-start | bytes 147460
  340.6 33.0 %copy-start.2 = (bf16[512,384]{1,0:T(8,128)(2,1)S(1)}, bf16[512,384]{1,0:T(8,128)(2,1)}, u32[]{:S(2)}) copy-start(bf16[512,384]{1,0:T(8,128)(2,1)} %param.15) | copy-start | bytes 1179652
  340.7 1.8 collective-permute-start.3
  342.6 34.0 %collective-permute-start.4 = (f32[128,384]{1,0:T(8,128)S(1)}, f32[128,384]{1,0:T(8,128)S(1)}, u32[]{:S(2)}, u32[]{:S(2)}) collective-permute-start(f32[128,384]{1,0:T(8,128)S(1)} %slice_select_fusion), channel_id=1, source_target_pairs={{0,2},{1,3},{2,0},{3,1},{4,6},{5,7},{6,4},{7,5},{8,10},{9,11},{10,... | collective-permute-start | bytes 589832 | tf_op jit(solution)/shard_map/ppermute | solution.py:140
  373.6 45.0 %copy-start.7 = (bf16[3,3,64,64]{3,2,1,0:T(8,128)(2,1)S(1)}, bf16[3,3,64,64]{3,2,1,0:T(8,128)(2,1)}, u32[]{:S(2)}) copy-start(bf16[3,3,64,64]{3,2,1,0:T(8,128)(2,1)} %param.26) | copy-start | bytes 221188
  373.9 46.5 %copy-start.3 = (bf16[512,384]{1,0:T(8,128)(2,1)}, bf16[512,384]{1,0:T(8,128)(2,1)S(1)}, u32[]{:S(2)}) copy-start(bf16[512,384]{1,0:T(8,128)(2,1)S(1)} %get-tuple-element.21) | copy-start | bytes 1179652
  373.9 45.9 %copy-start.12 = (f32[8,512]{1,0:T(8,128)S(1)}, f32[8,512]{1,0:T(8,128)}, u32[]{:S(2)}) copy-start(f32[8,512]{1,0:T(8,128)} %param.27) | copy-start | bytes 49156
  374.5 3.1 collective-permute-start.7
  377.7 14.0 %collective-permute-start.8 = (f32[514,66]{0,1:T(8,128)S(1)}, f32[514,66]{0,1:T(8,128)S(1)}, u32[]{:S(2)}, u32[]{:S(2)}) collective-permute-start(f32[514,66]{0,1:T(8,128)S(1)} %fusion.83), channel_id=1, source_target_pairs={{0,2},{1,3},{2,0},{3,1},{4,6},{5,7},{6,4},{7,5},{8,10},{9,11},{10,... | collective-permute-start | bytes 407096 | tf_op jit(solution)/shard_map/ppermute | solution.py:35
  378.9 16.3 %collective-permute-start.5 = (f32[64,384]{1,0:T(8,128)S(1)}, f32[64,384]{1,0:T(8,128)S(1)}, u32[]{:S(2)}, u32[]{:S(2)}) collective-permute-start(f32[64,384]{1,0:T(8,128)S(1)} %slice_select_fusion.1), channel_id=1, source_target_pairs={{0,4},{1,5},{2,6},{3,7},{4,0},{5,1},{6,2},{7,3},{8,12},{9,13},{10,... | collective-permute-start | bytes 294920 | tf_op jit(solution)/shard_map/ppermute | solution.py:140
  391.7 16.2 %collective-permute-start.9 = (f32[514,66]{0,1:T(8,128)S(1)}, f32[514,66]{0,1:T(8,128)S(1)}, u32[]{:S(2)}, u32[]{:S(2)}) collective-permute-start(f32[514,66]{0,1:T(8,128)S(1)} %add.295), channel_id=1, source_target_pairs={{0,4},{1,5},{2,6},{3,7},{4,0},{5,1},{6,2},{7,3},{8,12},{9,13},{10,... | collective-permute-start | bytes 407096 | tf_op jit(solution)/shard_map/ppermute | solution.py:35
  395.1 19.4 %collective-permute-start.6 = (f32[64,384]{1,0:T(8,128)S(1)}, f32[64,384]{1,0:T(8,128)S(1)}, u32[]{:S(2)}, u32[]{:S(2)}) collective-permute-start(f32[64,384]{1,0:T(8,128)S(1)} %select_add_fusion.2), channel_id=1, source_target_pairs={{0,0},{1,8},{2,16},{3,24},{4,32},{5,40},{6,48},{7,56},{8,1},{9,9},... | collective-permute-start | bytes 294920 | tf_op jit(solution)/shard_map/ppermute | solution.py:147
  408.5 6.9 %collective-permute-start.10 = (bf16[1,4096]{1,0:T(2,128)(2,1)S(1)}, bf16[1,4096]{1,0:T(2,128)(2,1)S(1)}, u32[]{:S(2)}, u32[]{:S(2)}) collective-permute-start(bf16[1,4096]{1,0:T(2,128)(2,1)S(1)} %slice.267), channel_id=1, source_target_pairs={{0,8},{8,16},{16,24},{24,32},{32,40},{40,48},{48,56},{1,9},{9,17},... | collective-permute-start | bytes 24584 | tf_op jit(solution)/shard_map/ppermute | solution.py:23
  410.6 7.7 %collective-permute-start.11 = (bf16[1,4096]{1,0:T(2,128)(2,1)S(1)}, bf16[1,4096]{1,0:T(2,128)(2,1)S(1)}, u32[]{:S(2)}, u32[]{:S(2)}) collective-permute-start(bf16[1,4096]{1,0:T(2,128)(2,1)S(1)} %slice.269), channel_id=1, source_target_pairs={{8,0},{16,8},{24,16},{32,24},{40,32},{48,40},{56,48},{9,1},{17,9},... | collective-permute-start | bytes 24584 | tf_op jit(solution)/shard_map/ppermute | solution.py:26
  419.8 0.6 copy-start.10
Sparse Core Ops, SparseCore 0:
  9.9 46.9 all-gather.4
  58.7 82.4 all-gather.6
  143.8 40.0 reduce-scatter.4
  185.6 77.7 all-gather.8
  265.0 43.9 all-gather.10
  315.6 56.6 reduce-scatter.6

commit v12 on v11

--- a/solution.py
+++ b/solution.py
@@ -137,7 +137,8 @@
         upper = bit_of(at, step) == 1
         kept = jnp.where(upper, high, low)
         sent = jnp.where(upper, low, high)
-        block = kept + lax.ppermute(sent, axis, [(i, i ^ step) for i in range(count)])
+        moved = lax.ppermute(sent.astype(jnp.bfloat16), axis, [(i, i ^ step) for i in range(count)])
+        block = kept + moved.astype(block.dtype)
     return block
 
 

time: 429 us -> 423 us (0.986)
  no operation moved by 1% of the time
where the time goes in v12:
time: 423 us; the launch traced here: 421 us
  waiting for transfers between devices  256 us (61%)
  blocking collectives  52.1 us (12%)
  starting transfers between devices  26.5 us (6%)
  Pallas kernels  20.1 us (5%)
  other arithmetic  19.9 us (5%)
  between operations  16.3 us (4%)
  local copies, waits for them, and re-layouts  15.4 us (4%)
  matrix products  14.9 us (4%)
    all_gather x1, waiting for transfers between devices, per_device(): img_weights = lax.all_gather(img_qkv, 'seq', axis=0, tiled=True)  57.2 us
    all_gather x1, waiting for transfers between devices, per_device(): lax.all_gather(jnp.concatenate([img_key.reshape(img_rows, kv_width), img_...  42.1 us
    all_gather x1, blocking collectives, per_device(): lax.all_gather(jnp.concatenate([txt_key.reshape(txt_rows, kv_width), txt_...  33.5 us
    unnamed x7, waiting for transfers between devices  28.1 us
    reduce_scatter x1, waiting for transfers between devices, per_device(): lax.psum_scatter(add_rows(txt_norm_rows, txt_qkv).astype(jnp.bfloat16), '...  27.1 us
    all_gather x1, waiting for transfers between devices, per_device(): lax.all_gather(img_hidden, 'tp', axis=1, tiled=True)  26.5 us
    all_gather x1, waiting for transfers between devices, per_device(): img_out_full = lax.all_gather(img_out_w, 'seq', axis=1, tiled=True)  25.6 us
    pallas_call x1, Pallas kernels, attention(): pl.pallas_call(functools.partial(attend_block, scale=head_dim ** (-0.5)),...  20.1 us
  transfers between devices with their start and end apart: 19, of which 15 were waited for; matrix products, arithmetic and copies ran while one was open for 10% of the time, Pallas kernels for 5%

profile of v12, /device:TPU:26, one launch (start us, length us, event | category | flops | bytes accessed | tf_op | source)
XLA Modules:
  0.0 421.4 jit_solution(3333506102113782799)
XLA Ops:
  7.3 0.7 all-gather.5.cloned.1.call-update
  8.0 2.3 copy.75
  10.3 0.7 convert_element_type.140
  11.1 18.6 %all_gather.18 = bf16[64,3072]{1,0:T(8,128)(2,1)S(1)} all-gather(bf16[64,384]{1,0:T(8,128)(2,1)S(1)} %copy-done.6), channel_id=1, replica_groups=mesh['req'=4,'seq'=8,'tp'=8] {'tp'}, dimensions={1}, use_global_device_ids=true | all-gather | bytes 442368 | tf_op jit(solution)/shard_map/all_gather | solution.py:235
  30.4 26.5 %all-gather.5.cloned.1.call-done = bf16[512,3072]{1,0:T(8,128)(2,1)} async-done(((bf16[512,384]{1,0:T(8,128)(2,1)}), bf16[512,3072]{1,0:T(8,128)(2,1)}) %all-gather.5.cloned.1.call-update) | async-done | bytes 3145744 | tf_op jit(solution)/shard_map/all_gather | solution.py:234
  56.9 2.5 convert_reduce_fusion
  59.5 0.3 copy-done.1
  59.8 1.0 fusion.2
  60.8 3.5 fusion.5
  64.3 0.8 copy.103
  65.1 5.6 %all-to-all-start = ((bf16[64,8,384]{2,0,1:T(8,128)(2,1)}), bf16[64,8,384]{2,0,1:T(8,128)(2,1)S(1)}, u32[]{:S(2)}, u32[]{:S(2)}) async-start(bf16[64,8,384]{2,0,1:T(8,128)(2,1)} %bitcast.169), calls=%async_computation | async-start | bytes 786432 | tf_op jit(solution)/shard_map/all_to_all | solution.py:245
  71.0 2.4 copy.72
  73.5 0.5 fusion.23
  74.0 8.0 %all-to-all-done = bf16[64,8,384]{2,0,1:T(8,128)(2,1)S(1)} async-done(((bf16[64,8,384]{2,0,1:T(8,128)(2,1)}), bf16[64,8,384]{2,0,1:T(8,128)(2,1)S(1)}, u32[]{:S(2)}, u32[]{:S(2)}) %all-to-all-start) | async-done | bytes 393248 | tf_op jit(solution)/shard_map/all_to_all | solution.py:245
  82.0 1.8 convolution_convert_fusion.1
  84.1 57.2 %all-gather.7.cloned.1.call-done = bf16[3072,3,384]{0,2,1:T(8,128)(2,1)} async-done(((bf16[384,3,384]{0,2,1:T(8,128)(2,1)}), bf16[3072,3,384]{0,2,1:T(8,128)(2,1)}) %all-gather.7.cloned.1.call-update) | async-done | bytes 7077904 | tf_op jit(solution)/shard_map/all_gather | solution.py:240
  141.2 7.1 %fusion.6 = f32[512,3,3,128]{0,3,2,1:T(8,128)S(1)} fusion(bf16[3,3,128,3072]{3,2,1,0:T(8,128)(2,1)} %bitcast.205, bf16[512,3072]{1,0:T(8,128)(2,1)} %fusion.5), kind=kOutput, calls=%fused_computation.9 | convolution fusion | flops 3623878656 | bytes 12582912 | tf_op jit(solution)/shard_map/dot_general | solution.py:207
  148.4 0.3 multiply_reduce_fusion
  148.7 0.5 squeeze.59
  149.1 0.5 squeeze.61
  149.6 0.3 multiply_multiply_fusion.1
  150.0 0.3 multiply_multiply_fusion
  150.4 2.1 subtract_convert_fusion
  152.4 0.9 pad_maximum_fusion.3
  153.9 1.0 pad_maximum_fusion
  155.0 0.5 all-gather.11.cloned.1.call-update
  156.3 0.6 compare_convert_fusion.keep_ref
  156.9 27.1 %reduce-scatter.5.cloned.1.call-done = bf16[64,1152]{1,0:T(8,128)(2,1)} async-done(((bf16[512,1152]{1,0:T(8,128)(2,1)}), bf16[64,1152]{1,0:T(8,128)(2,1)}) %reduce-scatter.5.cloned.1.call-update) | async-done | bytes 147472 | tf_op jit(solution)/shard_map/reduce_scatter | solution.py:246
  183.9 1.0 reshape.283
  185.6 33.5 %all_gather.21.tkey_ref.tvalue_ref = bf16[512,768]{1,0:T(8,128)(2,1)} all-gather(bf16[64,768]{1,0:T(8,128)(2,1)S(1)} %pad_maximum_fusion.9), channel_id=1, replica_groups=mesh['req'=4,'seq'=8,'tp'=8] {'seq'}, dimensions={0}, use_global_device_ids=true | all-gather | bytes 884736 | tf_op jit(solution)/shard_map/all_gather | solution.py:269
  219.1 0.9 pad_maximum_fusion.2
  220.4 0.8 pad_maximum_fusion.1.query_ref
  221.3 42.1 %all-gather.9.cloned.1.call-done.ikey_ref.ivalue_ref = bf16[4096,768]{1,0:T(8,128)(2,1)} async-done(((bf16[512,768]{1,0:T(8,128)(2,1)}), bf16[4096,768]{1,0:T(8,128)(2,1)}) %all-gather.9.cloned.1.call-update) | async-done | bytes 6291472 | tf_op jit(solution)/shard_map/all_gather | solution.py:261
  263.4 20.1 %shard_map.182 = bf16[576,384]{1,0:T(8,128)(2,1)} custom-call(f32[1,512]{1,0:T(1,128)} %compare_convert_fusion.keep_ref, bf16[576,384]{1,0:T(8,128)(2,1)} %pad_maximum_fusion.1.query_ref, bf16[512,768]{1,0:T(8,128)(2,1)} %all_gather.21.tkey_ref.tvalue_ref, bf16[512,768]{1,0:T(8,128)(2,1)} %all_gather.21.tkey_ref.tvalue_ref, ...), custom_call_target="tpu_custom_call" | custom-call | tf_op jit(solution)/shard_map/pallas_call | solution.py:83
  283.5 25.6 %all-gather.11.cloned.1.call-done = bf16[384,3072]{1,0:T(8,128)(2,1)} async-done(((bf16[384,384]{1,0:T(8,128)(2,1)}), bf16[384,3072]{1,0:T(8,128)(2,1)}) %all-gather.11.cloned.1.call-update) | async-done | bytes 2359312 | tf_op jit(solution)/shard_map/all_gather | solution.py:242
  309.1 3.6 convolution_convert_fusion
  312.7 2.8 copy.87
  315.5 0.8 slice_bitcast_fusion
  316.3 1.6 collective-permute-start
  317.9 4.5 %collective-permute-done = bf16[1,64,384]{2,1,0:T(8,128)(2,1)S(1)} collective-permute-done((bf16[1,64,384]{2,1,0:T(8,128)(2,1)S(1)}, bf16[1,64,384]{2,1,0:T(8,128)(2,1)S(1)}, u32[]{:S(2)}, u32[]{:S(2)}) %collective-permute-start) | collective-permute-done | bytes 49184 | tf_op jit(solution)/shard_map/ppermute | solution.py:108
  322.4 0.8 select_bitcast_fusion.5
  323.2 1.2 collective-permute-start.1
  324.4 3.4 collective-permute-done.1
  328.0 1.5 collective-permute-start.2
  329.6 10.4 %collective-permute-done.2 = bf16[4,64,384]{2,1,0:T(8,128)(2,1)S(1)} collective-permute-done((bf16[4,64,384]{2,1,0:T(8,128)(2,1)S(1)}, bf16[4,64,384]{2,1,0:T(8,128)(2,1)S(1)}, u32[]{:S(2)}, u32[]{:S(2)}) %collective-permute-start.2) | collective-permute-done | bytes 196640 | tf_op jit(solution)/shard_map/ppermute | solution.py:108
  340.2 0.4 fusion.8
  341.1 1.1 collective-permute-done.3
  342.3 2.5 collective-permute-start.4
  344.9 26.9 %reduce-scatter.7.cloned.1.call-done = bf16[384,512]{1,0:T(8,128)(2,1)} async-done(((bf16[3072,512]{1,0:T(8,128)(2,1)}), bf16[384,512]{1,0:T(8,128)(2,1)}) %reduce-scatter.7.cloned.1.call-update) | async-done | bytes 393232
  371.7 1.2 copy.88
  373.0 0.3 convert_reduce_fusion.1
  373.3 0.6 fusion.15
  374.1 1.4 collective-permute-done.7
  375.4 1.1 collective-permute-start.8
  376.6 2.4 collective-permute-start.5
  379.8 8.0 %collective-permute-done.8 = f32[514,66]{0,1:T(8,128)S(1)} collective-permute-done((f32[514,66]{0,1:T(8,128)S(1)}, f32[514,66]{0,1:T(8,128)S(1)}, u32[]{:S(2)}, u32[]{:S(2)}) %collective-permute-start.8) | collective-permute-done | bytes 135728 | tf_op jit(solution)/shard_map/ppermute | solution.py:35
  387.7 2.3 collective-permute-start.9
  390.0 1.9 collective-permute-start.6
  391.9 10.1 %collective-permute-done.9 = f32[514,66]{0,1:T(8,128)S(1)} collective-permute-done((f32[514,66]{0,1:T(8,128)S(1)}, f32[514,66]{0,1:T(8,128)S(1)}, u32[]{:S(2)}, u32[]{:S(2)}) %collective-permute-start.9) | collective-permute-done | bytes 135728 | tf_op jit(solution)/shard_map/ppermute | solution.py:35
  402.6 1.9 collective-permute-start.10
  404.7 3.9 collective-permute-start.11
  408.7 0.7 fusion.24
  409.7 2.8 collective-permute-done.11
  413.9 0.6 multiply_subtract_fusion
  (138 shorter events, 6.9 us)
Async XLA Ops:
  7.2 333.0 %copy-start = (bf16[384,384]{1,0:T(8,128)(2,1)S(1)}, bf16[384,384]{1,0:T(8,128)(2,1)}, u32[]{:S(2)}) copy-start(bf16[384,384]{1,0:T(8,128)(2,1)} %param.23) | copy-start | bytes 884740
  7.2 22.9 %copy-start.8 = (bf16[3,3072]{1,0:T(4,128)(2,1)S(1)}, bf16[3,3072]{1,0:T(4,128)(2,1)}, u32[]{:S(2)}) copy-start(bf16[3,3072]{1,0:T(4,128)(2,1)} %param.17) | copy-start | bytes 55300
  7.2 3.9 copy-start.9
  7.2 3.9 copy-start.6
  7.2 49.7 %all-gather.5.cloned.1.call-start = ((), (), s32[]{:S(2)}) async-start(), calls=%async_computation.3 | async-start | bytes 3538944 | tf_op jit(solution)/shard_map/all_gather | solution.py:234
  7.9 133.3 %all-gather.7.cloned.1.call-start = ((), (), s32[]{:S(2)}) async-start(), calls=%async_computation.5 | async-start | bytes 7962624 | tf_op jit(solution)/shard_map/all_gather | solution.py:240
  56.9 2.8 copy-start.1
  60.7 9.9 %copy-start.13 = (f32[4,128]{1,0:T(4,128)S(1)}, f32[4,128]{1,0:T(4,128)}, u32[]{:S(2)}) copy-start(f32[4,128]{1,0:T(4,128)} %param.21) | copy-start | bytes 6148
  60.7 10.2 %copy-start.4 = (bf16[384,3,384]{2,0,1:T(8,128)(2,1)S(1)}, bf16[384,3,384]{2,0,1:T(8,128)(2,1)}, u32[]{:S(2)}) copy-start(bf16[384,3,384]{2,0,1:T(8,128)(2,1)} %param.20) | copy-start | bytes 2654212
  65.1 16.9 %all-to-all-start = ((bf16[64,8,384]{2,0,1:T(8,128)(2,1)}), bf16[64,8,384]{2,0,1:T(8,128)(2,1)S(1)}, u32[]{:S(2)}, u32[]{:S(2)}) async-start(bf16[64,8,384]{2,0,1:T(8,128)(2,1)} %bitcast.169), calls=%async_computation | async-start | bytes 786432 | tf_op jit(solution)/shard_map/all_to_all | solution.py:245
  70.7 113.3 %reduce-scatter.5.cloned.1.call-start = ((), (), s32[]{:S(2)}) async-start(), calls=%async_computation.4 | async-start | bytes 1327104 | tf_op jit(solution)/shard_map/reduce_scatter | solution.py:246
  83.8 179.5 %all-gather.9.cloned.1.call-start = ((), (), s32[]{:S(2)}) async-start(), calls=%async_computation.6 | async-start | bytes 7077888 | tf_op jit(solution)/shard_map/all_gather | solution.py:261
  155.0 154.1 %all-gather.11.cloned.1.call-start = ((), (), s32[]{:S(2)}) async-start(), calls=%async_computation.7 | async-start | bytes 2654208 | tf_op jit(solution)/shard_map/all_gather | solution.py:242
  155.6 216.1 %reduce-scatter.7.cloned.1.call-start = ((), (), s32[]{:S(2)}) async-start(), calls=%async_computation.8 | async-start | bytes 3538944
  315.5 8.9 %copy-start.11 = (bf16[2,3072]{1,0:T(2,128)(2,1)S(1)}, bf16[2,3072]{1,0:T(2,128)(2,1)}, u32[]{:S(2)}) copy-start(bf16[2,3072]{1,0:T(2,128)(2,1)} %param.24) | copy-start | bytes 36868
  315.5 14.0 %copy-start.5 = (bf16[384,64]{0,1:T(8,128)(2,1)S(1)}, bf16[384,64]{0,1:T(8,128)(2,1)}, u32[]{:S(2)}) copy-start(bf16[384,64]{0,1:T(8,128)(2,1)} %param.25) | copy-start | bytes 147460
  316.3 6.0 %collective-permute-start = (bf16[1,64,384]{2,1,0:T(8,128)(2,1)S(1)}, bf16[1,64,384]{2,1,0:T(8,128)(2,1)S(1)}, u32[]{:S(2)}, u32[]{:S(2)}) collective-permute-start(bf16[1,64,384]{2,1,0:T(8,128)(2,1)S(1)} %slice_bitcast_fusion), channel_id=1, source_target_pairs={{0,16},{8,24},{16,0},{24,8},{32,48},{40,56},{48,32},{56,40},{1,17}... | collective-permute-start | bytes 147464 | tf_op jit(solution)/shard_map/ppermute | solution.py:108
  323.2 4.7 %collective-permute-start.1 = (bf16[2,64,384]{2,1,0:T(8,128)(2,1)S(1)}, bf16[2,64,384]{2,1,0:T(8,128)(2,1)S(1)}, u32[]{:S(2)}, u32[]{:S(2)}) collective-permute-start(bf16[2,64,384]{2,1,0:T(8,128)(2,1)S(1)} %maximum_bitcast_fusion), channel_id=1, source_target_pairs={{0,8},{8,0},{16,24},{24,16},{32,40},{40,32},{48,56},{56,48},{1,9},... | collective-permute-start | bytes 294920 | tf_op jit(solution)/shard_map/ppermute | solution.py:108
  328.0 12.0 %collective-permute-start.2 = (bf16[4,64,384]{2,1,0:T(8,128)(2,1)S(1)}, bf16[4,64,384]{2,1,0:T(8,128)(2,1)S(1)}, u32[]{:S(2)}, u32[]{:S(2)}) collective-permute-start(bf16[4,64,384]{2,1,0:T(8,128)(2,1)S(1)} %bitcast.185), channel_id=1, source_target_pairs={{0,32},{8,40},{16,48},{24,56},{32,0},{40,8},{48,16},{56,24},{1,33}... | collective-permute-start | bytes 589832 | tf_op jit(solution)/shard_map/ppermute | solution.py:108
  340.2 32.7 %copy-start.2 = (bf16[512,384]{1,0:T(8,128)(2,1)S(1)}, bf16[512,384]{1,0:T(8,128)(2,1)}, u32[]{:S(2)}) copy-start(bf16[512,384]{1,0:T(8,128)(2,1)} %param.15) | copy-start | bytes 1179652
  340.7 1.5 collective-permute-start.3
  342.3 31.7 %collective-permute-start.4 = (bf16[128,384]{1,0:T(8,128)(2,1)S(1)}, bf16[128,384]{1,0:T(8,128)(2,1)S(1)}, u32[]{:S(2)}, u32[]{:S(2)}) collective-permute-start(bf16[128,384]{1,0:T(8,128)(2,1)S(1)} %select_convert_fusion.1), channel_id=1, source_target_pairs={{0,2},{1,3},{2,0},{3,1},{4,6},{5,7},{6,4},{7,5},{8,10},{9,11},{10,... | collective-permute-start | bytes 294920 | tf_op jit(solution)/shard_map/ppermute | solution.py:140
  373.0 39.7 %copy-start.7 = (bf16[3,3,64,64]{3,2,1,0:T(8,128)(2,1)S(1)}, bf16[3,3,64,64]{3,2,1,0:T(8,128)(2,1)}, u32[]{:S(2)}) copy-start(bf16[3,3,64,64]{3,2,1,0:T(8,128)(2,1)} %param.26) | copy-start | bytes 221188
  373.3 41.3 %copy-start.3 = (bf16[512,384]{1,0:T(8,128)(2,1)}, bf16[512,384]{1,0:T(8,128)(2,1)S(1)}, u32[]{:S(2)}) copy-start(bf16[512,384]{1,0:T(8,128)(2,1)S(1)} %get-tuple-element.21) | copy-start | bytes 1179652
  373.3 40.6 %copy-start.12 = (f32[8,512]{1,0:T(8,128)S(1)}, f32[8,512]{1,0:T(8,128)}, u32[]{:S(2)}) copy-start(f32[8,512]{1,0:T(8,128)} %param.27) | copy-start | bytes 49156
  373.9 1.5 collective-permute-start.7
  375.4 12.3 %collective-permute-start.8 = (f32[514,66]{0,1:T(8,128)S(1)}, f32[514,66]{0,1:T(8,128)S(1)}, u32[]{:S(2)}, u32[]{:S(2)}) collective-permute-start(f32[514,66]{0,1:T(8,128)S(1)} %fusion.82), channel_id=1, source_target_pairs={{0,2},{1,3},{2,0},{3,1},{4,6},{5,7},{6,4},{7,5},{8,10},{9,11},{10,... | collective-permute-start | bytes 407096 | tf_op jit(solution)/shard_map/ppermute | solution.py:35
  376.6 13.4 %collective-permute-start.5 = (bf16[64,384]{1,0:T(8,128)(2,1)S(1)}, bf16[64,384]{1,0:T(8,128)(2,1)S(1)}, u32[]{:S(2)}, u32[]{:S(2)}) collective-permute-start(bf16[64,384]{1,0:T(8,128)(2,1)S(1)} %select_convert_fusion.2), channel_id=1, source_target_pairs={{0,4},{1,5},{2,6},{3,7},{4,0},{5,1},{6,2},{7,3},{8,12},{9,13},{10,... | collective-permute-start | bytes 147464 | tf_op jit(solution)/shard_map/ppermute | solution.py:140
  387.7 14.3 %collective-permute-start.9 = (f32[514,66]{0,1:T(8,128)S(1)}, f32[514,66]{0,1:T(8,128)S(1)}, u32[]{:S(2)}, u32[]{:S(2)}) collective-permute-start(f32[514,66]{0,1:T(8,128)S(1)} %add.295), channel_id=1, source_target_pairs={{0,4},{1,5},{2,6},{3,7},{4,0},{5,1},{6,2},{7,3},{8,12},{9,13},{10,... | collective-permute-start | bytes 407096 | tf_op jit(solution)/shard_map/ppermute | solution.py:35
  390.0 18.7 %collective-permute-start.6 = (f32[64,384]{1,0:T(8,128)S(1)}, f32[64,384]{1,0:T(8,128)S(1)}, u32[]{:S(2)}, u32[]{:S(2)}) collective-permute-start(f32[64,384]{1,0:T(8,128)S(1)} %convert_add_fusion.2), channel_id=1, source_target_pairs={{0,0},{1,8},{2,16},{3,24},{4,32},{5,40},{6,48},{7,56},{8,1},{9,9},... | collective-permute-start | bytes 294920 | tf_op jit(solution)/shard_map/ppermute | solution.py:148
  402.6 6.9 %collective-permute-start.10 = (bf16[1,4096]{1,0:T(2,128)(2,1)S(1)}, bf16[1,4096]{1,0:T(2,128)(2,1)S(1)}, u32[]{:S(2)}, u32[]{:S(2)}) collective-permute-start(bf16[1,4096]{1,0:T(2,128)(2,1)S(1)} %slice.267), channel_id=1, source_target_pairs={{0,8},{8,16},{16,24},{24,32},{32,40},{40,48},{48,56},{1,9},{9,17},... | collective-permute-start | bytes 24584 | tf_op jit(solution)/shard_map/ppermute | solution.py:23
  404.7 7.7 %collective-permute-start.11 = (bf16[1,4096]{1,0:T(2,128)(2,1)S(1)}, bf16[1,4096]{1,0:T(2,128)(2,1)S(1)}, u32[]{:S(2)}, u32[]{:S(2)}) collective-permute-start(bf16[1,4096]{1,0:T(2,128)(2,1)S(1)} %slice.269), channel_id=1, source_target_pairs={{8,0},{16,8},{24,16},{32,24},{40,32},{48,40},{56,48},{9,1},{17,9},... | collective-permute-start | bytes 24584 | tf_op jit(solution)/shard_map/ppermute | solution.py:26
  413.9 0.6 copy-start.10
Sparse Core Ops, SparseCore 0:
  9.9 46.9 all-gather.4
  58.7 82.4 all-gather.6
  143.8 40.0 reduce-scatter.4
  185.6 77.7 all-gather.8
  265.0 43.9 all-gather.10
  315.6 56.0 reduce-scatter.6

commit v13 on v12

--- a/solution.py
+++ b/solution.py
@@ -290,8 +290,10 @@
         preferred_element_type=jnp.float32,
     )
     txt_out = transpose_devices(
-        halving_scatter(txt_term.astype(jnp.bfloat16).astype(jnp.float32), "tp", 0, (1, 2, 4))
-    )
+        halving_scatter(txt_term.astype(jnp.bfloat16).astype(jnp.float32), "tp", 0, (1, 2, 4)).astype(
+            jnp.bfloat16
+        )
+    ).astype(jnp.float32)
     img_out = lax.psum_scatter(
         img_term.astype(jnp.bfloat16), "tp", scatter_dimension=1, tiled=True
     ).astype(jnp.float32)

time: 423 us -> 422 us (level)
  no operation moved by 1% of the time
where the time goes in v13:
time: 422 us; the launch traced here: 421 us
  waiting for transfers between devices  256 us (61%)
  blocking collectives  52.1 us (12%)
  starting transfers between devices  26.5 us (6%)
  Pallas kernels  20.1 us (5%)
  other arithmetic  19.9 us (5%)
  between operations  16.3 us (4%)
  local copies, waits for them, and re-layouts  15.4 us (4%)
  matrix products  14.9 us (4%)
    all_gather x1, waiting for transfers between devices, per_device(): img_weights = lax.all_gather(img_qkv, 'seq', axis=0, tiled=True)  57.2 us
    all_gather x1, waiting for transfers between devices, per_device(): lax.all_gather(jnp.concatenate([img_key.reshape(img_rows, kv_width), img_...  42.1 us
    all_gather x1, blocking collectives, per_device(): lax.all_gather(jnp.concatenate([txt_key.reshape(txt_rows, kv_width), txt_...  33.5 us
    unnamed x7, waiting for transfers between devices  28.1 us
    reduce_scatter x1, waiting for transfers between devices, per_device(): lax.psum_scatter(add_rows(txt_norm_rows, txt_qkv).astype(jnp.bfloat16), '...  27.1 us
    all_gather x1, waiting for transfers between devices, per_device(): lax.all_gather(img_hidden, 'tp', axis=1, tiled=True)  26.5 us
    all_gather x1, waiting for transfers between devices, per_device(): img_out_full = lax.all_gather(img_out_w, 'seq', axis=1, tiled=True)  25.6 us
    pallas_call x1, Pallas kernels, attention(): pl.pallas_call(functools.partial(attend_block, scale=head_dim ** (-0.5)),...  20.1 us
  transfers between devices with their start and end apart: 19, of which 15 were waited for; matrix products, arithmetic and copies ran while one was open for 10% of the time, Pallas kernels for 5%

profile of v13, /device:TPU:26, one launch (start us, length us, event | category | flops | bytes accessed | tf_op | source)
XLA Modules:
  0.0 421.0 jit_solution(14736387937501469338)
XLA Ops:
  7.3 0.7 all-gather.5.cloned.1.call-update
  8.0 2.3 copy.75
  10.3 0.7 convert_element_type.146
  11.1 18.6 %all_gather.18 = bf16[64,3072]{1,0:T(8,128)(2,1)S(1)} all-gather(bf16[64,384]{1,0:T(8,128)(2,1)S(1)} %copy-done.6), channel_id=1, replica_groups=mesh['req'=4,'seq'=8,'tp'=8] {'tp'}, dimensions={1}, use_global_device_ids=true | all-gather | bytes 442368 | tf_op jit(solution)/shard_map/all_gather | solution.py:235
  30.4 26.5 %all-gather.5.cloned.1.call-done = bf16[512,3072]{1,0:T(8,128)(2,1)} async-done(((bf16[512,384]{1,0:T(8,128)(2,1)}), bf16[512,3072]{1,0:T(8,128)(2,1)}) %all-gather.5.cloned.1.call-update) | async-done | bytes 3145744 | tf_op jit(solution)/shard_map/all_gather | solution.py:234
  56.9 2.5 convert_reduce_fusion
  59.5 0.3 copy-done.1
  59.8 1.0 fusion.2
  60.8 3.5 fusion.5
  64.3 0.8 copy.103
  65.1 5.6 %all-to-all-start = ((bf16[64,8,384]{2,0,1:T(8,128)(2,1)}), bf16[64,8,384]{2,0,1:T(8,128)(2,1)S(1)}, u32[]{:S(2)}, u32[]{:S(2)}) async-start(bf16[64,8,384]{2,0,1:T(8,128)(2,1)} %bitcast.169), calls=%async_computation | async-start | bytes 786432 | tf_op jit(solution)/shard_map/all_to_all | solution.py:245
  71.0 2.4 copy.72
  73.5 0.5 fusion.23
  74.0 8.0 %all-to-all-done = bf16[64,8,384]{2,0,1:T(8,128)(2,1)S(1)} async-done(((bf16[64,8,384]{2,0,1:T(8,128)(2,1)}), bf16[64,8,384]{2,0,1:T(8,128)(2,1)S(1)}, u32[]{:S(2)}, u32[]{:S(2)}) %all-to-all-start) | async-done | bytes 393248 | tf_op jit(solution)/shard_map/all_to_all | solution.py:245
  82.0 1.8 convolution_convert_fusion.1
  84.1 57.2 %all-gather.7.cloned.1.call-done = bf16[3072,3,384]{0,2,1:T(8,128)(2,1)} async-done(((bf16[384,3,384]{0,2,1:T(8,128)(2,1)}), bf16[3072,3,384]{0,2,1:T(8,128)(2,1)}) %all-gather.7.cloned.1.call-update) | async-done | bytes 7077904 | tf_op jit(solution)/shard_map/all_gather | solution.py:240
  141.2 7.1 %fusion.6 = f32[512,3,3,128]{0,3,2,1:T(8,128)S(1)} fusion(bf16[3,3,128,3072]{3,2,1,0:T(8,128)(2,1)} %bitcast.205, bf16[512,3072]{1,0:T(8,128)(2,1)} %fusion.5), kind=kOutput, calls=%fused_computation.9 | convolution fusion | flops 3623878656 | bytes 12582912 | tf_op jit(solution)/shard_map/dot_general | solution.py:207
  148.4 0.3 multiply_reduce_fusion
  148.7 0.5 squeeze.59
  149.1 0.5 squeeze.61
  149.6 0.3 multiply_multiply_fusion.1
  150.0 0.3 multiply_multiply_fusion
  150.4 2.1 subtract_convert_fusion
  152.4 0.9 pad_maximum_fusion.3
  153.9 1.0 pad_maximum_fusion
  155.0 0.5 all-gather.11.cloned.1.call-update
  156.3 0.6 compare_convert_fusion.keep_ref
  156.9 27.1 %reduce-scatter.5.cloned.1.call-done = bf16[64,1152]{1,0:T(8,128)(2,1)} async-done(((bf16[512,1152]{1,0:T(8,128)(2,1)}), bf16[64,1152]{1,0:T(8,128)(2,1)}) %reduce-scatter.5.cloned.1.call-update) | async-done | bytes 147472 | tf_op jit(solution)/shard_map/reduce_scatter | solution.py:246
  183.9 1.0 reshape.283
  185.6 33.5 %all_gather.21.tkey_ref.tvalue_ref = bf16[512,768]{1,0:T(8,128)(2,1)} all-gather(bf16[64,768]{1,0:T(8,128)(2,1)S(1)} %pad_maximum_fusion.9), channel_id=1, replica_groups=mesh['req'=4,'seq'=8,'tp'=8] {'seq'}, dimensions={0}, use_global_device_ids=true | all-gather | bytes 884736 | tf_op jit(solution)/shard_map/all_gather | solution.py:269
  219.1 0.9 pad_maximum_fusion.2
  220.4 0.8 pad_maximum_fusion.1.query_ref
  221.3 42.1 %all-gather.9.cloned.1.call-done.ikey_ref.ivalue_ref = bf16[4096,768]{1,0:T(8,128)(2,1)} async-done(((bf16[512,768]{1,0:T(8,128)(2,1)}), bf16[4096,768]{1,0:T(8,128)(2,1)}) %all-gather.9.cloned.1.call-update) | async-done | bytes 6291472 | tf_op jit(solution)/shard_map/all_gather | solution.py:261
  263.4 20.1 %shard_map.182 = bf16[576,384]{1,0:T(8,128)(2,1)} custom-call(f32[1,512]{1,0:T(1,128)} %compare_convert_fusion.keep_ref, bf16[576,384]{1,0:T(8,128)(2,1)} %pad_maximum_fusion.1.query_ref, bf16[512,768]{1,0:T(8,128)(2,1)} %all_gather.21.tkey_ref.tvalue_ref, bf16[512,768]{1,0:T(8,128)(2,1)} %all_gather.21.tkey_ref.tvalue_ref, ...), custom_call_target="tpu_custom_call" | custom-call | tf_op jit(solution)/shard_map/pallas_call | solution.py:83
  283.5 25.6 %all-gather.11.cloned.1.call-done = bf16[384,3072]{1,0:T(8,128)(2,1)} async-done(((bf16[384,384]{1,0:T(8,128)(2,1)}), bf16[384,3072]{1,0:T(8,128)(2,1)}) %all-gather.11.cloned.1.call-update) | async-done | bytes 2359312 | tf_op jit(solution)/shard_map/all_gather | solution.py:242
  309.1 3.6 convolution_convert_fusion
  312.7 2.8 copy.87
  315.5 0.8 slice_bitcast_fusion
  316.3 1.6 collective-permute-start
  317.9 4.5 %collective-permute-done = bf16[1,64,384]{2,1,0:T(8,128)(2,1)S(1)} collective-permute-done((bf16[1,64,384]{2,1,0:T(8,128)(2,1)S(1)}, bf16[1,64,384]{2,1,0:T(8,128)(2,1)S(1)}, u32[]{:S(2)}, u32[]{:S(2)}) %collective-permute-start) | collective-permute-done | bytes 49184 | tf_op jit(solution)/shard_map/ppermute | solution.py:108
  322.4 0.8 select_bitcast_fusion.5
  323.2 1.2 collective-permute-start.1
  324.4 3.4 collective-permute-done.1
  328.0 1.5 collective-permute-start.2
  329.6 10.4 %collective-permute-done.2 = bf16[4,64,384]{2,1,0:T(8,128)(2,1)S(1)} collective-permute-done((bf16[4,64,384]{2,1,0:T(8,128)(2,1)S(1)}, bf16[4,64,384]{2,1,0:T(8,128)(2,1)S(1)}, u32[]{:S(2)}, u32[]{:S(2)}) %collective-permute-start.2) | collective-permute-done | bytes 196640 | tf_op jit(solution)/shard_map/ppermute | solution.py:108
  340.2 0.4 fusion.8
  341.1 1.1 collective-permute-done.3
  342.3 2.5 collective-permute-start.4
  344.9 26.9 %reduce-scatter.7.cloned.1.call-done = bf16[384,512]{1,0:T(8,128)(2,1)} async-done(((bf16[3072,512]{1,0:T(8,128)(2,1)}), bf16[384,512]{1,0:T(8,128)(2,1)}) %reduce-scatter.7.cloned.1.call-update) | async-done | bytes 393232
  371.7 1.2 copy.88
  373.0 0.3 convert_reduce_fusion.1
  373.3 0.6 fusion.15
  374.1 1.4 collective-permute-done.7
  375.4 1.1 collective-permute-start.8
  376.6 2.4 collective-permute-start.5
  379.8 8.0 %collective-permute-done.8 = f32[514,66]{0,1:T(8,128)S(1)} collective-permute-done((f32[514,66]{0,1:T(8,128)S(1)}, f32[514,66]{0,1:T(8,128)S(1)}, u32[]{:S(2)}, u32[]{:S(2)}) %collective-permute-start.8) | collective-permute-done | bytes 135728 | tf_op jit(solution)/shard_map/ppermute | solution.py:35
  387.7 2.3 collective-permute-start.9
  390.0 1.9 collective-permute-start.6
  391.9 9.0 %collective-permute-done.9 = f32[514,66]{0,1:T(8,128)S(1)} collective-permute-done((f32[514,66]{0,1:T(8,128)S(1)}, f32[514,66]{0,1:T(8,128)S(1)}, u32[]{:S(2)}, u32[]{:S(2)}) %collective-permute-start.9) | collective-permute-done | bytes 135728 | tf_op jit(solution)/shard_map/ppermute | solution.py:35
  401.6 2.6 collective-permute-start.10
  404.3 3.3 collective-permute-start.11
  407.6 0.7 fusion.24
  408.6 3.5 collective-permute-done.11
  413.5 0.6 multiply_subtract_fusion
  (138 shorter events, 6.9 us)
Async XLA Ops:
  7.2 333.0 %copy-start = (bf16[384,384]{1,0:T(8,128)(2,1)S(1)}, bf16[384,384]{1,0:T(8,128)(2,1)}, u32[]{:S(2)}) copy-start(bf16[384,384]{1,0:T(8,128)(2,1)} %param.23) | copy-start | bytes 884740
  7.2 22.9 %copy-start.8 = (bf16[3,3072]{1,0:T(4,128)(2,1)S(1)}, bf16[3,3072]{1,0:T(4,128)(2,1)}, u32[]{:S(2)}) copy-start(bf16[3,3072]{1,0:T(4,128)(2,1)} %param.17) | copy-start | bytes 55300
  7.2 3.9 copy-start.9
  7.2 3.9 copy-start.6
  7.2 49.7 %all-gather.5.cloned.1.call-start = ((), (), s32[]{:S(2)}) async-start(), calls=%async_computation.3 | async-start | bytes 3538944 | tf_op jit(solution)/shard_map/all_gather | solution.py:234
  7.9 133.3 %all-gather.7.cloned.1.call-start = ((), (), s32[]{:S(2)}) async-start(), calls=%async_computation.5 | async-start | bytes 7962624 | tf_op jit(solution)/shard_map/all_gather | solution.py:240
  56.9 2.8 copy-start.1
  60.7 9.9 %copy-start.13 = (f32[4,128]{1,0:T(4,128)S(1)}, f32[4,128]{1,0:T(4,128)}, u32[]{:S(2)}) copy-start(f32[4,128]{1,0:T(4,128)} %param.21) | copy-start | bytes 6148
  60.7 10.2 %copy-start.4 = (bf16[384,3,384]{2,0,1:T(8,128)(2,1)S(1)}, bf16[384,3,384]{2,0,1:T(8,128)(2,1)}, u32[]{:S(2)}) copy-start(bf16[384,3,384]{2,0,1:T(8,128)(2,1)} %param.20) | copy-start | bytes 2654212
  65.1 16.9 %all-to-all-start = ((bf16[64,8,384]{2,0,1:T(8,128)(2,1)}), bf16[64,8,384]{2,0,1:T(8,128)(2,1)S(1)}, u32[]{:S(2)}, u32[]{:S(2)}) async-start(bf16[64,8,384]{2,0,1:T(8,128)(2,1)} %bitcast.169), calls=%async_computation | async-start | bytes 786432 | tf_op jit(solution)/shard_map/all_to_all | solution.py:245
  70.7 113.3 %reduce-scatter.5.cloned.1.call-start = ((), (), s32[]{:S(2)}) async-start(), calls=%async_computation.4 | async-start | bytes 1327104 | tf_op jit(solution)/shard_map/reduce_scatter | solution.py:246
  83.8 179.5 %all-gather.9.cloned.1.call-start = ((), (), s32[]{:S(2)}) async-start(), calls=%async_computation.6 | async-start | bytes 7077888 | tf_op jit(solution)/shard_map/all_gather | solution.py:261
  155.0 154.1 %all-gather.11.cloned.1.call-start = ((), (), s32[]{:S(2)}) async-start(), calls=%async_computation.7 | async-start | bytes 2654208 | tf_op jit(solution)/shard_map/all_gather | solution.py:242
  155.6 216.1 %reduce-scatter.7.cloned.1.call-start = ((), (), s32[]{:S(2)}) async-start(), calls=%async_computation.8 | async-start | bytes 3538944
  315.5 8.9 %copy-start.11 = (bf16[2,3072]{1,0:T(2,128)(2,1)S(1)}, bf16[2,3072]{1,0:T(2,128)(2,1)}, u32[]{:S(2)}) copy-start(bf16[2,3072]{1,0:T(2,128)(2,1)} %param.24) | copy-start | bytes 36868
  315.5 14.0 %copy-start.5 = (bf16[384,64]{0,1:T(8,128)(2,1)S(1)}, bf16[384,64]{0,1:T(8,128)(2,1)}, u32[]{:S(2)}) copy-start(bf16[384,64]{0,1:T(8,128)(2,1)} %param.25) | copy-start | bytes 147460
  316.3 6.0 %collective-permute-start = (bf16[1,64,384]{2,1,0:T(8,128)(2,1)S(1)}, bf16[1,64,384]{2,1,0:T(8,128)(2,1)S(1)}, u32[]{:S(2)}, u32[]{:S(2)}) collective-permute-start(bf16[1,64,384]{2,1,0:T(8,128)(2,1)S(1)} %slice_bitcast_fusion), channel_id=1, source_target_pairs={{0,16},{8,24},{16,0},{24,8},{32,48},{40,56},{48,32},{56,40},{1,17}... | collective-permute-start | bytes 147464 | tf_op jit(solution)/shard_map/ppermute | solution.py:108
  323.2 4.7 %collective-permute-start.1 = (bf16[2,64,384]{2,1,0:T(8,128)(2,1)S(1)}, bf16[2,64,384]{2,1,0:T(8,128)(2,1)S(1)}, u32[]{:S(2)}, u32[]{:S(2)}) collective-permute-start(bf16[2,64,384]{2,1,0:T(8,128)(2,1)S(1)} %maximum_bitcast_fusion), channel_id=1, source_target_pairs={{0,8},{8,0},{16,24},{24,16},{32,40},{40,32},{48,56},{56,48},{1,9},... | collective-permute-start | bytes 294920 | tf_op jit(solution)/shard_map/ppermute | solution.py:108
  328.0 12.0 %collective-permute-start.2 = (bf16[4,64,384]{2,1,0:T(8,128)(2,1)S(1)}, bf16[4,64,384]{2,1,0:T(8,128)(2,1)S(1)}, u32[]{:S(2)}, u32[]{:S(2)}) collective-permute-start(bf16[4,64,384]{2,1,0:T(8,128)(2,1)S(1)} %bitcast.185), channel_id=1, source_target_pairs={{0,32},{8,40},{16,48},{24,56},{32,0},{40,8},{48,16},{56,24},{1,33}... | collective-permute-start | bytes 589832 | tf_op jit(solution)/shard_map/ppermute | solution.py:108
  340.2 32.7 %copy-start.2 = (bf16[512,384]{1,0:T(8,128)(2,1)S(1)}, bf16[512,384]{1,0:T(8,128)(2,1)}, u32[]{:S(2)}) copy-start(bf16[512,384]{1,0:T(8,128)(2,1)} %param.15) | copy-start | bytes 1179652
  340.7 1.5 collective-permute-start.3
  342.3 31.7 %collective-permute-start.4 = (bf16[128,384]{1,0:T(8,128)(2,1)S(1)}, bf16[128,384]{1,0:T(8,128)(2,1)S(1)}, u32[]{:S(2)}, u32[]{:S(2)}) collective-permute-start(bf16[128,384]{1,0:T(8,128)(2,1)S(1)} %select_convert_fusion.1), channel_id=1, source_target_pairs={{0,2},{1,3},{2,0},{3,1},{4,6},{5,7},{6,4},{7,5},{8,10},{9,11},{10,... | collective-permute-start | bytes 294920 | tf_op jit(solution)/shard_map/ppermute | solution.py:140
  373.0 39.3 %copy-start.7 = (bf16[3,3,64,64]{3,2,1,0:T(8,128)(2,1)S(1)}, bf16[3,3,64,64]{3,2,1,0:T(8,128)(2,1)}, u32[]{:S(2)}) copy-start(bf16[3,3,64,64]{3,2,1,0:T(8,128)(2,1)} %param.26) | copy-start | bytes 221188
  373.3 40.9 %copy-start.3 = (bf16[512,384]{1,0:T(8,128)(2,1)}, bf16[512,384]{1,0:T(8,128)(2,1)S(1)}, u32[]{:S(2)}) copy-start(bf16[512,384]{1,0:T(8,128)(2,1)S(1)} %get-tuple-element.21) | copy-start | bytes 1179652
  373.3 40.2 %copy-start.12 = (f32[8,512]{1,0:T(8,128)S(1)}, f32[8,512]{1,0:T(8,128)}, u32[]{:S(2)}) copy-start(f32[8,512]{1,0:T(8,128)} %param.27) | copy-start | bytes 49156
  373.9 1.5 collective-permute-start.7
  375.4 12.3 %collective-permute-start.8 = (f32[514,66]{0,1:T(8,128)S(1)}, f32[514,66]{0,1:T(8,128)S(1)}, u32[]{:S(2)}, u32[]{:S(2)}) collective-permute-start(f32[514,66]{0,1:T(8,128)S(1)} %fusion.82), channel_id=1, source_target_pairs={{0,2},{1,3},{2,0},{3,1},{4,6},{5,7},{6,4},{7,5},{8,10},{9,11},{10,... | collective-permute-start | bytes 407096 | tf_op jit(solution)/shard_map/ppermute | solution.py:35
  376.6 13.4 %collective-permute-start.5 = (bf16[64,384]{1,0:T(8,128)(2,1)S(1)}, bf16[64,384]{1,0:T(8,128)(2,1)S(1)}, u32[]{:S(2)}, u32[]{:S(2)}) collective-permute-start(bf16[64,384]{1,0:T(8,128)(2,1)S(1)} %select_convert_fusion.2), channel_id=1, source_target_pairs={{0,4},{1,5},{2,6},{3,7},{4,0},{5,1},{6,2},{7,3},{8,12},{9,13},{10,... | collective-permute-start | bytes 147464 | tf_op jit(solution)/shard_map/ppermute | solution.py:140
  387.7 13.2 %collective-permute-start.9 = (f32[514,66]{0,1:T(8,128)S(1)}, f32[514,66]{0,1:T(8,128)S(1)}, u32[]{:S(2)}, u32[]{:S(2)}) collective-permute-start(f32[514,66]{0,1:T(8,128)S(1)} %add.295), channel_id=1, source_target_pairs={{0,4},{1,5},{2,6},{3,7},{4,0},{5,1},{6,2},{7,3},{8,12},{9,13},{10,... | collective-permute-start | bytes 407096 | tf_op jit(solution)/shard_map/ppermute | solution.py:35
  390.0 17.6 %collective-permute-start.6 = (bf16[64,384]{1,0:T(8,128)(2,1)S(1)}, bf16[64,384]{1,0:T(8,128)(2,1)S(1)}, u32[]{:S(2)}, u32[]{:S(2)}) collective-permute-start(bf16[64,384]{1,0:T(8,128)(2,1)S(1)} %add_convert_fusion.3), channel_id=1, source_target_pairs={{0,0},{1,8},{2,16},{3,24},{4,32},{5,40},{6,48},{7,56},{8,1},{9,9},... | collective-permute-start | bytes 147464 | tf_op jit(solution)/shard_map/ppermute | solution.py:148
  401.6 6.9 %collective-permute-start.10 = (bf16[1,4096]{1,0:T(2,128)(2,1)S(1)}, bf16[1,4096]{1,0:T(2,128)(2,1)S(1)}, u32[]{:S(2)}, u32[]{:S(2)}) collective-permute-start(bf16[1,4096]{1,0:T(2,128)(2,1)S(1)} %slice.267), channel_id=1, source_target_pairs={{0,8},{8,16},{16,24},{24,32},{32,40},{40,48},{48,56},{1,9},{9,17},... | collective-permute-start | bytes 24584 | tf_op jit(solution)/shard_map/ppermute | solution.py:23
  404.3 7.7 %collective-permute-start.11 = (bf16[1,4096]{1,0:T(2,128)(2,1)S(1)}, bf16[1,4096]{1,0:T(2,128)(2,1)S(1)}, u32[]{:S(2)}, u32[]{:S(2)}) collective-permute-start(bf16[1,4096]{1,0:T(2,128)(2,1)S(1)} %slice.269), channel_id=1, source_target_pairs={{8,0},{16,8},{24,16},{32,24},{40,32},{48,40},{56,48},{9,1},{17,9},... | collective-permute-start | bytes 24584 | tf_op jit(solution)/shard_map/ppermute | solution.py:26
  413.5 0.6 copy-start.10
Sparse Core Ops, SparseCore 0:
  9.9 46.9 all-gather.4
  58.7 82.4 all-gather.6
  143.8 40.0 reduce-scatter.4
  185.6 77.7 all-gather.8
  265.0 43.9 all-gather.10
  315.6 56.0 reduce-scatter.6
